TPU v7x, 32 devices: a whole 2x2x4 slice. The times are simulated.
32 devices in a mesh: seq: 8 (over z, y), rep: 4 (over x, core).
Axes of the slice: x: 2, y: 2, z: 4, core: 2. Of those that a mesh axis runs over, the one named last changes fastest.
Arguments:
- queries: bfloat16 [8192, 512], P(('rep', 'seq')), parts along dimension 0, may hold values from -40 to 40
- key_tokens: bfloat16 [8192, 512], P(('rep', 'seq')), parts along dimension 0, may hold values from -8 to 8
- value_tokens: bfloat16 [8192, 512], P(('rep', 'seq')), parts along dimension 0, may hold values from -6 to 6
- grad_out: bfloat16 [8192, 512], P(('rep', 'seq')), parts along dimension 0, may hold values from -6 to 6
Outputs:
- attended: bfloat16 [8192, 512], P(('rep', 'seq')), parts along dimension 0
- grad_queries: bfloat16 [8192, 512], P(('rep', 'seq')), parts along dimension 0
- grad_keys: bfloat16 [8192, 512], P(('rep', 'seq')), parts along dimension 0
- grad_values: bfloat16 [8192, 512], P(('rep', 'seq')), parts along dimension 0
There are 4 independent parts, one for each index of `rep`. A program takes and returns all parts, laid end to end along the dimension named above; each array names one. Nothing has to cross between parts.
All inputs are finite; a program needn't handle non-finite values.
Results may differ from a plain program's by a relative error of at most 0.04.
Values may be sent and summed in bfloat16 or wider, within the bound.
No kernel may reach another device: no remote copies, remote signals or barrier semaphores. Data moves between devices by JAX's collectives and lax.ppermute only.
A program may use at most 64 MiB of HBM per device.

v0:
```python
import math

import jax
import jax.numpy as jnp
from jax import lax
from jax.sharding import PartitionSpec as P

HEADS = 4
HD = 128
BLK = 128
WINDOW = 4


NEG = -1e30


def passed_along(value, axis, steps):
    count = lax.axis_size(axis)
    first, last = (max(0, -steps), min(count, count - steps))
    return lax.ppermute(value, axis, [(source, source + steps) for source in range(first, last)])


def offset_lists(block_total):
    near_list = list(range(WINDOW + 1))
    far_list = []
    stride = 1
    while stride < block_total:
        if stride > WINDOW:
            far_list.append(stride)
        stride = stride * 2
    return (near_list, far_list)


def allowed_mask(first_block, blocks_dev, offsets):
    block_ids = first_block + jnp.arange(blocks_dev, dtype=jnp.int32)
    offset_arr = jnp.array(offsets, dtype=jnp.int32)
    block_live = block_ids[:, None] - offset_arr[None, :] >= 0
    row_ids = jnp.arange(BLK, dtype=jnp.int32)
    causal = row_ids[:, None] >= row_ids[None, :]
    later_slab = offset_arr > 0
    slab_causal = jnp.logical_or(later_slab[None, :, None], causal[:, None, :])
    allowed = jnp.logical_and(block_live[:, None, :, None], slab_causal[None, :, :, :])
    return allowed.reshape(blocks_dev, BLK, len(offsets) * BLK)


def head_cols(array_in, col_start):
    return array_in[..., col_start : col_start + HD]


def to_blocks(array_in, block_count):
    return array_in.reshape(block_count, BLK, array_in.shape[-1])


def place_slabs(gradient, near_list, lead, span_blocks):
    blocks_dev = gradient.shape[0]
    placed = []
    for slot_index, offset in enumerate(near_list):
        before = lead - offset
        after = span_blocks - before - blocks_dev
        placed.append(jnp.pad(gradient[:, slot_index], ((before, after), (0, 0), (0, 0))))
    total = placed[0]
    for item in placed[1:]:
        total = total + item
    return total


def head_pass(query_per_head, output_gradient_heads, key_slabs, value_slabs, allowed, logit_scale):
    block_count = key_slabs.shape[0]
    key_row_block = key_slabs.reshape(block_count, -1, HD)
    value_row_block = value_slabs.reshape(block_count, -1, HD)
    score_matrix = (
        jnp.einsum(
            "nmv,njv->nmj", query_per_head, key_row_block, preferred_element_type=jnp.float32
        )
        * logit_scale
    )
    score_matrix = jnp.where(allowed, score_matrix, NEG)
    row_max = jnp.max(score_matrix, axis=-1, keepdims=True)
    log_total = row_max + jnp.log(jnp.sum(jnp.exp(score_matrix - row_max), axis=-1, keepdims=True))
    probabilities = jnp.exp(score_matrix - log_total)
    attention_weight = probabilities.astype(jnp.bfloat16)
    attended_per_head = jnp.einsum(
        "jym,jmo->jyo", attention_weight, value_row_block, preferred_element_type=jnp.float32
    ).astype(jnp.bfloat16)
    out_dot = jnp.sum(
        output_gradient_heads.astype(jnp.float32) * attended_per_head.astype(jnp.float32),
        axis=-1,
        keepdims=True,
    )
    probability_gradient = jnp.einsum(
        "nmv,njv->nmj", output_gradient_heads, value_row_block, preferred_element_type=jnp.float32
    )
    score_gradient = (probabilities * (probability_gradient - out_dot)).astype(jnp.bfloat16)
    query_gradient_heads = (
        jnp.einsum(
            "jym,jmo->jyo", score_gradient, key_row_block, preferred_element_type=jnp.float32
        )
        * logit_scale
    ).astype(jnp.bfloat16)
    key_gradient = (
        jnp.einsum(
            "uwj,uwn->ujn", score_gradient, query_per_head, preferred_element_type=jnp.float32
        )
        * logit_scale
    )
    value_gradient = jnp.einsum(
        "uwj,uwn->ujn", attention_weight, output_gradient_heads, preferred_element_type=jnp.float32
    )
    return (
        attended_per_head,
        query_gradient_heads,
        key_gradient,
        value_gradient,
        log_total[..., 0],
        out_dot[..., 0],
    )


def body(queries, key_tokens, value_tokens, grad_out):
    row_width = queries.shape[1]
    tok_count = queries.shape[0]
    blocks_dev = tok_count // BLK
    rim = (WINDOW + blocks_dev - 1) // blocks_dev
    devices = lax.axis_size("seq")
    near_list, far_list = offset_lists(devices * blocks_dev)
    offsets = near_list + far_list
    near_count = len(near_list)
    logit_scale = 1.0 / math.sqrt(HD)
    span_blocks = (rim + 1) * blocks_dev
    lead = rim * blocks_dev
    earlier_keys = []
    earlier_values = []
    for back in range(rim, 0, -1):
        got_keys, got_values = passed_along((key_tokens, value_tokens), "seq", back)
        earlier_keys.append(got_keys)
        earlier_values.append(got_values)
    span_keys = to_blocks(jnp.concatenate(earlier_keys + [key_tokens], axis=0), span_blocks)
    span_values = to_blocks(jnp.concatenate(earlier_values + [value_tokens], axis=0), span_blocks)
    far_keys = []
    far_values = []
    for stride in far_list:
        got_keys, got_values = passed_along((key_tokens, value_tokens), "seq", stride // blocks_dev)
        far_keys.append(to_blocks(got_keys, blocks_dev))
        far_values.append(to_blocks(got_values, blocks_dev))
    position = lax.axis_index("seq")
    allowed = allowed_mask(position * blocks_dev, blocks_dev, offsets)
    query_blocks = to_blocks(queries, blocks_dev)
    grad_blocks = to_blocks(grad_out, blocks_dev)
    attended_heads = []
    grad_query_heads = []
    near_key_heads = []
    near_value_heads = []
    total_heads = []
    dot_heads = []
    far_key_parts = [[] for stride in far_list]
    far_value_parts = [[] for stride in far_list]
    for head_index in range(HEADS):
        col_start = head_index * HD
        key_slabs = jnp.stack(
            [
                head_cols(span_keys[lead - offset : lead + blocks_dev - offset], col_start)
                for offset in near_list
            ]
            + [head_cols(item, col_start) for item in far_keys],
            axis=1,
        )
        value_slabs = jnp.stack(
            [
                head_cols(span_values[lead - offset : lead + blocks_dev - offset], col_start)
                for offset in near_list
            ]
            + [head_cols(item, col_start) for item in far_values],
            axis=1,
        )
        (
            attended_per_head,
            query_gradient_heads,
            key_gradient,
            value_gradient,
            log_total,
            out_dot,
        ) = head_pass(
            head_cols(query_blocks, col_start),
            head_cols(grad_blocks, col_start),
            key_slabs,
            value_slabs,
            allowed,
            logit_scale,
        )
        key_gradient = key_gradient.reshape(blocks_dev, -1, BLK, HD)
        value_gradient = value_gradient.reshape(blocks_dev, -1, BLK, HD)
        near_key_heads.append(place_slabs(key_gradient, near_list, lead, span_blocks))
        near_value_heads.append(place_slabs(value_gradient, near_list, lead, span_blocks))
        for level_index in range(len(far_list)):
            far_key_parts[level_index].append(
                key_gradient[:, near_count + level_index].astype(jnp.bfloat16)
            )
            far_value_parts[level_index].append(
                value_gradient[:, near_count + level_index].astype(jnp.bfloat16)
            )
        attended_heads.append(attended_per_head)
        grad_query_heads.append(query_gradient_heads)
        total_heads.append(log_total)
        dot_heads.append(out_dot)
    attended = jnp.concatenate(attended_heads, axis=-1).reshape(tok_count, row_width)
    grad_queries = jnp.concatenate(grad_query_heads, axis=-1).reshape(tok_count, row_width)
    near_keys = jnp.concatenate(near_key_heads, axis=-1).reshape((rim + 1) * tok_count, row_width)
    near_values = jnp.concatenate(near_value_heads, axis=-1).reshape(
        (rim + 1) * tok_count, row_width
    )
    total_keys = near_keys[lead * BLK :].astype(jnp.bfloat16).astype(jnp.float32)
    total_values = near_values[lead * BLK :].astype(jnp.bfloat16).astype(jnp.float32)
    for back in range(1, rim + 1):
        piece_start = (rim - back) * tok_count
        part_keys = near_keys[piece_start : piece_start + tok_count].astype(jnp.bfloat16)
        part_values = near_values[piece_start : piece_start + tok_count].astype(jnp.bfloat16)
        back_keys, back_values = passed_along((part_keys, part_values), "seq", -back)
        total_keys = total_keys + back_keys.astype(jnp.float32)
        total_values = total_values + back_values.astype(jnp.float32)
    for level_index, stride in enumerate(far_list):
        part_keys = jnp.concatenate(far_key_parts[level_index], axis=-1).reshape(
            tok_count, row_width
        )
        part_values = jnp.concatenate(far_value_parts[level_index], axis=-1).reshape(
            tok_count, row_width
        )
        got_keys, got_values = passed_along(
            (part_keys, part_values), "seq", -(stride // blocks_dev)
        )
        total_keys = total_keys + got_keys.astype(jnp.float32)
        total_values = total_values + got_values.astype(jnp.float32)
    return (
        attended,
        grad_queries,
        total_keys.astype(jnp.bfloat16),
        total_values.astype(jnp.bfloat16),
    )


def solution(mesh):
    placed = (
        P(("rep", "seq"), None),
        P(("rep", "seq"), None),
        P(("rep", "seq"), None),
        P(("rep", "seq"), None),
    )
    return jax.shard_map(
        body,
        mesh=mesh,
        in_specs=placed,
        out_specs=(
            P(("rep", "seq"), None),
            P(("rep", "seq"), None),
            P(("rep", "seq"), None),
            P(("rep", "seq"), None),
        ),
        check_vma=False,
    )
```

profile of v0, /device:TPU:14, one launch (start us, length us, event | category | flops | bytes accessed | tf_op | source)
XLA Modules:
  0.0 98.7 jit_solution(18210573907532908393)
XLA Ops:
  0.7 3.4 %collective-permute-start.3 = (bf16[256,512]{1,0:T(8,128)(2,1)}, bf16[256,512]{1,0:T(8,128)(2,1)S(1)}, u32[]{:S(2)}, u32[]{:S(2)}) collective-permute-start(bf16[256,512]{1,0:T(8,128)(2,1)} %param.7), channel_id=1, source_target_pairs={{0,4},{4,8},{8,12},{12,16},{16,20},{20,24},{24,28},{1,5},{5,9},{9,... | collective-permute-start | bytes 786440 | tf_op jit(solution)/shard_map/ppermute | solution.py:20
  4.1 3.5 %collective-permute-start.4 = (bf16[256,512]{1,0:T(8,128)(2,1)}, bf16[256,512]{1,0:T(8,128)(2,1)S(1)}, u32[]{:S(2)}, u32[]{:S(2)}) collective-permute-start(bf16[256,512]{1,0:T(8,128)(2,1)} %param.7), channel_id=1, source_target_pairs={{0,8},{4,12},{8,16},{12,20},{16,24},{20,28},{1,9},{5,13},{9,17},{1... | collective-permute-start | bytes 786440 | tf_op jit(solution)/shard_map/ppermute | solution.py:20
  7.6 2.0 %collective-permute-start.5 = (bf16[256,512]{1,0:T(8,128)(2,1)}, bf16[256,512]{1,0:T(8,128)(2,1)}, u32[]{:S(2)}, u32[]{:S(2)}) collective-permute-start(bf16[256,512]{1,0:T(8,128)(2,1)} %param.7), channel_id=1, source_target_pairs={{0,16},{4,20},{8,24},{12,28},{1,17},{5,21},{9,25},{13,29},{2,18},{... | collective-permute-start | bytes 786440 | tf_op jit(solution)/shard_map/ppermute | solution.py:20
  9.6 2.7 %collective-permute-start = (bf16[256,512]{1,0:T(8,128)(2,1)}, bf16[256,512]{1,0:T(8,128)(2,1)S(1)}, u32[]{:S(2)}, u32[]{:S(2)}) collective-permute-start(bf16[256,512]{1,0:T(8,128)(2,1)} %param.6), channel_id=1, source_target_pairs={{0,4},{4,8},{8,12},{12,16},{16,20},{20,24},{24,28},{1,5},{5,9},{9,... | collective-permute-start | bytes 786440 | tf_op jit(solution)/shard_map/ppermute | solution.py:20
  12.3 1.9 %collective-permute-start.1 = (bf16[256,512]{1,0:T(8,128)(2,1)}, bf16[256,512]{1,0:T(8,128)(2,1)S(1)}, u32[]{:S(2)}, u32[]{:S(2)}) collective-permute-start(bf16[256,512]{1,0:T(8,128)(2,1)} %param.6), channel_id=1, source_target_pairs={{0,8},{4,12},{8,16},{12,20},{16,24},{20,28},{1,9},{5,13},{9,17},{1... | collective-permute-start | bytes 786440 | tf_op jit(solution)/shard_map/ppermute | solution.py:20
  14.3 1.0 constant_dynamic-update-slice_fusion.17
  16.1 1.0 %fusion.60 = (bf16[2,128,128]{2,1,0:T(8,128)(2,1)S(1)}, bf16[2,128,128]{2,1,0:T(8,128)(2,1)S(1)}, bf16[2,128,128]{2,1,0:T(8,128)(2,1)S(1)}, bf16[2,128,128]{2,1,0:T(8,128)(2,1)S(1)}) fusion(bf16[2,128,512]{2,1,0:T(8,128)(2,1)} %bitcast.505), kind=kLoop, calls=%fused_computation.263 | loop fusion | bytes 524288
  18.1 21.1 %collective-permute-done = bf16[256,512]{1,0:T(8,128)(2,1)S(1)} collective-permute-done((bf16[256,512]{1,0:T(8,128)(2,1)}, bf16[256,512]{1,0:T(8,128)(2,1)S(1)}, u32[]{:S(2)}, u32[]{:S(2)}) %collective-permute-start) | collective-permute-done | bytes 262176 | tf_op jit(solution)/shard_map/ppermute | solution.py:20
  39.2 1.3 %collective-permute-start.2 = (bf16[256,512]{1,0:T(8,128)(2,1)S(1)}, bf16[256,512]{1,0:T(8,128)(2,1)S(1)}, u32[]{:S(2)}, u32[]{:S(2)}) collective-permute-start(bf16[256,512]{1,0:T(8,128)(2,1)S(1)} %copy-done.1), channel_id=1, source_target_pairs={{0,16},{4,20},{8,24},{12,28},{1,17},{5,21},{9,25},{13,29},{2,18},{... | collective-permute-start | bytes 786440 | tf_op jit(solution)/shard_map/ppermute | solution.py:20
  40.5 4.3 %collective-permute-done.1 = bf16[256,512]{1,0:T(8,128)(2,1)S(1)} collective-permute-done((bf16[256,512]{1,0:T(8,128)(2,1)}, bf16[256,512]{1,0:T(8,128)(2,1)S(1)}, u32[]{:S(2)}, u32[]{:S(2)}) %collective-permute-start.1) | collective-permute-done | bytes 262176 | tf_op jit(solution)/shard_map/ppermute | solution.py:20
  45.4 1.0 constant_dynamic-update-slice_fusion.6
  46.5 2.7 %collective-permute-done.2 = bf16[256,512]{1,0:T(8,128)(2,1)S(1)} collective-permute-done((bf16[256,512]{1,0:T(8,128)(2,1)S(1)}, bf16[256,512]{1,0:T(8,128)(2,1)S(1)}, u32[]{:S(2)}, u32[]{:S(2)}) %collective-permute-start.2) | collective-permute-done | bytes 262176 | tf_op jit(solution)/shard_map/ppermute | solution.py:20
  58.6 1.3 %collective-permute-start.8 = (bf16[256,512]{1,0:T(8,128)(2,1)S(1)}, bf16[256,512]{1,0:T(8,128)(2,1)S(1)}, u32[]{:S(2)}, u32[]{:S(2)}) collective-permute-start(bf16[256,512]{1,0:T(8,128)(2,1)S(1)} %pad_maximum_fusion.6), channel_id=1, source_target_pairs={{16,0},{20,4},{24,8},{28,12},{17,1},{21,5},{25,9},{29,13},{18,2},{... | collective-permute-start | bytes 786440 | tf_op jit(solution)/shard_map/ppermute | solution.py:20
  60.3 1.9 %collective-permute-start.7 = (bf16[256,512]{1,0:T(8,128)(2,1)S(1)}, bf16[256,512]{1,0:T(8,128)(2,1)S(1)}, u32[]{:S(2)}, u32[]{:S(2)}) collective-permute-start(bf16[256,512]{1,0:T(8,128)(2,1)S(1)} %bitcast.550), channel_id=1, source_target_pairs={{8,0},{12,4},{16,8},{20,12},{24,16},{28,20},{9,1},{13,5},{17,9},{2... | collective-permute-start | bytes 786440 | tf_op jit(solution)/shard_map/ppermute | solution.py:20
  62.2 3.0 %collective-permute-start.6 = (bf16[256,512]{1,0:T(8,128)(2,1)S(1)}, bf16[256,512]{1,0:T(8,128)(2,1)S(1)}, u32[]{:S(2)}, u32[]{:S(2)}) collective-permute-start(bf16[256,512]{1,0:T(8,128)(2,1)S(1)} %bitcast.549), channel_id=1, source_target_pairs={{4,0},{8,4},{12,8},{16,12},{20,16},{24,20},{28,24},{5,1},{9,5},{13... | collective-permute-start | bytes 786440 | tf_op jit(solution)/shard_map/ppermute | solution.py:20
  65.2 1.3 %collective-permute-start.11 = (bf16[256,512]{1,0:T(8,128)(2,1)S(1)}, bf16[256,512]{1,0:T(8,128)(2,1)S(1)}, u32[]{:S(2)}, u32[]{:S(2)}) collective-permute-start(bf16[256,512]{1,0:T(8,128)(2,1)S(1)} %pad_maximum_fusion.7), channel_id=1, source_target_pairs={{16,0},{20,4},{24,8},{28,12},{17,1},{21,5},{25,9},{29,13},{18,2},{... | collective-permute-start | bytes 786440 | tf_op jit(solution)/shard_map/ppermute | solution.py:20
  67.7 1.9 %collective-permute-start.10 = (bf16[256,512]{1,0:T(8,128)(2,1)}, bf16[256,512]{1,0:T(8,128)(2,1)S(1)}, u32[]{:S(2)}, u32[]{:S(2)}) collective-permute-start(bf16[256,512]{1,0:T(8,128)(2,1)} %bitcast.144), channel_id=1, source_target_pairs={{8,0},{12,4},{16,8},{20,12},{24,16},{28,20},{9,1},{13,5},{17,9},{2... | collective-permute-start | bytes 786440 | tf_op jit(solution)/shard_map/ppermute | solution.py:20
  69.6 1.0 %collective-permute-done.8 = bf16[256,512]{1,0:T(8,128)(2,1)S(1)} collective-permute-done((bf16[256,512]{1,0:T(8,128)(2,1)S(1)}, bf16[256,512]{1,0:T(8,128)(2,1)S(1)}, u32[]{:S(2)}, u32[]{:S(2)}) %collective-permute-start.8) | collective-permute-done | bytes 262176 | tf_op jit(solution)/shard_map/ppermute | solution.py:20
  70.7 1.9 %collective-permute-start.9 = (bf16[256,512]{1,0:T(8,128)(2,1)}, bf16[256,512]{1,0:T(8,128)(2,1)S(1)}, u32[]{:S(2)}, u32[]{:S(2)}) collective-permute-start(bf16[256,512]{1,0:T(8,128)(2,1)} %bitcast.143), channel_id=1, source_target_pairs={{4,0},{8,4},{12,8},{16,12},{20,16},{24,20},{28,24},{5,1},{9,5},{13... | collective-permute-start | bytes 786440 | tf_op jit(solution)/shard_map/ppermute | solution.py:20
  74.3 8.7 %collective-permute-done.7 = bf16[256,512]{1,0:T(8,128)(2,1)S(1)} collective-permute-done((bf16[256,512]{1,0:T(8,128)(2,1)S(1)}, bf16[256,512]{1,0:T(8,128)(2,1)S(1)}, u32[]{:S(2)}, u32[]{:S(2)}) %collective-permute-start.7) | collective-permute-done | bytes 262176 | tf_op jit(solution)/shard_map/ppermute | solution.py:20
  83.5 0.9 fusion.29
  84.3 8.5 %collective-permute-done.10 = bf16[256,512]{1,0:T(8,128)(2,1)S(1)} collective-permute-done((bf16[256,512]{1,0:T(8,128)(2,1)}, bf16[256,512]{1,0:T(8,128)(2,1)S(1)}, u32[]{:S(2)}, u32[]{:S(2)}) %collective-permute-start.10) | collective-permute-done | bytes 262176 | tf_op jit(solution)/shard_map/ppermute | solution.py:20
  92.8 5.0 %collective-permute-done.9 = bf16[256,512]{1,0:T(8,128)(2,1)S(1)} collective-permute-done((bf16[256,512]{1,0:T(8,128)(2,1)}, bf16[256,512]{1,0:T(8,128)(2,1)S(1)}, u32[]{:S(2)}, u32[]{:S(2)}) %collective-permute-start.9) | collective-permute-done | bytes 262176 | tf_op jit(solution)/shard_map/ppermute | solution.py:20
  97.8 0.9 fusion.26
  (115 shorter events, 15.1 us)
Async XLA Ops:
  0.6 16.5 %copy-start.5 = (pred[6]{0:T(512)(128)(4,1)S(1)}, pred[6]{0:T(512)(128)(4,1)}, u32[]{:S(2)}) copy-start(pred[6]{0:T(512)(128)(4,1)} %constant.107) | copy-start | bytes 22
  0.6 16.5 %copy-start.4 = (s32[6]{0:T(128)S(1)}, s32[6]{0:T(128)}, u32[]{:S(2)}) copy-start(s32[6]{0:T(128)} %constant.106) | copy-start | bytes 76
  0.7 44.3 %collective-permute-start.3 = (bf16[256,512]{1,0:T(8,128)(2,1)}, bf16[256,512]{1,0:T(8,128)(2,1)S(1)}, u32[]{:S(2)}, u32[]{:S(2)}) collective-permute-start(bf16[256,512]{1,0:T(8,128)(2,1)} %param.7), channel_id=1, source_target_pairs={{0,4},{4,8},{8,12},{12,16},{16,20},{20,24},{24,28},{1,5},{5,9},{9,... | collective-permute-start | bytes 786440 | tf_op jit(solution)/shard_map/ppermute | solution.py:20
  4.1 40.9 %collective-permute-start.4 = (bf16[256,512]{1,0:T(8,128)(2,1)}, bf16[256,512]{1,0:T(8,128)(2,1)S(1)}, u32[]{:S(2)}, u32[]{:S(2)}) collective-permute-start(bf16[256,512]{1,0:T(8,128)(2,1)} %param.7), channel_id=1, source_target_pairs={{0,8},{4,12},{8,16},{12,20},{16,24},{20,28},{1,9},{5,13},{9,17},{1... | collective-permute-start | bytes 786440 | tf_op jit(solution)/shard_map/ppermute | solution.py:20
  7.6 37.8 %collective-permute-start.5 = (bf16[256,512]{1,0:T(8,128)(2,1)}, bf16[256,512]{1,0:T(8,128)(2,1)}, u32[]{:S(2)}, u32[]{:S(2)}) collective-permute-start(bf16[256,512]{1,0:T(8,128)(2,1)} %param.7), channel_id=1, source_target_pairs={{0,16},{4,20},{8,24},{12,28},{1,17},{5,21},{9,25},{13,29},{2,18},{... | collective-permute-start | bytes 786440 | tf_op jit(solution)/shard_map/ppermute | solution.py:20
  9.6 29.7 %collective-permute-start = (bf16[256,512]{1,0:T(8,128)(2,1)}, bf16[256,512]{1,0:T(8,128)(2,1)S(1)}, u32[]{:S(2)}, u32[]{:S(2)}) collective-permute-start(bf16[256,512]{1,0:T(8,128)(2,1)} %param.6), channel_id=1, source_target_pairs={{0,4},{4,8},{8,12},{12,16},{16,20},{20,24},{24,28},{1,5},{5,9},{9,... | collective-permute-start | bytes 786440 | tf_op jit(solution)/shard_map/ppermute | solution.py:20
  12.3 32.5 %collective-permute-start.1 = (bf16[256,512]{1,0:T(8,128)(2,1)}, bf16[256,512]{1,0:T(8,128)(2,1)S(1)}, u32[]{:S(2)}, u32[]{:S(2)}) collective-permute-start(bf16[256,512]{1,0:T(8,128)(2,1)} %param.6), channel_id=1, source_target_pairs={{0,8},{4,12},{8,16},{12,20},{16,24},{20,28},{1,9},{5,13},{9,17},{1... | collective-permute-start | bytes 786440 | tf_op jit(solution)/shard_map/ppermute | solution.py:20
  14.3 3.8 %copy-start.2 = (bf16[256,512]{1,0:T(8,128)(2,1)S(1)}, bf16[256,512]{1,0:T(8,128)(2,1)}, u32[]{:S(2)}) copy-start(bf16[256,512]{1,0:T(8,128)(2,1)} %param.7) | copy-start | bytes 786436
  16.1 23.2 %copy-start.1 = (bf16[256,512]{1,0:T(8,128)(2,1)S(1)}, bf16[256,512]{1,0:T(8,128)(2,1)}, u32[]{:S(2)}) copy-start(bf16[256,512]{1,0:T(8,128)(2,1)} %param.6) | copy-start | bytes 786436
  39.2 10.0 %collective-permute-start.2 = (bf16[256,512]{1,0:T(8,128)(2,1)S(1)}, bf16[256,512]{1,0:T(8,128)(2,1)S(1)}, u32[]{:S(2)}, u32[]{:S(2)}) collective-permute-start(bf16[256,512]{1,0:T(8,128)(2,1)S(1)} %copy-done.1), channel_id=1, source_target_pairs={{0,16},{4,20},{8,24},{12,28},{1,17},{5,21},{9,25},{13,29},{2,18},{... | collective-permute-start | bytes 786440 | tf_op jit(solution)/shard_map/ppermute | solution.py:20
  46.5 2.9 %copy-start.3 = (bf16[256,512]{1,0:T(8,128)(2,1)S(1)}, bf16[256,512]{1,0:T(8,128)(2,1)}, u32[]{:S(2)}) copy-start(bf16[256,512]{1,0:T(8,128)(2,1)} %param.5) | copy-start | bytes 786436
  49.8 1.0 copy-start
  58.6 12.0 %collective-permute-start.8 = (bf16[256,512]{1,0:T(8,128)(2,1)S(1)}, bf16[256,512]{1,0:T(8,128)(2,1)S(1)}, u32[]{:S(2)}, u32[]{:S(2)}) collective-permute-start(bf16[256,512]{1,0:T(8,128)(2,1)S(1)} %pad_maximum_fusion.6), channel_id=1, source_target_pairs={{16,0},{20,4},{24,8},{28,12},{17,1},{21,5},{25,9},{29,13},{18,2},{... | collective-permute-start | bytes 786440 | tf_op jit(solution)/shard_map/ppermute | solution.py:20
  60.3 22.8 %collective-permute-start.7 = (bf16[256,512]{1,0:T(8,128)(2,1)S(1)}, bf16[256,512]{1,0:T(8,128)(2,1)S(1)}, u32[]{:S(2)}, u32[]{:S(2)}) collective-permute-start(bf16[256,512]{1,0:T(8,128)(2,1)S(1)} %bitcast.550), channel_id=1, source_target_pairs={{8,0},{12,4},{16,8},{20,12},{24,16},{28,20},{9,1},{13,5},{17,9},{2... | collective-permute-start | bytes 786440 | tf_op jit(solution)/shard_map/ppermute | solution.py:20
  62.2 21.3 %collective-permute-start.6 = (bf16[256,512]{1,0:T(8,128)(2,1)S(1)}, bf16[256,512]{1,0:T(8,128)(2,1)S(1)}, u32[]{:S(2)}, u32[]{:S(2)}) collective-permute-start(bf16[256,512]{1,0:T(8,128)(2,1)S(1)} %bitcast.549), channel_id=1, source_target_pairs={{4,0},{8,4},{12,8},{16,12},{20,16},{24,20},{28,24},{5,1},{9,5},{13... | collective-permute-start | bytes 786440 | tf_op jit(solution)/shard_map/ppermute | solution.py:20
  65.2 19.1 %collective-permute-start.11 = (bf16[256,512]{1,0:T(8,128)(2,1)S(1)}, bf16[256,512]{1,0:T(8,128)(2,1)S(1)}, u32[]{:S(2)}, u32[]{:S(2)}) collective-permute-start(bf16[256,512]{1,0:T(8,128)(2,1)S(1)} %pad_maximum_fusion.7), channel_id=1, source_target_pairs={{16,0},{20,4},{24,8},{28,12},{17,1},{21,5},{25,9},{29,13},{18,2},{... | collective-permute-start | bytes 786440 | tf_op jit(solution)/shard_map/ppermute | solution.py:20
  67.7 25.1 %collective-permute-start.10 = (bf16[256,512]{1,0:T(8,128)(2,1)}, bf16[256,512]{1,0:T(8,128)(2,1)S(1)}, u32[]{:S(2)}, u32[]{:S(2)}) collective-permute-start(bf16[256,512]{1,0:T(8,128)(2,1)} %bitcast.144), channel_id=1, source_target_pairs={{8,0},{12,4},{16,8},{20,12},{24,16},{28,20},{9,1},{13,5},{17,9},{2... | collective-permute-start | bytes 786440 | tf_op jit(solution)/shard_map/ppermute | solution.py:20
  70.7 27.1 %collective-permute-start.9 = (bf16[256,512]{1,0:T(8,128)(2,1)}, bf16[256,512]{1,0:T(8,128)(2,1)S(1)}, u32[]{:S(2)}, u32[]{:S(2)}) collective-permute-start(bf16[256,512]{1,0:T(8,128)(2,1)} %bitcast.143), channel_id=1, source_target_pairs={{4,0},{8,4},{12,8},{16,12},{20,16},{24,20},{28,24},{5,1},{9,5},{13... | collective-permute-start | bytes 786440 | tf_op jit(solution)/shard_map/ppermute | solution.py:20
where the time goes:
time: 99.2 us; the launch traced here: 98.7 us
  waiting for transfers between devices  51.8 us (52%)
  starting transfers between devices  26.2 us (26%)
  local copies, waits for them, and re-layouts  8.96 us (9%)
  matrix products  7.11 us (7%)
  other arithmetic  3.21 us (3%)
  between operations  1.4 us (1%)
    ppermute x12, waiting for transfers between devices, passed_along(): lax.ppermute(value, axis, [(source, source + steps) for source in range(f...  51.8 us
    ppermute x12, starting transfers between devices, passed_along(): lax.ppermute(value, axis, [(source, source + steps) for source in range(f...  26.2 us
    unnamed x34, local copies, waits for them, and re-layouts  4.59 us
  transfers between devices with their start and end apart: 12, of which 8 were waited for; matrix products, arithmetic and copies ran while one was open for 9% of the time, Pallas kernels for 0%

commit v1 on v0

--- a/solution.py
+++ b/solution.py
@@ -116,6 +116,14 @@
     )
 
 
+def swap_pairs(count):
+    return [(source, source ^ 1) for source in range(count) if source ^ 1 < count]
+
+
+def relay_ok(count, blocks_dev, rim, far_shifts):
+    return count % 2 == 0 and blocks_dev == 2 and rim == 2 and (not far_shifts or far_shifts[0] == 4)
+
+
 def body(queries, key_tokens, value_tokens, grad_out):
     row_width = queries.shape[1]
     tok_count = queries.shape[0]
@@ -128,21 +136,41 @@
     logit_scale = 1.0 / math.sqrt(HD)
     span_blocks = (rim + 1) * blocks_dev
     lead = rim * blocks_dev
-    earlier_keys = []
-    earlier_values = []
-    for back in range(rim, 0, -1):
-        got_keys, got_values = passed_along((key_tokens, value_tokens), "seq", back)
-        earlier_keys.append(got_keys)
-        earlier_values.append(got_values)
+    far_shifts = [stride // blocks_dev for stride in far_list]
+    relay = relay_ok(devices, blocks_dev, rim, far_shifts)
+    position = lax.axis_index("seq")
+    odd = (position % 2) == 1
+    if relay:
+        both = jnp.concatenate([key_tokens, value_tokens], axis=1)
+        back2 = passed_along(both, "seq", 2)
+        back1 = lax.ppermute(jnp.where(odd, back2, both), "seq", swap_pairs(devices))
+        far_both = []
+        for level_index, shift in enumerate(far_shifts):
+            if level_index == 0:
+                far_both.append(passed_along(back2, "seq", 2))
+            else:
+                far_both.append(passed_along(both, "seq", shift))
+        earlier_keys = [back2[:, :row_width], back1[:, :row_width]]
+        earlier_values = [back2[:, row_width:], back1[:, row_width:]]
+        far_keys = [to_blocks(item[:, :row_width], blocks_dev) for item in far_both]
+        far_values = [to_blocks(item[:, row_width:], blocks_dev) for item in far_both]
+    else:
+        earlier_keys = []
+        earlier_values = []
+        for back in range(rim, 0, -1):
+            got_keys, got_values = passed_along((key_tokens, value_tokens), "seq", back)
+            earlier_keys.append(got_keys)
+            earlier_values.append(got_values)
+        far_keys = []
+        far_values = []
+        for stride in far_list:
+            got_keys, got_values = passed_along(
+                (key_tokens, value_tokens), "seq", stride // blocks_dev
+            )
+            far_keys.append(to_blocks(got_keys, blocks_dev))
+            far_values.append(to_blocks(got_values, blocks_dev))
     span_keys = to_blocks(jnp.concatenate(earlier_keys + [key_tokens], axis=0), span_blocks)
     span_values = to_blocks(jnp.concatenate(earlier_values + [value_tokens], axis=0), span_blocks)
-    far_keys = []
-    far_values = []
-    for stride in far_list:
-        got_keys, got_values = passed_along((key_tokens, value_tokens), "seq", stride // blocks_dev)
-        far_keys.append(to_blocks(got_keys, blocks_dev))
-        far_values.append(to_blocks(got_values, blocks_dev))
-    position = lax.axis_index("seq")
     allowed = allowed_mask(position * blocks_dev, blocks_dev, offsets)
     query_blocks = to_blocks(queries, blocks_dev)
     grad_blocks = to_blocks(grad_out, blocks_dev)
@@ -150,8 +178,6 @@
     grad_query_heads = []
     near_key_heads = []
     near_value_heads = []
-    total_heads = []
-    dot_heads = []
     far_key_parts = [[] for stride in far_list]
     far_value_parts = [[] for stride in far_list]
     for head_index in range(HEADS):
@@ -192,43 +218,63 @@
         near_key_heads.append(place_slabs(key_gradient, near_list, lead, span_blocks))
         near_value_heads.append(place_slabs(value_gradient, near_list, lead, span_blocks))
         for level_index in range(len(far_list)):
-            far_key_parts[level_index].append(
-                key_gradient[:, near_count + level_index].astype(jnp.bfloat16)
-            )
-            far_value_parts[level_index].append(
-                value_gradient[:, near_count + level_index].astype(jnp.bfloat16)
-            )
+            far_key_parts[level_index].append(key_gradient[:, near_count + level_index])
+            far_value_parts[level_index].append(value_gradient[:, near_count + level_index])
         attended_heads.append(attended_per_head)
         grad_query_heads.append(query_gradient_heads)
-        total_heads.append(log_total)
-        dot_heads.append(out_dot)
     attended = jnp.concatenate(attended_heads, axis=-1).reshape(tok_count, row_width)
     grad_queries = jnp.concatenate(grad_query_heads, axis=-1).reshape(tok_count, row_width)
     near_keys = jnp.concatenate(near_key_heads, axis=-1).reshape((rim + 1) * tok_count, row_width)
     near_values = jnp.concatenate(near_value_heads, axis=-1).reshape(
         (rim + 1) * tok_count, row_width
     )
+    far_parts = []
+    for level_index in range(len(far_list)):
+        part_keys = jnp.concatenate(far_key_parts[level_index], axis=-1).reshape(
+            tok_count, row_width
+        )
+        part_values = jnp.concatenate(far_value_parts[level_index], axis=-1).reshape(
+            tok_count, row_width
+        )
+        far_parts.append((part_keys, part_values))
     total_keys = near_keys[lead * BLK :].astype(jnp.bfloat16).astype(jnp.float32)
     total_values = near_values[lead * BLK :].astype(jnp.bfloat16).astype(jnp.float32)
-    for back in range(1, rim + 1):
-        piece_start = (rim - back) * tok_count
-        part_keys = near_keys[piece_start : piece_start + tok_count].astype(jnp.bfloat16)
-        part_values = near_values[piece_start : piece_start + tok_count].astype(jnp.bfloat16)
-        back_keys, back_values = passed_along((part_keys, part_values), "seq", -back)
-        total_keys = total_keys + back_keys.astype(jnp.float32)
-        total_values = total_values + back_values.astype(jnp.float32)
-    for level_index, stride in enumerate(far_list):
-        part_keys = jnp.concatenate(far_key_parts[level_index], axis=-1).reshape(
-            tok_count, row_width
-        )
-        part_values = jnp.concatenate(far_value_parts[level_index], axis=-1).reshape(
-            tok_count, row_width
-        )
-        got_keys, got_values = passed_along(
-            (part_keys, part_values), "seq", -(stride // blocks_dev)
-        )
-        total_keys = total_keys + got_keys.astype(jnp.float32)
-        total_values = total_values + got_values.astype(jnp.float32)
+    if relay:
+        near_both = jnp.concatenate([near_keys, near_values], axis=1)
+        part_two = near_both[:tok_count]
+        part_one = near_both[tok_count : 2 * tok_count].astype(jnp.bfloat16)
+        swapped = lax.ppermute(part_one, "seq", swap_pairs(devices)).astype(jnp.float32)
+        zero = jnp.zeros_like(swapped)
+        relayed = part_two + jnp.where(odd, swapped, zero)
+        for level_index, shift in enumerate(far_shifts):
+            far_both = jnp.concatenate(far_parts[level_index], axis=1).astype(jnp.bfloat16)
+            if level_index == 0:
+                relayed = relayed + passed_along(far_both, "seq", -2).astype(jnp.float32)
+            else:
+                got = passed_along(far_both, "seq", -shift).astype(jnp.float32)
+                total_keys = total_keys + got[:, :row_width]
+                total_values = total_values + got[:, row_width:]
+        arrived = passed_along(relayed.astype(jnp.bfloat16), "seq", -2).astype(jnp.float32)
+        arrived = arrived + jnp.where(odd, zero, swapped)
+        total_keys = total_keys + arrived[:, :row_width]
+        total_values = total_values + arrived[:, row_width:]
+    else:
+        for back in range(1, rim + 1):
+            piece_start = (rim - back) * tok_count
+            part_keys = near_keys[piece_start : piece_start + tok_count].astype(jnp.bfloat16)
+            part_values = near_values[piece_start : piece_start + tok_count].astype(jnp.bfloat16)
+            back_keys, back_values = passed_along((part_keys, part_values), "seq", -back)
+            total_keys = total_keys + back_keys.astype(jnp.float32)
+            total_values = total_values + back_values.astype(jnp.float32)
+        for level_index, stride in enumerate(far_list):
+            part_keys, part_values = far_parts[level_index]
+            got_keys, got_values = passed_along(
+                (part_keys.astype(jnp.bfloat16), part_values.astype(jnp.bfloat16)),
+                "seq",
+                -(stride // blocks_dev),
+            )
+            total_keys = total_keys + got_keys.astype(jnp.float32)
+            total_values = total_values + got_values.astype(jnp.float32)
     return (
         attended,
         grad_queries,

time: 99.2 us -> 77.9 us (0.79)
  the two profiles are of different devices: /device:TPU:14 before, /device:TPU:0 now
where the time goes in v1:
time: 77.9 us; the launch traced here: 77.4 us
  waiting for transfers between devices  36.3 us (47%)
  starting transfers between devices  14 us (18%)
  local copies, waits for them, and re-layouts  12.8 us (16%)
  matrix products  8.35 us (11%)
  other arithmetic  4.49 us (6%)
  between operations  1.43 us (2%)
    ppermute x4, waiting for transfers between devices, passed_along(): lax.ppermute(value, axis, [(source, source + steps) for source in range(f...  32.5 us
    ppermute x4, starting transfers between devices, passed_along(): lax.ppermute(value, axis, [(source, source + steps) for source in range(f...  12 us
    unnamed x42, local copies, waits for them, and re-layouts  7.38 us
    ppermute x1, waiting for transfers between devices, body(): lax.ppermute(jnp.where(odd, back2, both), 'seq', swap_pairs(devices))  3.78 us
    dot_general x4, matrix products, head_pass(): jnp.einsum('jym,jmo->jyo', attention_weight, value_row_block, preferred_e...  2.61 us
  transfers between devices with their start and end apart: 6, of which 5 were waited for; matrix products, arithmetic and copies ran while one was open for 16% of the time, Pallas kernels for 0%

profile of v1, /device:TPU:0, one launch (start us, length us, event | category | flops | bytes accessed | tf_op | source)
XLA Modules:
  0.0 77.4 jit_solution(7903451363814488191)
XLA Ops:
  0.6 1.0 %constant_dynamic-update-slice_fusion.1 = bf16[256,1024]{1,0:T(8,128)(2,1)S(1)} fusion(bf16[256,512]{1,0:T(8,128)(2,1)} %param.6), kind=kLoop, calls=%fused_computation.144 | loop fusion | bytes 524288
  1.7 1.0 %constant_dynamic-update-slice_fusion = bf16[256,1024]{1,0:T(8,128)(2,1)S(1)} fusion(bf16[256,1024]{1,0:T(8,128)(2,1)S(1)} %constant_dynamic-update-slice_fusion.1, bf16[256,512]{1,0:T(8,128)(2,1)} %param.7), kind=kLoop, calls=%fused_computation.143 | loop fusion | bytes 524288 | tf_op jit(solution)/shard_map/concatenate | solution.py:144
  2.6 5.0 %collective-permute-start = (bf16[256,1024]{1,0:T(8,128)(2,1)S(1)}, bf16[256,1024]{1,0:T(8,128)(2,1)S(1)}, u32[]{:S(2)}, u32[]{:S(2)}) collective-permute-start(bf16[256,1024]{1,0:T(8,128)(2,1)S(1)} %constant_dynamic-update-slice_fusion), channel_id=1, source_target_pairs={{0,8},{4,12},{8,16},{12,20},{16,24},{20,28},{1,9},{5,13},{9,17},{1... | collective-permute-start | bytes 1572872 | tf_op jit(solution)/shard_map/ppermute | solution.py:20
  7.6 0.8 %constant_dynamic-update-slice_fusion.7 = bf16[2,6,128,128]{3,2,1,0:T(8,128)(2,1)S(1)} fusion(bf16[2,128,512]{2,1,0:T(8,128)(2,1)} %bitcast.517), kind=kLoop, calls=%fused_computation.150 | loop fusion | bytes 131072
  10.0 1.0 %constant_dynamic-update-slice_fusion.19 = (bf16[2,6,128,128]{3,2,0,1:T(8,128)(2,1)S(1)}, bf16[2,6,128,128]{3,2,0,1:T(8,128)(2,1)S(1)}, bf16[2,6,128,128]{3,2,0,1:T(8,128)(2,1)S(1)}) fusion(bf16[2,128,512]{2,1,0:T(8,128)(2,1)} %bitcast.518), kind=kLoop, calls=%fused_computation.162 | loop fusion | bytes 393216
  11.7 7.1 %collective-permute-done = bf16[256,1024]{1,0:T(8,128)(2,1)S(1)} collective-permute-done((bf16[256,1024]{1,0:T(8,128)(2,1)S(1)}, bf16[256,1024]{1,0:T(8,128)(2,1)S(1)}, u32[]{:S(2)}, u32[]{:S(2)}) %collective-permute-start) | collective-permute-done | bytes 524320 | tf_op jit(solution)/shard_map/ppermute | solution.py:20
  18.7 0.8 %broadcast_select_fusion = bf16[256,1024]{1,0:T(8,128)(2,1)} fusion(bf16[256,1024]{1,0:T(8,128)(2,1)S(1)} %collective-permute-done, bf16[256,1024]{1,0:T(8,128)(2,1)S(1)} %constant_dynamic-update-slice_fusion, pred[]{:T(512)S(6)} %eq.5), kind=kLoop, calls=%fused_computation.75 | loop fusion | flops 262144 | bytes 1572865 | tf_op jit(solution)/shard_map/jit(_where)/select_n | solution.py:146
  19.6 1.5 %collective-permute-start.1 = (bf16[256,1024]{1,0:T(8,128)(2,1)}, bf16[256,1024]{1,0:T(8,128)(2,1)}, u32[]{:S(2)}, u32[]{:S(2)}) collective-permute-start(bf16[256,1024]{1,0:T(8,128)(2,1)} %broadcast_select_fusion), channel_id=1, source_target_pairs={{0,4},{4,0},{8,12},{12,8},{16,20},{20,16},{24,28},{28,24},{1,5},{5... | collective-permute-start | bytes 1572872 | tf_op jit(solution)/shard_map/ppermute | solution.py:146
  21.3 1.0 %copy.208 = bf16[2,128,128]{1,2,0:T(8,128)(2,1)S(1)} copy(bf16[2,128,128]{2,1,0:T(8,128)(2,1)} %get-tuple-element.54) | data formatting | bytes 131072
  22.3 1.0 %copy.209 = bf16[2,128,128]{1,2,0:T(8,128)(2,1)S(1)} copy(bf16[2,128,128]{2,1,0:T(8,128)(2,1)} %get-tuple-element.53) | data formatting | bytes 131072
  23.3 1.0 %copy.210 = bf16[2,128,128]{1,2,0:T(8,128)(2,1)S(1)} copy(bf16[2,128,128]{2,1,0:T(8,128)(2,1)} %get-tuple-element.55) | data formatting | bytes 131072
  24.5 4.4 %collective-permute-start.2 = (bf16[256,1024]{1,0:T(8,128)(2,1)S(1)}, bf16[256,1024]{1,0:T(8,128)(2,1)S(1)}, u32[]{:S(2)}, u32[]{:S(2)}) collective-permute-start(bf16[256,1024]{1,0:T(8,128)(2,1)S(1)} %collective-permute-done), channel_id=1, source_target_pairs={{0,8},{4,12},{8,16},{12,20},{16,24},{20,28},{1,9},{5,13},{9,17},{1... | collective-permute-start | bytes 1572872 | tf_op jit(solution)/shard_map/ppermute | solution.py:20
  28.9 3.8 %collective-permute-done.1 = bf16[256,1024]{1,0:T(8,128)(2,1)} collective-permute-done((bf16[256,1024]{1,0:T(8,128)(2,1)}, bf16[256,1024]{1,0:T(8,128)(2,1)}, u32[]{:S(2)}, u32[]{:S(2)}) %collective-permute-start.1) | collective-permute-done | bytes 524320 | tf_op jit(solution)/shard_map/ppermute | solution.py:146
  32.7 1.1 %fusion.62 = (bf16[256,512]{1,0:T(8,128)(2,1)S(1)}, bf16[256,512]{1,0:T(8,128)(2,1)S(1)}) fusion(bf16[256,1024]{1,0:T(8,128)(2,1)} %collective-permute-done.1), kind=kLoop, calls=%fused_computation.281 | loop fusion | bytes 1048576 | tf_op jit(solution)/shard_map/slice | solution.py:153
  34.0 4.9 %collective-permute-done.2 = bf16[256,1024]{1,0:T(8,128)(2,1)S(1)} collective-permute-done((bf16[256,1024]{1,0:T(8,128)(2,1)S(1)}, bf16[256,1024]{1,0:T(8,128)(2,1)S(1)}, u32[]{:S(2)}, u32[]{:S(2)}) %collective-permute-start.2) | collective-permute-done | bytes 524320 | tf_op jit(solution)/shard_map/ppermute | solution.py:20
  40.1 1.0 %multiply_reduce_fusion.3 = (f32[2,128]{1,0:T(2,128)S(1)}, bf16[2,128,128]{1,2,0:T(8,128)(2,1)}) fusion(bf16[2,128,128]{1,2,0:T(8,128)(2,1)S(1)} %copy.207, bf16[2,768,128]{2,1,0:T(8,128)(2,1)S(1)} %bitcast.483, f32[2,128,768]{1,2,0:T(8,128)S(1)} %get-tuple-element.109, f32[2,128]{1,0:T(2,128)S(1)} %log_add_fusion.3), kind=kOutput, calls=%fused_computation.142 | convolution fusion | flops 50888448 | bytes 1312768 | tf_op jit(solution)/shard_map/jym,jmo->jyo/dot_general | solution.py:82
  46.3 1.0 %multiply_reduce_fusion = (f32[2,128]{1,0:T(2,128)S(1)}, bf16[2,128,128]{1,2,0:T(8,128)(2,1)}) fusion(bf16[2,128,128]{1,2,0:T(8,128)(2,1)S(1)} %copy.210, bf16[2,768,128]{2,1,0:T(8,128)(2,1)S(1)} %bitcast.489, f32[2,128,768]{1,2,0:T(8,128)S(1)} %get-tuple-element.103, f32[2,128]{1,0:T(2,128)S(1)} %log_add_fusion), kind=kOutput, calls=%fused_computation.139 | convolution fusion | flops 50888448 | bytes 1312768 | tf_op jit(solution)/shard_map/jym,jmo->jyo/dot_general | solution.py:82
  48.4 1.3 %collective-permute-start.4 = (bf16[256,1024]{1,0:T(8,128)(2,1)S(1)}, bf16[256,1024]{1,0:T(8,128)(2,1)S(1)}, u32[]{:S(2)}, u32[]{:S(2)}) collective-permute-start(bf16[256,1024]{1,0:T(8,128)(2,1)S(1)} %constant_dynamic-update-slice_fusion.50), channel_id=1, source_target_pairs={{8,0},{12,4},{16,8},{20,12},{24,16},{28,20},{9,1},{13,5},{17,9},{2... | collective-permute-start | bytes 1572872 | tf_op jit(solution)/shard_map/ppermute | solution.py:20
  51.6 11.0 %collective-permute-done.4 = bf16[256,1024]{1,0:T(8,128)(2,1)S(1)} collective-permute-done((bf16[256,1024]{1,0:T(8,128)(2,1)S(1)}, bf16[256,1024]{1,0:T(8,128)(2,1)S(1)}, u32[]{:S(2)}, u32[]{:S(2)}) %collective-permute-start.4) | collective-permute-done | bytes 524320 | tf_op jit(solution)/shard_map/ppermute | solution.py:20
  62.9 1.3 %collective-permute-start.5 = (bf16[256,1024]{1,0:T(8,128)(2,1)S(1)}, bf16[256,1024]{1,0:T(8,128)(2,1)S(1)}, u32[]{:S(2)}, u32[]{:S(2)}) collective-permute-start(bf16[256,1024]{1,0:T(8,128)(2,1)S(1)} %fusion.22), channel_id=1, source_target_pairs={{8,0},{12,4},{16,8},{20,12},{24,16},{28,20},{9,1},{13,5},{17,9},{2... | collective-permute-start | bytes 1572872 | tf_op jit(solution)/shard_map/ppermute | solution.py:20
  65.0 0.9 %copy.140 = bf16[2,128,512]{2,1,0:T(8,128)(2,1)} copy(bf16[2,128,512]{1,2,0:T(8,128)(2,1)S(1)} %pad_maximum_fusion.8) | data formatting | bytes 524288 | tf_op jit(solution)/shard_map/concatenate | solution.py:226
  65.8 0.9 %copy.123 = bf16[2,128,512]{2,1,0:T(8,128)(2,1)} copy(bf16[2,128,512]{1,2,0:T(8,128)(2,1)S(1)} %pad_maximum_fusion.7) | data formatting | bytes 524288 | tf_op jit(solution)/shard_map/concatenate | solution.py:225
  66.7 9.6 %collective-permute-done.5 = bf16[256,1024]{1,0:T(8,128)(2,1)S(1)} collective-permute-done((bf16[256,1024]{1,0:T(8,128)(2,1)S(1)}, bf16[256,1024]{1,0:T(8,128)(2,1)S(1)}, u32[]{:S(2)}, u32[]{:S(2)}) %collective-permute-start.5) | collective-permute-done | bytes 524320 | tf_op jit(solution)/shard_map/ppermute | solution.py:20
  76.4 1.0 %fusion.30 = (bf16[256,512]{1,0:T(8,128)(2,1)}, bf16[256,512]{1,0:T(8,128)(2,1)}) fusion(f32[256,1024]{1,0:T(8,128)S(1)} %fusion.23, bf16[2,128,512]{2,1,0:T(8,128)(2,1)S(1)} %slice.929, bf16[2,128,512]{2,1,0:T(8,128)(2,1)S(1)} %slice.930), kind=kLoop, calls=%fused_computation.70 | loop fusion | flops 786432 | bytes 2097152 | tf_op jit(solution)/shard_map/convert_element_type | solution.py:282
  (120 shorter events, 12.9 us)
Async XLA Ops:
  0.6 10.3 %copy-start = (bf16[256,512]{1,0:T(8,128)(2,1)S(1)}, bf16[256,512]{1,0:T(8,128)(2,1)}, u32[]{:S(2)}) copy-start(bf16[256,512]{1,0:T(8,128)(2,1)} %param.8) | copy-start | bytes 786436
  2.6 16.1 %collective-permute-start = (bf16[256,1024]{1,0:T(8,128)(2,1)S(1)}, bf16[256,1024]{1,0:T(8,128)(2,1)S(1)}, u32[]{:S(2)}, u32[]{:S(2)}) collective-permute-start(bf16[256,1024]{1,0:T(8,128)(2,1)S(1)} %constant_dynamic-update-slice_fusion), channel_id=1, source_target_pairs={{0,8},{4,12},{8,16},{12,20},{16,24},{20,28},{1,9},{5,13},{9,17},{1... | collective-permute-start | bytes 1572872 | tf_op jit(solution)/shard_map/ppermute | solution.py:20
  10.0 14.4 %copy-start.1 = (bf16[256,512]{1,0:T(8,128)(2,1)S(1)}, bf16[256,512]{1,0:T(8,128)(2,1)}, u32[]{:S(2)}) copy-start(bf16[256,512]{1,0:T(8,128)(2,1)} %param.7) | copy-start | bytes 786436
  19.6 13.1 %collective-permute-start.1 = (bf16[256,1024]{1,0:T(8,128)(2,1)}, bf16[256,1024]{1,0:T(8,128)(2,1)}, u32[]{:S(2)}, u32[]{:S(2)}) collective-permute-start(bf16[256,1024]{1,0:T(8,128)(2,1)} %broadcast_select_fusion), channel_id=1, source_target_pairs={{0,4},{4,0},{8,12},{12,8},{16,20},{20,16},{24,28},{28,24},{1,5},{5... | collective-permute-start | bytes 1572872 | tf_op jit(solution)/shard_map/ppermute | solution.py:146
  21.3 12.5 %copy-start.2 = (bf16[256,512]{1,0:T(8,128)(2,1)S(1)}, bf16[256,512]{1,0:T(8,128)(2,1)}, u32[]{:S(2)}) copy-start(bf16[256,512]{1,0:T(8,128)(2,1)} %param.6) | copy-start | bytes 786436
  24.5 14.4 %collective-permute-start.2 = (bf16[256,1024]{1,0:T(8,128)(2,1)S(1)}, bf16[256,1024]{1,0:T(8,128)(2,1)S(1)}, u32[]{:S(2)}, u32[]{:S(2)}) collective-permute-start(bf16[256,1024]{1,0:T(8,128)(2,1)S(1)} %collective-permute-done), channel_id=1, source_target_pairs={{0,8},{4,12},{8,16},{12,20},{16,24},{20,28},{1,9},{5,13},{9,17},{1... | collective-permute-start | bytes 1572872 | tf_op jit(solution)/shard_map/ppermute | solution.py:20
  33.8 5.1 %copy-start.3 = (bf16[256,512]{1,0:T(8,128)(2,1)S(1)}, bf16[256,512]{1,0:T(8,128)(2,1)}, u32[]{:S(2)}) copy-start(bf16[256,512]{1,0:T(8,128)(2,1)} %param.5) | copy-start | bytes 786436
  48.4 14.2 %collective-permute-start.4 = (bf16[256,1024]{1,0:T(8,128)(2,1)S(1)}, bf16[256,1024]{1,0:T(8,128)(2,1)S(1)}, u32[]{:S(2)}, u32[]{:S(2)}) collective-permute-start(bf16[256,1024]{1,0:T(8,128)(2,1)S(1)} %constant_dynamic-update-slice_fusion.50), channel_id=1, source_target_pairs={{8,0},{12,4},{16,8},{20,12},{24,16},{28,20},{9,1},{13,5},{17,9},{2... | collective-permute-start | bytes 1572872 | tf_op jit(solution)/shard_map/ppermute | solution.py:20
  50.4 12.2 %collective-permute-start.3 = (bf16[256,1024]{1,0:T(8,128)(2,1)S(1)}, bf16[256,1024]{1,0:T(8,128)(2,1)S(1)}, u32[]{:S(2)}, u32[]{:S(2)}) collective-permute-start(bf16[256,1024]{1,0:T(8,128)(2,1)S(1)} %fusion.25), channel_id=1, source_target_pairs={{0,4},{4,0},{8,12},{12,8},{16,20},{20,16},{24,28},{28,24},{1,5},{5... | collective-permute-start | bytes 1572872 | tf_op jit(solution)/shard_map/ppermute | solution.py:246
  62.9 13.4 %collective-permute-start.5 = (bf16[256,1024]{1,0:T(8,128)(2,1)S(1)}, bf16[256,1024]{1,0:T(8,128)(2,1)S(1)}, u32[]{:S(2)}, u32[]{:S(2)}) collective-permute-start(bf16[256,1024]{1,0:T(8,128)(2,1)S(1)} %fusion.22), channel_id=1, source_target_pairs={{8,0},{12,4},{16,8},{20,12},{24,16},{28,20},{9,1},{13,5},{17,9},{2... | collective-permute-start | bytes 1572872 | tf_op jit(solution)/shard_map/ppermute | solution.py:20
  64.5 1.3 %copy-start.4 = (bf16[2,128,128]{1,2,0:T(8,128)(2,1)S(1)}, bf16[2,128,128]{1,2,0:T(8,128)(2,1)}, u32[]{:S(2)}) copy-start(bf16[2,128,128]{1,2,0:T(8,128)(2,1)} %get-tuple-element.117) | copy-start | bytes 196612
  64.5 1.3 %copy-start.5 = (bf16[2,128,128]{1,2,0:T(8,128)(2,1)S(1)}, bf16[2,128,128]{1,2,0:T(8,128)(2,1)}, u32[]{:S(2)}) copy-start(bf16[2,128,128]{1,2,0:T(8,128)(2,1)} %get-tuple-element.111) | copy-start | bytes 196612

commit v2 on v0

--- a/solution.py
+++ b/solution.py
@@ -12,6 +12,7 @@
 
 
 NEG = -1e30
+CHUNKS = 2
 
 
 def passed_along(value, axis, steps):
@@ -116,7 +117,7 @@
     )
 
 
-def body(queries, key_tokens, value_tokens, grad_out):
+def legacy_body(queries, key_tokens, value_tokens, grad_out):
     row_width = queries.shape[1]
     tok_count = queries.shape[0]
     blocks_dev = tok_count // BLK
@@ -237,6 +238,181 @@
     )
 
 
+def swap_pairs(count):
+    return [(source, source ^ 1) for source in range(count) if source ^ 1 < count]
+
+
+def relay_ok(count, blocks_dev, rim, far_shifts):
+    return count % 2 == 0 and blocks_dev == 2 and rim == 2 and (not far_shifts or far_shifts[0] == 4)
+
+
+def plan(tok_count, devices):
+    blocks_dev = tok_count // BLK
+    rim = (WINDOW + blocks_dev - 1) // blocks_dev
+    near_list, far_list = offset_lists(devices * blocks_dev)
+    far_shifts = [stride // blocks_dev for stride in far_list]
+    return blocks_dev, rim, near_list, far_list, far_shifts
+
+
+def forward_round_two(both, back2, odd, devices, far_shifts):
+    back1 = lax.ppermute(jnp.where(odd, back2, both), "seq", swap_pairs(devices))
+    far_both = []
+    for level_index, shift in enumerate(far_shifts):
+        if level_index == 0:
+            far_both.append(passed_along(back2, "seq", 2))
+        else:
+            far_both.append(passed_along(both, "seq", shift))
+    return back1, far_both
+
+
+def chunk_compute(queries, grad_out, both, back2, back1, far_both, devices):
+    row_width = queries.shape[1]
+    tok_count = queries.shape[0]
+    blocks_dev, rim, near_list, far_list, far_shifts = plan(tok_count, devices)
+    offsets = near_list + far_list
+    near_count = len(near_list)
+    logit_scale = 1.0 / math.sqrt(HD)
+    span_blocks = (rim + 1) * blocks_dev
+    lead = rim * blocks_dev
+    position = lax.axis_index("seq")
+    span_both = jnp.concatenate([back2, back1, both], axis=0)
+    span_keys = to_blocks(span_both[:, :row_width], span_blocks)
+    span_values = to_blocks(span_both[:, row_width:], span_blocks)
+    far_keys = [to_blocks(item[:, :row_width], blocks_dev) for item in far_both]
+    far_values = [to_blocks(item[:, row_width:], blocks_dev) for item in far_both]
+    allowed = allowed_mask(position * blocks_dev, blocks_dev, offsets)
+    query_blocks = to_blocks(queries, blocks_dev)
+    grad_blocks = to_blocks(grad_out, blocks_dev)
+    attended_heads = []
+    grad_query_heads = []
+    near_key_heads = []
+    near_value_heads = []
+    far_key_parts = [[] for stride in far_list]
+    far_value_parts = [[] for stride in far_list]
+    for head_index in range(row_width // HD):
+        col_start = head_index * HD
+        key_slabs = jnp.stack(
+            [
+                head_cols(span_keys[lead - offset : lead + blocks_dev - offset], col_start)
+                for offset in near_list
+            ]
+            + [head_cols(item, col_start) for item in far_keys],
+            axis=1,
+        )
+        value_slabs = jnp.stack(
+            [
+                head_cols(span_values[lead - offset : lead + blocks_dev - offset], col_start)
+                for offset in near_list
+            ]
+            + [head_cols(item, col_start) for item in far_values],
+            axis=1,
+        )
+        attended_per_head, query_gradient_heads, key_gradient, value_gradient, _, _ = head_pass(
+            head_cols(query_blocks, col_start),
+            head_cols(grad_blocks, col_start),
+            key_slabs,
+            value_slabs,
+            allowed,
+            logit_scale,
+        )
+        key_gradient = key_gradient.reshape(blocks_dev, -1, BLK, HD)
+        value_gradient = value_gradient.reshape(blocks_dev, -1, BLK, HD)
+        near_key_heads.append(place_slabs(key_gradient, near_list, lead, span_blocks))
+        near_value_heads.append(place_slabs(value_gradient, near_list, lead, span_blocks))
+        for level_index in range(len(far_list)):
+            far_key_parts[level_index].append(key_gradient[:, near_count + level_index])
+            far_value_parts[level_index].append(value_gradient[:, near_count + level_index])
+        attended_heads.append(attended_per_head)
+        grad_query_heads.append(query_gradient_heads)
+    attended = jnp.concatenate(attended_heads, axis=-1).reshape(tok_count, row_width)
+    grad_queries = jnp.concatenate(grad_query_heads, axis=-1).reshape(tok_count, row_width)
+    near_keys = jnp.concatenate(near_key_heads, axis=-1).reshape((rim + 1) * tok_count, row_width)
+    near_values = jnp.concatenate(near_value_heads, axis=-1).reshape(
+        (rim + 1) * tok_count, row_width
+    )
+    near_both = jnp.concatenate([near_keys, near_values], axis=1)
+    own = near_both[2 * tok_count :].astype(jnp.bfloat16).astype(jnp.float32)
+    part_two = near_both[:tok_count]
+    part_one = near_both[tok_count : 2 * tok_count].astype(jnp.bfloat16)
+    far_sends = []
+    for level_index in range(len(far_list)):
+        part_keys = jnp.concatenate(far_key_parts[level_index], axis=-1).reshape(
+            tok_count, row_width
+        )
+        part_values = jnp.concatenate(far_value_parts[level_index], axis=-1).reshape(
+            tok_count, row_width
+        )
+        far_sends.append(jnp.concatenate([part_keys, part_values], axis=1).astype(jnp.bfloat16))
+    return attended, grad_queries, own, part_two, part_one, far_sends
+
+
+def backward_round_one(own, part_one, far_sends, devices, far_shifts):
+    swapped = lax.ppermute(part_one, "seq", swap_pairs(devices)).astype(jnp.float32)
+    far_first = None
+    for level_index, shift in enumerate(far_shifts):
+        if level_index == 0:
+            far_first = passed_along(far_sends[0], "seq", -2).astype(jnp.float32)
+        else:
+            own = own + passed_along(far_sends[level_index], "seq", -shift).astype(jnp.float32)
+    return own, swapped, far_first
+
+
+def backward_round_two(own, part_two, swapped, far_first, odd):
+    zero = jnp.zeros_like(swapped)
+    relayed = part_two + jnp.where(odd, swapped, zero)
+    if far_first is not None:
+        relayed = relayed + far_first
+    arrived = passed_along(relayed.astype(jnp.bfloat16), "seq", -2).astype(jnp.float32)
+    return own + arrived + jnp.where(odd, zero, swapped)
+
+
+def body(queries, key_tokens, value_tokens, grad_out):
+    row_width = queries.shape[1]
+    tok_count = queries.shape[0]
+    devices = lax.axis_size("seq")
+    blocks_dev, rim, near_list, far_list, far_shifts = plan(tok_count, devices)
+    if not relay_ok(devices, blocks_dev, rim, far_shifts):
+        return legacy_body(queries, key_tokens, value_tokens, grad_out)
+    odd = (lax.axis_index("seq") % 2) == 1
+    width = row_width // CHUNKS
+    cols = [slice(chunk * width, (chunk + 1) * width) for chunk in range(CHUNKS)]
+    boths = [jnp.concatenate([key_tokens[:, c], value_tokens[:, c]], axis=1) for c in cols]
+    back2s = []
+    for chunk in range(CHUNKS):
+        if chunk > 0:
+            boths[chunk], back2s[chunk - 1] = lax.optimization_barrier(
+                (boths[chunk], back2s[chunk - 1])
+            )
+        back2s.append(passed_along(boths[chunk], "seq", 2))
+    arrivals = [
+        forward_round_two(boths[chunk], back2s[chunk], odd, devices, far_shifts)
+        for chunk in range(CHUNKS)
+    ]
+    outs = []
+    pending = None
+    for chunk in range(CHUNKS + 1):
+        if chunk < CHUNKS:
+            chunk_inputs = (queries[:, cols[chunk]], grad_out[:, cols[chunk]]) + arrivals[chunk]
+            if pending is not None:
+                chunk_inputs, pending = lax.optimization_barrier((chunk_inputs, pending))
+        if pending is not None:
+            attended, grad_queries, own, part_two, swapped, far_first = pending
+            total = backward_round_two(own, part_two, swapped, far_first, odd)
+            outs.append((attended, grad_queries, total[:, :width], total[:, width:]))
+        if chunk == CHUNKS:
+            break
+        chunk_queries, chunk_grads, back1, far_both = chunk_inputs
+        attended, grad_queries, own, part_two, part_one, far_sends = chunk_compute(
+            chunk_queries, chunk_grads, boths[chunk], back2s[chunk], back1, far_both, devices
+        )
+        own, swapped, far_first = backward_round_one(own, part_one, far_sends, devices, far_shifts)
+        pending = (attended, grad_queries, own, part_two, swapped, far_first)
+    return tuple(
+        jnp.concatenate([item[index] for item in outs], axis=1).astype(jnp.bfloat16)
+        for index in range(4)
+    )
+
+
 def solution(mesh):
     placed = (
         P(("rep", "seq"), None),

time: 99.2 us -> 91.8 us (0.925)
  the two profiles are of different devices: /device:TPU:14 before, /device:TPU:0 now
where the time goes in v2:
time: 91.8 us; the launch traced here: 91.1 us
  starting transfers between devices  27.9 us (30%)
  local copies, waits for them, and re-layouts  22 us (24%)
  waiting for transfers between devices  18.7 us (20%)
  other arithmetic  12.8 us (14%)
  matrix products  7.69 us (8%)
  between operations  1.99 us (2%)
    ppermute x8, starting transfers between devices, passed_along(): lax.ppermute(value, axis, [(source, source + steps) for source in range(f...  22.8 us
    ppermute x8, waiting for transfers between devices, passed_along(): lax.ppermute(value, axis, [(source, source + steps) for source in range(f...  13.7 us
    unnamed x126, local copies, waits for them, and re-layouts  13.3 us
    ppermute x2, waiting for transfers between devices, forward_round_two(): lax.ppermute(jnp.where(odd, back2, both), 'seq', swap_pairs(devices))  4.95 us
    concatenate x4, other arithmetic, body(): jnp.concatenate([item[index] for item in outs], axis=1).astype(jnp.bfloat16)  3.85 us
    ppermute x2, starting transfers between devices, backward_round_one(): lax.ppermute(part_one, 'seq', swap_pairs(devices)).astype(jnp.float32)  3.03 us
    ppermute x2, starting transfers between devices, forward_round_two(): lax.ppermute(jnp.where(odd, back2, both), 'seq', swap_pairs(devices))  2.08 us
    dot_general x4, matrix products, head_pass(): jnp.einsum('jym,jmo->jyo', attention_weight, value_row_block, preferred_e...  2 us
  transfers between devices with their start and end apart: 12, of which 6 were waited for; matrix products, arithmetic and copies ran while one was open for 23% of the time, Pallas kernels for 0%

profile of v2, /device:TPU:0, one launch (start us, length us, event | category | flops | bytes accessed | tf_op | source)
XLA Modules:
  0.0 91.1 jit_solution(16154607227555976542)
XLA Ops:
  0.7 1.2 %fusion.71 = (bf16[256,256]{1,0:T(8,128)(2,1)S(1)}, bf16[256,256]{1,0:T(8,128)(2,1)S(1)}, bf16[256,256]{1,0:T(8,128)(2,1)S(1)}, bf16[256,256]{1,0:T(8,128)(2,1)S(1)}) fusion(bf16[256,512]{1,0:T(8,128)(2,1)} %param.7, bf16[256,512]{1,0:T(8,128)(2,1)} %param.8), kind=kLoop, calls=%fused_computation.300 | loop fusion | bytes 1048576 | tf_op jit(solution)/shard_map/slice | solution.py:379
  1.9 4.9 %collective-permute-start = (bf16[256,512]{1,0:T(8,128)(2,1)S(1)}, bf16[256,512]{1,0:T(8,128)(2,1)S(1)}, u32[]{:S(2)}, u32[]{:S(2)}) collective-permute-start(bf16[256,512]{1,0:T(8,128)(2,1)S(1)} %pad_maximum_fusion.7), channel_id=1, source_target_pairs={{0,8},{4,12},{8,16},{12,20},{16,24},{20,28},{1,9},{5,13},{9,17},{1... | collective-permute-start | bytes 786440 | tf_op jit(solution)/shard_map/ppermute | solution.py:21
  9.6 2.7 %collective-permute-done = bf16[256,512]{1,0:T(8,128)(2,1)S(1)} collective-permute-done((bf16[256,512]{1,0:T(8,128)(2,1)S(1)}, bf16[256,512]{1,0:T(8,128)(2,1)S(1)}, u32[]{:S(2)}, u32[]{:S(2)}) %collective-permute-start) | collective-permute-done | bytes 262176 | tf_op jit(solution)/shard_map/ppermute | solution.py:21
  12.4 4.4 %collective-permute-start.1 = (bf16[256,512]{1,0:T(8,128)(2,1)S(1)}, bf16[256,512]{1,0:T(8,128)(2,1)S(1)}, u32[]{:S(2)}, u32[]{:S(2)}) collective-permute-start(bf16[256,512]{1,0:T(8,128)(2,1)S(1)} %pad_maximum_fusion.6), channel_id=1, source_target_pairs={{0,8},{4,12},{8,16},{12,20},{16,24},{20,28},{1,9},{5,13},{9,17},{1... | collective-permute-start | bytes 786440 | tf_op jit(solution)/shard_map/ppermute | solution.py:21
  16.8 3.5 %collective-permute-start.5 = (bf16[256,512]{1,0:T(8,128)(2,1)S(1)}, bf16[256,512]{1,0:T(8,128)(2,1)S(1)}, u32[]{:S(2)}, u32[]{:S(2)}) collective-permute-start(bf16[256,512]{1,0:T(8,128)(2,1)S(1)} %collective-permute-done), channel_id=1, source_target_pairs={{0,8},{4,12},{8,16},{12,20},{16,24},{20,28},{1,9},{5,13},{9,17},{1... | collective-permute-start | bytes 786440 | tf_op jit(solution)/shard_map/ppermute | solution.py:21
  20.4 1.6 %collective-permute-start.4 = (bf16[256,512]{1,0:T(8,128)(2,1)S(1)}, bf16[256,512]{1,0:T(8,128)(2,1)S(1)}, u32[]{:S(2)}, u32[]{:S(2)}) collective-permute-start(bf16[256,512]{1,0:T(8,128)(2,1)S(1)} %get-tuple-element.105), channel_id=1, source_target_pairs={{0,4},{4,0},{8,12},{12,8},{16,20},{20,16},{24,28},{28,24},{1,5},{5... | collective-permute-start | bytes 786440 | tf_op jit(solution)/shard_map/ppermute | solution.py:258
  23.9 3.1 %collective-permute-done.4 = bf16[256,512]{1,0:T(8,128)(2,1)S(1)} collective-permute-done((bf16[256,512]{1,0:T(8,128)(2,1)S(1)}, bf16[256,512]{1,0:T(8,128)(2,1)S(1)}, u32[]{:S(2)}, u32[]{:S(2)}) %collective-permute-start.4) | collective-permute-done | bytes 262176 | tf_op jit(solution)/shard_map/ppermute | solution.py:258
  34.3 1.3 %collective-permute-start.7 = (bf16[256,512]{1,0:T(8,128)(2,1)S(1)}, bf16[256,512]{1,0:T(8,128)(2,1)S(1)}, u32[]{:S(2)}, u32[]{:S(2)}) collective-permute-start(bf16[256,512]{1,0:T(8,128)(2,1)S(1)} %pad_maximum_fusion.8), channel_id=1, source_target_pairs={{8,0},{12,4},{16,8},{20,12},{24,16},{28,20},{9,1},{13,5},{17,9},{2... | collective-permute-start | bytes 786440 | tf_op jit(solution)/shard_map/ppermute | solution.py:21
  36.5 1.5 %collective-permute-start.6 = (bf16[256,512]{1,0:T(8,128)(2,1)S(1)}, bf16[256,512]{1,0:T(8,128)(2,1)S(1)}, u32[]{:S(2)}, u32[]{:S(2)}) collective-permute-start(bf16[256,512]{1,0:T(8,128)(2,1)S(1)} %get-tuple-element.48), channel_id=1, source_target_pairs={{0,4},{4,0},{8,12},{12,8},{16,20},{20,16},{24,28},{28,24},{1,5},{5... | collective-permute-start | bytes 786440 | tf_op jit(solution)/shard_map/ppermute | solution.py:350
  39.6 4.9 %collective-permute-start.3 = (bf16[256,512]{1,0:T(8,128)(2,1)S(1)}, bf16[256,512]{1,0:T(8,128)(2,1)S(1)}, u32[]{:S(2)}, u32[]{:S(2)}) collective-permute-start(bf16[256,512]{1,0:T(8,128)(2,1)S(1)} %collective-permute-done.1), channel_id=1, source_target_pairs={{0,8},{4,12},{8,16},{12,20},{16,24},{20,28},{1,9},{5,13},{9,17},{1... | collective-permute-start | bytes 786440 | tf_op jit(solution)/shard_map/ppermute | solution.py:21
  46.4 1.8 %collective-permute-done.2 = bf16[256,512]{1,0:T(8,128)(2,1)S(1)} collective-permute-done((bf16[256,512]{1,0:T(8,128)(2,1)S(1)}, bf16[256,512]{1,0:T(8,128)(2,1)S(1)}, u32[]{:S(2)}, u32[]{:S(2)}) %collective-permute-start.2) | collective-permute-done | bytes 262176 | tf_op jit(solution)/shard_map/ppermute | solution.py:258
  49.9 1.1 %fusion.58 = (bf16[256,256]{1,0:T(8,128)(2,1)S(1)}, bf16[256,256]{1,0:T(8,128)(2,1)S(1)}) fusion(bf16[512,512]{1,0:T(8,128)(2,1)} %get-tuple-element.90), kind=kLoop, calls=%fused_computation.287 | loop fusion | bytes 524288 | tf_op jit(solution)/shard_map/slice | solution.py:296
  54.7 1.0 %multiply_reduce_fusion.1 = (f32[2,128]{1,0:T(2,128)S(1)}, bf16[2,128,128]{1,2,0:T(8,128)(2,1)}) fusion(bf16[2,128,128]{1,2,0:T(8,128)(2,1)S(1)} %copy.246, bf16[2,768,128]{2,1,0:T(8,128)(2,1)S(1)} %bitcast.485, f32[2,128,768]{1,2,0:T(8,128)S(1)} %get-tuple-element.149, f32[2,128]{1,0:T(2,128)S(1)} %log_add_fusion.1), kind=kOutput, calls=%fused_computation.151 | convolution fusion | flops 50888448 | bytes 1312768 | tf_op jit(solution)/shard_map/jym,jmo->jyo/dot_general | solution.py:83
  62.8 0.9 copy-done.11
  65.0 0.9 add_convert_fusion.1
  65.9 1.3 %collective-permute-start.8 = (bf16[256,512]{1,0:T(8,128)(2,1)}, bf16[256,512]{1,0:T(8,128)(2,1)}, u32[]{:S(2)}, u32[]{:S(2)}) collective-permute-start(bf16[256,512]{1,0:T(8,128)(2,1)} %add_convert_fusion.1), channel_id=1, source_target_pairs={{8,0},{12,4},{16,8},{20,12},{24,16},{28,20},{9,1},{13,5},{17,9},{2... | collective-permute-start | bytes 786440 | tf_op jit(solution)/shard_map/ppermute | solution.py:21
  67.9 1.3 %collective-permute-start.10 = (bf16[256,512]{1,0:T(8,128)(2,1)}, bf16[256,512]{1,0:T(8,128)(2,1)}, u32[]{:S(2)}, u32[]{:S(2)}) collective-permute-start(bf16[256,512]{1,0:T(8,128)(2,1)} %pad_maximum_fusion.11), channel_id=1, source_target_pairs={{8,0},{12,4},{16,8},{20,12},{24,16},{28,20},{9,1},{13,5},{17,9},{2... | collective-permute-start | bytes 786440 | tf_op jit(solution)/shard_map/ppermute | solution.py:21
  70.4 1.5 %collective-permute-start.9 = (bf16[256,512]{1,0:T(8,128)(2,1)}, bf16[256,512]{1,0:T(8,128)(2,1)S(1)}, u32[]{:S(2)}, u32[]{:S(2)}) collective-permute-start(bf16[256,512]{1,0:T(8,128)(2,1)} %slice.858), channel_id=1, source_target_pairs={{0,4},{4,0},{8,12},{12,8},{16,20},{20,16},{24,28},{28,24},{1,5},{5... | collective-permute-start | bytes 786440 | tf_op jit(solution)/shard_map/ppermute | solution.py:350
  72.8 1.7 %pad_maximum_fusion.10 = bf16[256,512]{1,0:T(8,128)(2,1)} fusion(bf16[256,256]{1,0:T(8,128)(2,1)} %bitcast.566, bf16[256,256]{1,0:T(8,128)(2,1)} %bitcast.537), kind=kLoop, calls=%fused_computation.89 | loop fusion | flops 524288 | bytes 524288 | tf_op jit(solution)/shard_map/concatenate | solution.py:411
  75.2 5.0 %collective-permute-done.10 = bf16[256,512]{1,0:T(8,128)(2,1)} collective-permute-done((bf16[256,512]{1,0:T(8,128)(2,1)}, bf16[256,512]{1,0:T(8,128)(2,1)}, u32[]{:S(2)}, u32[]{:S(2)}) %collective-permute-start.10) | collective-permute-done | bytes 262176 | tf_op jit(solution)/shard_map/ppermute | solution.py:21
  80.2 1.1 %fusion.24 = bf16[256,512]{1,0:T(8,128)(2,1)S(1)} fusion(bf16[256,512]{1,0:T(8,128)(2,1)S(1)} %collective-permute-done.9, f32[768,256]{1,0:T(8,128)S(1)} %bitcast.478, f32[768,256]{1,0:T(8,128)S(1)} %bitcast.480, bf16[256,512]{1,0:T(8,128)(2,1)} %collective-permute-done.10, pred[]{:T(512)S(6)} %eq.5), kind=kLoop, calls=%fused_computation.68 | loop fusion | flops 917504 | bytes 2359297 | tf_op jit(solution)/shard_map/convert_element_type | solution.py:365
  81.3 1.3 %collective-permute-start.11 = (bf16[256,512]{1,0:T(8,128)(2,1)S(1)}, bf16[256,512]{1,0:T(8,128)(2,1)S(1)}, u32[]{:S(2)}, u32[]{:S(2)}) collective-permute-start(bf16[256,512]{1,0:T(8,128)(2,1)S(1)} %fusion.24), channel_id=1, source_target_pairs={{8,0},{12,4},{16,8},{20,12},{24,16},{28,20},{9,1},{13,5},{17,9},{2... | collective-permute-start | bytes 786440 | tf_op jit(solution)/shard_map/ppermute | solution.py:21
  82.6 1.1 %add_convert_fusion = bf16[256,512]{1,0:T(8,128)(2,1)S(1)} fusion(f32[256,512]{1,0:T(8,128)S(1)} %convert_element_type.168, f32[256,512]{1,0:T(8,128)S(1)} %copy-done, bf16[256,512]{1,0:T(8,128)(2,1)} %collective-permute-done.8, pred[]{:T(512)S(6)} %eq.5), kind=kLoop, calls=%fused_computation.73 | loop fusion | flops 655360 | bytes 1572865 | tf_op jit(solution)/shard_map/convert.7
  83.7 5.8 %collective-permute-done.11 = bf16[256,512]{1,0:T(8,128)(2,1)S(1)} collective-permute-done((bf16[256,512]{1,0:T(8,128)(2,1)S(1)}, bf16[256,512]{1,0:T(8,128)(2,1)S(1)}, u32[]{:S(2)}, u32[]{:S(2)}) %collective-permute-start.11) | collective-permute-done | bytes 262176 | tf_op jit(solution)/shard_map/ppermute | solution.py:21
  (249 shorter events, 34.3 us)
Async XLA Ops:
  0.6 6.3 %copy-start.43 = (s32[6]{0:T(128)S(1)}, s32[6]{0:T(128)}, u32[]{:S(2)}) copy-start(s32[6]{0:T(128)} %constant.118) | copy-start | bytes 76
  0.6 6.4 %copy-start.42 = (pred[6]{0:T(512)(128)(4,1)S(1)}, pred[6]{0:T(512)(128)(4,1)}, u32[]{:S(2)}) copy-start(pred[6]{0:T(512)(128)(4,1)} %constant.119) | copy-start | bytes 22
  0.7 6.5 %copy-start.37 = (bf16[256,512]{1,0:T(8,128)(2,1)S(1)}, bf16[256,512]{1,0:T(8,128)(2,1)}, u32[]{:S(2)}) copy-start(bf16[256,512]{1,0:T(8,128)(2,1)} %param.6) | copy-start | bytes 786436
  0.7 6.5 %copy-start.36 = (bf16[256,512]{1,0:T(8,128)(2,1)S(1)}, bf16[256,512]{1,0:T(8,128)(2,1)}, u32[]{:S(2)}) copy-start(bf16[256,512]{1,0:T(8,128)(2,1)} %param.9) | copy-start | bytes 786436
  1.9 10.5 %collective-permute-start = (bf16[256,512]{1,0:T(8,128)(2,1)S(1)}, bf16[256,512]{1,0:T(8,128)(2,1)S(1)}, u32[]{:S(2)}, u32[]{:S(2)}) collective-permute-start(bf16[256,512]{1,0:T(8,128)(2,1)S(1)} %pad_maximum_fusion.7), channel_id=1, source_target_pairs={{0,8},{4,12},{8,16},{12,20},{16,24},{20,28},{1,9},{5,13},{9,17},{1... | collective-permute-start | bytes 786440 | tf_op jit(solution)/shard_map/ppermute | solution.py:21
  9.6 20.4 %copy-start.39 = (pred[128,768]{0,1:T(8,128)(4,1)}, pred[128,768]{0,1:T(8,128)(4,1)S(1)}, u32[]{:S(2)}) copy-start(pred[128,768]{0,1:T(8,128)(4,1)S(1)} %bitcast_or_fusion) | copy-start | bytes 294916
  12.4 26.0 %collective-permute-start.1 = (bf16[256,512]{1,0:T(8,128)(2,1)S(1)}, bf16[256,512]{1,0:T(8,128)(2,1)S(1)}, u32[]{:S(2)}, u32[]{:S(2)}) collective-permute-start(bf16[256,512]{1,0:T(8,128)(2,1)S(1)} %pad_maximum_fusion.6), channel_id=1, source_target_pairs={{0,8},{4,12},{8,16},{12,20},{16,24},{20,28},{1,9},{5,13},{9,17},{1... | collective-permute-start | bytes 786440 | tf_op jit(solution)/shard_map/ppermute | solution.py:21
  16.8 10.4 %collective-permute-start.5 = (bf16[256,512]{1,0:T(8,128)(2,1)S(1)}, bf16[256,512]{1,0:T(8,128)(2,1)S(1)}, u32[]{:S(2)}, u32[]{:S(2)}) collective-permute-start(bf16[256,512]{1,0:T(8,128)(2,1)S(1)} %collective-permute-done), channel_id=1, source_target_pairs={{0,8},{4,12},{8,16},{12,20},{16,24},{20,28},{1,9},{5,13},{9,17},{1... | collective-permute-start | bytes 786440 | tf_op jit(solution)/shard_map/ppermute | solution.py:21
  20.4 6.7 %collective-permute-start.4 = (bf16[256,512]{1,0:T(8,128)(2,1)S(1)}, bf16[256,512]{1,0:T(8,128)(2,1)S(1)}, u32[]{:S(2)}, u32[]{:S(2)}) collective-permute-start(bf16[256,512]{1,0:T(8,128)(2,1)S(1)} %get-tuple-element.105), channel_id=1, source_target_pairs={{0,4},{4,0},{8,12},{12,8},{16,20},{20,16},{24,28},{28,24},{1,5},{5... | collective-permute-start | bytes 786440 | tf_op jit(solution)/shard_map/ppermute | solution.py:258
  34.3 11.1 %collective-permute-start.7 = (bf16[256,512]{1,0:T(8,128)(2,1)S(1)}, bf16[256,512]{1,0:T(8,128)(2,1)S(1)}, u32[]{:S(2)}, u32[]{:S(2)}) collective-permute-start(bf16[256,512]{1,0:T(8,128)(2,1)S(1)} %pad_maximum_fusion.8), channel_id=1, source_target_pairs={{8,0},{12,4},{16,8},{20,12},{24,16},{28,20},{9,1},{13,5},{17,9},{2... | collective-permute-start | bytes 786440 | tf_op jit(solution)/shard_map/ppermute | solution.py:21
  36.5 9.8 %collective-permute-start.6 = (bf16[256,512]{1,0:T(8,128)(2,1)S(1)}, bf16[256,512]{1,0:T(8,128)(2,1)S(1)}, u32[]{:S(2)}, u32[]{:S(2)}) collective-permute-start(bf16[256,512]{1,0:T(8,128)(2,1)S(1)} %get-tuple-element.48), channel_id=1, source_target_pairs={{0,4},{4,0},{8,12},{12,8},{16,20},{20,16},{24,28},{28,24},{1,5},{5... | collective-permute-start | bytes 786440 | tf_op jit(solution)/shard_map/ppermute | solution.py:350
  39.1 9.1 %collective-permute-start.2 = (bf16[256,512]{1,0:T(8,128)(2,1)S(1)}, bf16[256,512]{1,0:T(8,128)(2,1)S(1)}, u32[]{:S(2)}, u32[]{:S(2)}) collective-permute-start(bf16[256,512]{1,0:T(8,128)(2,1)S(1)} %get-tuple-element.93), channel_id=1, source_target_pairs={{0,4},{4,0},{8,12},{12,8},{16,20},{20,16},{24,28},{28,24},{1,5},{5... | collective-permute-start | bytes 786440 | tf_op jit(solution)/shard_map/ppermute | solution.py:258
  39.6 8.7 %collective-permute-start.3 = (bf16[256,512]{1,0:T(8,128)(2,1)S(1)}, bf16[256,512]{1,0:T(8,128)(2,1)S(1)}, u32[]{:S(2)}, u32[]{:S(2)}) collective-permute-start(bf16[256,512]{1,0:T(8,128)(2,1)S(1)} %collective-permute-done.1), channel_id=1, source_target_pairs={{0,8},{4,12},{8,16},{12,20},{16,24},{20,28},{1,9},{5,13},{9,17},{1... | collective-permute-start | bytes 786440 | tf_op jit(solution)/shard_map/ppermute | solution.py:21
  45.4 5.7 %copy-start.12 = (bf16[256,256]{1,0:T(8,128)(2,1)}, bf16[256,256]{1,0:T(8,128)(2,1)S(1)}, u32[]{:S(2)}) copy-start(bf16[256,256]{1,0:T(8,128)(2,1)S(1)} %get-tuple-element.84) | copy-start | bytes 393220
  65.0 4.2 %copy-start.25 = (f32[2,128,128]{2,1,0:T(8,128)S(1)}, f32[2,128,128]{2,1,0:T(8,128)}, u32[]{:S(2)}) copy-start(f32[2,128,128]{2,1,0:T(8,128)} %get-tuple-element.28) | copy-start | bytes 393220
  65.0 4.2 %copy-start.26 = (f32[2,128,128]{2,1,0:T(8,128)S(1)}, f32[2,128,128]{2,1,0:T(8,128)}, u32[]{:S(2)}) copy-start(f32[2,128,128]{2,1,0:T(8,128)} %get-tuple-element.29) | copy-start | bytes 393220
  65.0 4.2 %copy-start.27 = (f32[2,128,128]{2,1,0:T(8,128)S(1)}, f32[2,128,128]{2,1,0:T(8,128)}, u32[]{:S(2)}) copy-start(f32[2,128,128]{2,1,0:T(8,128)} %get-tuple-element.30) | copy-start | bytes 393220
  65.0 4.2 %copy-start.28 = (f32[2,128,128]{2,1,0:T(8,128)S(1)}, f32[2,128,128]{2,1,0:T(8,128)}, u32[]{:S(2)}) copy-start(f32[2,128,128]{2,1,0:T(8,128)} %get-tuple-element.31) | copy-start | bytes 393220
  65.0 4.2 %copy-start.29 = (f32[2,128,128]{2,1,0:T(8,128)S(1)}, f32[2,128,128]{2,1,0:T(8,128)}, u32[]{:S(2)}) copy-start(f32[2,128,128]{2,1,0:T(8,128)} %get-tuple-element.32) | copy-start | bytes 393220
  65.9 16.7 %collective-permute-start.8 = (bf16[256,512]{1,0:T(8,128)(2,1)}, bf16[256,512]{1,0:T(8,128)(2,1)}, u32[]{:S(2)}, u32[]{:S(2)}) collective-permute-start(bf16[256,512]{1,0:T(8,128)(2,1)} %add_convert_fusion.1), channel_id=1, source_target_pairs={{8,0},{12,4},{16,8},{20,12},{24,16},{28,20},{9,1},{13,5},{17,9},{2... | collective-permute-start | bytes 786440 | tf_op jit(solution)/shard_map/ppermute | solution.py:21
  67.9 12.3 %collective-permute-start.10 = (bf16[256,512]{1,0:T(8,128)(2,1)}, bf16[256,512]{1,0:T(8,128)(2,1)}, u32[]{:S(2)}, u32[]{:S(2)}) collective-permute-start(bf16[256,512]{1,0:T(8,128)(2,1)} %pad_maximum_fusion.11), channel_id=1, source_target_pairs={{8,0},{12,4},{16,8},{20,12},{24,16},{28,20},{9,1},{13,5},{17,9},{2... | collective-permute-start | bytes 786440 | tf_op jit(solution)/shard_map/ppermute | solution.py:21
  70.4 9.8 %collective-permute-start.9 = (bf16[256,512]{1,0:T(8,128)(2,1)}, bf16[256,512]{1,0:T(8,128)(2,1)S(1)}, u32[]{:S(2)}, u32[]{:S(2)}) collective-permute-start(bf16[256,512]{1,0:T(8,128)(2,1)} %slice.858), channel_id=1, source_target_pairs={{0,4},{4,0},{8,12},{12,8},{16,20},{20,16},{24,28},{28,24},{1,5},{5... | collective-permute-start | bytes 786440 | tf_op jit(solution)/shard_map/ppermute | solution.py:350
  75.2 7.4 %copy-start = (f32[256,512]{1,0:T(8,128)S(1)}, f32[256,512]{1,0:T(8,128)}, u32[]{:S(2)}) copy-start(f32[256,512]{1,0:T(8,128)} %get-tuple-element.24) | copy-start | bytes 1572868
  81.3 8.3 %collective-permute-start.11 = (bf16[256,512]{1,0:T(8,128)(2,1)S(1)}, bf16[256,512]{1,0:T(8,128)(2,1)S(1)}, u32[]{:S(2)}, u32[]{:S(2)}) collective-permute-start(bf16[256,512]{1,0:T(8,128)(2,1)S(1)} %fusion.24), channel_id=1, source_target_pairs={{8,0},{12,4},{16,8},{20,12},{24,16},{28,20},{9,1},{13,5},{17,9},{2... | collective-permute-start | bytes 786440 | tf_op jit(solution)/shard_map/ppermute | solution.py:21
  (32 other events, 40.3 us)

commit v3 on v0

--- a/solution.py
+++ b/solution.py
@@ -12,6 +12,7 @@
 
 
 NEG = -1e30
+CHUNKS = 2
 
 
 def passed_along(value, axis, steps):
@@ -116,7 +117,7 @@
     )
 
 
-def body(queries, key_tokens, value_tokens, grad_out):
+def legacy_body(queries, key_tokens, value_tokens, grad_out):
     row_width = queries.shape[1]
     tok_count = queries.shape[0]
     blocks_dev = tok_count // BLK
@@ -237,6 +238,223 @@
     )
 
 
+def swap_pairs(count):
+    return [(source, source ^ 1) for source in range(count) if source ^ 1 < count]
+
+
+def relay_ok(count, blocks_dev, rim, far_shifts):
+    return count % 2 == 0 and blocks_dev == 2 and rim == 2 and (not far_shifts or far_shifts[0] == 4)
+
+
+def plan(tok_count, devices):
+    blocks_dev = tok_count // BLK
+    rim = (WINDOW + blocks_dev - 1) // blocks_dev
+    near_list, far_list = offset_lists(devices * blocks_dev)
+    far_shifts = [stride // blocks_dev for stride in far_list]
+    return blocks_dev, rim, near_list, far_list, far_shifts
+
+
+def row_pass(query_per_head, output_gradient_heads, key_slabs, value_slabs, allowed, logit_scale):
+    block_count = key_slabs.shape[0]
+    key_row_block = key_slabs.reshape(block_count, -1, HD)
+    value_row_block = value_slabs.reshape(block_count, -1, HD)
+    score_matrix = (
+        jnp.einsum(
+            "nmv,njv->nmj", query_per_head, key_row_block, preferred_element_type=jnp.float32
+        )
+        * logit_scale
+    )
+    score_matrix = jnp.where(allowed, score_matrix, NEG)
+    row_max = jnp.max(score_matrix, axis=-1, keepdims=True)
+    log_total = row_max + jnp.log(jnp.sum(jnp.exp(score_matrix - row_max), axis=-1, keepdims=True))
+    probabilities = jnp.exp(score_matrix - log_total)
+    attention_weight = probabilities.astype(jnp.bfloat16)
+    attended_per_head = jnp.einsum(
+        "jym,jmo->jyo", attention_weight, value_row_block, preferred_element_type=jnp.float32
+    ).astype(jnp.bfloat16)
+    out_dot = jnp.sum(
+        output_gradient_heads.astype(jnp.float32) * attended_per_head.astype(jnp.float32),
+        axis=-1,
+        keepdims=True,
+    )
+    probability_gradient = jnp.einsum(
+        "nmv,njv->nmj", output_gradient_heads, value_row_block, preferred_element_type=jnp.float32
+    )
+    score_gradient = (probabilities * (probability_gradient - out_dot)).astype(jnp.bfloat16)
+    query_gradient_heads = (
+        jnp.einsum(
+            "jym,jmo->jyo", score_gradient, key_row_block, preferred_element_type=jnp.float32
+        )
+        * logit_scale
+    ).astype(jnp.bfloat16)
+    return attended_per_head, query_gradient_heads, log_total[..., 0], out_dot[..., 0]
+
+
+def key_pass(key_per_head, value_per_head, query_slabs, grad_slabs, total_slabs, dot_slabs, allowed, logit_scale):
+    block_count = query_slabs.shape[0]
+    query_rows = query_slabs.reshape(block_count, -1, HD)
+    grad_rows = grad_slabs.reshape(block_count, -1, HD)
+    score_matrix = (
+        jnp.einsum("nmv,njv->nmj", query_rows, key_per_head, preferred_element_type=jnp.float32)
+        * logit_scale
+    )
+    total_rows = total_slabs.reshape(block_count, -1, 1)
+    dot_rows = dot_slabs.reshape(block_count, -1, 1)
+    probabilities = jnp.where(allowed, jnp.exp(score_matrix - total_rows), 0.0)
+    probability_gradient = jnp.einsum(
+        "nmv,njv->nmj", grad_rows, value_per_head, preferred_element_type=jnp.float32
+    )
+    score_gradient = (probabilities * (probability_gradient - dot_rows)).astype(jnp.bfloat16)
+    attention_weight = probabilities.astype(jnp.bfloat16)
+    key_gradient = (
+        jnp.einsum("nmj,nmv->njv", score_gradient, query_rows, preferred_element_type=jnp.float32)
+        * logit_scale
+    )
+    value_gradient = jnp.einsum(
+        "nmj,nmv->njv", attention_weight, grad_rows, preferred_element_type=jnp.float32
+    )
+    return key_gradient, value_gradient
+
+
+def key_allowed(first_block, blocks_dev, offsets, block_total):
+    block_ids = first_block + jnp.arange(blocks_dev, dtype=jnp.int32)
+    offset_arr = jnp.array(offsets, dtype=jnp.int32)
+    query_live = block_ids[:, None] + offset_arr[None, :] < block_total
+    row_ids = jnp.arange(BLK, dtype=jnp.int32)
+    causal = row_ids[:, None] >= row_ids[None, :]
+    later_slab = offset_arr > 0
+    slab_causal = jnp.logical_or(later_slab[:, None, None], causal[None, :, :])
+    allowed = jnp.logical_and(query_live[:, :, None, None], slab_causal[None, :, :, :])
+    return allowed.reshape(blocks_dev, len(offsets) * BLK, BLK)
+
+
+def body(queries, key_tokens, value_tokens, grad_out):
+    row_width = queries.shape[1]
+    tok_count = queries.shape[0]
+    devices = lax.axis_size("seq")
+    blocks_dev, rim, near_list, far_list, far_shifts = plan(tok_count, devices)
+    if not relay_ok(devices, blocks_dev, rim, far_shifts):
+        return legacy_body(queries, key_tokens, value_tokens, grad_out)
+    heads = row_width // HD
+    offsets = near_list + far_list
+    logit_scale = 1.0 / math.sqrt(HD)
+    span_blocks = (rim + 1) * blocks_dev
+    lead = rim * blocks_dev
+    position = lax.axis_index("seq")
+    odd = (position % 2) == 1
+    pairs = swap_pairs(devices)
+    keys_values = jnp.concatenate([key_tokens, value_tokens], axis=1)
+    queries_grads = jnp.concatenate([queries, grad_out], axis=1)
+    back2 = passed_along(keys_values, "seq", 2)
+    ahead2 = passed_along(queries_grads, "seq", -2)
+    swap_one = lax.ppermute(jnp.where(odd, queries_grads, keys_values), "seq", pairs)
+    back4 = passed_along(back2, "seq", 2)
+    ahead4 = passed_along(ahead2, "seq", -2)
+    swap_two = lax.ppermute(jnp.where(odd, back2, ahead2), "seq", pairs)
+    back1 = jnp.where(odd, swap_one, swap_two)
+    ahead1 = jnp.where(odd, swap_two, swap_one)
+    far_back = [back4] + [passed_along(keys_values, "seq", shift) for shift in far_shifts[1:]]
+    far_ahead = [ahead4] + [passed_along(queries_grads, "seq", -shift) for shift in far_shifts[1:]]
+    far_back = far_back[: len(far_shifts)]
+    far_ahead = far_ahead[: len(far_shifts)]
+
+    span_both = to_blocks(jnp.concatenate([back2, back1, keys_values], axis=0), span_blocks)
+    far_both = [to_blocks(item, blocks_dev) for item in far_back]
+    allowed = allowed_mask(position * blocks_dev, blocks_dev, offsets)
+    query_blocks = to_blocks(queries, blocks_dev)
+    grad_blocks = to_blocks(grad_out, blocks_dev)
+    attended_heads = []
+    grad_query_heads = []
+    total_heads = []
+    dot_heads = []
+    for head_index in range(heads):
+        key_col = head_index * HD
+        value_col = row_width + head_index * HD
+        key_slabs = jnp.stack(
+            [
+                head_cols(span_both[lead - offset : lead + blocks_dev - offset], key_col)
+                for offset in near_list
+            ]
+            + [head_cols(item, key_col) for item in far_both],
+            axis=1,
+        )
+        value_slabs = jnp.stack(
+            [
+                head_cols(span_both[lead - offset : lead + blocks_dev - offset], value_col)
+                for offset in near_list
+            ]
+            + [head_cols(item, value_col) for item in far_both],
+            axis=1,
+        )
+        attended_per_head, query_gradient_heads, log_total, out_dot = row_pass(
+            head_cols(query_blocks, key_col),
+            head_cols(grad_blocks, key_col),
+            key_slabs,
+            value_slabs,
+            allowed,
+            logit_scale,
+        )
+        attended_heads.append(attended_per_head.reshape(tok_count, HD))
+        grad_query_heads.append(query_gradient_heads.reshape(tok_count, HD))
+        total_heads.append(log_total.reshape(tok_count, 1))
+        dot_heads.append(out_dot.reshape(tok_count, 1))
+    attended = jnp.concatenate(attended_heads, axis=-1)
+    grad_queries = jnp.concatenate(grad_query_heads, axis=-1)
+    stats = jnp.concatenate(total_heads + dot_heads, axis=-1)
+    stats_one = passed_along(stats, "seq", -1)
+    stats_two = passed_along(stats, "seq", -2)
+    far_stats = [passed_along(stats, "seq", -shift) for shift in far_shifts]
+
+    span_rows = to_blocks(jnp.concatenate([queries_grads, ahead1, ahead2], axis=0), span_blocks)
+    span_stats = to_blocks(jnp.concatenate([stats, stats_one, stats_two], axis=0), span_blocks)
+    far_rows = [to_blocks(item, blocks_dev) for item in far_ahead]
+    far_stat_blocks = [to_blocks(item, blocks_dev) for item in far_stats]
+    row_slabs = jnp.stack(
+        [
+            jnp.stack(
+                [span_rows[block + offset] for offset in near_list]
+                + [item[block] for item in far_rows],
+                axis=0,
+            )
+            for block in range(blocks_dev)
+        ],
+        axis=0,
+    )
+    stat_slabs = jnp.stack(
+        [
+            jnp.stack(
+                [span_stats[block + offset] for offset in near_list]
+                + [item[block] for item in far_stat_blocks],
+                axis=0,
+            )
+            for block in range(blocks_dev)
+        ],
+        axis=0,
+    )
+    permitted = key_allowed(position * blocks_dev, blocks_dev, offsets, devices * blocks_dev)
+    key_blocks = to_blocks(key_tokens, blocks_dev)
+    value_blocks = to_blocks(value_tokens, blocks_dev)
+    key_grad_heads = []
+    value_grad_heads = []
+    for head_index in range(heads):
+        col = head_index * HD
+        key_gradient, value_gradient = key_pass(
+            head_cols(key_blocks, col),
+            head_cols(value_blocks, col),
+            head_cols(row_slabs, col),
+            head_cols(row_slabs, row_width + col),
+            stat_slabs[..., head_index],
+            stat_slabs[..., heads + head_index],
+            permitted,
+            logit_scale,
+        )
+        key_grad_heads.append(key_gradient.reshape(tok_count, HD))
+        value_grad_heads.append(value_gradient.reshape(tok_count, HD))
+    grad_keys = jnp.concatenate(key_grad_heads, axis=-1).astype(jnp.bfloat16)
+    grad_values = jnp.concatenate(value_grad_heads, axis=-1).astype(jnp.bfloat16)
+    return attended, grad_queries, grad_keys, grad_values
+
+
 def solution(mesh):
     placed = (
         P(("rep", "seq"), None),

time: 99.2 us -> 99.1 us (level)
  the two profiles are of different devices: /device:TPU:14 before, /device:TPU:24 now
where the time goes in v3:
time: 99.1 us; the launch traced here: 98 us
  local copies, waits for them, and re-layouts  25.7 us (26%)
  starting transfers between devices  25.3 us (26%)
  matrix products  24.5 us (25%)
  other arithmetic  11.2 us (11%)
  waiting for transfers between devices  9.8 us (10%)
  between operations  1.53 us (2%)
    ppermute x7, starting transfers between devices, passed_along(): lax.ppermute(value, axis, [(source, source + steps) for source in range(f...  23.3 us
    unnamed x156, local copies, waits for them, and re-layouts  21 us
    dot_general x4, matrix products, row_pass(): jnp.einsum('jym,jmo->jyo', score_gradient, key_row_block, preferred_eleme...  7.57 us
    ppermute x7, waiting for transfers between devices, passed_along(): lax.ppermute(value, axis, [(source, source + steps) for source in range(f...  6.49 us
    dot_general x4, matrix products, key_pass(): jnp.einsum('nmv,njv->nmj', query_rows, key_per_head, preferred_element_ty...  5.53 us
    dot_general x4, matrix products, key_pass(): jnp.einsum('nmj,nmv->njv', score_gradient, query_rows, preferred_element_...  4.63 us
    dot_general x4, matrix products, row_pass(): jnp.einsum('jym,jmo->jyo', attention_weight, value_row_block, preferred_e...  3.51 us
    ppermute x1, waiting for transfers between devices, body(): swap_two = lax.ppermute(jnp.where(odd, back2, ahead2), 'seq', pairs)  3.31 us
  transfers between devices with their start and end apart: 9, of which 4 were waited for; matrix products, arithmetic and copies ran while one was open for 40% of the time, Pallas kernels for 0%

profile of v3, /device:TPU:24, one launch (start us, length us, event | category | flops | bytes accessed | tf_op | source)
XLA Modules:
  0.0 98.0 jit_solution(10738157967173400374)
XLA Ops:
  5.0 5.4 %collective-permute-start.2 = (bf16[256,1024]{1,0:T(8,128)(2,1)S(1)}, bf16[256,1024]{1,0:T(8,128)(2,1)}, u32[]{:S(2)}, u32[]{:S(2)}) collective-permute-start(bf16[256,1024]{1,0:T(8,128)(2,1)S(1)} %constant_dynamic-update-slice_fusion.2), channel_id=1, source_target_pairs={{8,0},{12,4},{16,8},{20,12},{24,16},{28,20},{9,1},{13,5},{17,9},{2... | collective-permute-start | bytes 1572872 | tf_op jit(solution)/shard_map/ppermute | solution.py:21
  11.2 1.5 %collective-permute-start = (bf16[256,1024]{1,0:T(8,128)(2,1)}, bf16[256,1024]{1,0:T(8,128)(2,1)S(1)}, u32[]{:S(2)}, u32[]{:S(2)}) collective-permute-start(bf16[256,1024]{1,0:T(8,128)(2,1)} %broadcast_select_fusion.3), channel_id=1, source_target_pairs={{0,4},{4,0},{8,12},{12,8},{16,20},{20,16},{24,28},{28,24},{1,5},{5... | collective-permute-start | bytes 1572872 | tf_op jit(solution)/shard_map/ppermute | solution.py:350
  14.5 3.8 %collective-permute-done.1 = bf16[256,1024]{1,0:T(8,128)(2,1)S(1)} collective-permute-done((bf16[256,1024]{1,0:T(8,128)(2,1)S(1)}, bf16[256,1024]{1,0:T(8,128)(2,1)S(1)}, u32[]{:S(2)}, u32[]{:S(2)}) %collective-permute-start.1) | collective-permute-done | bytes 524320 | tf_op jit(solution)/shard_map/ppermute | solution.py:21
  18.3 2.2 %collective-permute-done.2 = bf16[256,1024]{1,0:T(8,128)(2,1)} collective-permute-done((bf16[256,1024]{1,0:T(8,128)(2,1)S(1)}, bf16[256,1024]{1,0:T(8,128)(2,1)}, u32[]{:S(2)}, u32[]{:S(2)}) %collective-permute-start.2) | collective-permute-done | bytes 524320 | tf_op jit(solution)/shard_map/ppermute | solution.py:21
  20.5 1.9 %broadcast_select_fusion.2 = bf16[256,1024]{1,0:T(8,128)(2,1)} fusion(bf16[256,1024]{1,0:T(8,128)(2,1)S(1)} %collective-permute-done.1, bf16[256,1024]{1,0:T(8,128)(2,1)} %collective-permute-done.2, pred[]{:T(512)S(6)} %eq.5), kind=kLoop, calls=%fused_computation.118 | loop fusion | flops 262144 | bytes 1572865 | tf_op jit(solution)/shard_map/jit(_where)/select_n | solution.py:353
  26.6 5.9 %collective-permute-start.5 = (bf16[256,1024]{1,0:T(8,128)(2,1)}, bf16[256,1024]{1,0:T(8,128)(2,1)}, u32[]{:S(2)}, u32[]{:S(2)}) collective-permute-start(bf16[256,1024]{1,0:T(8,128)(2,1)} %collective-permute-done.2), channel_id=1, source_target_pairs={{8,0},{12,4},{16,8},{20,12},{24,16},{28,20},{9,1},{13,5},{17,9},{2... | collective-permute-start | bytes 1572872 | tf_op jit(solution)/shard_map/ppermute | solution.py:21
  32.6 3.3 %collective-permute-done.3 = bf16[256,1024]{1,0:T(8,128)(2,1)} collective-permute-done((bf16[256,1024]{1,0:T(8,128)(2,1)}, bf16[256,1024]{1,0:T(8,128)(2,1)}, u32[]{:S(2)}, u32[]{:S(2)}) %collective-permute-start.3) | collective-permute-done | bytes 524320 | tf_op jit(solution)/shard_map/ppermute | solution.py:353
  35.9 1.9 %broadcast_select_fusion = (bf16[256,1024]{1,0:T(8,128)(2,1)}, bf16[256,1024]{1,0:T(8,128)(2,1)S(1)}) fusion(bf16[256,1024]{1,0:T(8,128)(2,1)} %collective-permute-done.3, bf16[256,1024]{1,0:T(8,128)(2,1)S(1)} %collective-permute-done, pred[]{:T(512)S(6)} %eq.5), kind=kLoop, calls=%fused_computation.116 | loop fusion | flops 524288 | bytes 2097153 | tf_op jit(solution)/shard_map/jit(_where)/select_n | solution.py:355
  46.8 2.5 %multiply_reduce_fusion.3 = (f32[2,128]{1,0:T(2,128)}, f32[2,128]{1,0:T(2,128)}, f32[2,128]{1,0:T(2,128)}, f32[2,128]{1,0:T(2,128)}, bf16[2,128,128]{2,1,0:T(8,128)(2,1)}) fusion(bf16[2,128,512]{2,1,0:T(8,128)(2,1)} %bitcast.522, bf16[2,128,128]{2,1,0:T(8,128)(2,1)S(1)} %convolution_convert_fusion.6, ...), kind=kOutput, calls=%fused_computation.241 | convolution fusion | flops 51280896 | bytes 1709056 | tf_op jit(solution)/shard_map/jym,jmo->jyo/dot_general | solution.py:272
  49.3 2.3 %fusion.52 = bf16[2,128,128]{2,1,0:T(8,128)(2,1)} fusion(bf16[2,768,128]{2,1,0:T(8,128)(2,1)} %bitcast.519, bf16[2,768,128]{2,1,0:T(8,128)(2,1)} %bitcast.499, f32[2,128,768]{1,2,0:T(8,128)S(1)} %get-tuple-element.93, f32[2,128]{1,0:T(2,128)} %get-tuple-element.7, f32[2,128]{1,0:T(2,128)S(1)} %log_add_fusion, bf16[2,128,512]{2,1,0:T(8,128)(2,1)} %bitcast.523), kind=kOutput, calls=%fused_computation.90 | convolution fusion | flops 101515264 | bytes 1705984 | tf_op jit(solution)/shard_map/jym,jmo->jyo/dot_general | solution.py:285
  51.6 2.3 %fusion.53 = bf16[2,128,128]{2,1,0:T(8,128)(2,1)} fusion(bf16[2,768,128]{2,1,0:T(8,128)(2,1)} %bitcast.521, bf16[2,768,128]{2,1,0:T(8,128)(2,1)} %bitcast.501, f32[2,128,768]{1,2,0:T(8,128)S(1)} %get-tuple-element.95, f32[2,128]{1,0:T(2,128)} %get-tuple-element.6, f32[2,128]{1,0:T(2,128)S(1)} %log_add_fusion.1, bf16[2,128,512]{2,1,0:T(8,128)(2,1)} %bitcast.524), kind=kOutput, calls=%fused_computation.91 | convolution fusion | flops 101515264 | bytes 1705984 | tf_op jit(solution)/shard_map/jym,jmo->jyo/dot_general | solution.py:285
  54.7 4.6 %collective-permute-start.6 = (f32[256,8]{0,1:T(8,128)S(1)}, f32[256,8]{0,1:T(8,128)}, u32[]{:S(2)}, u32[]{:S(2)}) collective-permute-start(f32[256,8]{0,1:T(8,128)S(1)} %concatenate.38), channel_id=1, source_target_pairs={{4,0},{8,4},{12,8},{16,12},{20,16},{24,20},{28,24},{5,1},{9,5},{13... | collective-permute-start | bytes 24584 | tf_op jit(solution)/shard_map/ppermute | solution.py:21
  59.3 3.0 %collective-permute-start.7 = (f32[256,8]{0,1:T(8,128)S(1)}, f32[256,8]{0,1:T(8,128)}, u32[]{:S(2)}, u32[]{:S(2)}) collective-permute-start(f32[256,8]{0,1:T(8,128)S(1)} %concatenate.38), channel_id=1, source_target_pairs={{8,0},{12,4},{16,8},{20,12},{24,16},{28,20},{9,1},{13,5},{17,9},{2... | collective-permute-start | bytes 24584 | tf_op jit(solution)/shard_map/ppermute | solution.py:21
  62.3 1.9 %collective-permute-start.8 = (f32[256,8]{0,1:T(8,128)S(1)}, f32[256,8]{0,1:T(8,128)}, u32[]{:S(2)}, u32[]{:S(2)}) collective-permute-start(f32[256,8]{0,1:T(8,128)S(1)} %concatenate.38), channel_id=1, source_target_pairs={{16,0},{20,4},{24,8},{28,12},{17,1},{21,5},{25,9},{29,13},{18,2},{... | collective-permute-start | bytes 24584 | tf_op jit(solution)/shard_map/ppermute | solution.py:21
  67.1 1.7 %fusion.101 = bf16[6,128,1024]{2,1,0:T(8,128)(2,1)} fusion(bf16[6,128,1024]{2,1,0:T(8,128)(2,1)} %get-tuple-element.30, bf16[256,1024]{1,0:T(8,128)(2,1)} %collective-permute-done.2), kind=kLoop, calls=%fused_computation.172 | loop fusion | bytes 524288
  68.8 1.9 %fusion.92 = (bf16[6,128,1024]{2,1,0:T(8,128)(2,1)}, bf16[6,128,1024]{2,1,0:T(8,128)(2,1)}) fusion(bf16[6,128,1024]{2,1,0:T(8,128)(2,1)} %fusion.101, bf16[256,1024]{1,0:T(8,128)(2,1)} %collective-permute-done.2, bf16[6,128,1024]{2,1,0:T(8,128)(2,1)} %get-tuple-element.31), kind=kLoop, calls=%fused_computation.153 | loop fusion | bytes 1048576
  70.7 1.8 %fusion.54 = bf16[2,128,128]{2,1,0:T(8,128)(2,1)} fusion(bf16[2,768,128]{2,1,0:T(8,128)(2,1)S(1)} %bitcast.517, bf16[2,768,128]{2,1,0:T(8,128)(2,1)S(1)} %bitcast.495, f32[2,128,768]{1,2,0:T(8,128)S(1)} %get-tuple-element.97, f32[2,128]{1,0:T(2,128)} %get-tuple-element.5, f32[2,128]{1,0:T(2,128)S(1)} %log_add_fusion.2, bf16[2,128,512]{2,1,0:T(8,128)(2,1)S(1)} %bitcast.525), kind=kOutput, calls=%fused_computation.92 | convolution fusion | flops 101515264 | bytes 1705984 | tf_op jit(solution)/shard_map/jym,jmo->jyo/dot_general | solution.py:285
  73.7 1.8 %fusion.91 = (bf16[6,128,1024]{2,1,0:T(8,128)(2,1)}, bf16[6,128,1024]{2,1,0:T(8,128)(2,1)}) fusion(bf16[6,128,1024]{2,1,0:T(8,128)(2,1)} %get-tuple-element.28, bf16[256,1024]{1,0:T(8,128)(2,1)} %collective-permute-done.5, bf16[6,128,1024]{2,1,0:T(8,128)(2,1)} %get-tuple-element.29), kind=kLoop, calls=%fused_computation.151 | loop fusion | bytes 1048576 | tf_op jit(solution)/shard_map/stack | solution.py:414
  75.6 2.4 %fusion.62 = (bf16[2,6,128,128]{3,2,1,0:T(8,128)(2,1)S(1)}, bf16[2,6,128,128]{3,2,1,0:T(8,128)(2,1)S(1)}, bf16[2,6,128,128]{3,2,1,0:T(8,128)(2,1)S(1)}, bf16[2,6...) fusion(bf16[1,6,128,1024]{3,2,1,0:T(8,128)(2,1)} %bitcast.503, ...), kind=kLoop, calls=%fused_computation.122 | loop fusion | flops 6291456 | bytes 6291456 | tf_op jit(solution)/shard_map/stack | solution.py:412
  84.9 1.3 %and_select_fusion = f32[2,768,128]{2,1,0:T(8,128)S(1)} fusion(bf16[2,768,128]{2,1,0:T(8,128)(2,1)S(1)} %bitcast.514, f32[2,768]{1,0:T(2,128)S(1)} %bitcast.582, pred[768,128]{1,0:T(8,128)(4,1)S(1)} %copy-done.39, pred[2,768]{1,0:T(4,128)(4,1)S(1)} %bitcast.586, bf16[2,128,512]{2,1,0:T(8,128)(2,1)} %bitcast.547), kind=kOutput, calls=%fused_computation.14 | convolution fusion | flops 51118080 | bytes 1351168 | tf_op jit(solution)/shard_map/nmv,njv->nmj/dot_general | solution.py:298
  87.1 2.3 %fusion.48 = bf16[2,128,128]{2,1,0:T(8,128)(2,1)} fusion(bf16[2,768,128]{2,1,0:T(8,128)(2,1)} %bitcast.515, f32[2,768,128]{2,1,0:T(8,128)S(1)} %and_select_fusion, bf16[2,768,128]{2,1,0:T(8,128)(2,1)S(1)} %bitcast.493, f32[2,768]{1,0:T(2,128)} %bitcast.570, bf16[2,128,512]{2,1,0:T(8,128)(2,1)} %bitcast.527), kind=kOutput, calls=%fused_computation.86 | convolution fusion | flops 101318656 | bytes 1710080 | tf_op jit(solution)/shard_map/nmj,nmv->njv/dot_general | solution.py:310
  89.4 1.5 %and_select_fusion.1 = f32[2,768,128]{2,1,0:T(8,128)S(1)} fusion(bf16[2,768,128]{2,1,0:T(8,128)(2,1)S(1)} %bitcast.512, f32[2,768]{1,0:T(2,128)} %bitcast.581, pred[768,128]{1,0:T(8,128)(4,1)} %bitcast_or_fusion, pred[2,768]{1,0:T(4,128)(4,1)} %bitcast.585, bf16[2,128,512]{2,1,0:T(8,128)(2,1)} %bitcast.548), kind=kOutput, calls=%fused_computation.15 | convolution fusion | flops 51118080 | bytes 1352704 | tf_op jit(solution)/shard_map/nmv,njv->nmj/dot_general | solution.py:298
  92.5 1.4 %and_select_fusion.2 = f32[2,768,128]{2,1,0:T(8,128)S(1)} fusion(bf16[2,768,128]{2,1,0:T(8,128)(2,1)S(1)} %bitcast.510, f32[2,768]{1,0:T(2,128)S(1)} %bitcast.584, pred[768,128]{1,0:T(8,128)(4,1)} %bitcast_or_fusion, pred[2,768]{1,0:T(4,128)(4,1)S(1)} %bitcast.587, bf16[2,128,512]{2,1,0:T(8,128)(2,1)} %bitcast.549), kind=kOutput, calls=%fused_computation.16 | convolution fusion | flops 51118080 | bytes 1351168 | tf_op jit(solution)/shard_map/nmv,njv->nmj/dot_general | solution.py:298
  94.9 1.3 %and_select_fusion.3 = f32[2,768,128]{2,1,0:T(8,128)S(1)} fusion(bf16[2,768,128]{2,1,0:T(8,128)(2,1)S(1)} %bitcast.508, f32[2,768]{1,0:T(2,128)S(1)} %bitcast.583, pred[768,128]{1,0:T(8,128)(4,1)S(1)} %copy-done.40, pred[2,768]{1,0:T(4,128)(4,1)S(1)} %bitcast.588, bf16[2,128,512]{2,1,0:T(8,128)(2,1)} %bitcast.550), kind=kOutput, calls=%fused_computation.17 | convolution fusion | flops 51118080 | bytes 1351168 | tf_op jit(solution)/shard_map/nmv,njv->nmj/dot_general | solution.py:298
  (211 shorter events, 36.5 us)
Async XLA Ops:
  1.7 11.1 %copy-start.57 = (s32[6]{0:T(128)S(1)}, s32[6]{0:T(128)}, u32[]{:S(2)}) copy-start(s32[6]{0:T(128)} %constant.36.clone) | copy-start | bytes 76
  1.7 11.1 %copy-start.58 = (s32[6]{0:T(128)S(1)}, s32[6]{0:T(128)}, u32[]{:S(2)}) copy-start(s32[6]{0:T(128)} %constant.37) | copy-start | bytes 76
  1.7 11.3 %copy-start.59 = (pred[6]{0:T(512)(128)(4,1)S(1)}, pred[6]{0:T(512)(128)(4,1)}, u32[]{:S(2)}) copy-start(pred[6]{0:T(512)(128)(4,1)} %constant.38) | copy-start | bytes 22
  2.7 15.6 %collective-permute-start.1 = (bf16[256,1024]{1,0:T(8,128)(2,1)S(1)}, bf16[256,1024]{1,0:T(8,128)(2,1)S(1)}, u32[]{:S(2)}, u32[]{:S(2)}) collective-permute-start(bf16[256,1024]{1,0:T(8,128)(2,1)S(1)} %constant_dynamic-update-slice_fusion), channel_id=1, source_target_pairs={{0,8},{4,12},{8,16},{12,20},{16,24},{20,28},{1,9},{5,13},{9,17},{1... | collective-permute-start | bytes 1572872 | tf_op jit(solution)/shard_map/ppermute | solution.py:21
  5.0 15.4 %collective-permute-start.2 = (bf16[256,1024]{1,0:T(8,128)(2,1)S(1)}, bf16[256,1024]{1,0:T(8,128)(2,1)}, u32[]{:S(2)}, u32[]{:S(2)}) collective-permute-start(bf16[256,1024]{1,0:T(8,128)(2,1)S(1)} %constant_dynamic-update-slice_fusion.2), channel_id=1, source_target_pairs={{8,0},{12,4},{16,8},{20,12},{24,16},{28,20},{9,1},{13,5},{17,9},{2... | collective-permute-start | bytes 1572872 | tf_op jit(solution)/shard_map/ppermute | solution.py:21
  11.2 21.3 %collective-permute-start = (bf16[256,1024]{1,0:T(8,128)(2,1)}, bf16[256,1024]{1,0:T(8,128)(2,1)S(1)}, u32[]{:S(2)}, u32[]{:S(2)}) collective-permute-start(bf16[256,1024]{1,0:T(8,128)(2,1)} %broadcast_select_fusion.3), channel_id=1, source_target_pairs={{0,4},{4,0},{8,12},{12,8},{16,20},{20,16},{24,28},{28,24},{1,5},{5... | collective-permute-start | bytes 1572872 | tf_op jit(solution)/shard_map/ppermute | solution.py:350
  18.3 21.3 %copy-start = (bf16[256,1024]{1,0:T(8,128)(2,1)}, bf16[256,1024]{1,0:T(8,128)(2,1)S(1)}, u32[]{:S(2)}) copy-start(bf16[256,1024]{1,0:T(8,128)(2,1)S(1)} %collective-permute-done.1) | copy-start | bytes 1572868
  22.4 13.5 %collective-permute-start.3 = (bf16[256,1024]{1,0:T(8,128)(2,1)}, bf16[256,1024]{1,0:T(8,128)(2,1)}, u32[]{:S(2)}, u32[]{:S(2)}) collective-permute-start(bf16[256,1024]{1,0:T(8,128)(2,1)} %broadcast_select_fusion.2), channel_id=1, source_target_pairs={{0,4},{4,0},{8,12},{12,8},{16,20},{20,16},{24,28},{28,24},{1,5},{5... | collective-permute-start | bytes 1572872 | tf_op jit(solution)/shard_map/ppermute | solution.py:353
  25.3 7.2 %copy-start.5 = (bf16[6,128,1024]{2,1,0:T(8,128)(2,1)}, bf16[6,128,1024]{2,1,0:T(8,128)(2,1)S(1)}, u32[]{:S(2)}) copy-start(bf16[6,128,1024]{2,1,0:T(8,128)(2,1)S(1)} %get-tuple-element.35) | copy-start | bytes 4718596
  25.3 14.9 %collective-permute-start.4 = (bf16[256,1024]{1,0:T(8,128)(2,1)S(1)}, bf16[256,1024]{1,0:T(8,128)(2,1)S(1)}, u32[]{:S(2)}, u32[]{:S(2)}) collective-permute-start(bf16[256,1024]{1,0:T(8,128)(2,1)S(1)} %collective-permute-done.1), channel_id=1, source_target_pairs={{0,8},{4,12},{8,16},{12,20},{16,24},{20,28},{1,9},{5,13},{9,17},{1... | collective-permute-start | bytes 1572872 | tf_op jit(solution)/shard_map/ppermute | solution.py:21
  26.6 47.0 %collective-permute-start.5 = (bf16[256,1024]{1,0:T(8,128)(2,1)}, bf16[256,1024]{1,0:T(8,128)(2,1)}, u32[]{:S(2)}, u32[]{:S(2)}) collective-permute-start(bf16[256,1024]{1,0:T(8,128)(2,1)} %collective-permute-done.2), channel_id=1, source_target_pairs={{8,0},{12,4},{16,8},{20,12},{24,16},{28,20},{9,1},{13,5},{17,9},{2... | collective-permute-start | bytes 1572872 | tf_op jit(solution)/shard_map/ppermute | solution.py:21
  41.7 7.6 %copy-start.47 = (f32[2,128]{1,0:T(2,128)}, f32[2,128]{1,0:T(2,128)S(1)}, u32[]{:S(2)}) copy-start(f32[2,128]{1,0:T(2,128)S(1)} %log_add_fusion) | copy-start | bytes 3076
  42.3 9.4 %copy-start.49 = (f32[2,128]{1,0:T(2,128)}, f32[2,128]{1,0:T(2,128)S(1)}, u32[]{:S(2)}) copy-start(f32[2,128]{1,0:T(2,128)S(1)} %log_add_fusion.1) | copy-start | bytes 3076
  51.6 13.7 %copy-start.6 = (bf16[256,1024]{1,0:T(8,128)(2,1)S(1)}, bf16[256,1024]{1,0:T(8,128)(2,1)}, u32[]{:S(2)}) copy-start(bf16[256,1024]{1,0:T(8,128)(2,1)} %get-tuple-element.24) | copy-start | bytes 1572868
  54.7 24.3 %collective-permute-start.6 = (f32[256,8]{0,1:T(8,128)S(1)}, f32[256,8]{0,1:T(8,128)}, u32[]{:S(2)}, u32[]{:S(2)}) collective-permute-start(f32[256,8]{0,1:T(8,128)S(1)} %concatenate.38), channel_id=1, source_target_pairs={{4,0},{8,4},{12,8},{16,12},{20,16},{24,20},{28,24},{5,1},{9,5},{13... | collective-permute-start | bytes 24584 | tf_op jit(solution)/shard_map/ppermute | solution.py:21
  59.3 21.0 %collective-permute-start.7 = (f32[256,8]{0,1:T(8,128)S(1)}, f32[256,8]{0,1:T(8,128)}, u32[]{:S(2)}, u32[]{:S(2)}) collective-permute-start(f32[256,8]{0,1:T(8,128)S(1)} %concatenate.38), channel_id=1, source_target_pairs={{8,0},{12,4},{16,8},{20,12},{24,16},{28,20},{9,1},{13,5},{17,9},{2... | collective-permute-start | bytes 24584 | tf_op jit(solution)/shard_map/ppermute | solution.py:21
  62.3 19.4 %collective-permute-start.8 = (f32[256,8]{0,1:T(8,128)S(1)}, f32[256,8]{0,1:T(8,128)}, u32[]{:S(2)}, u32[]{:S(2)}) collective-permute-start(f32[256,8]{0,1:T(8,128)S(1)} %concatenate.38), channel_id=1, source_target_pairs={{16,0},{20,4},{24,8},{28,12},{17,1},{21,5},{25,9},{29,13},{18,2},{... | collective-permute-start | bytes 24584 | tf_op jit(solution)/shard_map/ppermute | solution.py:21
  65.4 5.4 %copy-start.13 = (bf16[256,512]{1,0:T(8,128)(2,1)S(1)}, bf16[256,512]{1,0:T(8,128)(2,1)}, u32[]{:S(2)}) copy-start(bf16[256,512]{1,0:T(8,128)(2,1)} %param.9) | copy-start | bytes 786436
  67.1 5.4 %copy-start.2 = (bf16[2,6,128,128]{3,2,1,0:T(8,128)(2,1)S(1)}, bf16[2,6,128,128]{3,2,1,0:T(8,128)(2,1)}, u32[]{:S(2)}) copy-start(bf16[2,6,128,128]{3,2,1,0:T(8,128)(2,1)} %copy-done.1) | copy-start | bytes 1179652
  67.1 5.4 %copy-start.29 = (bf16[2,6,128,128]{3,2,1,0:T(8,128)(2,1)S(1)}, bf16[2,6,128,128]{3,2,1,0:T(8,128)(2,1)}, u32[]{:S(2)}) copy-start(bf16[2,6,128,128]{3,2,1,0:T(8,128)(2,1)} %copy-done.28) | copy-start | bytes 1179652
  67.1 5.4 %copy-start.51 = (f32[2,128]{1,0:T(2,128)S(1)}, f32[2,128]{1,0:T(2,128)}, u32[]{:S(2)}) copy-start(f32[2,128]{1,0:T(2,128)} %get-tuple-element.4) | copy-start | bytes 3076
  75.6 9.3 %copy-start.39 = (pred[768,128]{1,0:T(8,128)(4,1)S(1)}, pred[768,128]{1,0:T(8,128)(4,1)}, u32[]{:S(2)}) copy-start(pred[768,128]{1,0:T(8,128)(4,1)} %bitcast_or_fusion) | copy-start | bytes 294916
  75.6 9.3 %copy-start.55 = (pred[1,2,6,128]{3,1,2,0:T(4,128)(4,1)S(1)}, pred[1,2,6,128]{3,1,2,0:T(4,128)(4,1)}, u32[]{:S(2)}) copy-start(pred[1,2,6,128]{3,1,2,0:T(4,128)(4,1)} %copy.75) | copy-start | bytes 4612
  78.0 8.2 %copy-start.7 = (bf16[2,6,128,128]{3,2,1,0:T(8,128)(2,1)}, bf16[2,6,128,128]{3,2,1,0:T(8,128)(2,1)S(1)}, u32[]{:S(2)}) copy-start(bf16[2,6,128,128]{3,2,1,0:T(8,128)(2,1)S(1)} %get-tuple-element.23) | copy-start | bytes 1179652
  (45 other events, 96.0 us)

commit v4 on v3

--- a/solution.py
+++ b/solution.py
@@ -1,8 +1,11 @@
+import functools
 import math
 
 import jax
 import jax.numpy as jnp
 from jax import lax
+from jax.experimental import pallas as pl
+from jax.experimental.pallas import tpu as pltpu
 from jax.sharding import PartitionSpec as P
 
 HEADS = 4
@@ -328,6 +331,146 @@
     return allowed.reshape(blocks_dev, len(offsets) * BLK, BLK)
 
 
+TRANS_B = (((1,), (1,)), ((), ()))
+
+
+def row_kernel(near_list, far_list, heads, *refs):
+    far_count = len(far_list)
+    position_ref, query_ref, grad_ref, back2_ref, back1_ref, own_ref = refs[:6]
+    far_refs = refs[6 : 6 + far_count]
+    attended_ref, grad_query_ref, stats_ref = refs[6 + far_count :]
+    span = (back2_ref, back1_ref, own_ref)
+    width = heads * HD
+    scale = 1.0 / math.sqrt(HD)
+    first = 2 * position_ref[0]
+    row_ids = lax.broadcasted_iota(jnp.int32, (BLK, BLK), 0)
+    col_ids = lax.broadcasted_iota(jnp.int32, (BLK, BLK), 1)
+    causal = row_ids >= col_ids
+    lane_ids = lax.broadcasted_iota(jnp.int32, (BLK, 2 * heads), 1)
+    for block in range(2):
+        rows = pl.ds(block * BLK, BLK)
+        slabs = []
+        for offset in near_list:
+            index = 4 + block - offset
+            slabs.append((span[index // 2], (index % 2) * BLK, offset))
+        for level, offset in enumerate(far_list):
+            slabs.append((far_refs[level], block * BLK, offset))
+        stats_tile = jnp.zeros((BLK, 2 * heads), jnp.float32)
+        for head in range(heads):
+            cols = pl.ds(head * HD, HD)
+            value_cols = pl.ds(width + head * HD, HD)
+            query = query_ref[rows, cols]
+            grad = grad_ref[rows, cols]
+            scores = []
+            for source, start, offset in slabs:
+                key = source[pl.ds(start, BLK), cols]
+                score = lax.dot_general(query, key, TRANS_B, preferred_element_type=jnp.float32)
+                score = score * scale
+                live = first + block - offset >= 0
+                mask = jnp.logical_and(causal, live) if offset == 0 else jnp.logical_and(
+                    row_ids >= 0, live
+                )
+                scores.append(jnp.where(mask, score, NEG))
+            row_max = scores[0].max(axis=-1, keepdims=True)
+            for score in scores[1:]:
+                row_max = jnp.maximum(row_max, score.max(axis=-1, keepdims=True))
+            row_sum = jnp.exp(scores[0] - row_max).sum(axis=-1, keepdims=True)
+            for score in scores[1:]:
+                row_sum = row_sum + jnp.exp(score - row_max).sum(axis=-1, keepdims=True)
+            log_total = row_max + jnp.log(row_sum)
+            probs = [jnp.exp(score - log_total) for score in scores]
+            attended = jnp.zeros((BLK, HD), jnp.float32)
+            for prob, (source, start, offset) in zip(probs, slabs):
+                value = source[pl.ds(start, BLK), value_cols]
+                attended = attended + jnp.dot(
+                    prob.astype(jnp.bfloat16), value, preferred_element_type=jnp.float32
+                )
+            attended = attended.astype(jnp.bfloat16)
+            attended_ref[rows, cols] = attended
+            out_dot = jnp.sum(
+                grad.astype(jnp.float32) * attended.astype(jnp.float32), axis=-1, keepdims=True
+            )
+            grad_query = jnp.zeros((BLK, HD), jnp.float32)
+            for prob, (source, start, offset) in zip(probs, slabs):
+                value = source[pl.ds(start, BLK), value_cols]
+                key = source[pl.ds(start, BLK), cols]
+                prob_grad = lax.dot_general(grad, value, TRANS_B, preferred_element_type=jnp.float32)
+                score_grad = (prob * (prob_grad - out_dot)).astype(jnp.bfloat16)
+                grad_query = grad_query + jnp.dot(
+                    score_grad, key, preferred_element_type=jnp.float32
+                )
+            grad_query_ref[rows, cols] = (grad_query * scale).astype(jnp.bfloat16)
+            stats_tile = stats_tile + jnp.where(lane_ids == head, log_total, 0.0)
+            stats_tile = stats_tile + jnp.where(lane_ids == heads + head, out_dot, 0.0)
+        stats_ref[rows, :] = stats_tile
+
+
+def key_kernel(near_list, far_list, heads, block_total, *refs):
+    far_count = len(far_list)
+    position_ref, own_ref, rows0_ref, rows1_ref, rows2_ref = refs[:5]
+    far_rows = refs[5 : 5 + far_count]
+    stats0_ref, stats1_ref, stats2_ref = refs[5 + far_count : 8 + far_count]
+    far_stats = refs[8 + far_count : 8 + 2 * far_count]
+    grad_key_ref, grad_value_ref = refs[8 + 2 * far_count :]
+    span_rows = (rows0_ref, rows1_ref, rows2_ref)
+    span_stats = (stats0_ref, stats1_ref, stats2_ref)
+    width = heads * HD
+    scale = 1.0 / math.sqrt(HD)
+    first = 2 * position_ref[0]
+    row_ids = lax.broadcasted_iota(jnp.int32, (BLK, BLK), 0)
+    col_ids = lax.broadcasted_iota(jnp.int32, (BLK, BLK), 1)
+    causal = row_ids >= col_ids
+    lane_ids = lax.broadcasted_iota(jnp.int32, (BLK, 2 * heads), 1)
+    for block in range(2):
+        rows = pl.ds(block * BLK, BLK)
+        slabs = []
+        for offset in near_list:
+            index = block + offset
+            slabs.append((span_rows[index // 2], span_stats[index // 2], (index % 2) * BLK, offset))
+        for level, offset in enumerate(far_list):
+            slabs.append((far_rows[level], far_stats[level], block * BLK, offset))
+        for head in range(heads):
+            cols = pl.ds(head * HD, HD)
+            value_cols = pl.ds(width + head * HD, HD)
+            key = own_ref[rows, cols]
+            value = own_ref[rows, value_cols]
+            grad_key = jnp.zeros((BLK, HD), jnp.float32)
+            grad_value = jnp.zeros((BLK, HD), jnp.float32)
+            for source, stats, start, offset in slabs:
+                query = source[pl.ds(start, BLK), cols]
+                grad = source[pl.ds(start, BLK), value_cols]
+                tile = stats[pl.ds(start, BLK), :]
+                log_total = jnp.sum(jnp.where(lane_ids == head, tile, 0.0), axis=-1, keepdims=True)
+                out_dot = jnp.sum(
+                    jnp.where(lane_ids == heads + head, tile, 0.0), axis=-1, keepdims=True
+                )
+                score = lax.dot_general(query, key, TRANS_B, preferred_element_type=jnp.float32)
+                score = score * scale
+                live = first + block + offset < block_total
+                mask = jnp.logical_and(causal, live) if offset == 0 else jnp.logical_and(
+                    row_ids >= 0, live
+                )
+                prob = jnp.where(mask, jnp.exp(score - log_total), 0.0)
+                prob_grad = lax.dot_general(grad, value, TRANS_B, preferred_element_type=jnp.float32)
+                score_grad = prob * (prob_grad - out_dot)
+                grad_value = grad_value + jnp.dot(
+                    prob.T.astype(jnp.bfloat16), grad, preferred_element_type=jnp.float32
+                )
+                grad_key = grad_key + jnp.dot(
+                    score_grad.T.astype(jnp.bfloat16), query, preferred_element_type=jnp.float32
+                )
+            grad_key_ref[rows, cols] = (grad_key * scale).astype(jnp.bfloat16)
+            grad_value_ref[rows, cols] = grad_value.astype(jnp.bfloat16)
+
+
+def smem_spec():
+    return pl.BlockSpec(memory_space=pltpu.SMEM)
+
+
+def vmem_spec():
+    return pl.BlockSpec(memory_space=pltpu.VMEM)
+
+
 def body(queries, key_tokens, value_tokens, grad_out):
     row_width = queries.shape[1]
     tok_count = queries.shape[0]
@@ -358,100 +501,43 @@
     far_back = far_back[: len(far_shifts)]
     far_ahead = far_ahead[: len(far_shifts)]
 
-    span_both = to_blocks(jnp.concatenate([back2, back1, keys_values], axis=0), span_blocks)
-    far_both = [to_blocks(item, blocks_dev) for item in far_back]
-    allowed = allowed_mask(position * blocks_dev, blocks_dev, offsets)
-    query_blocks = to_blocks(queries, blocks_dev)
-    grad_blocks = to_blocks(grad_out, blocks_dev)
-    attended_heads = []
-    grad_query_heads = []
-    total_heads = []
-    dot_heads = []
-    for head_index in range(heads):
-        key_col = head_index * HD
-        value_col = row_width + head_index * HD
-        key_slabs = jnp.stack(
-            [
-                head_cols(span_both[lead - offset : lead + blocks_dev - offset], key_col)
-                for offset in near_list
-            ]
-            + [head_cols(item, key_col) for item in far_both],
-            axis=1,
-        )
-        value_slabs = jnp.stack(
-            [
-                head_cols(span_both[lead - offset : lead + blocks_dev - offset], value_col)
-                for offset in near_list
-            ]
-            + [head_cols(item, value_col) for item in far_both],
-            axis=1,
-        )
-        attended_per_head, query_gradient_heads, log_total, out_dot = row_pass(
-            head_cols(query_blocks, key_col),
-            head_cols(grad_blocks, key_col),
-            key_slabs,
-            value_slabs,
-            allowed,
-            logit_scale,
-        )
-        attended_heads.append(attended_per_head.reshape(tok_count, HD))
-        grad_query_heads.append(query_gradient_heads.reshape(tok_count, HD))
-        total_heads.append(log_total.reshape(tok_count, 1))
-        dot_heads.append(out_dot.reshape(tok_count, 1))
-    attended = jnp.concatenate(attended_heads, axis=-1)
-    grad_queries = jnp.concatenate(grad_query_heads, axis=-1)
-    stats = jnp.concatenate(total_heads + dot_heads, axis=-1)
+    position_arr = jnp.reshape(position, (1,)).astype(jnp.int32)
+    far_offsets = list(far_list)
+    attended, grad_queries, stats = pl.pallas_call(
+        functools.partial(row_kernel, near_list, far_offsets, heads),
+        out_shape=(
+            jax.ShapeDtypeStruct((tok_count, row_width), jnp.bfloat16),
+            jax.ShapeDtypeStruct((tok_count, row_width), jnp.bfloat16),
+            jax.ShapeDtypeStruct((tok_count, 2 * heads), jnp.float32),
+        ),
+        in_specs=[smem_spec()] + [vmem_spec()] * (5 + len(far_back)),
+        out_specs=(vmem_spec(), vmem_spec(), vmem_spec()),
+        name="rows_pass",
+    )(position_arr, queries, grad_out, back2, back1, keys_values, *far_back)
     stats_one = passed_along(stats, "seq", -1)
     stats_two = passed_along(stats, "seq", -2)
     far_stats = [passed_along(stats, "seq", -shift) for shift in far_shifts]
-
-    span_rows = to_blocks(jnp.concatenate([queries_grads, ahead1, ahead2], axis=0), span_blocks)
-    span_stats = to_blocks(jnp.concatenate([stats, stats_one, stats_two], axis=0), span_blocks)
-    far_rows = [to_blocks(item, blocks_dev) for item in far_ahead]
-    far_stat_blocks = [to_blocks(item, blocks_dev) for item in far_stats]
-    row_slabs = jnp.stack(
-        [
-            jnp.stack(
-                [span_rows[block + offset] for offset in near_list]
-                + [item[block] for item in far_rows],
-                axis=0,
-            )
-            for block in range(blocks_dev)
-        ],
-        axis=0,
-    )
-    stat_slabs = jnp.stack(
-        [
-            jnp.stack(
-                [span_stats[block + offset] for offset in near_list]
-                + [item[block] for item in far_stat_blocks],
-                axis=0,
-            )
-            for block in range(blocks_dev)
-        ],
-        axis=0,
-    )
-    permitted = key_allowed(position * blocks_dev, blocks_dev, offsets, devices * blocks_dev)
-    key_blocks = to_blocks(key_tokens, blocks_dev)
-    value_blocks = to_blocks(value_tokens, blocks_dev)
-    key_grad_heads = []
-    value_grad_heads = []
-    for head_index in range(heads):
-        col = head_index * HD
-        key_gradient, value_gradient = key_pass(
-            head_cols(key_blocks, col),
-            head_cols(value_blocks, col),
-            head_cols(row_slabs, col),
-            head_cols(row_slabs, row_width + col),
-            stat_slabs[..., head_index],
-            stat_slabs[..., heads + head_index],
-            permitted,
-            logit_scale,
-        )
-        key_grad_heads.append(key_gradient.reshape(tok_count, HD))
-        value_grad_heads.append(value_gradient.reshape(tok_count, HD))
-    grad_keys = jnp.concatenate(key_grad_heads, axis=-1).astype(jnp.bfloat16)
-    grad_values = jnp.concatenate(value_grad_heads, axis=-1).astype(jnp.bfloat16)
+    grad_keys, grad_values = pl.pallas_call(
+        functools.partial(key_kernel, near_list, far_offsets, heads, devices * blocks_dev),
+        out_shape=(
+            jax.ShapeDtypeStruct((tok_count, row_width), jnp.bfloat16),
+            jax.ShapeDtypeStruct((tok_count, row_width), jnp.bfloat16),
+        ),
+        in_specs=[smem_spec()] + [vmem_spec()] * (7 + 2 * len(far_ahead)),
+        out_specs=(vmem_spec(), vmem_spec()),
+        name="keys_pass",
+    )(
+        position_arr,
+        keys_values,
+        queries_grads,
+        ahead1,
+        ahead2,
+        *far_ahead,
+        stats,
+        stats_one,
+        stats_two,
+        *far_stats,
+    )
     return attended, grad_queries, grad_keys, grad_values
 
 

time: 99.1 us -> 78.1 us (0.79)
  the two profiles are of different devices: /device:TPU:24 before, /device:TPU:0 now
where the time goes in v4:
time: 78.1 us; the launch traced here: 77.7 us
  waiting for transfers between devices  31.3 us (40%)
  Pallas kernels  23.5 us (30%)
  starting transfers between devices  18.4 us (24%)
  local copies, waits for them, and re-layouts  2.54 us (3%)
  other arithmetic  1.15 us (1%)
  between operations  0.87 us (1%)
    ppermute x7, waiting for transfers between devices, passed_along(): lax.ppermute(value, axis, [(source, source + steps) for source in range(f...  25.2 us
    ppermute x7, starting transfers between devices, passed_along(): lax.ppermute(value, axis, [(source, source + steps) for source in range(f...  15.2 us
    pallas_call x1, Pallas kernels, body(): pl.pallas_call(functools.partial(key_kernel, near_list, far_offsets, head...  12.8 us
    pallas_call x1, Pallas kernels, body(): pl.pallas_call(functools.partial(row_kernel, near_list, far_offsets, head...  10.7 us
    ppermute x1, waiting for transfers between devices, body(): swap_two = lax.ppermute(jnp.where(odd, back2, ahead2), 'seq', pairs)  6.15 us
    unnamed x26, local copies, waits for them, and re-layouts  2.5 us
    ppermute x1, starting transfers between devices, body(): lax.ppermute(jnp.where(odd, queries_grads, keys_values), 'seq', pairs)  1.58 us
    ppermute x1, starting transfers between devices, body(): swap_two = lax.ppermute(jnp.where(odd, back2, ahead2), 'seq', pairs)  1.58 us
  transfers between devices with their start and end apart: 9, of which 7 were waited for; matrix products, arithmetic and copies ran while one was open for 2% of the time, Pallas kernels for 14%

profile of v4, /device:TPU:0, one launch (start us, length us, event | category | flops | bytes accessed | tf_op | source)
XLA Modules:
  0.0 77.7 jit_solution(16387581392875301037)
XLA Ops:
  0.6 1.0 %constant_dynamic-update-slice_fusion.1 = bf16[256,1024]{1,0:T(8,128)(2,1)S(1)} fusion(bf16[256,512]{1,0:T(8,128)(2,1)} %param.5), kind=kLoop, calls=%fused_computation.5 | loop fusion | bytes 524288
  1.7 5.1 %collective-permute-start = (bf16[256,1024]{1,0:T(8,128)(2,1)S(1)}, bf16[256,1024]{1,0:T(8,128)(2,1)S(1)}, u32[]{:S(2)}, u32[]{:S(2)}) collective-permute-start(bf16[256,1024]{1,0:T(8,128)(2,1)S(1)} %constant_dynamic-update-slice_fusion.refs_5_.refs_1_), channel_id=1, source_target_pairs={{0,8},{4,12},{8,16},{12,20},{16,24},{20,28},{1,9},{5,13},{9,17},{1... | collective-permute-start | bytes 1572872 | tf_op jit(solution)/shard_map/ppermute | solution.py:24
  6.9 1.3 %collective-permute-start.2 = (bf16[256,1024]{1,0:T(8,128)(2,1)S(1)}, bf16[256,1024]{1,0:T(8,128)(2,1)S(1)}, u32[]{:S(2)}, u32[]{:S(2)}) collective-permute-start(bf16[256,1024]{1,0:T(8,128)(2,1)S(1)} %constant_dynamic-update-slice_fusion.2.refs_2_), channel_id=1, source_target_pairs={{8,0},{12,4},{16,8},{20,12},{24,16},{28,20},{9,1},{13,5},{17,9},{2... | collective-permute-start | bytes 1572872 | tf_op jit(solution)/shard_map/ppermute | solution.py:24
  8.3 0.1 broadcast_select_fusion.3
  8.3 1.6 %collective-permute-start.1 = (bf16[256,1024]{1,0:T(8,128)(2,1)S(1)}, bf16[256,1024]{1,0:T(8,128)(2,1)S(1)}, u32[]{:S(2)}, u32[]{:S(2)}) collective-permute-start(bf16[256,1024]{1,0:T(8,128)(2,1)S(1)} %broadcast_select_fusion.3), channel_id=1, source_target_pairs={{0,4},{4,0},{8,12},{12,8},{16,20},{20,16},{24,28},{28,24},{1,5},{5... | collective-permute-start | bytes 1572872 | tf_op jit(solution)/shard_map/ppermute | solution.py:493
  9.9 8.1 %collective-permute-done.refs_3_ = bf16[256,1024]{1,0:T(8,128)(2,1)S(1)} collective-permute-done((bf16[256,1024]{1,0:T(8,128)(2,1)S(1)}, bf16[256,1024]{1,0:T(8,128)(2,1)S(1)}, u32[]{:S(2)}, u32[]{:S(2)}) %collective-permute-start) | collective-permute-done | bytes 524320 | tf_op jit(solution)/shard_map/ppermute | solution.py:24
  18.0 4.2 %collective-permute-done.2.refs_4_ = bf16[256,1024]{1,0:T(8,128)(2,1)S(1)} collective-permute-done((bf16[256,1024]{1,0:T(8,128)(2,1)S(1)}, bf16[256,1024]{1,0:T(8,128)(2,1)S(1)}, u32[]{:S(2)}, u32[]{:S(2)}) %collective-permute-start.2) | collective-permute-done | bytes 524320 | tf_op jit(solution)/shard_map/ppermute | solution.py:24
  22.2 0.1 broadcast_select_fusion.2
  22.3 1.6 %collective-permute-start.3 = (bf16[256,1024]{1,0:T(8,128)(2,1)S(1)}, bf16[256,1024]{1,0:T(8,128)(2,1)S(1)}, u32[]{:S(2)}, u32[]{:S(2)}) collective-permute-start(bf16[256,1024]{1,0:T(8,128)(2,1)S(1)} %broadcast_select_fusion.2), channel_id=1, source_target_pairs={{0,4},{4,0},{8,12},{12,8},{16,20},{20,16},{24,28},{28,24},{1,5},{5... | collective-permute-start | bytes 1572872 | tf_op jit(solution)/shard_map/ppermute | solution.py:496
  23.9 3.5 %collective-permute-start.4 = (bf16[256,1024]{1,0:T(8,128)(2,1)S(1)}, bf16[256,1024]{1,0:T(8,128)(2,1)S(1)}, u32[]{:S(2)}, u32[]{:S(2)}) collective-permute-start(bf16[256,1024]{1,0:T(8,128)(2,1)S(1)} %collective-permute-done.refs_3_), channel_id=1, source_target_pairs={{0,8},{4,12},{8,16},{12,20},{16,24},{20,28},{1,9},{5,13},{9,17},{1... | collective-permute-start | bytes 1572872 | tf_op jit(solution)/shard_map/ppermute | solution.py:24
  27.3 1.3 %collective-permute-start.5 = (bf16[256,1024]{1,0:T(8,128)(2,1)S(1)}, bf16[256,1024]{1,0:T(8,128)(2,1)S(1)}, u32[]{:S(2)}, u32[]{:S(2)}) collective-permute-start(bf16[256,1024]{1,0:T(8,128)(2,1)S(1)} %collective-permute-done.2.refs_4_), channel_id=1, source_target_pairs={{8,0},{12,4},{16,8},{20,12},{24,16},{28,20},{9,1},{13,5},{17,9},{2... | collective-permute-start | bytes 1572872 | tf_op jit(solution)/shard_map/ppermute | solution.py:24
  28.7 6.1 %collective-permute-done.3 = bf16[256,1024]{1,0:T(8,128)(2,1)S(1)} collective-permute-done((bf16[256,1024]{1,0:T(8,128)(2,1)S(1)}, bf16[256,1024]{1,0:T(8,128)(2,1)S(1)}, u32[]{:S(2)}, u32[]{:S(2)}) %collective-permute-start.3) | collective-permute-done | bytes 524320 | tf_op jit(solution)/shard_map/ppermute | solution.py:496
  34.8 1.0 %broadcast_select_fusion = (bf16[256,1024]{1,0:T(8,128)(2,1)}, bf16[256,1024]{1,0:T(8,128)(2,1)}) fusion(bf16[256,1024]{1,0:T(8,128)(2,1)S(1)} %collective-permute-done.3, bf16[256,1024]{1,0:T(8,128)(2,1)S(1)} %collective-permute-done.1, pred[]{:T(512)S(6)} %eq.5), kind=kLoop, calls=%fused_computation | loop fusion | flops 524288 | bytes 2097153 | tf_op jit(solution)/shard_map/jit(_where)/select_n | solution.py:498
  35.8 1.2 %collective-permute-done.4.refs_6_ = bf16[256,1024]{1,0:T(8,128)(2,1)S(1)} collective-permute-done((bf16[256,1024]{1,0:T(8,128)(2,1)S(1)}, bf16[256,1024]{1,0:T(8,128)(2,1)S(1)}, u32[]{:S(2)}, u32[]{:S(2)}) %collective-permute-start.4) | collective-permute-done | bytes 524320 | tf_op jit(solution)/shard_map/ppermute | solution.py:24
  37.0 0.8 %copy-done.7 = bf16[256,1024]{1,0:T(8,128)(2,1)} copy-done((bf16[256,1024]{1,0:T(8,128)(2,1)}, bf16[256,1024]{1,0:T(8,128)(2,1)S(1)}, u32[]{:S(2)}) %copy-start.7) | copy-done | bytes 524312
  37.8 10.7 %rows_pass.1 = (bf16[256,512]{1,0:T(8,128)(2,1)}, bf16[256,512]{1,0:T(8,128)(2,1)}, f32[256,8]{1,0:T(8,128)}) custom-call(s32[1]{0:T(128)} %bitcast.refs_0_, bf16[256,512]{1,0:T(8,128)(2,1)} %refs_1_.1, bf16[256,512]{1,0:T(8,128)(2,1)} %refs_2_.1, bf16[256,1024]{1,0:T(8,128)(2,1)} %copy-done.3, bf16[256,1024]{1,0:T(8,128)(2,1)} %get-tuple-element.15.refs_4_, ...), custom_call_target="tpu_custom_call" | custom-call | tf_op jit(solution)/shard_map/rows_pass/pallas_call | solution.py:506
  48.4 1.3 %collective-permute-start.6 = (f32[256,8]{1,0:T(8,128)}, f32[256,8]{1,0:T(8,128)S(1)}, u32[]{:S(2)}, u32[]{:S(2)}) collective-permute-start(f32[256,8]{1,0:T(8,128)} %get-tuple-element.11.refs_6_), channel_id=1, source_target_pairs={{4,0},{8,4},{12,8},{16,12},{20,16},{24,20},{28,24},{5,1},{9,5},{13... | collective-permute-start | bytes 24584 | tf_op jit(solution)/shard_map/ppermute | solution.py:24
  49.7 1.3 %collective-permute-start.7 = (f32[256,8]{1,0:T(8,128)}, f32[256,8]{1,0:T(8,128)S(1)}, u32[]{:S(2)}, u32[]{:S(2)}) collective-permute-start(f32[256,8]{1,0:T(8,128)} %get-tuple-element.11.refs_6_), channel_id=1, source_target_pairs={{8,0},{12,4},{16,8},{20,12},{24,16},{28,20},{9,1},{13,5},{17,9},{2... | collective-permute-start | bytes 24584 | tf_op jit(solution)/shard_map/ppermute | solution.py:24
  51.0 1.5 %collective-permute-start.8 = (f32[256,8]{1,0:T(8,128)}, f32[256,8]{1,0:T(8,128)S(1)}, u32[]{:S(2)}, u32[]{:S(2)}) collective-permute-start(f32[256,8]{1,0:T(8,128)} %get-tuple-element.11.refs_6_), channel_id=1, source_target_pairs={{16,0},{20,4},{24,8},{28,12},{17,1},{21,5},{25,9},{29,13},{18,2},{... | collective-permute-start | bytes 24584 | tf_op jit(solution)/shard_map/ppermute | solution.py:24
  52.5 3.0 %collective-permute-done.6.refs_7_ = f32[256,8]{1,0:T(8,128)S(1)} collective-permute-done((f32[256,8]{1,0:T(8,128)}, f32[256,8]{1,0:T(8,128)S(1)}, u32[]{:S(2)}, u32[]{:S(2)}) %collective-permute-start.6) | collective-permute-done | bytes 8224 | tf_op jit(solution)/shard_map/ppermute | solution.py:24
  55.5 3.1 %collective-permute-done.7.refs_8_ = f32[256,8]{1,0:T(8,128)S(1)} collective-permute-done((f32[256,8]{1,0:T(8,128)}, f32[256,8]{1,0:T(8,128)S(1)}, u32[]{:S(2)}, u32[]{:S(2)}) %collective-permute-start.7) | collective-permute-done | bytes 8224 | tf_op jit(solution)/shard_map/ppermute | solution.py:24
  58.6 5.6 %collective-permute-done.8.refs_9_ = f32[256,8]{1,0:T(8,128)S(1)} collective-permute-done((f32[256,8]{1,0:T(8,128)}, f32[256,8]{1,0:T(8,128)S(1)}, u32[]{:S(2)}, u32[]{:S(2)}) %collective-permute-start.8) | collective-permute-done | bytes 8224 | tf_op jit(solution)/shard_map/ppermute | solution.py:24
  64.3 0.6 copy-done.11
  64.9 12.8 %keys_pass.1 = (bf16[256,512]{1,0:T(8,128)(2,1)}, bf16[256,512]{1,0:T(8,128)(2,1)}) custom-call(s32[1]{0:T(128)} %bitcast.refs_0_, bf16[256,1024]{1,0:T(8,128)(2,1)} %copy-done, bf16[256,1024]{1,0:T(8,128)(2,1)} %copy-done.1, bf16[256,1024]{1,0:T(8,128)(2,1)} %get-tuple-element.14.refs_3_, bf16[256,1024]{1,0:T(8,128)(2,1)} %copy-done.2, ...), custom_call_target="tpu_custom_call" | custom-call | tf_op jit(solution)/shard_map/keys_pass/pallas_call | solution.py:520
  (27 shorter events, 0.1 us)
Async XLA Ops:
  0.6 1.0 %copy-start.8 = (bf16[256,512]{1,0:T(8,128)(2,1)S(1)}, bf16[256,512]{1,0:T(8,128)(2,1)}, u32[]{:S(2)}) copy-start(bf16[256,512]{1,0:T(8,128)(2,1)} %param.6) | copy-start | bytes 786436
  1.7 5.2 %copy-start.4 = (bf16[256,512]{1,0:T(8,128)(2,1)S(1)}, bf16[256,512]{1,0:T(8,128)(2,1)}, u32[]{:S(2)}) copy-start(bf16[256,512]{1,0:T(8,128)(2,1)} %refs_1_.1) | copy-start | bytes 786436
  1.7 6.5 %copy-start = (bf16[256,1024]{1,0:T(8,128)(2,1)}, bf16[256,1024]{1,0:T(8,128)(2,1)S(1)}, u32[]{:S(2)}) copy-start(bf16[256,1024]{1,0:T(8,128)(2,1)S(1)} %constant_dynamic-update-slice_fusion.refs_5_.refs_1_) | copy-start | bytes 1572868
  1.7 5.2 %copy-start.5 = (bf16[256,512]{1,0:T(8,128)(2,1)S(1)}, bf16[256,512]{1,0:T(8,128)(2,1)}, u32[]{:S(2)}) copy-start(bf16[256,512]{1,0:T(8,128)(2,1)} %refs_2_.1) | copy-start | bytes 786436
  1.7 16.2 %collective-permute-start = (bf16[256,1024]{1,0:T(8,128)(2,1)S(1)}, bf16[256,1024]{1,0:T(8,128)(2,1)S(1)}, u32[]{:S(2)}, u32[]{:S(2)}) collective-permute-start(bf16[256,1024]{1,0:T(8,128)(2,1)S(1)} %constant_dynamic-update-slice_fusion.refs_5_.refs_1_), channel_id=1, source_target_pairs={{0,8},{4,12},{8,16},{12,20},{16,24},{20,28},{1,9},{5,13},{9,17},{1... | collective-permute-start | bytes 1572872 | tf_op jit(solution)/shard_map/ppermute | solution.py:24
  6.9 1.4 %copy-start.1 = (bf16[256,1024]{1,0:T(8,128)(2,1)}, bf16[256,1024]{1,0:T(8,128)(2,1)S(1)}, u32[]{:S(2)}) copy-start(bf16[256,1024]{1,0:T(8,128)(2,1)S(1)} %constant_dynamic-update-slice_fusion.2.refs_2_) | copy-start | bytes 1572868
  6.9 15.3 %collective-permute-start.2 = (bf16[256,1024]{1,0:T(8,128)(2,1)S(1)}, bf16[256,1024]{1,0:T(8,128)(2,1)S(1)}, u32[]{:S(2)}, u32[]{:S(2)}) collective-permute-start(bf16[256,1024]{1,0:T(8,128)(2,1)S(1)} %constant_dynamic-update-slice_fusion.2.refs_2_), channel_id=1, source_target_pairs={{8,0},{12,4},{16,8},{20,12},{24,16},{28,20},{9,1},{13,5},{17,9},{2... | collective-permute-start | bytes 1572872 | tf_op jit(solution)/shard_map/ppermute | solution.py:24
  8.3 20.3 %collective-permute-start.1 = (bf16[256,1024]{1,0:T(8,128)(2,1)S(1)}, bf16[256,1024]{1,0:T(8,128)(2,1)S(1)}, u32[]{:S(2)}, u32[]{:S(2)}) collective-permute-start(bf16[256,1024]{1,0:T(8,128)(2,1)S(1)} %broadcast_select_fusion.3), channel_id=1, source_target_pairs={{0,4},{4,0},{8,12},{12,8},{16,20},{20,16},{24,28},{28,24},{1,5},{5... | collective-permute-start | bytes 1572872 | tf_op jit(solution)/shard_map/ppermute | solution.py:493
  18.0 5.9 %copy-start.3 = (bf16[256,1024]{1,0:T(8,128)(2,1)}, bf16[256,1024]{1,0:T(8,128)(2,1)S(1)}, u32[]{:S(2)}) copy-start(bf16[256,1024]{1,0:T(8,128)(2,1)S(1)} %collective-permute-done.refs_3_) | copy-start | bytes 1572868
  22.2 5.1 %copy-start.2 = (bf16[256,1024]{1,0:T(8,128)(2,1)}, bf16[256,1024]{1,0:T(8,128)(2,1)S(1)}, u32[]{:S(2)}) copy-start(bf16[256,1024]{1,0:T(8,128)(2,1)S(1)} %collective-permute-done.2.refs_4_) | copy-start | bytes 1572868
  22.3 12.5 %collective-permute-start.3 = (bf16[256,1024]{1,0:T(8,128)(2,1)S(1)}, bf16[256,1024]{1,0:T(8,128)(2,1)S(1)}, u32[]{:S(2)}, u32[]{:S(2)}) collective-permute-start(bf16[256,1024]{1,0:T(8,128)(2,1)S(1)} %broadcast_select_fusion.2), channel_id=1, source_target_pairs={{0,4},{4,0},{8,12},{12,8},{16,20},{20,16},{24,28},{28,24},{1,5},{5... | collective-permute-start | bytes 1572872 | tf_op jit(solution)/shard_map/ppermute | solution.py:496
  23.9 13.1 %collective-permute-start.4 = (bf16[256,1024]{1,0:T(8,128)(2,1)S(1)}, bf16[256,1024]{1,0:T(8,128)(2,1)S(1)}, u32[]{:S(2)}, u32[]{:S(2)}) collective-permute-start(bf16[256,1024]{1,0:T(8,128)(2,1)S(1)} %collective-permute-done.refs_3_), channel_id=1, source_target_pairs={{0,8},{4,12},{8,16},{12,20},{16,24},{20,28},{1,9},{5,13},{9,17},{1... | collective-permute-start | bytes 1572872 | tf_op jit(solution)/shard_map/ppermute | solution.py:24
  27.3 25.2 %collective-permute-start.5 = (bf16[256,1024]{1,0:T(8,128)(2,1)S(1)}, bf16[256,1024]{1,0:T(8,128)(2,1)S(1)}, u32[]{:S(2)}, u32[]{:S(2)}) collective-permute-start(bf16[256,1024]{1,0:T(8,128)(2,1)S(1)} %collective-permute-done.2.refs_4_), channel_id=1, source_target_pairs={{8,0},{12,4},{16,8},{20,12},{24,16},{28,20},{9,1},{13,5},{17,9},{2... | collective-permute-start | bytes 1572872 | tf_op jit(solution)/shard_map/ppermute | solution.py:24
  37.0 0.8 %copy-start.7 = (bf16[256,1024]{1,0:T(8,128)(2,1)}, bf16[256,1024]{1,0:T(8,128)(2,1)S(1)}, u32[]{:S(2)}) copy-start(bf16[256,1024]{1,0:T(8,128)(2,1)S(1)} %collective-permute-done.4.refs_6_) | copy-start | bytes 1572868
  48.4 7.1 %collective-permute-start.6 = (f32[256,8]{1,0:T(8,128)}, f32[256,8]{1,0:T(8,128)S(1)}, u32[]{:S(2)}, u32[]{:S(2)}) collective-permute-start(f32[256,8]{1,0:T(8,128)} %get-tuple-element.11.refs_6_), channel_id=1, source_target_pairs={{4,0},{8,4},{12,8},{16,12},{20,16},{24,20},{28,24},{5,1},{9,5},{13... | collective-permute-start | bytes 24584 | tf_op jit(solution)/shard_map/ppermute | solution.py:24
  49.7 8.9 %collective-permute-start.7 = (f32[256,8]{1,0:T(8,128)}, f32[256,8]{1,0:T(8,128)S(1)}, u32[]{:S(2)}, u32[]{:S(2)}) collective-permute-start(f32[256,8]{1,0:T(8,128)} %get-tuple-element.11.refs_6_), channel_id=1, source_target_pairs={{8,0},{12,4},{16,8},{20,12},{24,16},{28,20},{9,1},{13,5},{17,9},{2... | collective-permute-start | bytes 24584 | tf_op jit(solution)/shard_map/ppermute | solution.py:24
  51.0 13.2 %collective-permute-start.8 = (f32[256,8]{1,0:T(8,128)}, f32[256,8]{1,0:T(8,128)S(1)}, u32[]{:S(2)}, u32[]{:S(2)}) collective-permute-start(f32[256,8]{1,0:T(8,128)} %get-tuple-element.11.refs_6_), channel_id=1, source_target_pairs={{16,0},{20,4},{24,8},{28,12},{17,1},{21,5},{25,9},{29,13},{18,2},{... | collective-permute-start | bytes 24584 | tf_op jit(solution)/shard_map/ppermute | solution.py:24
  52.5 11.7 %copy-start.6 = (bf16[256,1024]{1,0:T(8,128)(2,1)}, bf16[256,1024]{1,0:T(8,128)(2,1)S(1)}, u32[]{:S(2)}) copy-start(bf16[256,1024]{1,0:T(8,128)(2,1)S(1)} %collective-permute-done.5.refs_5_) | copy-start | bytes 1572868
  55.5 8.8 %copy-start.9 = (f32[256,8]{1,0:T(8,128)}, f32[256,8]{1,0:T(8,128)S(1)}, u32[]{:S(2)}) copy-start(f32[256,8]{1,0:T(8,128)S(1)} %collective-permute-done.6.refs_7_) | copy-start | bytes 24580
  58.6 5.6 %copy-start.10 = (f32[256,8]{1,0:T(8,128)}, f32[256,8]{1,0:T(8,128)S(1)}, u32[]{:S(2)}) copy-start(f32[256,8]{1,0:T(8,128)S(1)} %collective-permute-done.7.refs_8_) | copy-start | bytes 24580
  64.2 0.6 copy-start.11

commit v5 on v4

--- a/solution.py
+++ b/solution.py
@@ -334,54 +334,50 @@
 TRANS_B = (((1,), (1,)), ((), ()))
 
 
-def row_kernel(near_list, far_list, heads, *refs):
+def row_kernel(near_count, far_list, heads, *refs):
     far_count = len(far_list)
-    position_ref, query_ref, grad_ref, back2_ref, back1_ref, own_ref = refs[:6]
-    far_refs = refs[6 : 6 + far_count]
-    attended_ref, grad_query_ref, stats_ref = refs[6 + far_count :]
-    span = (back2_ref, back1_ref, own_ref)
+    position_ref, query_ref, grad_ref, span_ref = refs[:4]
+    far_refs = refs[4 : 4 + far_count]
+    attended_ref, grad_query_ref, stats_ref = refs[4 + far_count :]
     width = heads * HD
+    near_rows = near_count * BLK
     scale = 1.0 / math.sqrt(HD)
     first = 2 * position_ref[0]
-    row_ids = lax.broadcasted_iota(jnp.int32, (BLK, BLK), 0)
-    col_ids = lax.broadcasted_iota(jnp.int32, (BLK, BLK), 1)
-    causal = row_ids >= col_ids
+    near_row_ids = lax.broadcasted_iota(jnp.int32, (BLK, near_rows), 0)
+    near_col_ids = lax.broadcasted_iota(jnp.int32, (BLK, near_rows), 1)
+    near_offset = (near_count - 1) - near_col_ids // BLK
+    near_causal = jnp.logical_or(near_offset > 0, near_row_ids >= near_col_ids % BLK)
     lane_ids = lax.broadcasted_iota(jnp.int32, (BLK, 2 * heads), 1)
     for block in range(2):
         rows = pl.ds(block * BLK, BLK)
-        slabs = []
-        for offset in near_list:
-            index = 4 + block - offset
-            slabs.append((span[index // 2], (index % 2) * BLK, offset))
-        for level, offset in enumerate(far_list):
-            slabs.append((far_refs[level], block * BLK, offset))
+        near_span = pl.ds(block * BLK, near_rows)
+        near_mask = jnp.logical_and(near_causal, first + block - near_offset >= 0)
+        far_live = [first + block - offset >= 0 for offset in far_list]
         stats_tile = jnp.zeros((BLK, 2 * heads), jnp.float32)
         for head in range(heads):
             cols = pl.ds(head * HD, HD)
             value_cols = pl.ds(width + head * HD, HD)
             query = query_ref[rows, cols]
             grad = grad_ref[rows, cols]
+            keys = [span_ref[near_span, cols]] + [item[rows, cols] for item in far_refs]
+            values = [span_ref[near_span, value_cols]] + [item[rows, value_cols] for item in far_refs]
+            masks = [near_mask] + far_live
             scores = []
-            for source, start, offset in slabs:
-                key = source[pl.ds(start, BLK), cols]
+            for key, mask in zip(keys, masks):
                 score = lax.dot_general(query, key, TRANS_B, preferred_element_type=jnp.float32)
-                score = score * scale
-                live = first + block - offset >= 0
-                mask = jnp.logical_and(causal, live) if offset == 0 else jnp.logical_and(
-                    row_ids >= 0, live
-                )
-                scores.append(jnp.where(mask, score, NEG))
+                scores.append(jnp.where(mask, score * scale, NEG))
             row_max = scores[0].max(axis=-1, keepdims=True)
             for score in scores[1:]:
                 row_max = jnp.maximum(row_max, score.max(axis=-1, keepdims=True))
-            row_sum = jnp.exp(scores[0] - row_max).sum(axis=-1, keepdims=True)
-            for score in scores[1:]:
-                row_sum = row_sum + jnp.exp(score - row_max).sum(axis=-1, keepdims=True)
+            shifted = [jnp.exp(score - row_max) for score in scores]
+            row_sum = shifted[0].sum(axis=-1, keepdims=True)
+            for item in shifted[1:]:
+                row_sum = row_sum + item.sum(axis=-1, keepdims=True)
             log_total = row_max + jnp.log(row_sum)
-            probs = [jnp.exp(score - log_total) for score in scores]
+            inverse = 1.0 / row_sum
+            probs = [item * inverse for item in shifted]
             attended = jnp.zeros((BLK, HD), jnp.float32)
-            for prob, (source, start, offset) in zip(probs, slabs):
-                value = source[pl.ds(start, BLK), value_cols]
+            for prob, value in zip(probs, values):
                 attended = attended + jnp.dot(
                     prob.astype(jnp.bfloat16), value, preferred_element_type=jnp.float32
                 )
@@ -391,9 +387,7 @@
                 grad.astype(jnp.float32) * attended.astype(jnp.float32), axis=-1, keepdims=True
             )
             grad_query = jnp.zeros((BLK, HD), jnp.float32)
-            for prob, (source, start, offset) in zip(probs, slabs):
-                value = source[pl.ds(start, BLK), value_cols]
-                key = source[pl.ds(start, BLK), cols]
+            for prob, key, value in zip(probs, keys, values):
                 prob_grad = lax.dot_general(grad, value, TRANS_B, preferred_element_type=jnp.float32)
                 score_grad = (prob * (prob_grad - out_dot)).astype(jnp.bfloat16)
                 grad_query = grad_query + jnp.dot(
@@ -405,52 +399,44 @@
         stats_ref[rows, :] = stats_tile
 
 
-def key_kernel(near_list, far_list, heads, block_total, *refs):
+def key_kernel(near_count, far_list, heads, block_total, *refs):
     far_count = len(far_list)
-    position_ref, own_ref, rows0_ref, rows1_ref, rows2_ref = refs[:5]
-    far_rows = refs[5 : 5 + far_count]
-    stats0_ref, stats1_ref, stats2_ref = refs[5 + far_count : 8 + far_count]
-    far_stats = refs[8 + far_count : 8 + 2 * far_count]
-    grad_key_ref, grad_value_ref = refs[8 + 2 * far_count :]
-    span_rows = (rows0_ref, rows1_ref, rows2_ref)
-    span_stats = (stats0_ref, stats1_ref, stats2_ref)
+    position_ref, own_ref, span_ref, stats_span_ref = refs[:4]
+    far_rows = refs[4 : 4 + far_count]
+    far_stats = refs[4 + far_count : 4 + 2 * far_count]
+    grad_key_ref, grad_value_ref = refs[4 + 2 * far_count :]
     width = heads * HD
+    near_rows = near_count * BLK
     scale = 1.0 / math.sqrt(HD)
     first = 2 * position_ref[0]
-    row_ids = lax.broadcasted_iota(jnp.int32, (BLK, BLK), 0)
-    col_ids = lax.broadcasted_iota(jnp.int32, (BLK, BLK), 1)
-    causal = row_ids >= col_ids
-    lane_ids = lax.broadcasted_iota(jnp.int32, (BLK, 2 * heads), 1)
+    near_row_ids = lax.broadcasted_iota(jnp.int32, (near_rows, BLK), 0)
+    near_col_ids = lax.broadcasted_iota(jnp.int32, (near_rows, BLK), 1)
+    near_offset = near_row_ids // BLK
+    near_causal = jnp.logical_or(near_offset > 0, near_row_ids % BLK >= near_col_ids)
+    near_lanes = lax.broadcasted_iota(jnp.int32, (near_rows, 2 * heads), 1)
+    far_lanes = lax.broadcasted_iota(jnp.int32, (BLK, 2 * heads), 1)
     for block in range(2):
         rows = pl.ds(block * BLK, BLK)
-        slabs = []
-        for offset in near_list:
-            index = block + offset
-            slabs.append((span_rows[index // 2], span_stats[index // 2], (index % 2) * BLK, offset))
-        for level, offset in enumerate(far_list):
-            slabs.append((far_rows[level], far_stats[level], block * BLK, offset))
+        near_span = pl.ds(block * BLK, near_rows)
+        near_mask = jnp.logical_and(near_causal, first + block + near_offset < block_total)
+        far_live = [first + block + offset < block_total for offset in far_list]
+        masks = [near_mask] + far_live
+        stat_tiles = [stats_span_ref[near_span, :]] + [item[rows, :] for item in far_stats]
+        lanes = [near_lanes] + [far_lanes] * far_count
         for head in range(heads):
             cols = pl.ds(head * HD, HD)
             value_cols = pl.ds(width + head * HD, HD)
             key = own_ref[rows, cols]
             value = own_ref[rows, value_cols]
+            queries = [span_ref[near_span, cols]] + [item[rows, cols] for item in far_rows]
+            grads = [span_ref[near_span, value_cols]] + [item[rows, value_cols] for item in far_rows]
             grad_key = jnp.zeros((BLK, HD), jnp.float32)
             grad_value = jnp.zeros((BLK, HD), jnp.float32)
-            for source, stats, start, offset in slabs:
-                query = source[pl.ds(start, BLK), cols]
-                grad = source[pl.ds(start, BLK), value_cols]
-                tile = stats[pl.ds(start, BLK), :]
-                log_total = jnp.sum(jnp.where(lane_ids == head, tile, 0.0), axis=-1, keepdims=True)
-                out_dot = jnp.sum(
-                    jnp.where(lane_ids == heads + head, tile, 0.0), axis=-1, keepdims=True
-                )
+            for query, grad, tile, lane, mask in zip(queries, grads, stat_tiles, lanes, masks):
+                log_total = jnp.sum(jnp.where(lane == head, tile, 0.0), axis=-1, keepdims=True)
+                out_dot = jnp.sum(jnp.where(lane == heads + head, tile, 0.0), axis=-1, keepdims=True)
                 score = lax.dot_general(query, key, TRANS_B, preferred_element_type=jnp.float32)
-                score = score * scale
-                live = first + block + offset < block_total
-                mask = jnp.logical_and(causal, live) if offset == 0 else jnp.logical_and(
-                    row_ids >= 0, live
-                )
-                prob = jnp.where(mask, jnp.exp(score - log_total), 0.0)
+                prob = jnp.where(mask, jnp.exp(score * scale - log_total), 0.0)
                 prob_grad = lax.dot_general(grad, value, TRANS_B, preferred_element_type=jnp.float32)
                 score_grad = prob * (prob_grad - out_dot)
                 grad_value = grad_value + jnp.dot(
@@ -504,38 +490,40 @@
     position_arr = jnp.reshape(position, (1,)).astype(jnp.int32)
     far_offsets = list(far_list)
     attended, grad_queries, stats = pl.pallas_call(
-        functools.partial(row_kernel, near_list, far_offsets, heads),
+        functools.partial(row_kernel, len(near_list), far_offsets, heads),
         out_shape=(
             jax.ShapeDtypeStruct((tok_count, row_width), jnp.bfloat16),
             jax.ShapeDtypeStruct((tok_count, row_width), jnp.bfloat16),
             jax.ShapeDtypeStruct((tok_count, 2 * heads), jnp.float32),
         ),
-        in_specs=[smem_spec()] + [vmem_spec()] * (5 + len(far_back)),
+        in_specs=[smem_spec()] + [vmem_spec()] * (3 + len(far_back)),
         out_specs=(vmem_spec(), vmem_spec(), vmem_spec()),
         name="rows_pass",
-    )(position_arr, queries, grad_out, back2, back1, keys_values, *far_back)
+    )(
+        position_arr,
+        queries,
+        grad_out,
+        jnp.concatenate([back2, back1, keys_values], axis=0),
+        *far_back,
+    )
     stats_one = passed_along(stats, "seq", -1)
     stats_two = passed_along(stats, "seq", -2)
     far_stats = [passed_along(stats, "seq", -shift) for shift in far_shifts]
     grad_keys, grad_values = pl.pallas_call(
-        functools.partial(key_kernel, near_list, far_offsets, heads, devices * blocks_dev),
+        functools.partial(key_kernel, len(near_list), far_offsets, heads, devices * blocks_dev),
         out_shape=(
             jax.ShapeDtypeStruct((tok_count, row_width), jnp.bfloat16),
             jax.ShapeDtypeStruct((tok_count, row_width), jnp.bfloat16),
         ),
-        in_specs=[smem_spec()] + [vmem_spec()] * (7 + 2 * len(far_ahead)),
+        in_specs=[smem_spec()] + [vmem_spec()] * (3 + 2 * len(far_ahead)),
         out_specs=(vmem_spec(), vmem_spec()),
         name="keys_pass",
     )(
         position_arr,
         keys_values,
-        queries_grads,
-        ahead1,
-        ahead2,
+        jnp.concatenate([queries_grads, ahead1, ahead2], axis=0),
+        jnp.concatenate([stats, stats_one, stats_two], axis=0),
         *far_ahead,
-        stats,
-        stats_one,
-        stats_two,
         *far_stats,
     )
     return attended, grad_queries, grad_keys, grad_values

time: 78.1 us -> 72 us (0.922)
  Pallas kernels: 23.5 us -> 15.6 us
  other arithmetic: 1.15 us -> 3.56 us
  waiting for transfers between devices: 31.3 us -> 29.1 us
  local copies, waits for them, and re-layouts: 2.54 us -> 4.47 us
    pallas_call x2, Pallas kernels: 23.5 us -> 15.6 us  [the longest x1 8.5 us: body(): pl.pallas_call(functools.partial(row_kernel, len(near_list), far_offsets,...]
    concatenate x0 -> x3, other arithmetic: none -> 3.37 us  [the longest x1 1.29 us: body(): jnp.concatenate([back2, back1, keys_values], axis=0)]
    ppermute x7, waiting for transfers between devices: 25.2 us -> 22.9 us  [passed_along(): lax.ppermute(value, axis, [(source, source + steps) for source in range(f...]
    unnamed x26 -> x14, local copies, waits for them, and re-layouts: 2.5 us -> 3.47 us
    select_n x1, other arithmetic: 1.04 us -> 0.07 us  [body(): ahead1 = jnp.where(odd, swap_two, swap_one)]
    concatenate x1, local copies, waits for them, and re-layouts: 0.02 us -> 0.98 us  [body(): keys_values = jnp.concatenate([key_tokens, value_tokens], axis=1)]
  transfers between devices with their start and end apart: 9 -> 9, of which waited for: 7 -> 7; matrix products, arithmetic and copies ran while one was open for 2% -> 6% of each run, Pallas kernels for 14% -> 12%
where the time goes in v5:
time: 72 us; the launch traced here: 71.6 us
  waiting for transfers between devices  29.1 us (40%)
  starting transfers between devices  18.1 us (25%)
  Pallas kernels  15.6 us (22%)
  local copies, waits for them, and re-layouts  4.47 us (6%)
  other arithmetic  3.56 us (5%)
  between operations  0.8 us (1%)
    ppermute x7, waiting for transfers between devices, passed_along(): lax.ppermute(value, axis, [(source, source + steps) for source in range(f...  22.9 us
    ppermute x7, starting transfers between devices, passed_along(): lax.ppermute(value, axis, [(source, source + steps) for source in range(f...  14.9 us
    pallas_call x1, Pallas kernels, body(): pl.pallas_call(functools.partial(row_kernel, len(near_list), far_offsets,...  8.5 us
    pallas_call x1, Pallas kernels, body(): pl.pallas_call(functools.partial(key_kernel, len(near_list), far_offsets,...  7.14 us
    ppermute x1, waiting for transfers between devices, body(): swap_two = lax.ppermute(jnp.where(odd, back2, ahead2), 'seq', pairs)  6.16 us
    unnamed x14, local copies, waits for them, and re-layouts  3.47 us
    ppermute x1, starting transfers between devices, body(): lax.ppermute(jnp.where(odd, queries_grads, keys_values), 'seq', pairs)  1.58 us
    ppermute x1, starting transfers between devices, body(): swap_two = lax.ppermute(jnp.where(odd, back2, ahead2), 'seq', pairs)  1.58 us
  transfers between devices with their start and end apart: 9, of which 7 were waited for; matrix products, arithmetic and copies ran while one was open for 6% of the time, Pallas kernels for 12%

profile of v5, /device:TPU:0, one launch (start us, length us, event | category | flops | bytes accessed | tf_op | source)
XLA Modules:
  0.0 71.6 jit_solution(2958796290833449408)
XLA Ops:
  0.6 1.0 %constant_dynamic-update-slice_fusion.1 = bf16[256,1024]{1,0:T(8,128)(2,1)S(1)} fusion(bf16[256,512]{1,0:T(8,128)(2,1)} %param.5), kind=kLoop, calls=%fused_computation.8 | loop fusion | bytes 524288
  1.7 1.0 %constant_dynamic-update-slice_fusion.refs_1_ = bf16[256,1024]{1,0:T(8,128)(2,1)S(1)} fusion(bf16[256,1024]{1,0:T(8,128)(2,1)S(1)} %constant_dynamic-update-slice_fusion.1, bf16[256,512]{1,0:T(8,128)(2,1)} %param.6), kind=kLoop, calls=%fused_computation.7 | loop fusion | bytes 524288 | tf_op jit(solution)/shard_map/concatenate | solution.py:475
  2.7 5.0 %collective-permute-start = (bf16[256,1024]{1,0:T(8,128)(2,1)S(1)}, bf16[256,1024]{1,0:T(8,128)(2,1)S(1)}, u32[]{:S(2)}, u32[]{:S(2)}) collective-permute-start(bf16[256,1024]{1,0:T(8,128)(2,1)S(1)} %constant_dynamic-update-slice_fusion.refs_1_), channel_id=1, source_target_pairs={{0,8},{4,12},{8,16},{12,20},{16,24},{20,28},{1,9},{5,13},{9,17},{1... | collective-permute-start | bytes 1572872 | tf_op jit(solution)/shard_map/ppermute | solution.py:24
  7.6 1.0 %constant_dynamic-update-slice_fusion.3 = bf16[256,1024]{1,0:T(8,128)(2,1)S(1)} fusion(bf16[256,512]{1,0:T(8,128)(2,1)} %refs_1_.1), kind=kLoop, calls=%fused_computation.10 | loop fusion | bytes 524288
  8.7 1.3 %collective-permute-start.2 = (bf16[256,1024]{1,0:T(8,128)(2,1)S(1)}, bf16[256,1024]{1,0:T(8,128)(2,1)S(1)}, u32[]{:S(2)}, u32[]{:S(2)}) collective-permute-start(bf16[256,1024]{1,0:T(8,128)(2,1)S(1)} %constant_dynamic-update-slice_fusion.2), channel_id=1, source_target_pairs={{8,0},{12,4},{16,8},{20,12},{24,16},{28,20},{9,1},{13,5},{17,9},{2... | collective-permute-start | bytes 1572872 | tf_op jit(solution)/shard_map/ppermute | solution.py:24
  10.0 1.6 %collective-permute-start.1 = (bf16[256,1024]{1,0:T(8,128)(2,1)S(1)}, bf16[256,1024]{1,0:T(8,128)(2,1)S(1)}, u32[]{:S(2)}, u32[]{:S(2)}) collective-permute-start(bf16[256,1024]{1,0:T(8,128)(2,1)S(1)} %broadcast_select_fusion.3), channel_id=1, source_target_pairs={{0,4},{4,0},{8,12},{12,8},{16,20},{20,16},{24,28},{28,24},{1,5},{5... | collective-permute-start | bytes 1572872 | tf_op jit(solution)/shard_map/ppermute | solution.py:479
  11.6 7.1 %collective-permute-done = bf16[256,1024]{1,0:T(8,128)(2,1)S(1)} collective-permute-done((bf16[256,1024]{1,0:T(8,128)(2,1)S(1)}, bf16[256,1024]{1,0:T(8,128)(2,1)S(1)}, u32[]{:S(2)}, u32[]{:S(2)}) %collective-permute-start) | collective-permute-done | bytes 524320 | tf_op jit(solution)/shard_map/ppermute | solution.py:24
  18.8 5.2 %collective-permute-done.2 = bf16[256,1024]{1,0:T(8,128)(2,1)S(1)} collective-permute-done((bf16[256,1024]{1,0:T(8,128)(2,1)S(1)}, bf16[256,1024]{1,0:T(8,128)(2,1)S(1)}, u32[]{:S(2)}, u32[]{:S(2)}) %collective-permute-start.2) | collective-permute-done | bytes 524320 | tf_op jit(solution)/shard_map/ppermute | solution.py:24
  24.0 1.6 %collective-permute-start.3 = (bf16[256,1024]{1,0:T(8,128)(2,1)S(1)}, bf16[256,1024]{1,0:T(8,128)(2,1)S(1)}, u32[]{:S(2)}, u32[]{:S(2)}) collective-permute-start(bf16[256,1024]{1,0:T(8,128)(2,1)S(1)} %broadcast_select_fusion.2), channel_id=1, source_target_pairs={{0,4},{4,0},{8,12},{12,8},{16,20},{20,16},{24,28},{28,24},{1,5},{5... | collective-permute-start | bytes 1572872 | tf_op jit(solution)/shard_map/ppermute | solution.py:482
  25.6 3.5 %collective-permute-start.4 = (bf16[256,1024]{1,0:T(8,128)(2,1)S(1)}, bf16[256,1024]{1,0:T(8,128)(2,1)S(1)}, u32[]{:S(2)}, u32[]{:S(2)}) collective-permute-start(bf16[256,1024]{1,0:T(8,128)(2,1)S(1)} %collective-permute-done), channel_id=1, source_target_pairs={{0,8},{4,12},{8,16},{12,20},{16,24},{20,28},{1,9},{5,13},{9,17},{1... | collective-permute-start | bytes 1572872 | tf_op jit(solution)/shard_map/ppermute | solution.py:24
  29.1 1.3 %collective-permute-start.7 = (bf16[256,1024]{1,0:T(8,128)(2,1)S(1)}, bf16[256,1024]{1,0:T(8,128)(2,1)S(1)}, u32[]{:S(2)}, u32[]{:S(2)}) collective-permute-start(bf16[256,1024]{1,0:T(8,128)(2,1)S(1)} %collective-permute-done.2), channel_id=1, source_target_pairs={{8,0},{12,4},{16,8},{20,12},{24,16},{28,20},{9,1},{13,5},{17,9},{2... | collective-permute-start | bytes 1572872 | tf_op jit(solution)/shard_map/ppermute | solution.py:24
  30.4 6.2 %collective-permute-done.3 = bf16[256,1024]{1,0:T(8,128)(2,1)S(1)} collective-permute-done((bf16[256,1024]{1,0:T(8,128)(2,1)S(1)}, bf16[256,1024]{1,0:T(8,128)(2,1)S(1)}, u32[]{:S(2)}, u32[]{:S(2)}) %collective-permute-start.3) | collective-permute-done | bytes 524320 | tf_op jit(solution)/shard_map/ppermute | solution.py:482
  36.6 1.3 %pad_maximum_fusion.refs_3_ = bf16[768,1024]{1,0:T(8,128)(2,1)} fusion(bf16[256,1024]{1,0:T(8,128)(2,1)S(1)} %constant_dynamic-update-slice_fusion.refs_1_, bf16[256,1024]{1,0:T(8,128)(2,1)S(1)} %get-tuple-element.15, bf16[256,1024]{1,0:T(8,128)(2,1)S(1)} %collective-permute-done), kind=kLoop, calls=%fused_computation | loop fusion | flops 4718592 | bytes 3145728 | tf_op jit(solution)/shard_map/concatenate | solution.py:506
  37.9 0.8 %collective-permute-done.4.refs_4_ = bf16[256,1024]{1,0:T(8,128)(2,1)S(1)} collective-permute-done((bf16[256,1024]{1,0:T(8,128)(2,1)S(1)}, bf16[256,1024]{1,0:T(8,128)(2,1)S(1)}, u32[]{:S(2)}, u32[]{:S(2)}) %collective-permute-start.4) | collective-permute-done | bytes 524320 | tf_op jit(solution)/shard_map/ppermute | solution.py:24
  38.7 0.8 %copy-done.3 = bf16[256,1024]{1,0:T(8,128)(2,1)} copy-done((bf16[256,1024]{1,0:T(8,128)(2,1)}, bf16[256,1024]{1,0:T(8,128)(2,1)S(1)}, u32[]{:S(2)}) %copy-start.3) | copy-done | bytes 524312
  39.5 8.5 %rows_pass.1 = (bf16[256,512]{1,0:T(8,128)(2,1)}, bf16[256,512]{1,0:T(8,128)(2,1)}, f32[256,8]{1,0:T(8,128)}) custom-call(s32[1]{0:T(128)} %bitcast.refs_0_, bf16[256,512]{1,0:T(8,128)(2,1)} %refs_1_.1, bf16[256,512]{1,0:T(8,128)(2,1)} %refs_2_.1, bf16[768,1024]{1,0:T(8,128)(2,1)} %pad_maximum_fusion.refs_3_, bf16[256,1024]{1,0:T(8,128)(2,1)} %copy-done.3), custom_call_target="tpu_custom_call" | custom-call | tf_op jit(solution)/shard_map/rows_pass/pallas_call | solution.py:492
  48.0 1.3 %collective-permute-start.5 = (f32[256,8]{1,0:T(8,128)}, f32[256,8]{1,0:T(8,128)S(1)}, u32[]{:S(2)}, u32[]{:S(2)}) collective-permute-start(f32[256,8]{1,0:T(8,128)} %get-tuple-element.11), channel_id=1, source_target_pairs={{4,0},{8,4},{12,8},{16,12},{20,16},{24,20},{28,24},{5,1},{9,5},{13... | collective-permute-start | bytes 24584 | tf_op jit(solution)/shard_map/ppermute | solution.py:24
  49.3 1.3 %collective-permute-start.6 = (f32[256,8]{1,0:T(8,128)}, f32[256,8]{1,0:T(8,128)S(1)}, u32[]{:S(2)}, u32[]{:S(2)}) collective-permute-start(f32[256,8]{1,0:T(8,128)} %get-tuple-element.11), channel_id=1, source_target_pairs={{8,0},{12,4},{16,8},{20,12},{24,16},{28,20},{9,1},{13,5},{17,9},{2... | collective-permute-start | bytes 24584 | tf_op jit(solution)/shard_map/ppermute | solution.py:24
  50.6 1.3 %collective-permute-start.8 = (f32[256,8]{1,0:T(8,128)}, f32[256,8]{1,0:T(8,128)S(1)}, u32[]{:S(2)}, u32[]{:S(2)}) collective-permute-start(f32[256,8]{1,0:T(8,128)} %get-tuple-element.11), channel_id=1, source_target_pairs={{16,0},{20,4},{24,8},{28,12},{17,1},{21,5},{25,9},{29,13},{18,2},{... | collective-permute-start | bytes 24584 | tf_op jit(solution)/shard_map/ppermute | solution.py:24
  51.9 1.3 %pad_maximum_fusion.1.refs_2_ = bf16[768,1024]{1,0:T(8,128)(2,1)} fusion(bf16[256,1024]{1,0:T(8,128)(2,1)S(1)} %collective-permute-done.2, bf16[256,1024]{1,0:T(8,128)(2,1)S(1)} %get-tuple-element.14, bf16[256,1024]{1,0:T(8,128)(2,1)S(1)} %constant_dynamic-update-slice_fusion.2), kind=kLoop, calls=%fused_computation.1 | loop fusion | flops 4718592 | bytes 3145728 | tf_op jit(solution)/shard_map/concatenate | solution.py:524
  53.2 1.9 %collective-permute-done.5 = f32[256,8]{1,0:T(8,128)S(1)} collective-permute-done((f32[256,8]{1,0:T(8,128)}, f32[256,8]{1,0:T(8,128)S(1)}, u32[]{:S(2)}, u32[]{:S(2)}) %collective-permute-start.5) | collective-permute-done | bytes 8224 | tf_op jit(solution)/shard_map/ppermute | solution.py:24
  55.1 3.1 %collective-permute-done.6 = f32[256,8]{1,0:T(8,128)S(1)} collective-permute-done((f32[256,8]{1,0:T(8,128)}, f32[256,8]{1,0:T(8,128)S(1)}, u32[]{:S(2)}, u32[]{:S(2)}) %collective-permute-start.6) | collective-permute-done | bytes 8224 | tf_op jit(solution)/shard_map/ppermute | solution.py:24
  59.0 4.8 %collective-permute-done.8.refs_5_ = f32[256,8]{1,0:T(8,128)S(1)} collective-permute-done((f32[256,8]{1,0:T(8,128)}, f32[256,8]{1,0:T(8,128)S(1)}, u32[]{:S(2)}, u32[]{:S(2)}) %collective-permute-start.8) | collective-permute-done | bytes 8224 | tf_op jit(solution)/shard_map/ppermute | solution.py:24
  64.5 7.1 %keys_pass.1 = (bf16[256,512]{1,0:T(8,128)(2,1)}, bf16[256,512]{1,0:T(8,128)(2,1)}) custom-call(s32[1]{0:T(128)} %bitcast.refs_0_, bf16[256,1024]{1,0:T(8,128)(2,1)} %copy-done, bf16[768,1024]{1,0:T(8,128)(2,1)} %pad_maximum_fusion.1.refs_2_, f32[768,8]{1,0:T(8,128)} %pad_maximum_fusion.2.refs_3_, bf16[256,1024]{1,0:T(8,128)(2,1)} %copy-done.2, ...), custom_call_target="tpu_custom_call" | custom-call | tf_op jit(solution)/shard_map/keys_pass/pallas_call | solution.py:512
  (18 shorter events, 1.7 us)
Async XLA Ops:
  0.6 8.0 %copy-start.1 = (bf16[256,512]{1,0:T(8,128)(2,1)S(1)}, bf16[256,512]{1,0:T(8,128)(2,1)}, u32[]{:S(2)}) copy-start(bf16[256,512]{1,0:T(8,128)(2,1)} %refs_2_.1) | copy-start | bytes 786436
  2.6 34.0 %copy-start = (bf16[256,1024]{1,0:T(8,128)(2,1)}, bf16[256,1024]{1,0:T(8,128)(2,1)S(1)}, u32[]{:S(2)}) copy-start(bf16[256,1024]{1,0:T(8,128)(2,1)S(1)} %constant_dynamic-update-slice_fusion.refs_1_) | copy-start | bytes 1572868
  2.7 16.1 %collective-permute-start = (bf16[256,1024]{1,0:T(8,128)(2,1)S(1)}, bf16[256,1024]{1,0:T(8,128)(2,1)S(1)}, u32[]{:S(2)}, u32[]{:S(2)}) collective-permute-start(bf16[256,1024]{1,0:T(8,128)(2,1)S(1)} %constant_dynamic-update-slice_fusion.refs_1_), channel_id=1, source_target_pairs={{0,8},{4,12},{8,16},{12,20},{16,24},{20,28},{1,9},{5,13},{9,17},{1... | collective-permute-start | bytes 1572872 | tf_op jit(solution)/shard_map/ppermute | solution.py:24
  8.7 15.3 %collective-permute-start.2 = (bf16[256,1024]{1,0:T(8,128)(2,1)S(1)}, bf16[256,1024]{1,0:T(8,128)(2,1)S(1)}, u32[]{:S(2)}, u32[]{:S(2)}) collective-permute-start(bf16[256,1024]{1,0:T(8,128)(2,1)S(1)} %constant_dynamic-update-slice_fusion.2), channel_id=1, source_target_pairs={{8,0},{12,4},{16,8},{20,12},{24,16},{28,20},{9,1},{13,5},{17,9},{2... | collective-permute-start | bytes 1572872 | tf_op jit(solution)/shard_map/ppermute | solution.py:24
  10.0 20.3 %collective-permute-start.1 = (bf16[256,1024]{1,0:T(8,128)(2,1)S(1)}, bf16[256,1024]{1,0:T(8,128)(2,1)S(1)}, u32[]{:S(2)}, u32[]{:S(2)}) collective-permute-start(bf16[256,1024]{1,0:T(8,128)(2,1)S(1)} %broadcast_select_fusion.3), channel_id=1, source_target_pairs={{0,4},{4,0},{8,12},{12,8},{16,20},{20,16},{24,28},{28,24},{1,5},{5... | collective-permute-start | bytes 1572872 | tf_op jit(solution)/shard_map/ppermute | solution.py:479
  24.0 12.5 %collective-permute-start.3 = (bf16[256,1024]{1,0:T(8,128)(2,1)S(1)}, bf16[256,1024]{1,0:T(8,128)(2,1)S(1)}, u32[]{:S(2)}, u32[]{:S(2)}) collective-permute-start(bf16[256,1024]{1,0:T(8,128)(2,1)S(1)} %broadcast_select_fusion.2), channel_id=1, source_target_pairs={{0,4},{4,0},{8,12},{12,8},{16,20},{20,16},{24,28},{28,24},{1,5},{5... | collective-permute-start | bytes 1572872 | tf_op jit(solution)/shard_map/ppermute | solution.py:482
  25.6 13.1 %collective-permute-start.4 = (bf16[256,1024]{1,0:T(8,128)(2,1)S(1)}, bf16[256,1024]{1,0:T(8,128)(2,1)S(1)}, u32[]{:S(2)}, u32[]{:S(2)}) collective-permute-start(bf16[256,1024]{1,0:T(8,128)(2,1)S(1)} %collective-permute-done), channel_id=1, source_target_pairs={{0,8},{4,12},{8,16},{12,20},{16,24},{20,28},{1,9},{5,13},{9,17},{1... | collective-permute-start | bytes 1572872 | tf_op jit(solution)/shard_map/ppermute | solution.py:24
  29.1 29.9 %collective-permute-start.7 = (bf16[256,1024]{1,0:T(8,128)(2,1)S(1)}, bf16[256,1024]{1,0:T(8,128)(2,1)S(1)}, u32[]{:S(2)}, u32[]{:S(2)}) collective-permute-start(bf16[256,1024]{1,0:T(8,128)(2,1)S(1)} %collective-permute-done.2), channel_id=1, source_target_pairs={{8,0},{12,4},{16,8},{20,12},{24,16},{28,20},{9,1},{13,5},{17,9},{2... | collective-permute-start | bytes 1572872 | tf_op jit(solution)/shard_map/ppermute | solution.py:24
  38.7 0.8 %copy-start.3 = (bf16[256,1024]{1,0:T(8,128)(2,1)}, bf16[256,1024]{1,0:T(8,128)(2,1)S(1)}, u32[]{:S(2)}) copy-start(bf16[256,1024]{1,0:T(8,128)(2,1)S(1)} %collective-permute-done.4.refs_4_) | copy-start | bytes 1572868
  48.0 7.1 %collective-permute-start.5 = (f32[256,8]{1,0:T(8,128)}, f32[256,8]{1,0:T(8,128)S(1)}, u32[]{:S(2)}, u32[]{:S(2)}) collective-permute-start(f32[256,8]{1,0:T(8,128)} %get-tuple-element.11), channel_id=1, source_target_pairs={{4,0},{8,4},{12,8},{16,12},{20,16},{24,20},{28,24},{5,1},{9,5},{13... | collective-permute-start | bytes 24584 | tf_op jit(solution)/shard_map/ppermute | solution.py:24
  49.3 8.9 %collective-permute-start.6 = (f32[256,8]{1,0:T(8,128)}, f32[256,8]{1,0:T(8,128)S(1)}, u32[]{:S(2)}, u32[]{:S(2)}) collective-permute-start(f32[256,8]{1,0:T(8,128)} %get-tuple-element.11), channel_id=1, source_target_pairs={{8,0},{12,4},{16,8},{20,12},{24,16},{28,20},{9,1},{13,5},{17,9},{2... | collective-permute-start | bytes 24584 | tf_op jit(solution)/shard_map/ppermute | solution.py:24
  50.6 13.2 %collective-permute-start.8 = (f32[256,8]{1,0:T(8,128)}, f32[256,8]{1,0:T(8,128)S(1)}, u32[]{:S(2)}, u32[]{:S(2)}) collective-permute-start(f32[256,8]{1,0:T(8,128)} %get-tuple-element.11), channel_id=1, source_target_pairs={{16,0},{20,4},{24,8},{28,12},{17,1},{21,5},{25,9},{29,13},{18,2},{... | collective-permute-start | bytes 24584 | tf_op jit(solution)/shard_map/ppermute | solution.py:24
  51.9 6.3 %copy-start.4 = (f32[256,8]{1,0:T(8,128)S(1)}, f32[256,8]{1,0:T(8,128)}, u32[]{:S(2)}) copy-start(f32[256,8]{1,0:T(8,128)} %get-tuple-element.11) | copy-start | bytes 24580
  59.0 4.8 %copy-start.2 = (bf16[256,1024]{1,0:T(8,128)(2,1)}, bf16[256,1024]{1,0:T(8,128)(2,1)S(1)}, u32[]{:S(2)}) copy-start(bf16[256,1024]{1,0:T(8,128)(2,1)S(1)} %collective-permute-done.7.refs_4_) | copy-start | bytes 1572868
  63.8 0.7 copy-start.5

commit v6 on v5

--- a/solution.py
+++ b/solution.py
@@ -334,11 +334,14 @@
 TRANS_B = (((1,), (1,)), ((), ()))
 
 
-def row_kernel(near_count, far_list, heads, *refs):
+def row_kernel(near_count, far_list, heads, phase, *refs):
     far_count = len(far_list)
     position_ref, query_ref, grad_ref, span_ref = refs[:4]
     far_refs = refs[4 : 4 + far_count]
-    attended_ref, grad_query_ref, stats_ref = refs[4 + far_count :]
+    if phase == "stats":
+        attended_ref, stats_ref = refs[4 + far_count :]
+    else:
+        stats_in_ref, grad_query_ref = refs[4 + far_count :]
     width = heads * HD
     near_rows = near_count * BLK
     scale = 1.0 / math.sqrt(HD)
@@ -353,7 +356,11 @@
         near_span = pl.ds(block * BLK, near_rows)
         near_mask = jnp.logical_and(near_causal, first + block - near_offset >= 0)
         far_live = [first + block - offset >= 0 for offset in far_list]
-        stats_tile = jnp.zeros((BLK, 2 * heads), jnp.float32)
+        masks = [near_mask] + far_live
+        if phase == "stats":
+            stats_tile = jnp.zeros((BLK, 2 * heads), jnp.float32)
+        else:
+            stats_tile = stats_in_ref[rows, :]
         for head in range(heads):
             cols = pl.ds(head * HD, HD)
             value_cols = pl.ds(width + head * HD, HD)
@@ -361,11 +368,31 @@
             grad = grad_ref[rows, cols]
             keys = [span_ref[near_span, cols]] + [item[rows, cols] for item in far_refs]
             values = [span_ref[near_span, value_cols]] + [item[rows, value_cols] for item in far_refs]
-            masks = [near_mask] + far_live
-            scores = []
-            for key, mask in zip(keys, masks):
-                score = lax.dot_general(query, key, TRANS_B, preferred_element_type=jnp.float32)
-                scores.append(jnp.where(mask, score * scale, NEG))
+            scores = [
+                lax.dot_general(query, key, TRANS_B, preferred_element_type=jnp.float32) * scale
+                for key in keys
+            ]
+            if phase == "grad":
+                log_total = jnp.sum(jnp.where(lane_ids == head, stats_tile, 0.0), axis=-1, keepdims=True)
+                out_dot = jnp.sum(
+                    jnp.where(lane_ids == heads + head, stats_tile, 0.0), axis=-1, keepdims=True
+                )
+                probs = [
+                    jnp.where(mask, jnp.exp(score - log_total), 0.0)
+                    for score, mask in zip(scores, masks)
+                ]
+                grad_query = jnp.zeros((BLK, HD), jnp.float32)
+                for prob, key, value in zip(probs, keys, values):
+                    prob_grad = lax.dot_general(
+                        grad, value, TRANS_B, preferred_element_type=jnp.float32
+                    )
+                    score_grad = (prob * (prob_grad - out_dot)).astype(jnp.bfloat16)
+                    grad_query = grad_query + jnp.dot(
+                        score_grad, key, preferred_element_type=jnp.float32
+                    )
+                grad_query_ref[rows, cols] = (grad_query * scale).astype(jnp.bfloat16)
+                continue
+            scores = [jnp.where(mask, score, NEG) for score, mask in zip(scores, masks)]
             row_max = scores[0].max(axis=-1, keepdims=True)
             for score in scores[1:]:
                 row_max = jnp.maximum(row_max, score.max(axis=-1, keepdims=True))
@@ -375,28 +402,29 @@
                 row_sum = row_sum + item.sum(axis=-1, keepdims=True)
             log_total = row_max + jnp.log(row_sum)
             inverse = 1.0 / row_sum
-            probs = [item * inverse for item in shifted]
             attended = jnp.zeros((BLK, HD), jnp.float32)
-            for prob, value in zip(probs, values):
+            for item, value in zip(shifted, values):
                 attended = attended + jnp.dot(
-                    prob.astype(jnp.bfloat16), value, preferred_element_type=jnp.float32
+                    (item * inverse).astype(jnp.bfloat16), value, preferred_element_type=jnp.float32
                 )
             attended = attended.astype(jnp.bfloat16)
             attended_ref[rows, cols] = attended
             out_dot = jnp.sum(
                 grad.astype(jnp.float32) * attended.astype(jnp.float32), axis=-1, keepdims=True
             )
-            grad_query = jnp.zeros((BLK, HD), jnp.float32)
-            for prob, key, value in zip(probs, keys, values):
-                prob_grad = lax.dot_general(grad, value, TRANS_B, preferred_element_type=jnp.float32)
-                score_grad = (prob * (prob_grad - out_dot)).astype(jnp.bfloat16)
-                grad_query = grad_query + jnp.dot(
-                    score_grad, key, preferred_element_type=jnp.float32
-                )
-            grad_query_ref[rows, cols] = (grad_query * scale).astype(jnp.bfloat16)
             stats_tile = stats_tile + jnp.where(lane_ids == head, log_total, 0.0)
             stats_tile = stats_tile + jnp.where(lane_ids == heads + head, out_dot, 0.0)
-        stats_ref[rows, :] = stats_tile
+        if phase == "stats":
+            stats_ref[rows, :] = stats_tile
+
+
+def estimate(tok_count, row_width, slab_rows, matmuls, exps):
+    flops = 2 * tok_count * slab_rows * HD * matmuls * (row_width // HD)
+    return pl.CostEstimate(
+        flops=flops,
+        transcendentals=tok_count * slab_rows * exps * (row_width // HD),
+        bytes_accessed=8 * tok_count * row_width * 4,
+    )
 
 
 def key_kernel(near_count, far_list, heads, block_total, *refs):
@@ -489,26 +517,31 @@
 
     position_arr = jnp.reshape(position, (1,)).astype(jnp.int32)
     far_offsets = list(far_list)
-    attended, grad_queries, stats = pl.pallas_call(
-        functools.partial(row_kernel, len(near_list), far_offsets, heads),
+    row_span = jnp.concatenate([back2, back1, keys_values], axis=0)
+    slab_rows = (len(near_list) + len(far_list)) * BLK
+    row_inputs = (position_arr, queries, grad_out, row_span, *far_back)
+    attended, stats = pl.pallas_call(
+        functools.partial(row_kernel, len(near_list), far_offsets, heads, "stats"),
         out_shape=(
-            jax.ShapeDtypeStruct((tok_count, row_width), jnp.bfloat16),
             jax.ShapeDtypeStruct((tok_count, row_width), jnp.bfloat16),
             jax.ShapeDtypeStruct((tok_count, 2 * heads), jnp.float32),
         ),
         in_specs=[smem_spec()] + [vmem_spec()] * (3 + len(far_back)),
-        out_specs=(vmem_spec(), vmem_spec(), vmem_spec()),
-        name="rows_pass",
-    )(
-        position_arr,
-        queries,
-        grad_out,
-        jnp.concatenate([back2, back1, keys_values], axis=0),
-        *far_back,
-    )
+        out_specs=(vmem_spec(), vmem_spec()),
+        cost_estimate=estimate(tok_count, row_width, slab_rows, 2, 1),
+        name="rows_stats",
+    )(*row_inputs)
     stats_one = passed_along(stats, "seq", -1)
     stats_two = passed_along(stats, "seq", -2)
     far_stats = [passed_along(stats, "seq", -shift) for shift in far_shifts]
+    grad_queries = pl.pallas_call(
+        functools.partial(row_kernel, len(near_list), far_offsets, heads, "grad"),
+        out_shape=jax.ShapeDtypeStruct((tok_count, row_width), jnp.bfloat16),
+        in_specs=[smem_spec()] + [vmem_spec()] * (4 + len(far_back)),
+        out_specs=vmem_spec(),
+        cost_estimate=estimate(tok_count, row_width, slab_rows, 3, 1),
+        name="rows_grad",
+    )(*row_inputs, stats)
     grad_keys, grad_values = pl.pallas_call(
         functools.partial(key_kernel, len(near_list), far_offsets, heads, devices * blocks_dev),
         out_shape=(
@@ -517,6 +550,7 @@
         ),
         in_specs=[smem_spec()] + [vmem_spec()] * (3 + 2 * len(far_ahead)),
         out_specs=(vmem_spec(), vmem_spec()),
+        cost_estimate=estimate(tok_count, row_width, slab_rows, 4, 1),
         name="keys_pass",
     )(
         position_arr,

time: 72 us -> 69.8 us (0.969)
  waiting for transfers between devices: 29.1 us -> 24 us
  Pallas kernels: 15.6 us -> 18.6 us
    ppermute x7, waiting for transfers between devices: 22.9 us -> 17.9 us  [passed_along(): lax.ppermute(value, axis, [(source, source + steps) for source in range(f...]
    pallas_call x1 -> x2, Pallas kernels: 8.5 us -> 11.4 us  [body(): pl.pallas_call(functools.partial(row_kernel, len(near_list), far_offsets,...]
    unnamed x14 -> x12, local copies, waits for them, and re-layouts: 3.47 us -> 3.46 us
  transfers between devices with their start and end apart: 9 -> 9, of which waited for: 7 -> 5; matrix products, arithmetic and copies ran while one was open for 6% -> 7% of each run, Pallas kernels for 12% -> 16%
where the time goes in v6:
time: 69.8 us; the launch traced here: 69.4 us
  waiting for transfers between devices  24 us (34%)
  Pallas kernels  18.6 us (27%)
  starting transfers between devices  18.1 us (26%)
  local copies, waits for them, and re-layouts  4.46 us (6%)
  other arithmetic  3.53 us (5%)
  between operations  0.8 us (1%)
    ppermute x7, waiting for transfers between devices, passed_along(): lax.ppermute(value, axis, [(source, source + steps) for source in range(f...  17.9 us
    ppermute x7, starting transfers between devices, passed_along(): lax.ppermute(value, axis, [(source, source + steps) for source in range(f...  14.9 us
    pallas_call x2, Pallas kernels, body(): pl.pallas_call(functools.partial(row_kernel, len(near_list), far_offsets,...  11.4 us
    pallas_call x1, Pallas kernels, body(): pl.pallas_call(functools.partial(key_kernel, len(near_list), far_offsets,...  7.14 us
    ppermute x1, waiting for transfers between devices, body(): swap_two = lax.ppermute(jnp.where(odd, back2, ahead2), 'seq', pairs)  6.16 us
    unnamed x12, local copies, waits for them, and re-layouts  3.46 us
    ppermute x1, starting transfers between devices, body(): lax.ppermute(jnp.where(odd, queries_grads, keys_values), 'seq', pairs)  1.58 us
    ppermute x1, starting transfers between devices, body(): swap_two = lax.ppermute(jnp.where(odd, back2, ahead2), 'seq', pairs)  1.58 us
  transfers between devices with their start and end apart: 9, of which 5 were waited for; matrix products, arithmetic and copies ran while one was open for 7% of the time, Pallas kernels for 16%

profile of v6, /device:TPU:0, one launch (start us, length us, event | category | flops | bytes accessed | tf_op | source)
XLA Modules:
  0.0 69.4 jit_solution(16897219945303839217)
XLA Ops:
  0.6 1.0 %constant_dynamic-update-slice_fusion.1 = bf16[256,1024]{1,0:T(8,128)(2,1)S(1)} fusion(bf16[256,512]{1,0:T(8,128)(2,1)} %param.5), kind=kLoop, calls=%fused_computation.8 | loop fusion | bytes 524288
  1.7 1.0 %constant_dynamic-update-slice_fusion.refs_1_ = bf16[256,1024]{1,0:T(8,128)(2,1)S(1)} fusion(bf16[256,1024]{1,0:T(8,128)(2,1)S(1)} %constant_dynamic-update-slice_fusion.1, bf16[256,512]{1,0:T(8,128)(2,1)} %param.6), kind=kLoop, calls=%fused_computation.7 | loop fusion | bytes 524288 | tf_op jit(solution)/shard_map/concatenate | solution.py:503
  2.7 5.0 %collective-permute-start = (bf16[256,1024]{1,0:T(8,128)(2,1)S(1)}, bf16[256,1024]{1,0:T(8,128)(2,1)S(1)}, u32[]{:S(2)}, u32[]{:S(2)}) collective-permute-start(bf16[256,1024]{1,0:T(8,128)(2,1)S(1)} %constant_dynamic-update-slice_fusion.refs_1_), channel_id=1, source_target_pairs={{0,8},{4,12},{8,16},{12,20},{16,24},{20,28},{1,9},{5,13},{9,17},{1... | collective-permute-start | bytes 1572872 | tf_op jit(solution)/shard_map/ppermute | solution.py:24
  7.6 1.0 %constant_dynamic-update-slice_fusion.3 = bf16[256,1024]{1,0:T(8,128)(2,1)S(1)} fusion(bf16[256,512]{1,0:T(8,128)(2,1)} %refs_1_.3), kind=kLoop, calls=%fused_computation.10 | loop fusion | bytes 524288
  8.7 1.3 %collective-permute-start.2 = (bf16[256,1024]{1,0:T(8,128)(2,1)S(1)}, bf16[256,1024]{1,0:T(8,128)(2,1)S(1)}, u32[]{:S(2)}, u32[]{:S(2)}) collective-permute-start(bf16[256,1024]{1,0:T(8,128)(2,1)S(1)} %constant_dynamic-update-slice_fusion.2), channel_id=1, source_target_pairs={{8,0},{12,4},{16,8},{20,12},{24,16},{28,20},{9,1},{13,5},{17,9},{2... | collective-permute-start | bytes 1572872 | tf_op jit(solution)/shard_map/ppermute | solution.py:24
  10.0 1.6 %collective-permute-start.1 = (bf16[256,1024]{1,0:T(8,128)(2,1)S(1)}, bf16[256,1024]{1,0:T(8,128)(2,1)S(1)}, u32[]{:S(2)}, u32[]{:S(2)}) collective-permute-start(bf16[256,1024]{1,0:T(8,128)(2,1)S(1)} %broadcast_select_fusion.3), channel_id=1, source_target_pairs={{0,4},{4,0},{8,12},{12,8},{16,20},{20,16},{24,28},{28,24},{1,5},{5... | collective-permute-start | bytes 1572872 | tf_op jit(solution)/shard_map/ppermute | solution.py:507
  11.6 7.1 %collective-permute-done = bf16[256,1024]{1,0:T(8,128)(2,1)S(1)} collective-permute-done((bf16[256,1024]{1,0:T(8,128)(2,1)S(1)}, bf16[256,1024]{1,0:T(8,128)(2,1)S(1)}, u32[]{:S(2)}, u32[]{:S(2)}) %collective-permute-start) | collective-permute-done | bytes 524320 | tf_op jit(solution)/shard_map/ppermute | solution.py:24
  18.8 5.2 %collective-permute-done.2 = bf16[256,1024]{1,0:T(8,128)(2,1)S(1)} collective-permute-done((bf16[256,1024]{1,0:T(8,128)(2,1)S(1)}, bf16[256,1024]{1,0:T(8,128)(2,1)S(1)}, u32[]{:S(2)}, u32[]{:S(2)}) %collective-permute-start.2) | collective-permute-done | bytes 524320 | tf_op jit(solution)/shard_map/ppermute | solution.py:24
  24.0 1.6 %collective-permute-start.3 = (bf16[256,1024]{1,0:T(8,128)(2,1)S(1)}, bf16[256,1024]{1,0:T(8,128)(2,1)S(1)}, u32[]{:S(2)}, u32[]{:S(2)}) collective-permute-start(bf16[256,1024]{1,0:T(8,128)(2,1)S(1)} %broadcast_select_fusion.2), channel_id=1, source_target_pairs={{0,4},{4,0},{8,12},{12,8},{16,20},{20,16},{24,28},{28,24},{1,5},{5... | collective-permute-start | bytes 1572872 | tf_op jit(solution)/shard_map/ppermute | solution.py:510
  25.6 3.5 %collective-permute-start.4 = (bf16[256,1024]{1,0:T(8,128)(2,1)S(1)}, bf16[256,1024]{1,0:T(8,128)(2,1)S(1)}, u32[]{:S(2)}, u32[]{:S(2)}) collective-permute-start(bf16[256,1024]{1,0:T(8,128)(2,1)S(1)} %collective-permute-done), channel_id=1, source_target_pairs={{0,8},{4,12},{8,16},{12,20},{16,24},{20,28},{1,9},{5,13},{9,17},{1... | collective-permute-start | bytes 1572872 | tf_op jit(solution)/shard_map/ppermute | solution.py:24
  29.1 1.3 %collective-permute-start.7 = (bf16[256,1024]{1,0:T(8,128)(2,1)S(1)}, bf16[256,1024]{1,0:T(8,128)(2,1)}, u32[]{:S(2)}, u32[]{:S(2)}) collective-permute-start(bf16[256,1024]{1,0:T(8,128)(2,1)S(1)} %collective-permute-done.2), channel_id=1, source_target_pairs={{8,0},{12,4},{16,8},{20,12},{24,16},{28,20},{9,1},{13,5},{17,9},{2... | collective-permute-start | bytes 1572872 | tf_op jit(solution)/shard_map/ppermute | solution.py:24
  30.4 6.2 %collective-permute-done.3 = bf16[256,1024]{1,0:T(8,128)(2,1)S(1)} collective-permute-done((bf16[256,1024]{1,0:T(8,128)(2,1)S(1)}, bf16[256,1024]{1,0:T(8,128)(2,1)S(1)}, u32[]{:S(2)}, u32[]{:S(2)}) %collective-permute-start.3) | collective-permute-done | bytes 524320 | tf_op jit(solution)/shard_map/ppermute | solution.py:510
  36.6 1.3 %pad_maximum_fusion.refs_3_ = bf16[768,1024]{1,0:T(8,128)(2,1)} fusion(bf16[256,1024]{1,0:T(8,128)(2,1)S(1)} %constant_dynamic-update-slice_fusion.refs_1_, bf16[256,1024]{1,0:T(8,128)(2,1)S(1)} %get-tuple-element.13, bf16[256,1024]{1,0:T(8,128)(2,1)S(1)} %collective-permute-done), kind=kLoop, calls=%fused_computation | loop fusion | flops 4718592 | bytes 3145728 | tf_op jit(solution)/shard_map/concatenate | solution.py:520
  37.9 0.8 %collective-permute-done.4.refs_4_ = bf16[256,1024]{1,0:T(8,128)(2,1)S(1)} collective-permute-done((bf16[256,1024]{1,0:T(8,128)(2,1)S(1)}, bf16[256,1024]{1,0:T(8,128)(2,1)S(1)}, u32[]{:S(2)}, u32[]{:S(2)}) %collective-permute-start.4) | collective-permute-done | bytes 524320 | tf_op jit(solution)/shard_map/ppermute | solution.py:24
  38.7 0.8 %copy-done.2 = bf16[256,1024]{1,0:T(8,128)(2,1)} copy-done((bf16[256,1024]{1,0:T(8,128)(2,1)}, bf16[256,1024]{1,0:T(8,128)(2,1)S(1)}, u32[]{:S(2)}) %copy-start.2) | copy-done | bytes 524312
  39.5 6.2 %rows_stats.1 = (bf16[256,512]{1,0:T(8,128)(2,1)}, f32[256,8]{1,0:T(8,128)}) custom-call(s32[1]{0:T(128)} %bitcast.refs_0_, bf16[256,512]{1,0:T(8,128)(2,1)} %refs_1_.3, bf16[256,512]{1,0:T(8,128)(2,1)} %refs_2_.3, bf16[768,1024]{1,0:T(8,128)(2,1)} %pad_maximum_fusion.refs_3_, bf16[256,1024]{1,0:T(8,128)(2,1)} %copy-done.2), custom_call_target="tpu_custom_call" | custom-call | flops 402653184 | bytes 4194304 | tf_op jit(solution)/shard_map/rows_stats/pallas_call | solution.py:523
  45.7 1.3 %collective-permute-start.6 = (f32[256,8]{1,0:T(8,128)}, f32[256,8]{1,0:T(8,128)S(1)}, u32[]{:S(2)}, u32[]{:S(2)}) collective-permute-start(f32[256,8]{1,0:T(8,128)} %get-tuple-element.9.refs_5_), channel_id=1, source_target_pairs={{8,0},{12,4},{16,8},{20,12},{24,16},{28,20},{9,1},{13,5},{17,9},{2... | collective-permute-start | bytes 24584 | tf_op jit(solution)/shard_map/ppermute | solution.py:24
  47.0 1.3 %collective-permute-start.5 = (f32[256,8]{1,0:T(8,128)}, f32[256,8]{1,0:T(8,128)S(1)}, u32[]{:S(2)}, u32[]{:S(2)}) collective-permute-start(f32[256,8]{1,0:T(8,128)} %get-tuple-element.9.refs_5_), channel_id=1, source_target_pairs={{4,0},{8,4},{12,8},{16,12},{20,16},{24,20},{28,24},{5,1},{9,5},{13... | collective-permute-start | bytes 24584 | tf_op jit(solution)/shard_map/ppermute | solution.py:24
  48.3 1.3 %collective-permute-start.8 = (f32[256,8]{1,0:T(8,128)}, f32[256,8]{1,0:T(8,128)S(1)}, u32[]{:S(2)}, u32[]{:S(2)}) collective-permute-start(f32[256,8]{1,0:T(8,128)} %get-tuple-element.9.refs_5_), channel_id=1, source_target_pairs={{16,0},{20,4},{24,8},{28,12},{17,1},{21,5},{25,9},{29,13},{18,2},{... | collective-permute-start | bytes 24584 | tf_op jit(solution)/shard_map/ppermute | solution.py:24
  49.6 1.3 %pad_maximum_fusion.1.refs_2_ = bf16[768,1024]{1,0:T(8,128)(2,1)} fusion(bf16[256,1024]{1,0:T(8,128)(2,1)S(1)} %collective-permute-done.2, bf16[256,1024]{1,0:T(8,128)(2,1)S(1)} %get-tuple-element.12, bf16[256,1024]{1,0:T(8,128)(2,1)S(1)} %constant_dynamic-update-slice_fusion.2), kind=kLoop, calls=%fused_computation.1 | loop fusion | flops 4718592 | bytes 3145728 | tf_op jit(solution)/shard_map/concatenate | solution.py:558
  50.9 5.2 %rows_grad.1 = bf16[256,512]{1,0:T(8,128)(2,1)} custom-call(s32[1]{0:T(128)} %bitcast.refs_0_, bf16[256,512]{1,0:T(8,128)(2,1)} %refs_1_.3, bf16[256,512]{1,0:T(8,128)(2,1)} %refs_2_.3, bf16[768,1024]{1,0:T(8,128)(2,1)} %pad_maximum_fusion.refs_3_, bf16[256,1024]{1,0:T(8,128)(2,1)} %copy-done.2, f32[256,8]{1,0:T(8,128)} %get-tuple-element.9.refs_5_), custom_call_target="tpu_custom_call" | custom-call | flops 603979776 | bytes 4194304 | tf_op jit(solution)/shard_map/rows_grad/pallas_call | solution.py:537
  56.1 0.8 %pad_maximum_fusion.2.refs_3_ = f32[768,8]{1,0:T(8,128)} fusion(f32[256,8]{1,0:T(8,128)S(1)} %collective-permute-done.6, f32[256,8]{1,0:T(8,128)S(1)} %collective-permute-done.5, f32[256,8]{1,0:T(8,128)S(1)} %copy-done.3), kind=kLoop, calls=%fused_computation.6 | loop fusion | flops 12288 | bytes 49152 | tf_op jit(solution)/shard_map/concatenate | solution.py:559
  56.9 4.7 %collective-permute-done.8.refs_5_ = f32[256,8]{1,0:T(8,128)S(1)} collective-permute-done((f32[256,8]{1,0:T(8,128)}, f32[256,8]{1,0:T(8,128)S(1)}, u32[]{:S(2)}, u32[]{:S(2)}) %collective-permute-start.8) | collective-permute-done | bytes 8224 | tf_op jit(solution)/shard_map/ppermute | solution.py:24
  62.3 7.1 %keys_pass.1 = (bf16[256,512]{1,0:T(8,128)(2,1)}, bf16[256,512]{1,0:T(8,128)(2,1)}) custom-call(s32[1]{0:T(128)} %bitcast.refs_0_, bf16[256,1024]{1,0:T(8,128)(2,1)} %copy-done, bf16[768,1024]{1,0:T(8,128)(2,1)} %pad_maximum_fusion.1.refs_2_, f32[768,8]{1,0:T(8,128)} %pad_maximum_fusion.2.refs_3_, bf16[256,1024]{1,0:T(8,128)(2,1)} %collective-permute-done.7.refs_4_, ...), custom_call_target="tpu_custom_call" | custom-call | flops 805306368 | bytes 4194304 | tf_op jit(solution)/shard_map/keys_pass/pallas_call | solution.py:545
  (17 shorter events, 0.9 us)
Async XLA Ops:
  0.6 8.0 %copy-start.1 = (bf16[256,512]{1,0:T(8,128)(2,1)S(1)}, bf16[256,512]{1,0:T(8,128)(2,1)}, u32[]{:S(2)}) copy-start(bf16[256,512]{1,0:T(8,128)(2,1)} %refs_2_.3) | copy-start | bytes 786436
  2.6 34.0 %copy-start = (bf16[256,1024]{1,0:T(8,128)(2,1)}, bf16[256,1024]{1,0:T(8,128)(2,1)S(1)}, u32[]{:S(2)}) copy-start(bf16[256,1024]{1,0:T(8,128)(2,1)S(1)} %constant_dynamic-update-slice_fusion.refs_1_) | copy-start | bytes 1572868
  2.7 16.1 %collective-permute-start = (bf16[256,1024]{1,0:T(8,128)(2,1)S(1)}, bf16[256,1024]{1,0:T(8,128)(2,1)S(1)}, u32[]{:S(2)}, u32[]{:S(2)}) collective-permute-start(bf16[256,1024]{1,0:T(8,128)(2,1)S(1)} %constant_dynamic-update-slice_fusion.refs_1_), channel_id=1, source_target_pairs={{0,8},{4,12},{8,16},{12,20},{16,24},{20,28},{1,9},{5,13},{9,17},{1... | collective-permute-start | bytes 1572872 | tf_op jit(solution)/shard_map/ppermute | solution.py:24
  8.7 15.3 %collective-permute-start.2 = (bf16[256,1024]{1,0:T(8,128)(2,1)S(1)}, bf16[256,1024]{1,0:T(8,128)(2,1)S(1)}, u32[]{:S(2)}, u32[]{:S(2)}) collective-permute-start(bf16[256,1024]{1,0:T(8,128)(2,1)S(1)} %constant_dynamic-update-slice_fusion.2), channel_id=1, source_target_pairs={{8,0},{12,4},{16,8},{20,12},{24,16},{28,20},{9,1},{13,5},{17,9},{2... | collective-permute-start | bytes 1572872 | tf_op jit(solution)/shard_map/ppermute | solution.py:24
  10.0 20.3 %collective-permute-start.1 = (bf16[256,1024]{1,0:T(8,128)(2,1)S(1)}, bf16[256,1024]{1,0:T(8,128)(2,1)S(1)}, u32[]{:S(2)}, u32[]{:S(2)}) collective-permute-start(bf16[256,1024]{1,0:T(8,128)(2,1)S(1)} %broadcast_select_fusion.3), channel_id=1, source_target_pairs={{0,4},{4,0},{8,12},{12,8},{16,20},{20,16},{24,28},{28,24},{1,5},{5... | collective-permute-start | bytes 1572872 | tf_op jit(solution)/shard_map/ppermute | solution.py:507
  24.0 12.5 %collective-permute-start.3 = (bf16[256,1024]{1,0:T(8,128)(2,1)S(1)}, bf16[256,1024]{1,0:T(8,128)(2,1)S(1)}, u32[]{:S(2)}, u32[]{:S(2)}) collective-permute-start(bf16[256,1024]{1,0:T(8,128)(2,1)S(1)} %broadcast_select_fusion.2), channel_id=1, source_target_pairs={{0,4},{4,0},{8,12},{12,8},{16,20},{20,16},{24,28},{28,24},{1,5},{5... | collective-permute-start | bytes 1572872 | tf_op jit(solution)/shard_map/ppermute | solution.py:510
  25.6 13.1 %collective-permute-start.4 = (bf16[256,1024]{1,0:T(8,128)(2,1)S(1)}, bf16[256,1024]{1,0:T(8,128)(2,1)S(1)}, u32[]{:S(2)}, u32[]{:S(2)}) collective-permute-start(bf16[256,1024]{1,0:T(8,128)(2,1)S(1)} %collective-permute-done), channel_id=1, source_target_pairs={{0,8},{4,12},{8,16},{12,20},{16,24},{20,28},{1,9},{5,13},{9,17},{1... | collective-permute-start | bytes 1572872 | tf_op jit(solution)/shard_map/ppermute | solution.py:24
  29.1 27.9 %collective-permute-start.7 = (bf16[256,1024]{1,0:T(8,128)(2,1)S(1)}, bf16[256,1024]{1,0:T(8,128)(2,1)}, u32[]{:S(2)}, u32[]{:S(2)}) collective-permute-start(bf16[256,1024]{1,0:T(8,128)(2,1)S(1)} %collective-permute-done.2), channel_id=1, source_target_pairs={{8,0},{12,4},{16,8},{20,12},{24,16},{28,20},{9,1},{13,5},{17,9},{2... | collective-permute-start | bytes 1572872 | tf_op jit(solution)/shard_map/ppermute | solution.py:24
  38.7 0.8 %copy-start.2 = (bf16[256,1024]{1,0:T(8,128)(2,1)}, bf16[256,1024]{1,0:T(8,128)(2,1)S(1)}, u32[]{:S(2)}) copy-start(bf16[256,1024]{1,0:T(8,128)(2,1)S(1)} %collective-permute-done.4.refs_4_) | copy-start | bytes 1572868
  45.7 10.4 %collective-permute-start.6 = (f32[256,8]{1,0:T(8,128)}, f32[256,8]{1,0:T(8,128)S(1)}, u32[]{:S(2)}, u32[]{:S(2)}) collective-permute-start(f32[256,8]{1,0:T(8,128)} %get-tuple-element.9.refs_5_), channel_id=1, source_target_pairs={{8,0},{12,4},{16,8},{20,12},{24,16},{28,20},{9,1},{13,5},{17,9},{2... | collective-permute-start | bytes 24584 | tf_op jit(solution)/shard_map/ppermute | solution.py:24
  47.0 9.1 %collective-permute-start.5 = (f32[256,8]{1,0:T(8,128)}, f32[256,8]{1,0:T(8,128)S(1)}, u32[]{:S(2)}, u32[]{:S(2)}) collective-permute-start(f32[256,8]{1,0:T(8,128)} %get-tuple-element.9.refs_5_), channel_id=1, source_target_pairs={{4,0},{8,4},{12,8},{16,12},{20,16},{24,20},{28,24},{5,1},{9,5},{13... | collective-permute-start | bytes 24584 | tf_op jit(solution)/shard_map/ppermute | solution.py:24
  48.3 13.3 %collective-permute-start.8 = (f32[256,8]{1,0:T(8,128)}, f32[256,8]{1,0:T(8,128)S(1)}, u32[]{:S(2)}, u32[]{:S(2)}) collective-permute-start(f32[256,8]{1,0:T(8,128)} %get-tuple-element.9.refs_5_), channel_id=1, source_target_pairs={{16,0},{20,4},{24,8},{28,12},{17,1},{21,5},{25,9},{29,13},{18,2},{... | collective-permute-start | bytes 24584 | tf_op jit(solution)/shard_map/ppermute | solution.py:24
  50.9 5.2 %copy-start.3 = (f32[256,8]{1,0:T(8,128)S(1)}, f32[256,8]{1,0:T(8,128)}, u32[]{:S(2)}) copy-start(f32[256,8]{1,0:T(8,128)} %get-tuple-element.9.refs_5_) | copy-start | bytes 24580
  61.6 0.7 copy-start.4

commit v7 on v6

--- a/solution.py
+++ b/solution.py
@@ -427,12 +427,15 @@
     )
 
 
-def key_kernel(near_count, far_list, heads, block_total, *refs):
+def key_kernel(near_count, far_list, heads, block_total, part, *refs):
     far_count = len(far_list)
-    position_ref, own_ref, span_ref, stats_span_ref = refs[:4]
-    far_rows = refs[4 : 4 + far_count]
-    far_stats = refs[4 + far_count : 4 + 2 * far_count]
-    grad_key_ref, grad_value_ref = refs[4 + 2 * far_count :]
+    position_ref, own_ref = refs[:2]
+    if part == "near":
+        span_ref, stats_span_ref, grad_key_ref, grad_value_ref = refs[2:]
+    else:
+        far_rows = refs[2 : 2 + far_count]
+        far_stats = refs[2 + far_count : 2 + 2 * far_count]
+        key_acc_ref, value_acc_ref, grad_key_ref, grad_value_ref = refs[2 + 2 * far_count :]
     width = heads * HD
     near_rows = near_count * BLK
     scale = 1.0 / math.sqrt(HD)
@@ -446,20 +449,29 @@
     for block in range(2):
         rows = pl.ds(block * BLK, BLK)
         near_span = pl.ds(block * BLK, near_rows)
-        near_mask = jnp.logical_and(near_causal, first + block + near_offset < block_total)
-        far_live = [first + block + offset < block_total for offset in far_list]
-        masks = [near_mask] + far_live
-        stat_tiles = [stats_span_ref[near_span, :]] + [item[rows, :] for item in far_stats]
-        lanes = [near_lanes] + [far_lanes] * far_count
+        if part == "near":
+            masks = [jnp.logical_and(near_causal, first + block + near_offset < block_total)]
+            stat_tiles = [stats_span_ref[near_span, :]]
+            lanes = [near_lanes]
+        else:
+            masks = [first + block + offset < block_total for offset in far_list]
+            stat_tiles = [item[rows, :] for item in far_stats]
+            lanes = [far_lanes] * far_count
         for head in range(heads):
             cols = pl.ds(head * HD, HD)
             value_cols = pl.ds(width + head * HD, HD)
             key = own_ref[rows, cols]
             value = own_ref[rows, value_cols]
-            queries = [span_ref[near_span, cols]] + [item[rows, cols] for item in far_rows]
-            grads = [span_ref[near_span, value_cols]] + [item[rows, value_cols] for item in far_rows]
-            grad_key = jnp.zeros((BLK, HD), jnp.float32)
-            grad_value = jnp.zeros((BLK, HD), jnp.float32)
+            if part == "near":
+                queries = [span_ref[near_span, cols]]
+                grads = [span_ref[near_span, value_cols]]
+                grad_key = jnp.zeros((BLK, HD), jnp.float32)
+                grad_value = jnp.zeros((BLK, HD), jnp.float32)
+            else:
+                queries = [item[rows, cols] for item in far_rows]
+                grads = [item[rows, value_cols] for item in far_rows]
+                grad_key = key_acc_ref[rows, cols]
+                grad_value = value_acc_ref[rows, cols]
             for query, grad, tile, lane, mask in zip(queries, grads, stat_tiles, lanes, masks):
                 log_total = jnp.sum(jnp.where(lane == head, tile, 0.0), axis=-1, keepdims=True)
                 out_dot = jnp.sum(jnp.where(lane == heads + head, tile, 0.0), axis=-1, keepdims=True)
@@ -473,8 +485,12 @@
                 grad_key = grad_key + jnp.dot(
                     score_grad.T.astype(jnp.bfloat16), query, preferred_element_type=jnp.float32
                 )
-            grad_key_ref[rows, cols] = (grad_key * scale).astype(jnp.bfloat16)
-            grad_value_ref[rows, cols] = grad_value.astype(jnp.bfloat16)
+            if part == "near":
+                grad_key_ref[rows, cols] = grad_key
+                grad_value_ref[rows, cols] = grad_value
+            else:
+                grad_key_ref[rows, cols] = (grad_key * scale).astype(jnp.bfloat16)
+                grad_value_ref[rows, cols] = grad_value.astype(jnp.bfloat16)
 
 
 def smem_spec():
@@ -531,9 +547,9 @@
         cost_estimate=estimate(tok_count, row_width, slab_rows, 2, 1),
         name="rows_stats",
     )(*row_inputs)
+    far_stats = [passed_along(stats, "seq", -shift) for shift in far_shifts]
     stats_one = passed_along(stats, "seq", -1)
     stats_two = passed_along(stats, "seq", -2)
-    far_stats = [passed_along(stats, "seq", -shift) for shift in far_shifts]
     grad_queries = pl.pallas_call(
         functools.partial(row_kernel, len(near_list), far_offsets, heads, "grad"),
         out_shape=jax.ShapeDtypeStruct((tok_count, row_width), jnp.bfloat16),
@@ -542,24 +558,33 @@
         cost_estimate=estimate(tok_count, row_width, slab_rows, 3, 1),
         name="rows_grad",
     )(*row_inputs, stats)
+    key_acc, value_acc = pl.pallas_call(
+        functools.partial(key_kernel, len(near_list), far_offsets, heads, devices * blocks_dev, "near"),
+        out_shape=(
+            jax.ShapeDtypeStruct((tok_count, row_width), jnp.float32),
+            jax.ShapeDtypeStruct((tok_count, row_width), jnp.float32),
+        ),
+        in_specs=[smem_spec()] + [vmem_spec()] * 3,
+        out_specs=(vmem_spec(), vmem_spec()),
+        cost_estimate=estimate(tok_count, row_width, len(near_list) * BLK, 4, 1),
+        name="keys_near",
+    )(
+        position_arr,
+        keys_values,
+        jnp.concatenate([queries_grads, ahead1, ahead2], axis=0),
+        jnp.concatenate([stats, stats_one, stats_two], axis=0),
+    )
     grad_keys, grad_values = pl.pallas_call(
-        functools.partial(key_kernel, len(near_list), far_offsets, heads, devices * blocks_dev),
+        functools.partial(key_kernel, len(near_list), far_offsets, heads, devices * blocks_dev, "far"),
         out_shape=(
             jax.ShapeDtypeStruct((tok_count, row_width), jnp.bfloat16),
             jax.ShapeDtypeStruct((tok_count, row_width), jnp.bfloat16),
         ),
         in_specs=[smem_spec()] + [vmem_spec()] * (3 + 2 * len(far_ahead)),
         out_specs=(vmem_spec(), vmem_spec()),
-        cost_estimate=estimate(tok_count, row_width, slab_rows, 4, 1),
-        name="keys_pass",
-    )(
-        position_arr,
-        keys_values,
-        jnp.concatenate([queries_grads, ahead1, ahead2], axis=0),
-        jnp.concatenate([stats, stats_one, stats_two], axis=0),
-        *far_ahead,
-        *far_stats,
-    )
+        cost_estimate=estimate(tok_count, row_width, len(far_list) * BLK, 4, 1),
+        name="keys_far",
+    )(position_arr, keys_values, *far_ahead, *far_stats, key_acc, value_acc)
     return attended, grad_queries, grad_keys, grad_values
 
 

time: 69.8 us -> 70.2 us (level)
  the two profiles are of different devices: /device:TPU:0 before, /device:TPU:14 now
where the time goes in v7:
time: 70.2 us; the launch traced here: 69.8 us
  Pallas kernels  21.7 us (31%)
  waiting for transfers between devices  19.8 us (28%)
  starting transfers between devices  19.5 us (28%)
  local copies, waits for them, and re-layouts  4.44 us (6%)
  other arithmetic  3.53 us (5%)
  between operations  0.81 us (1%)
    ppermute x7, starting transfers between devices, passed_along(): lax.ppermute(value, axis, [(source, source + steps) for source in range(f...  18.4 us
    ppermute x7, waiting for transfers between devices, passed_along(): lax.ppermute(value, axis, [(source, source + steps) for source in range(f...  13.7 us
    pallas_call x2, Pallas kernels, body(): pl.pallas_call(functools.partial(row_kernel, len(near_list), far_offsets,...  11.4 us
    pallas_call x2, Pallas kernels, body(): pl.pallas_call(functools.partial(key_kernel, len(near_list), far_offsets,...  10.2 us
    ppermute x1, waiting for transfers between devices, body(): swap_two = lax.ppermute(jnp.where(odd, back2, ahead2), 'seq', pairs)  6.08 us
    unnamed x12, local copies, waits for them, and re-layouts  3.44 us
  transfers between devices with their start and end apart: 9, of which 5 were waited for; matrix products, arithmetic and copies ran while one was open for 6% of the time, Pallas kernels for 25%

profile of v7, /device:TPU:14, one launch (start us, length us, event | category | flops | bytes accessed | tf_op | source)
XLA Modules:
  0.0 69.8 jit_solution(2924862416452535444)
XLA Ops:
  0.6 1.0 %constant_dynamic-update-slice_fusion.1 = bf16[256,1024]{1,0:T(8,128)(2,1)S(1)} fusion(bf16[256,512]{1,0:T(8,128)(2,1)} %param.5), kind=kLoop, calls=%fused_computation.8 | loop fusion | bytes 524288
  1.7 1.0 %constant_dynamic-update-slice_fusion.refs_1_ = bf16[256,1024]{1,0:T(8,128)(2,1)S(1)} fusion(bf16[256,1024]{1,0:T(8,128)(2,1)S(1)} %constant_dynamic-update-slice_fusion.1, bf16[256,512]{1,0:T(8,128)(2,1)} %param.6), kind=kLoop, calls=%fused_computation.7 | loop fusion | bytes 524288 | tf_op jit(solution)/shard_map/concatenate | solution.py:519
  2.7 3.5 %collective-permute-start = (bf16[256,1024]{1,0:T(8,128)(2,1)S(1)}, bf16[256,1024]{1,0:T(8,128)(2,1)S(1)}, u32[]{:S(2)}, u32[]{:S(2)}) collective-permute-start(bf16[256,1024]{1,0:T(8,128)(2,1)S(1)} %constant_dynamic-update-slice_fusion.refs_1_), channel_id=1, source_target_pairs={{0,8},{4,12},{8,16},{12,20},{16,24},{20,28},{1,9},{5,13},{9,17},{1... | collective-permute-start | bytes 1572872 | tf_op jit(solution)/shard_map/ppermute | solution.py:24
  6.2 1.0 %constant_dynamic-update-slice_fusion.3 = bf16[256,1024]{1,0:T(8,128)(2,1)S(1)} fusion(bf16[256,512]{1,0:T(8,128)(2,1)} %refs_1_.3), kind=kLoop, calls=%fused_computation.10 | loop fusion | bytes 524288
  7.2 2.4 %collective-permute-start.2 = (bf16[256,1024]{1,0:T(8,128)(2,1)S(1)}, bf16[256,1024]{1,0:T(8,128)(2,1)S(1)}, u32[]{:S(2)}, u32[]{:S(2)}) collective-permute-start(bf16[256,1024]{1,0:T(8,128)(2,1)S(1)} %constant_dynamic-update-slice_fusion.2), channel_id=1, source_target_pairs={{8,0},{12,4},{16,8},{20,12},{24,16},{28,20},{9,1},{13,5},{17,9},{2... | collective-permute-start | bytes 1572872 | tf_op jit(solution)/shard_map/ppermute | solution.py:24
  10.2 8.0 %collective-permute-done = bf16[256,1024]{1,0:T(8,128)(2,1)S(1)} collective-permute-done((bf16[256,1024]{1,0:T(8,128)(2,1)S(1)}, bf16[256,1024]{1,0:T(8,128)(2,1)S(1)}, u32[]{:S(2)}, u32[]{:S(2)}) %collective-permute-start) | collective-permute-done | bytes 524320 | tf_op jit(solution)/shard_map/ppermute | solution.py:24
  18.2 4.2 %collective-permute-done.2 = bf16[256,1024]{1,0:T(8,128)(2,1)S(1)} collective-permute-done((bf16[256,1024]{1,0:T(8,128)(2,1)S(1)}, bf16[256,1024]{1,0:T(8,128)(2,1)S(1)}, u32[]{:S(2)}, u32[]{:S(2)}) %collective-permute-start.2) | collective-permute-done | bytes 524320 | tf_op jit(solution)/shard_map/ppermute | solution.py:24
  23.1 3.5 %collective-permute-start.4 = (bf16[256,1024]{1,0:T(8,128)(2,1)S(1)}, bf16[256,1024]{1,0:T(8,128)(2,1)S(1)}, u32[]{:S(2)}, u32[]{:S(2)}) collective-permute-start(bf16[256,1024]{1,0:T(8,128)(2,1)S(1)} %collective-permute-done), channel_id=1, source_target_pairs={{0,8},{4,12},{8,16},{12,20},{16,24},{20,28},{1,9},{5,13},{9,17},{1... | collective-permute-start | bytes 1572872 | tf_op jit(solution)/shard_map/ppermute | solution.py:24
  26.6 2.4 %collective-permute-start.5 = (bf16[256,1024]{1,0:T(8,128)(2,1)S(1)}, bf16[256,1024]{1,0:T(8,128)(2,1)}, u32[]{:S(2)}, u32[]{:S(2)}) collective-permute-start(bf16[256,1024]{1,0:T(8,128)(2,1)S(1)} %collective-permute-done.2), channel_id=1, source_target_pairs={{8,0},{12,4},{16,8},{20,12},{24,16},{28,20},{9,1},{13,5},{17,9},{2... | collective-permute-start | bytes 1572872 | tf_op jit(solution)/shard_map/ppermute | solution.py:24
  29.0 6.1 %collective-permute-done.3 = bf16[256,1024]{1,0:T(8,128)(2,1)S(1)} collective-permute-done((bf16[256,1024]{1,0:T(8,128)(2,1)S(1)}, bf16[256,1024]{1,0:T(8,128)(2,1)S(1)}, u32[]{:S(2)}, u32[]{:S(2)}) %collective-permute-start.3) | collective-permute-done | bytes 524320 | tf_op jit(solution)/shard_map/ppermute | solution.py:526
  35.1 1.3 %pad_maximum_fusion.refs_3_ = bf16[768,1024]{1,0:T(8,128)(2,1)} fusion(bf16[256,1024]{1,0:T(8,128)(2,1)S(1)} %constant_dynamic-update-slice_fusion.refs_1_, bf16[256,1024]{1,0:T(8,128)(2,1)S(1)} %get-tuple-element.17, bf16[256,1024]{1,0:T(8,128)(2,1)S(1)} %collective-permute-done), kind=kLoop, calls=%fused_computation | loop fusion | flops 4718592 | bytes 3145728 | tf_op jit(solution)/shard_map/concatenate | solution.py:536
  36.4 0.8 %collective-permute-done.4.refs_4_ = bf16[256,1024]{1,0:T(8,128)(2,1)S(1)} collective-permute-done((bf16[256,1024]{1,0:T(8,128)(2,1)S(1)}, bf16[256,1024]{1,0:T(8,128)(2,1)S(1)}, u32[]{:S(2)}, u32[]{:S(2)}) %collective-permute-start.4) | collective-permute-done | bytes 524320 | tf_op jit(solution)/shard_map/ppermute | solution.py:24
  37.2 0.8 %copy-done.2 = bf16[256,1024]{1,0:T(8,128)(2,1)} copy-done((bf16[256,1024]{1,0:T(8,128)(2,1)}, bf16[256,1024]{1,0:T(8,128)(2,1)S(1)}, u32[]{:S(2)}) %copy-start.2) | copy-done | bytes 524312
  38.0 6.2 %rows_stats.1 = (bf16[256,512]{1,0:T(8,128)(2,1)}, f32[256,8]{1,0:T(8,128)}) custom-call(s32[1]{0:T(128)} %bitcast.refs_0_, bf16[256,512]{1,0:T(8,128)(2,1)} %refs_1_.3, bf16[256,512]{1,0:T(8,128)(2,1)} %refs_2_.3, bf16[768,1024]{1,0:T(8,128)(2,1)} %pad_maximum_fusion.refs_3_, bf16[256,1024]{1,0:T(8,128)(2,1)} %copy-done.2), custom_call_target="tpu_custom_call" | custom-call | flops 402653184 | bytes 4194304 | tf_op jit(solution)/shard_map/rows_stats/pallas_call | solution.py:539
  44.2 1.3 %collective-permute-start.6 = (f32[256,8]{1,0:T(8,128)}, f32[256,8]{1,0:T(8,128)S(1)}, u32[]{:S(2)}, u32[]{:S(2)}) collective-permute-start(f32[256,8]{1,0:T(8,128)} %get-tuple-element.11.refs_5_), channel_id=1, source_target_pairs={{16,0},{20,4},{24,8},{28,12},{17,1},{21,5},{25,9},{29,13},{18,2},{... | collective-permute-start | bytes 24584 | tf_op jit(solution)/shard_map/ppermute | solution.py:24
  45.4 1.9 %collective-permute-start.8 = (f32[256,8]{1,0:T(8,128)}, f32[256,8]{1,0:T(8,128)S(1)}, u32[]{:S(2)}, u32[]{:S(2)}) collective-permute-start(f32[256,8]{1,0:T(8,128)} %get-tuple-element.11.refs_5_), channel_id=1, source_target_pairs={{8,0},{12,4},{16,8},{20,12},{24,16},{28,20},{9,1},{13,5},{17,9},{2... | collective-permute-start | bytes 24584 | tf_op jit(solution)/shard_map/ppermute | solution.py:24
  47.4 3.4 %collective-permute-start.7 = (f32[256,8]{1,0:T(8,128)}, f32[256,8]{1,0:T(8,128)S(1)}, u32[]{:S(2)}, u32[]{:S(2)}) collective-permute-start(f32[256,8]{1,0:T(8,128)} %get-tuple-element.11.refs_5_), channel_id=1, source_target_pairs={{4,0},{8,4},{12,8},{16,12},{20,16},{24,20},{28,24},{5,1},{9,5},{13... | collective-permute-start | bytes 24584 | tf_op jit(solution)/shard_map/ppermute | solution.py:24
  50.8 1.3 %pad_maximum_fusion.1.refs_2_ = bf16[768,1024]{1,0:T(8,128)(2,1)} fusion(bf16[256,1024]{1,0:T(8,128)(2,1)S(1)} %collective-permute-done.2, bf16[256,1024]{1,0:T(8,128)(2,1)S(1)} %get-tuple-element.16, bf16[256,1024]{1,0:T(8,128)(2,1)S(1)} %constant_dynamic-update-slice_fusion.2), kind=kLoop, calls=%fused_computation.1 | loop fusion | flops 4718592 | bytes 3145728 | tf_op jit(solution)/shard_map/concatenate | solution.py:574
  52.1 5.2 %rows_grad.1 = bf16[256,512]{1,0:T(8,128)(2,1)} custom-call(s32[1]{0:T(128)} %bitcast.refs_0_, bf16[256,512]{1,0:T(8,128)(2,1)} %refs_1_.3, bf16[256,512]{1,0:T(8,128)(2,1)} %refs_2_.3, bf16[768,1024]{1,0:T(8,128)(2,1)} %pad_maximum_fusion.refs_3_, bf16[256,1024]{1,0:T(8,128)(2,1)} %copy-done.2, f32[256,8]{1,0:T(8,128)} %get-tuple-element.11.refs_5_), custom_call_target="tpu_custom_call" | custom-call | flops 603979776 | bytes 4194304 | tf_op jit(solution)/shard_map/rows_grad/pallas_call | solution.py:553
  57.3 0.7 %collective-permute-done.7 = f32[256,8]{1,0:T(8,128)S(1)} collective-permute-done((f32[256,8]{1,0:T(8,128)}, f32[256,8]{1,0:T(8,128)S(1)}, u32[]{:S(2)}, u32[]{:S(2)}) %collective-permute-start.7) | collective-permute-done | bytes 8224 | tf_op jit(solution)/shard_map/ppermute | solution.py:24
  58.1 0.8 %pad_maximum_fusion.2.refs_3_ = f32[768,8]{1,0:T(8,128)} fusion(f32[256,8]{1,0:T(8,128)S(1)} %collective-permute-done.8, f32[256,8]{1,0:T(8,128)S(1)} %collective-permute-done.7, f32[256,8]{1,0:T(8,128)S(1)} %copy-done.3), kind=kLoop, calls=%fused_computation.6 | loop fusion | flops 12288 | bytes 49152 | tf_op jit(solution)/shard_map/concatenate | solution.py:575
  58.9 5.8 %keys_near.1 = (f32[256,512]{1,0:T(8,128)}, f32[256,512]{1,0:T(8,128)}) custom-call(s32[1]{0:T(128)} %bitcast.refs_0_, bf16[256,1024]{1,0:T(8,128)(2,1)} %copy-done, bf16[768,1024]{1,0:T(8,128)(2,1)} %pad_maximum_fusion.1.refs_2_, f32[768,8]{1,0:T(8,128)} %pad_maximum_fusion.2.refs_3_), custom_call_target="tpu_custom_call" | custom-call | flops 671088640 | bytes 4194304 | tf_op jit(solution)/shard_map/keys_near/pallas_call | solution.py:561
  64.7 0.6 copy-done.4
  65.3 4.4 %keys_far.1 = (bf16[256,512]{1,0:T(8,128)(2,1)}, bf16[256,512]{1,0:T(8,128)(2,1)}) custom-call(s32[1]{0:T(128)} %bitcast.refs_0_, bf16[256,1024]{1,0:T(8,128)(2,1)} %copy-done, bf16[256,1024]{1,0:T(8,128)(2,1)} %collective-permute-done.5.refs_2_, f32[256,8]{1,0:T(8,128)} %copy-done.4, f32[256,512]{1,0:T(8,128)} %get-tuple-element.12.refs_4_, ...), custom_call_target="tpu_custom_call" | custom-call | flops 134217728 | bytes 4194304 | tf_op jit(solution)/shard_map/keys_far/pallas_call | solution.py:577
  (18 shorter events, 1.4 us)
Async XLA Ops:
  0.6 6.5 %copy-start.1 = (bf16[256,512]{1,0:T(8,128)(2,1)S(1)}, bf16[256,512]{1,0:T(8,128)(2,1)}, u32[]{:S(2)}) copy-start(bf16[256,512]{1,0:T(8,128)(2,1)} %refs_2_.3) | copy-start | bytes 786436
  2.6 32.5 %copy-start = (bf16[256,1024]{1,0:T(8,128)(2,1)}, bf16[256,1024]{1,0:T(8,128)(2,1)S(1)}, u32[]{:S(2)}) copy-start(bf16[256,1024]{1,0:T(8,128)(2,1)S(1)} %constant_dynamic-update-slice_fusion.refs_1_) | copy-start | bytes 1572868
  2.7 15.6 %collective-permute-start = (bf16[256,1024]{1,0:T(8,128)(2,1)S(1)}, bf16[256,1024]{1,0:T(8,128)(2,1)S(1)}, u32[]{:S(2)}, u32[]{:S(2)}) collective-permute-start(bf16[256,1024]{1,0:T(8,128)(2,1)S(1)} %constant_dynamic-update-slice_fusion.refs_1_), channel_id=1, source_target_pairs={{0,8},{4,12},{8,16},{12,20},{16,24},{20,28},{1,9},{5,13},{9,17},{1... | collective-permute-start | bytes 1572872 | tf_op jit(solution)/shard_map/ppermute | solution.py:24
  7.2 15.3 %collective-permute-start.2 = (bf16[256,1024]{1,0:T(8,128)(2,1)S(1)}, bf16[256,1024]{1,0:T(8,128)(2,1)S(1)}, u32[]{:S(2)}, u32[]{:S(2)}) collective-permute-start(bf16[256,1024]{1,0:T(8,128)(2,1)S(1)} %constant_dynamic-update-slice_fusion.2), channel_id=1, source_target_pairs={{8,0},{12,4},{16,8},{20,12},{24,16},{28,20},{9,1},{13,5},{17,9},{2... | collective-permute-start | bytes 1572872 | tf_op jit(solution)/shard_map/ppermute | solution.py:24
  9.6 19.3 %collective-permute-start.1 = (bf16[256,1024]{1,0:T(8,128)(2,1)S(1)}, bf16[256,1024]{1,0:T(8,128)(2,1)S(1)}, u32[]{:S(2)}, u32[]{:S(2)}) collective-permute-start(bf16[256,1024]{1,0:T(8,128)(2,1)S(1)} %broadcast_select_fusion.3), channel_id=1, source_target_pairs={{0,4},{4,0},{8,12},{12,8},{16,20},{20,16},{24,28},{28,24},{1,5},{5... | collective-permute-start | bytes 1572872 | tf_op jit(solution)/shard_map/ppermute | solution.py:523
  22.5 12.5 %collective-permute-start.3 = (bf16[256,1024]{1,0:T(8,128)(2,1)S(1)}, bf16[256,1024]{1,0:T(8,128)(2,1)S(1)}, u32[]{:S(2)}, u32[]{:S(2)}) collective-permute-start(bf16[256,1024]{1,0:T(8,128)(2,1)S(1)} %broadcast_select_fusion.2), channel_id=1, source_target_pairs={{0,4},{4,0},{8,12},{12,8},{16,20},{20,16},{24,28},{28,24},{1,5},{5... | collective-permute-start | bytes 1572872 | tf_op jit(solution)/shard_map/ppermute | solution.py:526
  23.1 14.1 %collective-permute-start.4 = (bf16[256,1024]{1,0:T(8,128)(2,1)S(1)}, bf16[256,1024]{1,0:T(8,128)(2,1)S(1)}, u32[]{:S(2)}, u32[]{:S(2)}) collective-permute-start(bf16[256,1024]{1,0:T(8,128)(2,1)S(1)} %collective-permute-done), channel_id=1, source_target_pairs={{0,8},{4,12},{8,16},{12,20},{16,24},{20,28},{1,9},{5,13},{9,17},{1... | collective-permute-start | bytes 1572872 | tf_op jit(solution)/shard_map/ppermute | solution.py:24
  26.6 38.1 %collective-permute-start.5 = (bf16[256,1024]{1,0:T(8,128)(2,1)S(1)}, bf16[256,1024]{1,0:T(8,128)(2,1)}, u32[]{:S(2)}, u32[]{:S(2)}) collective-permute-start(bf16[256,1024]{1,0:T(8,128)(2,1)S(1)} %collective-permute-done.2), channel_id=1, source_target_pairs={{8,0},{12,4},{16,8},{20,12},{24,16},{28,20},{9,1},{13,5},{17,9},{2... | collective-permute-start | bytes 1572872 | tf_op jit(solution)/shard_map/ppermute | solution.py:24
  37.2 0.8 %copy-start.2 = (bf16[256,1024]{1,0:T(8,128)(2,1)}, bf16[256,1024]{1,0:T(8,128)(2,1)S(1)}, u32[]{:S(2)}) copy-start(bf16[256,1024]{1,0:T(8,128)(2,1)S(1)} %collective-permute-done.4.refs_4_) | copy-start | bytes 1572868
  44.2 20.5 %collective-permute-start.6 = (f32[256,8]{1,0:T(8,128)}, f32[256,8]{1,0:T(8,128)S(1)}, u32[]{:S(2)}, u32[]{:S(2)}) collective-permute-start(f32[256,8]{1,0:T(8,128)} %get-tuple-element.11.refs_5_), channel_id=1, source_target_pairs={{16,0},{20,4},{24,8},{28,12},{17,1},{21,5},{25,9},{29,13},{18,2},{... | collective-permute-start | bytes 24584 | tf_op jit(solution)/shard_map/ppermute | solution.py:24
  45.4 11.9 %collective-permute-start.8 = (f32[256,8]{1,0:T(8,128)}, f32[256,8]{1,0:T(8,128)S(1)}, u32[]{:S(2)}, u32[]{:S(2)}) collective-permute-start(f32[256,8]{1,0:T(8,128)} %get-tuple-element.11.refs_5_), channel_id=1, source_target_pairs={{8,0},{12,4},{16,8},{20,12},{24,16},{28,20},{9,1},{13,5},{17,9},{2... | collective-permute-start | bytes 24584 | tf_op jit(solution)/shard_map/ppermute | solution.py:24
  47.4 10.7 %collective-permute-start.7 = (f32[256,8]{1,0:T(8,128)}, f32[256,8]{1,0:T(8,128)S(1)}, u32[]{:S(2)}, u32[]{:S(2)}) collective-permute-start(f32[256,8]{1,0:T(8,128)} %get-tuple-element.11.refs_5_), channel_id=1, source_target_pairs={{4,0},{8,4},{12,8},{16,12},{20,16},{24,20},{28,24},{5,1},{9,5},{13... | collective-permute-start | bytes 24584 | tf_op jit(solution)/shard_map/ppermute | solution.py:24
  52.1 6.0 %copy-start.3 = (f32[256,8]{1,0:T(8,128)S(1)}, f32[256,8]{1,0:T(8,128)}, u32[]{:S(2)}) copy-start(f32[256,8]{1,0:T(8,128)} %get-tuple-element.11.refs_5_) | copy-start | bytes 24580
  64.7 0.7 copy-start.4

commit v8 on v6

--- a/solution.py
+++ b/solution.py
@@ -339,7 +339,7 @@
     position_ref, query_ref, grad_ref, span_ref = refs[:4]
     far_refs = refs[4 : 4 + far_count]
     if phase == "stats":
-        attended_ref, stats_ref = refs[4 + far_count :]
+        attended_ref, stats_ref, stats_rows_ref = refs[4 + far_count :]
     else:
         stats_in_ref, grad_query_ref = refs[4 + far_count :]
     width = heads * HD
@@ -416,6 +416,12 @@
             stats_tile = stats_tile + jnp.where(lane_ids == heads + head, out_dot, 0.0)
         if phase == "stats":
             stats_ref[rows, :] = stats_tile
+            wide_lanes = lax.broadcasted_iota(jnp.int32, (BLK, BLK), 1)
+            wide = jnp.zeros((BLK, BLK), jnp.float32)
+            for lane in range(2 * heads):
+                column = jnp.sum(jnp.where(lane_ids == lane, stats_tile, 0.0), axis=-1, keepdims=True)
+                wide = wide + jnp.where(wide_lanes == lane, column, 0.0)
+            stats_rows_ref[:, rows] = wide.T[: 2 * heads, :]
 
 
 def estimate(tok_count, row_width, slab_rows, matmuls, exps):
@@ -437,20 +443,16 @@
     near_rows = near_count * BLK
     scale = 1.0 / math.sqrt(HD)
     first = 2 * position_ref[0]
-    near_row_ids = lax.broadcasted_iota(jnp.int32, (near_rows, BLK), 0)
-    near_col_ids = lax.broadcasted_iota(jnp.int32, (near_rows, BLK), 1)
-    near_offset = near_row_ids // BLK
-    near_causal = jnp.logical_or(near_offset > 0, near_row_ids % BLK >= near_col_ids)
-    near_lanes = lax.broadcasted_iota(jnp.int32, (near_rows, 2 * heads), 1)
-    far_lanes = lax.broadcasted_iota(jnp.int32, (BLK, 2 * heads), 1)
+    near_key_ids = lax.broadcasted_iota(jnp.int32, (BLK, near_rows), 0)
+    near_query_ids = lax.broadcasted_iota(jnp.int32, (BLK, near_rows), 1)
+    near_offset = near_query_ids // BLK
+    near_causal = jnp.logical_or(near_offset > 0, near_query_ids % BLK >= near_key_ids)
     for block in range(2):
         rows = pl.ds(block * BLK, BLK)
         near_span = pl.ds(block * BLK, near_rows)
         near_mask = jnp.logical_and(near_causal, first + block + near_offset < block_total)
         far_live = [first + block + offset < block_total for offset in far_list]
         masks = [near_mask] + far_live
-        stat_tiles = [stats_span_ref[near_span, :]] + [item[rows, :] for item in far_stats]
-        lanes = [near_lanes] + [far_lanes] * far_count
         for head in range(heads):
             cols = pl.ds(head * HD, HD)
             value_cols = pl.ds(width + head * HD, HD)
@@ -458,21 +460,23 @@
             value = own_ref[rows, value_cols]
             queries = [span_ref[near_span, cols]] + [item[rows, cols] for item in far_rows]
             grads = [span_ref[near_span, value_cols]] + [item[rows, value_cols] for item in far_rows]
+            totals = [stats_span_ref[pl.ds(head, 1), near_span]] + [
+                item[pl.ds(head, 1), rows] for item in far_stats
+            ]
+            dots = [stats_span_ref[pl.ds(heads + head, 1), near_span]] + [
+                item[pl.ds(heads + head, 1), rows] for item in far_stats
+            ]
             grad_key = jnp.zeros((BLK, HD), jnp.float32)
             grad_value = jnp.zeros((BLK, HD), jnp.float32)
-            for query, grad, tile, lane, mask in zip(queries, grads, stat_tiles, lanes, masks):
-                log_total = jnp.sum(jnp.where(lane == head, tile, 0.0), axis=-1, keepdims=True)
-                out_dot = jnp.sum(jnp.where(lane == heads + head, tile, 0.0), axis=-1, keepdims=True)
-                score = lax.dot_general(query, key, TRANS_B, preferred_element_type=jnp.float32)
+            for query, grad, log_total, out_dot, mask in zip(queries, grads, totals, dots, masks):
+                score = lax.dot_general(key, query, TRANS_B, preferred_element_type=jnp.float32)
                 prob = jnp.where(mask, jnp.exp(score * scale - log_total), 0.0)
-                prob_grad = lax.dot_general(grad, value, TRANS_B, preferred_element_type=jnp.float32)
-                score_grad = prob * (prob_grad - out_dot)
+                prob_grad = lax.dot_general(value, grad, TRANS_B, preferred_element_type=jnp.float32)
+                score_grad = (prob * (prob_grad - out_dot)).astype(jnp.bfloat16)
                 grad_value = grad_value + jnp.dot(
-                    prob.T.astype(jnp.bfloat16), grad, preferred_element_type=jnp.float32
+                    prob.astype(jnp.bfloat16), grad, preferred_element_type=jnp.float32
                 )
-                grad_key = grad_key + jnp.dot(
-                    score_grad.T.astype(jnp.bfloat16), query, preferred_element_type=jnp.float32
-                )
+                grad_key = grad_key + jnp.dot(score_grad, query, preferred_element_type=jnp.float32)
             grad_key_ref[rows, cols] = (grad_key * scale).astype(jnp.bfloat16)
             grad_value_ref[rows, cols] = grad_value.astype(jnp.bfloat16)
 
@@ -520,20 +524,21 @@
     row_span = jnp.concatenate([back2, back1, keys_values], axis=0)
     slab_rows = (len(near_list) + len(far_list)) * BLK
     row_inputs = (position_arr, queries, grad_out, row_span, *far_back)
-    attended, stats = pl.pallas_call(
+    attended, stats, stats_rows = pl.pallas_call(
         functools.partial(row_kernel, len(near_list), far_offsets, heads, "stats"),
         out_shape=(
             jax.ShapeDtypeStruct((tok_count, row_width), jnp.bfloat16),
             jax.ShapeDtypeStruct((tok_count, 2 * heads), jnp.float32),
+            jax.ShapeDtypeStruct((2 * heads, tok_count), jnp.float32),
         ),
         in_specs=[smem_spec()] + [vmem_spec()] * (3 + len(far_back)),
-        out_specs=(vmem_spec(), vmem_spec()),
+        out_specs=(vmem_spec(), vmem_spec(), vmem_spec()),
         cost_estimate=estimate(tok_count, row_width, slab_rows, 2, 1),
         name="rows_stats",
     )(*row_inputs)
-    stats_one = passed_along(stats, "seq", -1)
-    stats_two = passed_along(stats, "seq", -2)
-    far_stats = [passed_along(stats, "seq", -shift) for shift in far_shifts]
+    stats_one = passed_along(stats_rows, "seq", -1)
+    stats_two = passed_along(stats_rows, "seq", -2)
+    far_stats = [passed_along(stats_rows, "seq", -shift) for shift in far_shifts]
     grad_queries = pl.pallas_call(
         functools.partial(row_kernel, len(near_list), far_offsets, heads, "grad"),
         out_shape=jax.ShapeDtypeStruct((tok_count, row_width), jnp.bfloat16),
@@ -556,7 +561,7 @@
         position_arr,
         keys_values,
         jnp.concatenate([queries_grads, ahead1, ahead2], axis=0),
-        jnp.concatenate([stats, stats_one, stats_two], axis=0),
+        jnp.concatenate([stats_rows, stats_one, stats_two], axis=1),
         *far_ahead,
         *far_stats,
     )

time: 69.8 us -> 65.6 us (0.940)
  the two profiles are of different devices: /device:TPU:0 before, /device:TPU:28 now
where the time goes in v8:
time: 65.6 us; the launch traced here: 65.2 us
  starting transfers between devices  23 us (35%)
  Pallas kernels  17.1 us (26%)
  waiting for transfers between devices  16.6 us (25%)
  local copies, waits for them, and re-layouts  4.4 us (7%)
  other arithmetic  3.36 us (5%)
  between operations  0.79 us (1%)
    ppermute x7, starting transfers between devices, passed_along(): lax.ppermute(value, axis, [(source, source + steps) for source in range(f...  21.8 us
    pallas_call x2, Pallas kernels, body(): pl.pallas_call(functools.partial(row_kernel, len(near_list), far_offsets,...  11.6 us
    ppermute x7, waiting for transfers between devices, passed_along(): lax.ppermute(value, axis, [(source, source + steps) for source in range(f...  10.7 us
    ppermute x1, waiting for transfers between devices, body(): swap_two = lax.ppermute(jnp.where(odd, back2, ahead2), 'seq', pairs)  5.87 us
    pallas_call x1, Pallas kernels, body(): pl.pallas_call(functools.partial(key_kernel, len(near_list), far_offsets,...  5.42 us
    unnamed x12, local copies, waits for them, and re-layouts  3.4 us
  transfers between devices with their start and end apart: 9, of which 4 were waited for; matrix products, arithmetic and copies ran while one was open for 7% of the time, Pallas kernels for 18%

profile of v8, /device:TPU:28, one launch (start us, length us, event | category | flops | bytes accessed | tf_op | source)
XLA Modules:
  0.0 65.2 jit_solution(17078828036938460951)
XLA Ops:
  0.6 1.0 %constant_dynamic-update-slice_fusion.1 = bf16[256,1024]{1,0:T(8,128)(2,1)S(1)} fusion(bf16[256,512]{1,0:T(8,128)(2,1)} %param.5), kind=kLoop, calls=%fused_computation.8 | loop fusion | bytes 524288
  1.7 1.0 %constant_dynamic-update-slice_fusion.refs_1_ = bf16[256,1024]{1,0:T(8,128)(2,1)S(1)} fusion(bf16[256,1024]{1,0:T(8,128)(2,1)S(1)} %constant_dynamic-update-slice_fusion.1, bf16[256,512]{1,0:T(8,128)(2,1)} %param.6), kind=kLoop, calls=%fused_computation.7 | loop fusion | bytes 524288 | tf_op jit(solution)/shard_map/concatenate | solution.py:507
  2.7 1.3 %collective-permute-start = (bf16[256,1024]{1,0:T(8,128)(2,1)S(1)}, bf16[256,1024]{1,0:T(8,128)(2,1)S(1)}, u32[]{:S(2)}, u32[]{:S(2)}) collective-permute-start(bf16[256,1024]{1,0:T(8,128)(2,1)S(1)} %constant_dynamic-update-slice_fusion.refs_1_), channel_id=1, source_target_pairs={{0,8},{4,12},{8,16},{12,20},{16,24},{20,28},{1,9},{5,13},{9,17},{1... | collective-permute-start | bytes 1572872 | tf_op jit(solution)/shard_map/ppermute | solution.py:24
  4.0 1.0 %constant_dynamic-update-slice_fusion.3 = bf16[256,1024]{1,0:T(8,128)(2,1)S(1)} fusion(bf16[256,512]{1,0:T(8,128)(2,1)} %refs_1_.3), kind=kLoop, calls=%fused_computation.10 | loop fusion | bytes 524288
  5.0 4.6 %collective-permute-start.2 = (bf16[256,1024]{1,0:T(8,128)(2,1)S(1)}, bf16[256,1024]{1,0:T(8,128)(2,1)S(1)}, u32[]{:S(2)}, u32[]{:S(2)}) collective-permute-start(bf16[256,1024]{1,0:T(8,128)(2,1)S(1)} %constant_dynamic-update-slice_fusion.2), channel_id=1, source_target_pairs={{8,0},{12,4},{16,8},{20,12},{24,16},{28,20},{9,1},{13,5},{17,9},{2... | collective-permute-start | bytes 1572872 | tf_op jit(solution)/shard_map/ppermute | solution.py:24
  9.6 0.6 collective-permute-start.1
  10.2 8.0 %collective-permute-done = bf16[256,1024]{1,0:T(8,128)(2,1)S(1)} collective-permute-done((bf16[256,1024]{1,0:T(8,128)(2,1)S(1)}, bf16[256,1024]{1,0:T(8,128)(2,1)S(1)}, u32[]{:S(2)}, u32[]{:S(2)}) %collective-permute-start) | collective-permute-done | bytes 524320 | tf_op jit(solution)/shard_map/ppermute | solution.py:24
  18.2 2.2 %collective-permute-done.2 = bf16[256,1024]{1,0:T(8,128)(2,1)S(1)} collective-permute-done((bf16[256,1024]{1,0:T(8,128)(2,1)S(1)}, bf16[256,1024]{1,0:T(8,128)(2,1)S(1)}, u32[]{:S(2)}, u32[]{:S(2)}) %collective-permute-start.2) | collective-permute-done | bytes 524320 | tf_op jit(solution)/shard_map/ppermute | solution.py:24
  20.5 0.6 collective-permute-start.3
  21.1 1.3 %collective-permute-start.4 = (bf16[256,1024]{1,0:T(8,128)(2,1)S(1)}, bf16[256,1024]{1,0:T(8,128)(2,1)S(1)}, u32[]{:S(2)}, u32[]{:S(2)}) collective-permute-start(bf16[256,1024]{1,0:T(8,128)(2,1)S(1)} %collective-permute-done), channel_id=1, source_target_pairs={{0,8},{4,12},{8,16},{12,20},{16,24},{20,28},{1,9},{5,13},{9,17},{1... | collective-permute-start | bytes 1572872 | tf_op jit(solution)/shard_map/ppermute | solution.py:24
  22.3 5.8 %collective-permute-start.7 = (bf16[256,1024]{1,0:T(8,128)(2,1)S(1)}, bf16[256,1024]{1,0:T(8,128)(2,1)}, u32[]{:S(2)}, u32[]{:S(2)}) collective-permute-start(bf16[256,1024]{1,0:T(8,128)(2,1)S(1)} %collective-permute-done.2), channel_id=1, source_target_pairs={{8,0},{12,4},{16,8},{20,12},{24,16},{28,20},{9,1},{13,5},{17,9},{2... | collective-permute-start | bytes 1572872 | tf_op jit(solution)/shard_map/ppermute | solution.py:24
  28.2 5.9 %collective-permute-done.3 = bf16[256,1024]{1,0:T(8,128)(2,1)S(1)} collective-permute-done((bf16[256,1024]{1,0:T(8,128)(2,1)S(1)}, bf16[256,1024]{1,0:T(8,128)(2,1)S(1)}, u32[]{:S(2)}, u32[]{:S(2)}) %collective-permute-start.3) | collective-permute-done | bytes 524320 | tf_op jit(solution)/shard_map/ppermute | solution.py:514
  34.1 1.3 %pad_maximum_fusion.refs_3_ = bf16[768,1024]{1,0:T(8,128)(2,1)} fusion(bf16[256,1024]{1,0:T(8,128)(2,1)S(1)} %constant_dynamic-update-slice_fusion.refs_1_, bf16[256,1024]{1,0:T(8,128)(2,1)S(1)} %get-tuple-element.15, bf16[256,1024]{1,0:T(8,128)(2,1)S(1)} %collective-permute-done), kind=kLoop, calls=%fused_computation | loop fusion | flops 4718592 | bytes 3145728 | tf_op jit(solution)/shard_map/concatenate | solution.py:524
  35.4 0.5 collective-permute-done.4.refs_4_
  35.9 0.8 %copy-done.2 = bf16[256,1024]{1,0:T(8,128)(2,1)} copy-done((bf16[256,1024]{1,0:T(8,128)(2,1)}, bf16[256,1024]{1,0:T(8,128)(2,1)S(1)}, u32[]{:S(2)}) %copy-start.2) | copy-done | bytes 524312
  36.7 6.4 %rows_stats.1 = (bf16[256,512]{1,0:T(8,128)(2,1)}, f32[256,8]{1,0:T(8,128)}, f32[8,256]{1,0:T(8,128)}) custom-call(s32[1]{0:T(128)} %bitcast.refs_0_, bf16[256,512]{1,0:T(8,128)(2,1)} %refs_1_.3, bf16[256,512]{1,0:T(8,128)(2,1)} %refs_2_.3, bf16[768,1024]{1,0:T(8,128)(2,1)} %pad_maximum_fusion.refs_3_, bf16[256,1024]{1,0:T(8,128)(2,1)} %copy-done.2), custom_call_target="tpu_custom_call" | custom-call | flops 402653184 | bytes 4194304 | tf_op jit(solution)/shard_map/rows_stats/pallas_call | solution.py:527
  43.1 3.6 %collective-permute-start.6 = (f32[8,256]{1,0:T(8,128)}, f32[8,256]{1,0:T(8,128)S(1)}, u32[]{:S(2)}, u32[]{:S(2)}) collective-permute-start(f32[8,256]{1,0:T(8,128)} %get-tuple-element.11), channel_id=1, source_target_pairs={{8,0},{12,4},{16,8},{20,12},{24,16},{28,20},{9,1},{13,5},{17,9},{2... | collective-permute-start | bytes 24584 | tf_op jit(solution)/shard_map/ppermute | solution.py:24
  46.7 3.4 %collective-permute-start.5 = (f32[8,256]{1,0:T(8,128)}, f32[8,256]{1,0:T(8,128)S(1)}, u32[]{:S(2)}, u32[]{:S(2)}) collective-permute-start(f32[8,256]{1,0:T(8,128)} %get-tuple-element.11), channel_id=1, source_target_pairs={{4,0},{8,4},{12,8},{16,12},{20,16},{24,20},{28,24},{5,1},{9,5},{13... | collective-permute-start | bytes 24584 | tf_op jit(solution)/shard_map/ppermute | solution.py:24
  50.2 1.8 %collective-permute-start.8 = (f32[8,256]{1,0:T(8,128)}, f32[8,256]{1,0:T(8,128)S(1)}, u32[]{:S(2)}, u32[]{:S(2)}) collective-permute-start(f32[8,256]{1,0:T(8,128)} %get-tuple-element.11), channel_id=1, source_target_pairs={{16,0},{20,4},{24,8},{28,12},{17,1},{21,5},{25,9},{29,13},{18,2},{... | collective-permute-start | bytes 24584 | tf_op jit(solution)/shard_map/ppermute | solution.py:24
  52.0 1.3 %pad_maximum_fusion.1.refs_2_ = bf16[768,1024]{1,0:T(8,128)(2,1)} fusion(bf16[256,1024]{1,0:T(8,128)(2,1)S(1)} %collective-permute-done.2, bf16[256,1024]{1,0:T(8,128)(2,1)S(1)} %get-tuple-element.14, bf16[256,1024]{1,0:T(8,128)(2,1)S(1)} %constant_dynamic-update-slice_fusion.2), kind=kLoop, calls=%fused_computation.1 | loop fusion | flops 4718592 | bytes 3145728 | tf_op jit(solution)/shard_map/concatenate | solution.py:563
  53.3 5.2 %rows_grad.1 = bf16[256,512]{1,0:T(8,128)(2,1)} custom-call(s32[1]{0:T(128)} %bitcast.refs_0_, bf16[256,512]{1,0:T(8,128)(2,1)} %refs_1_.3, bf16[256,512]{1,0:T(8,128)(2,1)} %refs_2_.3, bf16[768,1024]{1,0:T(8,128)(2,1)} %pad_maximum_fusion.refs_3_, bf16[256,1024]{1,0:T(8,128)(2,1)} %copy-done.2, f32[256,8]{1,0:T(8,128)} %get-tuple-element.10.refs_5_), custom_call_target="tpu_custom_call" | custom-call | flops 603979776 | bytes 4194304 | tf_op jit(solution)/shard_map/rows_grad/pallas_call | solution.py:542
  58.5 0.6 pad_maximum_fusion.2.refs_3_
  59.1 0.6 copy-done.4
  59.7 5.4 %keys_pass.1 = (bf16[256,512]{1,0:T(8,128)(2,1)}, bf16[256,512]{1,0:T(8,128)(2,1)}) custom-call(s32[1]{0:T(128)} %bitcast.refs_0_, bf16[256,1024]{1,0:T(8,128)(2,1)} %copy-done, bf16[768,1024]{1,0:T(8,128)(2,1)} %pad_maximum_fusion.1.refs_2_, f32[8,768]{1,0:T(8,128)} %pad_maximum_fusion.2.refs_3_, bf16[256,1024]{1,0:T(8,128)(2,1)} %collective-permute-done.7.refs_4_, ...), custom_call_target="tpu_custom_call" | custom-call | flops 805306368 | bytes 4194304 | tf_op jit(solution)/shard_map/keys_pass/pallas_call | solution.py:550
  (17 shorter events, 0.2 us)
Async XLA Ops:
  0.6 4.3 %copy-start.1 = (bf16[256,512]{1,0:T(8,128)(2,1)S(1)}, bf16[256,512]{1,0:T(8,128)(2,1)}, u32[]{:S(2)}) copy-start(bf16[256,512]{1,0:T(8,128)(2,1)} %refs_2_.3) | copy-start | bytes 786436
  2.6 31.5 %copy-start = (bf16[256,1024]{1,0:T(8,128)(2,1)}, bf16[256,1024]{1,0:T(8,128)(2,1)S(1)}, u32[]{:S(2)}) copy-start(bf16[256,1024]{1,0:T(8,128)(2,1)S(1)} %constant_dynamic-update-slice_fusion.refs_1_) | copy-start | bytes 1572868
  2.7 15.6 %collective-permute-start = (bf16[256,1024]{1,0:T(8,128)(2,1)S(1)}, bf16[256,1024]{1,0:T(8,128)(2,1)S(1)}, u32[]{:S(2)}, u32[]{:S(2)}) collective-permute-start(bf16[256,1024]{1,0:T(8,128)(2,1)S(1)} %constant_dynamic-update-slice_fusion.refs_1_), channel_id=1, source_target_pairs={{0,8},{4,12},{8,16},{12,20},{16,24},{20,28},{1,9},{5,13},{9,17},{1... | collective-permute-start | bytes 1572872 | tf_op jit(solution)/shard_map/ppermute | solution.py:24
  5.0 15.4 %collective-permute-start.2 = (bf16[256,1024]{1,0:T(8,128)(2,1)S(1)}, bf16[256,1024]{1,0:T(8,128)(2,1)S(1)}, u32[]{:S(2)}, u32[]{:S(2)}) collective-permute-start(bf16[256,1024]{1,0:T(8,128)(2,1)S(1)} %constant_dynamic-update-slice_fusion.2), channel_id=1, source_target_pairs={{8,0},{12,4},{16,8},{20,12},{24,16},{28,20},{9,1},{13,5},{17,9},{2... | collective-permute-start | bytes 1572872 | tf_op jit(solution)/shard_map/ppermute | solution.py:24
  9.6 18.5 %collective-permute-start.1 = (bf16[256,1024]{1,0:T(8,128)(2,1)S(1)}, bf16[256,1024]{1,0:T(8,128)(2,1)S(1)}, u32[]{:S(2)}, u32[]{:S(2)}) collective-permute-start(bf16[256,1024]{1,0:T(8,128)(2,1)S(1)} %broadcast_select_fusion.3), channel_id=1, source_target_pairs={{0,4},{4,0},{8,12},{12,8},{16,20},{20,16},{24,28},{28,24},{1,5},{5... | collective-permute-start | bytes 1572872 | tf_op jit(solution)/shard_map/ppermute | solution.py:511
  20.5 13.6 %collective-permute-start.3 = (bf16[256,1024]{1,0:T(8,128)(2,1)S(1)}, bf16[256,1024]{1,0:T(8,128)(2,1)S(1)}, u32[]{:S(2)}, u32[]{:S(2)}) collective-permute-start(bf16[256,1024]{1,0:T(8,128)(2,1)S(1)} %broadcast_select_fusion.2), channel_id=1, source_target_pairs={{0,4},{4,0},{8,12},{12,8},{16,20},{20,16},{24,28},{28,24},{1,5},{5... | collective-permute-start | bytes 1572872 | tf_op jit(solution)/shard_map/ppermute | solution.py:514
  21.1 14.8 %collective-permute-start.4 = (bf16[256,1024]{1,0:T(8,128)(2,1)S(1)}, bf16[256,1024]{1,0:T(8,128)(2,1)S(1)}, u32[]{:S(2)}, u32[]{:S(2)}) collective-permute-start(bf16[256,1024]{1,0:T(8,128)(2,1)S(1)} %collective-permute-done), channel_id=1, source_target_pairs={{0,8},{4,12},{8,16},{12,20},{16,24},{20,28},{1,9},{5,13},{9,17},{1... | collective-permute-start | bytes 1572872 | tf_op jit(solution)/shard_map/ppermute | solution.py:24
  22.3 36.8 %collective-permute-start.7 = (bf16[256,1024]{1,0:T(8,128)(2,1)S(1)}, bf16[256,1024]{1,0:T(8,128)(2,1)}, u32[]{:S(2)}, u32[]{:S(2)}) collective-permute-start(bf16[256,1024]{1,0:T(8,128)(2,1)S(1)} %collective-permute-done.2), channel_id=1, source_target_pairs={{8,0},{12,4},{16,8},{20,12},{24,16},{28,20},{9,1},{13,5},{17,9},{2... | collective-permute-start | bytes 1572872 | tf_op jit(solution)/shard_map/ppermute | solution.py:24
  35.9 0.8 %copy-start.2 = (bf16[256,1024]{1,0:T(8,128)(2,1)}, bf16[256,1024]{1,0:T(8,128)(2,1)S(1)}, u32[]{:S(2)}) copy-start(bf16[256,1024]{1,0:T(8,128)(2,1)S(1)} %collective-permute-done.4.refs_4_) | copy-start | bytes 1572868
  43.1 15.4 %collective-permute-start.6 = (f32[8,256]{1,0:T(8,128)}, f32[8,256]{1,0:T(8,128)S(1)}, u32[]{:S(2)}, u32[]{:S(2)}) collective-permute-start(f32[8,256]{1,0:T(8,128)} %get-tuple-element.11), channel_id=1, source_target_pairs={{8,0},{12,4},{16,8},{20,12},{24,16},{28,20},{9,1},{13,5},{17,9},{2... | collective-permute-start | bytes 24584 | tf_op jit(solution)/shard_map/ppermute | solution.py:24
  46.7 11.8 %collective-permute-start.5 = (f32[8,256]{1,0:T(8,128)}, f32[8,256]{1,0:T(8,128)S(1)}, u32[]{:S(2)}, u32[]{:S(2)}) collective-permute-start(f32[8,256]{1,0:T(8,128)} %get-tuple-element.11), channel_id=1, source_target_pairs={{4,0},{8,4},{12,8},{16,12},{20,16},{24,20},{28,24},{5,1},{9,5},{13... | collective-permute-start | bytes 24584 | tf_op jit(solution)/shard_map/ppermute | solution.py:24
  50.2 9.0 %collective-permute-start.8 = (f32[8,256]{1,0:T(8,128)}, f32[8,256]{1,0:T(8,128)S(1)}, u32[]{:S(2)}, u32[]{:S(2)}) collective-permute-start(f32[8,256]{1,0:T(8,128)} %get-tuple-element.11), channel_id=1, source_target_pairs={{16,0},{20,4},{24,8},{28,12},{17,1},{21,5},{25,9},{29,13},{18,2},{... | collective-permute-start | bytes 24584 | tf_op jit(solution)/shard_map/ppermute | solution.py:24
  53.3 5.2 %copy-start.3 = (f32[8,256]{1,0:T(8,128)S(1)}, f32[8,256]{1,0:T(8,128)}, u32[]{:S(2)}) copy-start(f32[8,256]{1,0:T(8,128)} %get-tuple-element.11) | copy-start | bytes 24580
  59.1 0.6 copy-start.4

commit v9 on v8

--- a/solution.py
+++ b/solution.py
@@ -334,14 +334,29 @@
 TRANS_B = (((1,), (1,)), ((), ()))
 
 
+def span_load(refs, start, length, other, axis):
+    size = refs[0].shape[axis]
+    pieces = []
+    at = start
+    while length > 0:
+        index, offset = at // size, at % size
+        count = min(size - offset, length)
+        window = pl.ds(offset, count)
+        pieces.append(refs[index][window, other] if axis == 0 else refs[index][other, window])
+        at += count
+        length -= count
+    return pieces[0] if len(pieces) == 1 else jnp.concatenate(pieces, axis=axis)
+
+
 def row_kernel(near_count, far_list, heads, phase, *refs):
     far_count = len(far_list)
-    position_ref, query_ref, grad_ref, span_ref = refs[:4]
-    far_refs = refs[4 : 4 + far_count]
+    position_ref, query_ref, grad_ref = refs[:3]
+    span_refs = refs[3:6]
+    far_refs = refs[6 : 6 + far_count]
     if phase == "stats":
-        attended_ref, stats_ref, stats_rows_ref = refs[4 + far_count :]
+        attended_ref, stats_ref, stats_rows_ref = refs[6 + far_count :]
     else:
-        stats_in_ref, grad_query_ref = refs[4 + far_count :]
+        stats_in_ref, grad_query_ref = refs[6 + far_count :]
     width = heads * HD
     near_rows = near_count * BLK
     scale = 1.0 / math.sqrt(HD)
@@ -366,8 +381,10 @@
             value_cols = pl.ds(width + head * HD, HD)
             query = query_ref[rows, cols]
             grad = grad_ref[rows, cols]
-            keys = [span_ref[near_span, cols]] + [item[rows, cols] for item in far_refs]
-            values = [span_ref[near_span, value_cols]] + [item[rows, value_cols] for item in far_refs]
+            keys = [span_load(span_refs, block * BLK, near_rows, cols, 0)]
+            keys = keys + [item[rows, cols] for item in far_refs]
+            values = [span_load(span_refs, block * BLK, near_rows, value_cols, 0)]
+            values = values + [item[rows, value_cols] for item in far_refs]
             scores = [
                 lax.dot_general(query, key, TRANS_B, preferred_element_type=jnp.float32) * scale
                 for key in keys
@@ -435,10 +452,12 @@
 
 def key_kernel(near_count, far_list, heads, block_total, *refs):
     far_count = len(far_list)
-    position_ref, own_ref, span_ref, stats_span_ref = refs[:4]
-    far_rows = refs[4 : 4 + far_count]
-    far_stats = refs[4 + far_count : 4 + 2 * far_count]
-    grad_key_ref, grad_value_ref = refs[4 + 2 * far_count :]
+    position_ref, own_ref = refs[:2]
+    span_refs = refs[2:5]
+    stats_refs = refs[5:8]
+    far_rows = refs[8 : 8 + far_count]
+    far_stats = refs[8 + far_count : 8 + 2 * far_count]
+    grad_key_ref, grad_value_ref = refs[8 + 2 * far_count :]
     width = heads * HD
     near_rows = near_count * BLK
     scale = 1.0 / math.sqrt(HD)
@@ -458,12 +477,14 @@
             value_cols = pl.ds(width + head * HD, HD)
             key = own_ref[rows, cols]
             value = own_ref[rows, value_cols]
-            queries = [span_ref[near_span, cols]] + [item[rows, cols] for item in far_rows]
-            grads = [span_ref[near_span, value_cols]] + [item[rows, value_cols] for item in far_rows]
-            totals = [stats_span_ref[pl.ds(head, 1), near_span]] + [
+            queries = [span_load(span_refs, block * BLK, near_rows, cols, 0)]
+            queries = queries + [item[rows, cols] for item in far_rows]
+            grads = [span_load(span_refs, block * BLK, near_rows, value_cols, 0)]
+            grads = grads + [item[rows, value_cols] for item in far_rows]
+            totals = [span_load(stats_refs, block * BLK, near_rows, pl.ds(head, 1), 1)] + [
                 item[pl.ds(head, 1), rows] for item in far_stats
             ]
-            dots = [stats_span_ref[pl.ds(heads + head, 1), near_span]] + [
+            dots = [span_load(stats_refs, block * BLK, near_rows, pl.ds(heads + head, 1), 1)] + [
                 item[pl.ds(heads + head, 1), rows] for item in far_stats
             ]
             grad_key = jnp.zeros((BLK, HD), jnp.float32)
@@ -521,9 +542,8 @@
 
     position_arr = jnp.reshape(position, (1,)).astype(jnp.int32)
     far_offsets = list(far_list)
-    row_span = jnp.concatenate([back2, back1, keys_values], axis=0)
     slab_rows = (len(near_list) + len(far_list)) * BLK
-    row_inputs = (position_arr, queries, grad_out, row_span, *far_back)
+    row_inputs = (position_arr, queries, grad_out, back2, back1, keys_values, *far_back)
     attended, stats, stats_rows = pl.pallas_call(
         functools.partial(row_kernel, len(near_list), far_offsets, heads, "stats"),
         out_shape=(
@@ -531,7 +551,7 @@
             jax.ShapeDtypeStruct((tok_count, 2 * heads), jnp.float32),
             jax.ShapeDtypeStruct((2 * heads, tok_count), jnp.float32),
         ),
-        in_specs=[smem_spec()] + [vmem_spec()] * (3 + len(far_back)),
+        in_specs=[smem_spec()] + [vmem_spec()] * (5 + len(far_back)),
         out_specs=(vmem_spec(), vmem_spec(), vmem_spec()),
         cost_estimate=estimate(tok_count, row_width, slab_rows, 2, 1),
         name="rows_stats",
@@ -542,7 +562,7 @@
     grad_queries = pl.pallas_call(
         functools.partial(row_kernel, len(near_list), far_offsets, heads, "grad"),
         out_shape=jax.ShapeDtypeStruct((tok_count, row_width), jnp.bfloat16),
-        in_specs=[smem_spec()] + [vmem_spec()] * (4 + len(far_back)),
+        in_specs=[smem_spec()] + [vmem_spec()] * (6 + len(far_back)),
         out_specs=vmem_spec(),
         cost_estimate=estimate(tok_count, row_width, slab_rows, 3, 1),
         name="rows_grad",
@@ -553,15 +573,19 @@
             jax.ShapeDtypeStruct((tok_count, row_width), jnp.bfloat16),
             jax.ShapeDtypeStruct((tok_count, row_width), jnp.bfloat16),
         ),
-        in_specs=[smem_spec()] + [vmem_spec()] * (3 + 2 * len(far_ahead)),
+        in_specs=[smem_spec()] + [vmem_spec()] * (7 + 2 * len(far_ahead)),
         out_specs=(vmem_spec(), vmem_spec()),
         cost_estimate=estimate(tok_count, row_width, slab_rows, 4, 1),
         name="keys_pass",
     )(
         position_arr,
         keys_values,
-        jnp.concatenate([queries_grads, ahead1, ahead2], axis=0),
-        jnp.concatenate([stats_rows, stats_one, stats_two], axis=1),
+        queries_grads,
+        ahead1,
+        ahead2,
+        stats_rows,
+        stats_one,
+        stats_two,
         *far_ahead,
         *far_stats,
     )

time: 65.6 us -> 62 us (0.945)
  the two profiles are of different devices: /device:TPU:28 before, /device:TPU:0 now
where the time goes in v9:
time: 62 us; the launch traced here: 61.1 us
  waiting for transfers between devices  21.4 us (35%)
  starting transfers between devices  18.2 us (29%)
  Pallas kernels  17 us (27%)
  local copies, waits for them, and re-layouts  2.49 us (4%)
  other arithmetic  1.15 us (2%)
  between operations  0.88 us (1%)
    ppermute x7, waiting for transfers between devices, passed_along(): lax.ppermute(value, axis, [(source, source + steps) for source in range(f...  15.3 us
    ppermute x7, starting transfers between devices, passed_along(): lax.ppermute(value, axis, [(source, source + steps) for source in range(f...  15 us
    pallas_call x2, Pallas kernels, body(): pl.pallas_call(functools.partial(row_kernel, len(near_list), far_offsets,...  11.6 us
    ppermute x1, waiting for transfers between devices, body(): swap_two = lax.ppermute(jnp.where(odd, back2, ahead2), 'seq', pairs)  6.15 us
    pallas_call x1, Pallas kernels, body(): pl.pallas_call(functools.partial(key_kernel, len(near_list), far_offsets,...  5.42 us
    unnamed x26, local copies, waits for them, and re-layouts  2.44 us
    ppermute x1, starting transfers between devices, body(): lax.ppermute(jnp.where(odd, queries_grads, keys_values), 'seq', pairs)  1.58 us
    ppermute x1, starting transfers between devices, body(): swap_two = lax.ppermute(jnp.where(odd, back2, ahead2), 'seq', pairs)  1.58 us
  transfers between devices with their start and end apart: 9, of which 5 were waited for; matrix products, arithmetic and copies ran while one was open for 2% of the time, Pallas kernels for 19%

profile of v9, /device:TPU:0, one launch (start us, length us, event | category | flops | bytes accessed | tf_op | source)
XLA Modules:
  0.0 61.1 jit_solution(16677246221559800702)
XLA Ops:
  0.6 1.0 %constant_dynamic-update-slice_fusion.1 = bf16[256,1024]{1,0:T(8,128)(2,1)S(1)} fusion(bf16[256,512]{1,0:T(8,128)(2,1)} %param.5), kind=kLoop, calls=%fused_computation.5 | loop fusion | bytes 524288
  1.7 0.0 copy-start.2
  1.7 5.1 %collective-permute-start = (bf16[256,1024]{1,0:T(8,128)(2,1)S(1)}, bf16[256,1024]{1,0:T(8,128)(2,1)S(1)}, u32[]{:S(2)}, u32[]{:S(2)}) collective-permute-start(bf16[256,1024]{1,0:T(8,128)(2,1)S(1)} %constant_dynamic-update-slice_fusion.refs_5_.refs_1_), channel_id=1, source_target_pairs={{0,8},{4,12},{8,16},{12,20},{16,24},{20,28},{1,9},{5,13},{9,17},{1... | collective-permute-start | bytes 1572872 | tf_op jit(solution)/shard_map/ppermute | solution.py:24
  6.9 1.3 %collective-permute-start.2 = (bf16[256,1024]{1,0:T(8,128)(2,1)S(1)}, bf16[256,1024]{1,0:T(8,128)(2,1)S(1)}, u32[]{:S(2)}, u32[]{:S(2)}) collective-permute-start(bf16[256,1024]{1,0:T(8,128)(2,1)S(1)} %constant_dynamic-update-slice_fusion.2.refs_2_), channel_id=1, source_target_pairs={{8,0},{12,4},{16,8},{20,12},{24,16},{28,20},{9,1},{13,5},{17,9},{2... | collective-permute-start | bytes 1572872 | tf_op jit(solution)/shard_map/ppermute | solution.py:24
  8.3 0.1 broadcast_select_fusion.3
  8.3 1.6 %collective-permute-start.1 = (bf16[256,1024]{1,0:T(8,128)(2,1)S(1)}, bf16[256,1024]{1,0:T(8,128)(2,1)S(1)}, u32[]{:S(2)}, u32[]{:S(2)}) collective-permute-start(bf16[256,1024]{1,0:T(8,128)(2,1)S(1)} %broadcast_select_fusion.3), channel_id=1, source_target_pairs={{0,4},{4,0},{8,12},{12,8},{16,20},{20,16},{24,28},{28,24},{1,5},{5... | collective-permute-start | bytes 1572872 | tf_op jit(solution)/shard_map/ppermute | solution.py:532
  9.9 8.1 %collective-permute-done.refs_3_ = bf16[256,1024]{1,0:T(8,128)(2,1)S(1)} collective-permute-done((bf16[256,1024]{1,0:T(8,128)(2,1)S(1)}, bf16[256,1024]{1,0:T(8,128)(2,1)S(1)}, u32[]{:S(2)}, u32[]{:S(2)}) %collective-permute-start) | collective-permute-done | bytes 524320 | tf_op jit(solution)/shard_map/ppermute | solution.py:24
  18.0 4.2 %collective-permute-done.2.refs_4_ = bf16[256,1024]{1,0:T(8,128)(2,1)S(1)} collective-permute-done((bf16[256,1024]{1,0:T(8,128)(2,1)S(1)}, bf16[256,1024]{1,0:T(8,128)(2,1)S(1)}, u32[]{:S(2)}, u32[]{:S(2)}) %collective-permute-start.2) | collective-permute-done | bytes 524320 | tf_op jit(solution)/shard_map/ppermute | solution.py:24
  22.2 0.1 broadcast_select_fusion.2
  22.3 1.6 %collective-permute-start.3 = (bf16[256,1024]{1,0:T(8,128)(2,1)S(1)}, bf16[256,1024]{1,0:T(8,128)(2,1)S(1)}, u32[]{:S(2)}, u32[]{:S(2)}) collective-permute-start(bf16[256,1024]{1,0:T(8,128)(2,1)S(1)} %broadcast_select_fusion.2), channel_id=1, source_target_pairs={{0,4},{4,0},{8,12},{12,8},{16,20},{20,16},{24,28},{28,24},{1,5},{5... | collective-permute-start | bytes 1572872 | tf_op jit(solution)/shard_map/ppermute | solution.py:535
  23.9 3.5 %collective-permute-start.4 = (bf16[256,1024]{1,0:T(8,128)(2,1)S(1)}, bf16[256,1024]{1,0:T(8,128)(2,1)S(1)}, u32[]{:S(2)}, u32[]{:S(2)}) collective-permute-start(bf16[256,1024]{1,0:T(8,128)(2,1)S(1)} %collective-permute-done.refs_3_), channel_id=1, source_target_pairs={{0,8},{4,12},{8,16},{12,20},{16,24},{20,28},{1,9},{5,13},{9,17},{1... | collective-permute-start | bytes 1572872 | tf_op jit(solution)/shard_map/ppermute | solution.py:24
  27.3 1.3 %collective-permute-start.7 = (bf16[256,1024]{1,0:T(8,128)(2,1)S(1)}, bf16[256,1024]{1,0:T(8,128)(2,1)S(1)}, u32[]{:S(2)}, u32[]{:S(2)}) collective-permute-start(bf16[256,1024]{1,0:T(8,128)(2,1)S(1)} %collective-permute-done.2.refs_4_), channel_id=1, source_target_pairs={{8,0},{12,4},{16,8},{20,12},{24,16},{28,20},{9,1},{13,5},{17,9},{2... | collective-permute-start | bytes 1572872 | tf_op jit(solution)/shard_map/ppermute | solution.py:24
  28.7 6.1 %collective-permute-done.3 = bf16[256,1024]{1,0:T(8,128)(2,1)S(1)} collective-permute-done((bf16[256,1024]{1,0:T(8,128)(2,1)S(1)}, bf16[256,1024]{1,0:T(8,128)(2,1)S(1)}, u32[]{:S(2)}, u32[]{:S(2)}) %collective-permute-start.3) | collective-permute-done | bytes 524320 | tf_op jit(solution)/shard_map/ppermute | solution.py:535
  34.8 1.0 %broadcast_select_fusion = (bf16[256,1024]{1,0:T(8,128)(2,1)}, bf16[256,1024]{1,0:T(8,128)(2,1)}) fusion(bf16[256,1024]{1,0:T(8,128)(2,1)S(1)} %collective-permute-done.3, bf16[256,1024]{1,0:T(8,128)(2,1)S(1)} %collective-permute-done.1, pred[]{:T(512)S(6)} %eq.5), kind=kLoop, calls=%fused_computation | loop fusion | flops 524288 | bytes 2097153 | tf_op jit(solution)/shard_map/jit(_where)/select_n | solution.py:537
  35.8 1.2 %collective-permute-done.4.refs_6_ = bf16[256,1024]{1,0:T(8,128)(2,1)S(1)} collective-permute-done((bf16[256,1024]{1,0:T(8,128)(2,1)S(1)}, bf16[256,1024]{1,0:T(8,128)(2,1)S(1)}, u32[]{:S(2)}, u32[]{:S(2)}) %collective-permute-start.4) | collective-permute-done | bytes 524320 | tf_op jit(solution)/shard_map/ppermute | solution.py:24
  37.0 0.8 %copy-done.4 = bf16[256,1024]{1,0:T(8,128)(2,1)} copy-done((bf16[256,1024]{1,0:T(8,128)(2,1)}, bf16[256,1024]{1,0:T(8,128)(2,1)S(1)}, u32[]{:S(2)}) %copy-start.4) | copy-done | bytes 524312
  37.8 6.4 %rows_stats.1 = (bf16[256,512]{1,0:T(8,128)(2,1)}, f32[256,8]{1,0:T(8,128)}, f32[8,256]{1,0:T(8,128)}) custom-call(s32[1]{0:T(128)} %bitcast.refs_0_, bf16[256,512]{1,0:T(8,128)(2,1)} %refs_1_.3, bf16[256,512]{1,0:T(8,128)(2,1)} %refs_2_.3, bf16[256,1024]{1,0:T(8,128)(2,1)} %copy-done.1, bf16[256,1024]{1,0:T(8,128)(2,1)} %get-tuple-element.15.refs_4_, ...), custom_call_target="tpu_custom_call" | custom-call | flops 402653184 | bytes 4194304 | tf_op jit(solution)/shard_map/rows_stats/pallas_call | solution.py:547
  44.2 1.3 %collective-permute-start.5 = (f32[8,256]{1,0:T(8,128)}, f32[8,256]{1,0:T(8,128)S(1)}, u32[]{:S(2)}, u32[]{:S(2)}) collective-permute-start(f32[8,256]{1,0:T(8,128)} %get-tuple-element.11.refs_5_), channel_id=1, source_target_pairs={{4,0},{8,4},{12,8},{16,12},{20,16},{24,20},{28,24},{5,1},{9,5},{13... | collective-permute-start | bytes 24584 | tf_op jit(solution)/shard_map/ppermute | solution.py:24
  45.5 1.3 %collective-permute-start.6 = (f32[8,256]{1,0:T(8,128)}, f32[8,256]{1,0:T(8,128)S(1)}, u32[]{:S(2)}, u32[]{:S(2)}) collective-permute-start(f32[8,256]{1,0:T(8,128)} %get-tuple-element.11.refs_5_), channel_id=1, source_target_pairs={{8,0},{12,4},{16,8},{20,12},{24,16},{28,20},{9,1},{13,5},{17,9},{2... | collective-permute-start | bytes 24584 | tf_op jit(solution)/shard_map/ppermute | solution.py:24
  46.8 1.3 %collective-permute-start.8 = (f32[8,256]{1,0:T(8,128)}, f32[8,256]{1,0:T(8,128)S(1)}, u32[]{:S(2)}, u32[]{:S(2)}) collective-permute-start(f32[8,256]{1,0:T(8,128)} %get-tuple-element.11.refs_5_), channel_id=1, source_target_pairs={{16,0},{20,4},{24,8},{28,12},{17,1},{21,5},{25,9},{29,13},{18,2},{... | collective-permute-start | bytes 24584 | tf_op jit(solution)/shard_map/ppermute | solution.py:24
  48.1 5.2 %rows_grad.1 = bf16[256,512]{1,0:T(8,128)(2,1)} custom-call(s32[1]{0:T(128)} %bitcast.refs_0_, bf16[256,512]{1,0:T(8,128)(2,1)} %refs_1_.3, bf16[256,512]{1,0:T(8,128)(2,1)} %refs_2_.3, bf16[256,1024]{1,0:T(8,128)(2,1)} %copy-done.1, bf16[256,1024]{1,0:T(8,128)(2,1)} %get-tuple-element.15.refs_4_, bf16[256,1024]{1,0:T(8,128)(2,1)} %copy-done, ...), custom_call_target="tpu_custom_call" | custom-call | flops 603979776 | bytes 4194304 | tf_op jit(solution)/shard_map/rows_grad/pallas_call | solution.py:562
  53.3 1.8 %collective-permute-done.8.refs_9_ = f32[8,256]{1,0:T(8,128)S(1)} collective-permute-done((f32[8,256]{1,0:T(8,128)}, f32[8,256]{1,0:T(8,128)S(1)}, u32[]{:S(2)}, u32[]{:S(2)}) %collective-permute-start.8) | collective-permute-done | bytes 8224 | tf_op jit(solution)/shard_map/ppermute | solution.py:24
  55.1 0.6 copy-done.11
  55.7 5.4 %keys_pass.1 = (bf16[256,512]{1,0:T(8,128)(2,1)}, bf16[256,512]{1,0:T(8,128)(2,1)}) custom-call(s32[1]{0:T(128)} %bitcast.refs_0_, bf16[256,1024]{1,0:T(8,128)(2,1)} %copy-done, bf16[256,1024]{1,0:T(8,128)(2,1)} %copy-done.5, bf16[256,1024]{1,0:T(8,128)(2,1)} %get-tuple-element.14.refs_3_, bf16[256,1024]{1,0:T(8,128)(2,1)} %copy-done.6, ...), custom_call_target="tpu_custom_call" | custom-call | flops 805306368 | bytes 4194304 | tf_op jit(solution)/shard_map/keys_pass/pallas_call | solution.py:570
  (28 shorter events, 0.1 us)
Async XLA Ops:
  0.6 1.0 %copy-start.7 = (bf16[256,512]{1,0:T(8,128)(2,1)S(1)}, bf16[256,512]{1,0:T(8,128)(2,1)}, u32[]{:S(2)}) copy-start(bf16[256,512]{1,0:T(8,128)(2,1)} %param.6) | copy-start | bytes 786436
  1.7 5.2 %copy-start.2 = (bf16[256,512]{1,0:T(8,128)(2,1)S(1)}, bf16[256,512]{1,0:T(8,128)(2,1)}, u32[]{:S(2)}) copy-start(bf16[256,512]{1,0:T(8,128)(2,1)} %refs_1_.3) | copy-start | bytes 786436
  1.7 6.5 %copy-start = (bf16[256,1024]{1,0:T(8,128)(2,1)}, bf16[256,1024]{1,0:T(8,128)(2,1)S(1)}, u32[]{:S(2)}) copy-start(bf16[256,1024]{1,0:T(8,128)(2,1)S(1)} %constant_dynamic-update-slice_fusion.refs_5_.refs_1_) | copy-start | bytes 1572868
  1.7 5.2 %copy-start.3 = (bf16[256,512]{1,0:T(8,128)(2,1)S(1)}, bf16[256,512]{1,0:T(8,128)(2,1)}, u32[]{:S(2)}) copy-start(bf16[256,512]{1,0:T(8,128)(2,1)} %refs_2_.3) | copy-start | bytes 786436
  1.7 16.2 %collective-permute-start = (bf16[256,1024]{1,0:T(8,128)(2,1)S(1)}, bf16[256,1024]{1,0:T(8,128)(2,1)S(1)}, u32[]{:S(2)}, u32[]{:S(2)}) collective-permute-start(bf16[256,1024]{1,0:T(8,128)(2,1)S(1)} %constant_dynamic-update-slice_fusion.refs_5_.refs_1_), channel_id=1, source_target_pairs={{0,8},{4,12},{8,16},{12,20},{16,24},{20,28},{1,9},{5,13},{9,17},{1... | collective-permute-start | bytes 1572872 | tf_op jit(solution)/shard_map/ppermute | solution.py:24
  6.9 1.4 %copy-start.5 = (bf16[256,1024]{1,0:T(8,128)(2,1)}, bf16[256,1024]{1,0:T(8,128)(2,1)S(1)}, u32[]{:S(2)}) copy-start(bf16[256,1024]{1,0:T(8,128)(2,1)S(1)} %constant_dynamic-update-slice_fusion.2.refs_2_) | copy-start | bytes 1572868
  6.9 15.3 %collective-permute-start.2 = (bf16[256,1024]{1,0:T(8,128)(2,1)S(1)}, bf16[256,1024]{1,0:T(8,128)(2,1)S(1)}, u32[]{:S(2)}, u32[]{:S(2)}) collective-permute-start(bf16[256,1024]{1,0:T(8,128)(2,1)S(1)} %constant_dynamic-update-slice_fusion.2.refs_2_), channel_id=1, source_target_pairs={{8,0},{12,4},{16,8},{20,12},{24,16},{28,20},{9,1},{13,5},{17,9},{2... | collective-permute-start | bytes 1572872 | tf_op jit(solution)/shard_map/ppermute | solution.py:24
  8.3 20.3 %collective-permute-start.1 = (bf16[256,1024]{1,0:T(8,128)(2,1)S(1)}, bf16[256,1024]{1,0:T(8,128)(2,1)S(1)}, u32[]{:S(2)}, u32[]{:S(2)}) collective-permute-start(bf16[256,1024]{1,0:T(8,128)(2,1)S(1)} %broadcast_select_fusion.3), channel_id=1, source_target_pairs={{0,4},{4,0},{8,12},{12,8},{16,20},{20,16},{24,28},{28,24},{1,5},{5... | collective-permute-start | bytes 1572872 | tf_op jit(solution)/shard_map/ppermute | solution.py:532
  18.0 5.9 %copy-start.1 = (bf16[256,1024]{1,0:T(8,128)(2,1)}, bf16[256,1024]{1,0:T(8,128)(2,1)S(1)}, u32[]{:S(2)}) copy-start(bf16[256,1024]{1,0:T(8,128)(2,1)S(1)} %collective-permute-done.refs_3_) | copy-start | bytes 1572868
  22.2 5.1 %copy-start.6 = (bf16[256,1024]{1,0:T(8,128)(2,1)}, bf16[256,1024]{1,0:T(8,128)(2,1)S(1)}, u32[]{:S(2)}) copy-start(bf16[256,1024]{1,0:T(8,128)(2,1)S(1)} %collective-permute-done.2.refs_4_) | copy-start | bytes 1572868
  22.3 12.5 %collective-permute-start.3 = (bf16[256,1024]{1,0:T(8,128)(2,1)S(1)}, bf16[256,1024]{1,0:T(8,128)(2,1)S(1)}, u32[]{:S(2)}, u32[]{:S(2)}) collective-permute-start(bf16[256,1024]{1,0:T(8,128)(2,1)S(1)} %broadcast_select_fusion.2), channel_id=1, source_target_pairs={{0,4},{4,0},{8,12},{12,8},{16,20},{20,16},{24,28},{28,24},{1,5},{5... | collective-permute-start | bytes 1572872 | tf_op jit(solution)/shard_map/ppermute | solution.py:535
  23.9 13.1 %collective-permute-start.4 = (bf16[256,1024]{1,0:T(8,128)(2,1)S(1)}, bf16[256,1024]{1,0:T(8,128)(2,1)S(1)}, u32[]{:S(2)}, u32[]{:S(2)}) collective-permute-start(bf16[256,1024]{1,0:T(8,128)(2,1)S(1)} %collective-permute-done.refs_3_), channel_id=1, source_target_pairs={{0,8},{4,12},{8,16},{12,20},{16,24},{20,28},{1,9},{5,13},{9,17},{1... | collective-permute-start | bytes 1572872 | tf_op jit(solution)/shard_map/ppermute | solution.py:24
  27.3 25.9 %collective-permute-start.7 = (bf16[256,1024]{1,0:T(8,128)(2,1)S(1)}, bf16[256,1024]{1,0:T(8,128)(2,1)S(1)}, u32[]{:S(2)}, u32[]{:S(2)}) collective-permute-start(bf16[256,1024]{1,0:T(8,128)(2,1)S(1)} %collective-permute-done.2.refs_4_), channel_id=1, source_target_pairs={{8,0},{12,4},{16,8},{20,12},{24,16},{28,20},{9,1},{13,5},{17,9},{2... | collective-permute-start | bytes 1572872 | tf_op jit(solution)/shard_map/ppermute | solution.py:24
  37.0 0.8 %copy-start.4 = (bf16[256,1024]{1,0:T(8,128)(2,1)}, bf16[256,1024]{1,0:T(8,128)(2,1)S(1)}, u32[]{:S(2)}) copy-start(bf16[256,1024]{1,0:T(8,128)(2,1)S(1)} %collective-permute-done.4.refs_6_) | copy-start | bytes 1572868
  44.2 9.1 %collective-permute-start.5 = (f32[8,256]{1,0:T(8,128)}, f32[8,256]{1,0:T(8,128)S(1)}, u32[]{:S(2)}, u32[]{:S(2)}) collective-permute-start(f32[8,256]{1,0:T(8,128)} %get-tuple-element.11.refs_5_), channel_id=1, source_target_pairs={{4,0},{8,4},{12,8},{16,12},{20,16},{24,20},{28,24},{5,1},{9,5},{13... | collective-permute-start | bytes 24584 | tf_op jit(solution)/shard_map/ppermute | solution.py:24
  45.5 7.8 %collective-permute-start.6 = (f32[8,256]{1,0:T(8,128)}, f32[8,256]{1,0:T(8,128)S(1)}, u32[]{:S(2)}, u32[]{:S(2)}) collective-permute-start(f32[8,256]{1,0:T(8,128)} %get-tuple-element.11.refs_5_), channel_id=1, source_target_pairs={{8,0},{12,4},{16,8},{20,12},{24,16},{28,20},{9,1},{13,5},{17,9},{2... | collective-permute-start | bytes 24584 | tf_op jit(solution)/shard_map/ppermute | solution.py:24
  46.8 8.3 %collective-permute-start.8 = (f32[8,256]{1,0:T(8,128)}, f32[8,256]{1,0:T(8,128)S(1)}, u32[]{:S(2)}, u32[]{:S(2)}) collective-permute-start(f32[8,256]{1,0:T(8,128)} %get-tuple-element.11.refs_5_), channel_id=1, source_target_pairs={{16,0},{20,4},{24,8},{28,12},{17,1},{21,5},{25,9},{29,13},{18,2},{... | collective-permute-start | bytes 24584 | tf_op jit(solution)/shard_map/ppermute | solution.py:24
  53.3 1.8 %copy-start.8 = (bf16[256,1024]{1,0:T(8,128)(2,1)}, bf16[256,1024]{1,0:T(8,128)(2,1)S(1)}, u32[]{:S(2)}) copy-start(bf16[256,1024]{1,0:T(8,128)(2,1)S(1)} %collective-permute-done.7.refs_8_) | copy-start | bytes 1572868
  53.3 1.8 %copy-start.9 = (f32[8,256]{1,0:T(8,128)}, f32[8,256]{1,0:T(8,128)S(1)}, u32[]{:S(2)}) copy-start(f32[8,256]{1,0:T(8,128)S(1)} %collective-permute-done.5.refs_6_) | copy-start | bytes 24580
  53.3 1.8 %copy-start.10 = (f32[8,256]{1,0:T(8,128)}, f32[8,256]{1,0:T(8,128)S(1)}, u32[]{:S(2)}) copy-start(f32[8,256]{1,0:T(8,128)S(1)} %collective-permute-done.6.refs_7_) | copy-start | bytes 24580
  55.1 0.6 copy-start.11

commit v10 on v9

--- a/solution.py
+++ b/solution.py
@@ -334,7 +334,11 @@
 TRANS_B = (((1,), (1,)), ((), ()))
 
 
-def span_load(refs, start, length, other, axis):
+def ref_load(ref, window, other, axis):
+    return ref[window, other] if axis == 0 else ref[other, window]
+
+
+def span_load(refs, start, length, other, axis, odd=None):
     size = refs[0].shape[axis]
     pieces = []
     at = start
@@ -342,7 +346,17 @@
         index, offset = at // size, at % size
         count = min(size - offset, length)
         window = pl.ds(offset, count)
-        pieces.append(refs[index][window, other] if axis == 0 else refs[index][other, window])
+        if isinstance(refs[index], tuple):
+            when_odd, when_even = refs[index]
+            pieces.append(
+                jnp.where(
+                    odd,
+                    ref_load(when_odd, window, other, axis),
+                    ref_load(when_even, window, other, axis),
+                )
+            )
+        else:
+            pieces.append(ref_load(refs[index], window, other, axis))
         at += count
         length -= count
     return pieces[0] if len(pieces) == 1 else jnp.concatenate(pieces, axis=axis)
@@ -351,12 +365,13 @@
 def row_kernel(near_count, far_list, heads, phase, *refs):
     far_count = len(far_list)
     position_ref, query_ref, grad_ref = refs[:3]
-    span_refs = refs[3:6]
-    far_refs = refs[6 : 6 + far_count]
+    span_refs = (refs[3], (refs[4], refs[5]), refs[6])
+    far_refs = refs[7 : 7 + far_count]
     if phase == "stats":
-        attended_ref, stats_ref, stats_rows_ref = refs[6 + far_count :]
+        attended_ref, stats_ref, stats_rows_ref = refs[7 + far_count :]
     else:
-        stats_in_ref, grad_query_ref = refs[6 + far_count :]
+        stats_in_ref, grad_query_ref = refs[7 + far_count :]
+    odd = position_ref[0] % 2 == 1
     width = heads * HD
     near_rows = near_count * BLK
     scale = 1.0 / math.sqrt(HD)
@@ -381,9 +396,9 @@
             value_cols = pl.ds(width + head * HD, HD)
             query = query_ref[rows, cols]
             grad = grad_ref[rows, cols]
-            keys = [span_load(span_refs, block * BLK, near_rows, cols, 0)]
+            keys = [span_load(span_refs, block * BLK, near_rows, cols, 0, odd)]
             keys = keys + [item[rows, cols] for item in far_refs]
-            values = [span_load(span_refs, block * BLK, near_rows, value_cols, 0)]
+            values = [span_load(span_refs, block * BLK, near_rows, value_cols, 0, odd)]
             values = values + [item[rows, value_cols] for item in far_refs]
             scores = [
                 lax.dot_general(query, key, TRANS_B, preferred_element_type=jnp.float32) * scale
@@ -453,11 +468,12 @@
 def key_kernel(near_count, far_list, heads, block_total, *refs):
     far_count = len(far_list)
     position_ref, own_ref = refs[:2]
-    span_refs = refs[2:5]
-    stats_refs = refs[5:8]
-    far_rows = refs[8 : 8 + far_count]
-    far_stats = refs[8 + far_count : 8 + 2 * far_count]
-    grad_key_ref, grad_value_ref = refs[8 + 2 * far_count :]
+    span_refs = (refs[2], (refs[3], refs[4]), refs[5])
+    stats_refs = refs[6:9]
+    far_rows = refs[9 : 9 + far_count]
+    far_stats = refs[9 + far_count : 9 + 2 * far_count]
+    grad_key_ref, grad_value_ref = refs[9 + 2 * far_count :]
+    odd = position_ref[0] % 2 == 1
     width = heads * HD
     near_rows = near_count * BLK
     scale = 1.0 / math.sqrt(HD)
@@ -477,9 +493,9 @@
             value_cols = pl.ds(width + head * HD, HD)
             key = own_ref[rows, cols]
             value = own_ref[rows, value_cols]
-            queries = [span_load(span_refs, block * BLK, near_rows, cols, 0)]
+            queries = [span_load(span_refs, block * BLK, near_rows, cols, 0, odd)]
             queries = queries + [item[rows, cols] for item in far_rows]
-            grads = [span_load(span_refs, block * BLK, near_rows, value_cols, 0)]
+            grads = [span_load(span_refs, block * BLK, near_rows, value_cols, 0, odd)]
             grads = grads + [item[rows, value_cols] for item in far_rows]
             totals = [span_load(stats_refs, block * BLK, near_rows, pl.ds(head, 1), 1)] + [
                 item[pl.ds(head, 1), rows] for item in far_stats
@@ -533,8 +549,6 @@
     back4 = passed_along(back2, "seq", 2)
     ahead4 = passed_along(ahead2, "seq", -2)
     swap_two = lax.ppermute(jnp.where(odd, back2, ahead2), "seq", pairs)
-    back1 = jnp.where(odd, swap_one, swap_two)
-    ahead1 = jnp.where(odd, swap_two, swap_one)
     far_back = [back4] + [passed_along(keys_values, "seq", shift) for shift in far_shifts[1:]]
     far_ahead = [ahead4] + [passed_along(queries_grads, "seq", -shift) for shift in far_shifts[1:]]
     far_back = far_back[: len(far_shifts)]
@@ -543,7 +557,7 @@
     position_arr = jnp.reshape(position, (1,)).astype(jnp.int32)
     far_offsets = list(far_list)
     slab_rows = (len(near_list) + len(far_list)) * BLK
-    row_inputs = (position_arr, queries, grad_out, back2, back1, keys_values, *far_back)
+    row_inputs = (position_arr, queries, grad_out, back2, swap_one, swap_two, keys_values, *far_back)
     attended, stats, stats_rows = pl.pallas_call(
         functools.partial(row_kernel, len(near_list), far_offsets, heads, "stats"),
         out_shape=(
@@ -551,7 +565,7 @@
             jax.ShapeDtypeStruct((tok_count, 2 * heads), jnp.float32),
             jax.ShapeDtypeStruct((2 * heads, tok_count), jnp.float32),
         ),
-        in_specs=[smem_spec()] + [vmem_spec()] * (5 + len(far_back)),
+        in_specs=[smem_spec()] + [vmem_spec()] * (6 + len(far_back)),
         out_specs=(vmem_spec(), vmem_spec(), vmem_spec()),
         cost_estimate=estimate(tok_count, row_width, slab_rows, 2, 1),
         name="rows_stats",
@@ -562,7 +576,7 @@
     grad_queries = pl.pallas_call(
         functools.partial(row_kernel, len(near_list), far_offsets, heads, "grad"),
         out_shape=jax.ShapeDtypeStruct((tok_count, row_width), jnp.bfloat16),
-        in_specs=[smem_spec()] + [vmem_spec()] * (6 + len(far_back)),
+        in_specs=[smem_spec()] + [vmem_spec()] * (7 + len(far_back)),
         out_specs=vmem_spec(),
         cost_estimate=estimate(tok_count, row_width, slab_rows, 3, 1),
         name="rows_grad",
@@ -573,7 +587,7 @@
             jax.ShapeDtypeStruct((tok_count, row_width), jnp.bfloat16),
             jax.ShapeDtypeStruct((tok_count, row_width), jnp.bfloat16),
         ),
-        in_specs=[smem_spec()] + [vmem_spec()] * (7 + 2 * len(far_ahead)),
+        in_specs=[smem_spec()] + [vmem_spec()] * (8 + 2 * len(far_ahead)),
         out_specs=(vmem_spec(), vmem_spec()),
         cost_estimate=estimate(tok_count, row_width, slab_rows, 4, 1),
         name="keys_pass",
@@ -581,7 +595,8 @@
         position_arr,
         keys_values,
         queries_grads,
-        ahead1,
+        swap_two,
+        swap_one,
         ahead2,
         stats_rows,
         stats_one,

time: 62 us -> 63.3 us (1.021)
  the two profiles are of different devices: /device:TPU:0 before, /device:TPU:28 now
where the time goes in v10:
time: 63.3 us; the launch traced here: 63 us
  starting transfers between devices  22.3 us (35%)
  waiting for transfers between devices  18.6 us (29%)
  Pallas kernels  17.7 us (28%)
  local copies, waits for them, and re-layouts  3.27 us (5%)
  between operations  0.89 us (1%)
    ppermute x7, starting transfers between devices, passed_along(): lax.ppermute(value, axis, [(source, source + steps) for source in range(f...  21.2 us
    pallas_call x2, Pallas kernels, body(): pl.pallas_call(functools.partial(row_kernel, len(near_list), far_offsets,...  12.1 us
    ppermute x7, waiting for transfers between devices, passed_along(): lax.ppermute(value, axis, [(source, source + steps) for source in range(f...  12 us
    ppermute x1, waiting for transfers between devices, body(): swap_two = lax.ppermute(jnp.where(odd, back2, ahead2), 'seq', pairs)  6.64 us
    pallas_call x1, Pallas kernels, body(): pl.pallas_call(functools.partial(key_kernel, len(near_list), far_offsets,...  5.68 us
    unnamed x30, local copies, waits for them, and re-layouts  3.22 us
  transfers between devices with their start and end apart: 9, of which 4 were waited for; matrix products, arithmetic and copies ran while one was open for 0% of the time, Pallas kernels for 19%

profile of v10, /device:TPU:28, one launch (start us, length us, event | category | flops | bytes accessed | tf_op | source)
XLA Modules:
  0.0 63.0 jit_solution(3905551533307391459)
XLA Ops:
  0.6 1.0 %constant_dynamic-update-slice_fusion.1 = bf16[256,1024]{1,0:T(8,128)(2,1)S(1)} fusion(bf16[256,512]{1,0:T(8,128)(2,1)} %param.5), kind=kLoop, calls=%fused_computation.3 | loop fusion | bytes 524288
  1.7 0.0 copy-start.5
  1.7 0.0 copy-start.6
  1.7 1.4 %collective-permute-start = (bf16[256,1024]{1,0:T(8,128)(2,1)S(1)}, bf16[256,1024]{1,0:T(8,128)(2,1)S(1)}, u32[]{:S(2)}, u32[]{:S(2)}) collective-permute-start(bf16[256,1024]{1,0:T(8,128)(2,1)S(1)} %constant_dynamic-update-slice_fusion.refs_6_.refs_1_), channel_id=1, source_target_pairs={{0,8},{4,12},{8,16},{12,20},{16,24},{20,28},{1,9},{5,13},{9,17},{1... | collective-permute-start | bytes 1572872 | tf_op jit(solution)/shard_map/ppermute | solution.py:24
  3.3 4.6 %collective-permute-start.2 = (bf16[256,1024]{1,0:T(8,128)(2,1)S(1)}, bf16[256,1024]{1,0:T(8,128)(2,1)S(1)}, u32[]{:S(2)}, u32[]{:S(2)}) collective-permute-start(bf16[256,1024]{1,0:T(8,128)(2,1)S(1)} %constant_dynamic-update-slice_fusion.2.refs_2_), channel_id=1, source_target_pairs={{8,0},{12,4},{16,8},{20,12},{24,16},{28,20},{9,1},{13,5},{17,9},{2... | collective-permute-start | bytes 1572872 | tf_op jit(solution)/shard_map/ppermute | solution.py:24
  7.9 0.1 broadcast_select_fusion.1
  7.9 0.6 collective-permute-start.1
  8.5 8.9 %collective-permute-done.refs_3_ = bf16[256,1024]{1,0:T(8,128)(2,1)S(1)} collective-permute-done((bf16[256,1024]{1,0:T(8,128)(2,1)S(1)}, bf16[256,1024]{1,0:T(8,128)(2,1)S(1)}, u32[]{:S(2)}, u32[]{:S(2)}) %collective-permute-start) | collective-permute-done | bytes 524320 | tf_op jit(solution)/shard_map/ppermute | solution.py:24
  17.4 1.3 %collective-permute-done.2.refs_5_ = bf16[256,1024]{1,0:T(8,128)(2,1)S(1)} collective-permute-done((bf16[256,1024]{1,0:T(8,128)(2,1)S(1)}, bf16[256,1024]{1,0:T(8,128)(2,1)S(1)}, u32[]{:S(2)}, u32[]{:S(2)}) %collective-permute-start.2) | collective-permute-done | bytes 524320 | tf_op jit(solution)/shard_map/ppermute | solution.py:24
  18.7 0.1 broadcast_select_fusion
  18.8 0.6 collective-permute-start.3
  19.3 1.3 %collective-permute-start.4 = (bf16[256,1024]{1,0:T(8,128)(2,1)S(1)}, bf16[256,1024]{1,0:T(8,128)(2,1)S(1)}, u32[]{:S(2)}, u32[]{:S(2)}) collective-permute-start(bf16[256,1024]{1,0:T(8,128)(2,1)S(1)} %collective-permute-done.refs_3_), channel_id=1, source_target_pairs={{0,8},{4,12},{8,16},{12,20},{16,24},{20,28},{1,9},{5,13},{9,17},{1... | collective-permute-start | bytes 1572872 | tf_op jit(solution)/shard_map/ppermute | solution.py:24
  20.6 5.0 %collective-permute-start.7 = (bf16[256,1024]{1,0:T(8,128)(2,1)S(1)}, bf16[256,1024]{1,0:T(8,128)(2,1)S(1)}, u32[]{:S(2)}, u32[]{:S(2)}) collective-permute-start(bf16[256,1024]{1,0:T(8,128)(2,1)S(1)} %collective-permute-done.2.refs_5_), channel_id=1, source_target_pairs={{8,0},{12,4},{16,8},{20,12},{24,16},{28,20},{9,1},{13,5},{17,9},{2... | collective-permute-start | bytes 1572872 | tf_op jit(solution)/shard_map/ppermute | solution.py:24
  25.7 6.6 %collective-permute-done.3.refs_5_.refs_3_ = bf16[256,1024]{1,0:T(8,128)(2,1)S(1)} collective-permute-done((bf16[256,1024]{1,0:T(8,128)(2,1)S(1)}, bf16[256,1024]{1,0:T(8,128)(2,1)S(1)}, u32[]{:S(2)}, u32[]{:S(2)}) %collective-permute-start.3) | collective-permute-done | bytes 524320 | tf_op jit(solution)/shard_map/ppermute | solution.py:551
  32.4 1.8 %collective-permute-done.4.refs_7_ = bf16[256,1024]{1,0:T(8,128)(2,1)S(1)} collective-permute-done((bf16[256,1024]{1,0:T(8,128)(2,1)S(1)}, bf16[256,1024]{1,0:T(8,128)(2,1)S(1)}, u32[]{:S(2)}, u32[]{:S(2)}) %collective-permute-start.4) | collective-permute-done | bytes 524320 | tf_op jit(solution)/shard_map/ppermute | solution.py:24
  34.2 0.8 %copy-done.8 = bf16[256,1024]{1,0:T(8,128)(2,1)} copy-done((bf16[256,1024]{1,0:T(8,128)(2,1)}, bf16[256,1024]{1,0:T(8,128)(2,1)S(1)}, u32[]{:S(2)}) %copy-start.8) | copy-done | bytes 524312
  35.0 6.7 %rows_stats.1 = (bf16[256,512]{1,0:T(8,128)(2,1)}, f32[256,8]{1,0:T(8,128)}, f32[8,256]{1,0:T(8,128)}) custom-call(s32[1]{0:T(128)} %bitcast.refs_0_, bf16[256,512]{1,0:T(8,128)(2,1)} %refs_1_.3, bf16[256,512]{1,0:T(8,128)(2,1)} %refs_2_.3, bf16[256,1024]{1,0:T(8,128)(2,1)} %copy-done.1, bf16[256,1024]{1,0:T(8,128)(2,1)} %copy-done.2, ...), custom_call_target="tpu_custom_call" | custom-call | flops 402653184 | bytes 4194304 | tf_op jit(solution)/shard_map/rows_stats/pallas_call | solution.py:561
  41.7 3.4 %collective-permute-start.5 = (f32[8,256]{1,0:T(8,128)}, f32[8,256]{1,0:T(8,128)S(1)}, u32[]{:S(2)}, u32[]{:S(2)}) collective-permute-start(f32[8,256]{1,0:T(8,128)} %get-tuple-element.11.refs_6_), channel_id=1, source_target_pairs={{4,0},{8,4},{12,8},{16,12},{20,16},{24,20},{28,24},{5,1},{9,5},{13... | collective-permute-start | bytes 24584 | tf_op jit(solution)/shard_map/ppermute | solution.py:24
  45.1 3.6 %collective-permute-start.6 = (f32[8,256]{1,0:T(8,128)}, f32[8,256]{1,0:T(8,128)S(1)}, u32[]{:S(2)}, u32[]{:S(2)}) collective-permute-start(f32[8,256]{1,0:T(8,128)} %get-tuple-element.11.refs_6_), channel_id=1, source_target_pairs={{8,0},{12,4},{16,8},{20,12},{24,16},{28,20},{9,1},{13,5},{17,9},{2... | collective-permute-start | bytes 24584 | tf_op jit(solution)/shard_map/ppermute | solution.py:24
  48.7 1.8 %collective-permute-start.8 = (f32[8,256]{1,0:T(8,128)}, f32[8,256]{1,0:T(8,128)S(1)}, u32[]{:S(2)}, u32[]{:S(2)}) collective-permute-start(f32[8,256]{1,0:T(8,128)} %get-tuple-element.11.refs_6_), channel_id=1, source_target_pairs={{16,0},{20,4},{24,8},{28,12},{17,1},{21,5},{25,9},{29,13},{18,2},{... | collective-permute-start | bytes 24584 | tf_op jit(solution)/shard_map/ppermute | solution.py:24
  50.5 5.3 %rows_grad.1 = bf16[256,512]{1,0:T(8,128)(2,1)} custom-call(s32[1]{0:T(128)} %bitcast.refs_0_, bf16[256,512]{1,0:T(8,128)(2,1)} %refs_1_.3, bf16[256,512]{1,0:T(8,128)(2,1)} %refs_2_.3, bf16[256,1024]{1,0:T(8,128)(2,1)} %copy-done.1, bf16[256,1024]{1,0:T(8,128)(2,1)} %copy-done.2, bf16[256,1024]{1,0:T(8,128)(2,1)} %copy-done.3, bf16[256,1024]{1,0:T(8,128)(2,1)} %copy-done, ...), custom_call_target="tpu_custom_call" | custom-call | flops 603979776 | bytes 4194304 | tf_op jit(solution)/shard_map/rows_grad/pallas_call | solution.py:576
  55.9 0.8 %copy-done.9 = bf16[256,1024]{1,0:T(8,128)(2,1)} copy-done((bf16[256,1024]{1,0:T(8,128)(2,1)}, bf16[256,1024]{1,0:T(8,128)(2,1)S(1)}, u32[]{:S(2)}) %copy-start.9) | copy-done | bytes 524312
  56.7 0.6 copy-done.13
  57.3 5.7 %keys_pass.1 = (bf16[256,512]{1,0:T(8,128)(2,1)}, bf16[256,512]{1,0:T(8,128)(2,1)}) custom-call(s32[1]{0:T(128)} %bitcast.refs_0_, bf16[256,1024]{1,0:T(8,128)(2,1)} %copy-done, bf16[256,1024]{1,0:T(8,128)(2,1)} %copy-done.4, bf16[256,1024]{1,0:T(8,128)(2,1)} %copy-done.3, bf16[256,1024]{1,0:T(8,128)(2,1)} %copy-done.2, bf16[256,1024]{1,0:T(8,128)(2,1)} %copy-done.7, ...), custom_call_target="tpu_custom_call" | custom-call | flops 805306368 | bytes 4194304 | tf_op jit(solution)/shard_map/keys_pass/pallas_call | solution.py:584
  (31 shorter events, 0.1 us)
Async XLA Ops:
  0.6 1.0 %copy-start.10 = (bf16[256,512]{1,0:T(8,128)(2,1)S(1)}, bf16[256,512]{1,0:T(8,128)(2,1)}, u32[]{:S(2)}) copy-start(bf16[256,512]{1,0:T(8,128)(2,1)} %param.6) | copy-start | bytes 786436
  1.7 1.5 %copy-start.5 = (bf16[256,512]{1,0:T(8,128)(2,1)S(1)}, bf16[256,512]{1,0:T(8,128)(2,1)}, u32[]{:S(2)}) copy-start(bf16[256,512]{1,0:T(8,128)(2,1)} %refs_1_.3) | copy-start | bytes 786436
  1.7 6.1 %copy-start = (bf16[256,1024]{1,0:T(8,128)(2,1)}, bf16[256,1024]{1,0:T(8,128)(2,1)S(1)}, u32[]{:S(2)}) copy-start(bf16[256,1024]{1,0:T(8,128)(2,1)S(1)} %constant_dynamic-update-slice_fusion.refs_6_.refs_1_) | copy-start | bytes 1572868
  1.7 1.5 %copy-start.6 = (bf16[256,512]{1,0:T(8,128)(2,1)S(1)}, bf16[256,512]{1,0:T(8,128)(2,1)}, u32[]{:S(2)}) copy-start(bf16[256,512]{1,0:T(8,128)(2,1)} %refs_2_.3) | copy-start | bytes 786436
  1.7 15.7 %collective-permute-start = (bf16[256,1024]{1,0:T(8,128)(2,1)S(1)}, bf16[256,1024]{1,0:T(8,128)(2,1)S(1)}, u32[]{:S(2)}, u32[]{:S(2)}) collective-permute-start(bf16[256,1024]{1,0:T(8,128)(2,1)S(1)} %constant_dynamic-update-slice_fusion.refs_6_.refs_1_), channel_id=1, source_target_pairs={{0,8},{4,12},{8,16},{12,20},{16,24},{20,28},{1,9},{5,13},{9,17},{1... | collective-permute-start | bytes 1572872 | tf_op jit(solution)/shard_map/ppermute | solution.py:24
  3.3 4.7 %copy-start.4 = (bf16[256,1024]{1,0:T(8,128)(2,1)}, bf16[256,1024]{1,0:T(8,128)(2,1)S(1)}, u32[]{:S(2)}) copy-start(bf16[256,1024]{1,0:T(8,128)(2,1)S(1)} %constant_dynamic-update-slice_fusion.2.refs_2_) | copy-start | bytes 1572868
  3.3 15.4 %collective-permute-start.2 = (bf16[256,1024]{1,0:T(8,128)(2,1)S(1)}, bf16[256,1024]{1,0:T(8,128)(2,1)S(1)}, u32[]{:S(2)}, u32[]{:S(2)}) collective-permute-start(bf16[256,1024]{1,0:T(8,128)(2,1)S(1)} %constant_dynamic-update-slice_fusion.2.refs_2_), channel_id=1, source_target_pairs={{8,0},{12,4},{16,8},{20,12},{24,16},{28,20},{9,1},{13,5},{17,9},{2... | collective-permute-start | bytes 1572872 | tf_op jit(solution)/shard_map/ppermute | solution.py:24
  7.9 17.7 %collective-permute-start.1 = (bf16[256,1024]{1,0:T(8,128)(2,1)S(1)}, bf16[256,1024]{1,0:T(8,128)(2,1)S(1)}, u32[]{:S(2)}, u32[]{:S(2)}) collective-permute-start(bf16[256,1024]{1,0:T(8,128)(2,1)S(1)} %broadcast_select_fusion.1), channel_id=1, source_target_pairs={{0,4},{4,0},{8,12},{12,8},{16,20},{20,16},{24,28},{28,24},{1,5},{5... | collective-permute-start | bytes 1572872 | tf_op jit(solution)/shard_map/ppermute | solution.py:548
  17.4 1.9 %copy-start.1 = (bf16[256,1024]{1,0:T(8,128)(2,1)}, bf16[256,1024]{1,0:T(8,128)(2,1)S(1)}, u32[]{:S(2)}) copy-start(bf16[256,1024]{1,0:T(8,128)(2,1)S(1)} %collective-permute-done.refs_3_) | copy-start | bytes 1572868
  18.7 1.9 %copy-start.7 = (bf16[256,1024]{1,0:T(8,128)(2,1)}, bf16[256,1024]{1,0:T(8,128)(2,1)S(1)}, u32[]{:S(2)}) copy-start(bf16[256,1024]{1,0:T(8,128)(2,1)S(1)} %collective-permute-done.2.refs_5_) | copy-start | bytes 1572868
  18.8 13.6 %collective-permute-start.3 = (bf16[256,1024]{1,0:T(8,128)(2,1)S(1)}, bf16[256,1024]{1,0:T(8,128)(2,1)S(1)}, u32[]{:S(2)}, u32[]{:S(2)}) collective-permute-start(bf16[256,1024]{1,0:T(8,128)(2,1)S(1)} %broadcast_select_fusion), channel_id=1, source_target_pairs={{0,4},{4,0},{8,12},{12,8},{16,20},{20,16},{24,28},{28,24},{1,5},{5... | collective-permute-start | bytes 1572872 | tf_op jit(solution)/shard_map/ppermute | solution.py:551
  19.3 14.8 %collective-permute-start.4 = (bf16[256,1024]{1,0:T(8,128)(2,1)S(1)}, bf16[256,1024]{1,0:T(8,128)(2,1)S(1)}, u32[]{:S(2)}, u32[]{:S(2)}) collective-permute-start(bf16[256,1024]{1,0:T(8,128)(2,1)S(1)} %collective-permute-done.refs_3_), channel_id=1, source_target_pairs={{0,8},{4,12},{8,16},{12,20},{16,24},{20,28},{1,9},{5,13},{9,17},{1... | collective-permute-start | bytes 1572872 | tf_op jit(solution)/shard_map/ppermute | solution.py:24
  20.6 35.3 %collective-permute-start.7 = (bf16[256,1024]{1,0:T(8,128)(2,1)S(1)}, bf16[256,1024]{1,0:T(8,128)(2,1)S(1)}, u32[]{:S(2)}, u32[]{:S(2)}) collective-permute-start(bf16[256,1024]{1,0:T(8,128)(2,1)S(1)} %collective-permute-done.2.refs_5_), channel_id=1, source_target_pairs={{8,0},{12,4},{16,8},{20,12},{24,16},{28,20},{9,1},{13,5},{17,9},{2... | collective-permute-start | bytes 1572872 | tf_op jit(solution)/shard_map/ppermute | solution.py:24
  25.7 8.5 %copy-start.2 = (bf16[256,1024]{1,0:T(8,128)(2,1)}, bf16[256,1024]{1,0:T(8,128)(2,1)S(1)}, u32[]{:S(2)}) copy-start(bf16[256,1024]{1,0:T(8,128)(2,1)S(1)} %collective-permute-done.1.refs_4_) | copy-start | bytes 1572868
  32.4 1.8 %copy-start.3 = (bf16[256,1024]{1,0:T(8,128)(2,1)}, bf16[256,1024]{1,0:T(8,128)(2,1)S(1)}, u32[]{:S(2)}) copy-start(bf16[256,1024]{1,0:T(8,128)(2,1)S(1)} %collective-permute-done.3.refs_5_.refs_3_) | copy-start | bytes 1572868
  34.2 0.8 %copy-start.8 = (bf16[256,1024]{1,0:T(8,128)(2,1)}, bf16[256,1024]{1,0:T(8,128)(2,1)S(1)}, u32[]{:S(2)}) copy-start(bf16[256,1024]{1,0:T(8,128)(2,1)S(1)} %collective-permute-done.4.refs_7_) | copy-start | bytes 1572868
  41.7 14.2 %collective-permute-start.5 = (f32[8,256]{1,0:T(8,128)}, f32[8,256]{1,0:T(8,128)S(1)}, u32[]{:S(2)}, u32[]{:S(2)}) collective-permute-start(f32[8,256]{1,0:T(8,128)} %get-tuple-element.11.refs_6_), channel_id=1, source_target_pairs={{4,0},{8,4},{12,8},{16,12},{20,16},{24,20},{28,24},{5,1},{9,5},{13... | collective-permute-start | bytes 24584 | tf_op jit(solution)/shard_map/ppermute | solution.py:24
  45.1 10.8 %collective-permute-start.6 = (f32[8,256]{1,0:T(8,128)}, f32[8,256]{1,0:T(8,128)S(1)}, u32[]{:S(2)}, u32[]{:S(2)}) collective-permute-start(f32[8,256]{1,0:T(8,128)} %get-tuple-element.11.refs_6_), channel_id=1, source_target_pairs={{8,0},{12,4},{16,8},{20,12},{24,16},{28,20},{9,1},{13,5},{17,9},{2... | collective-permute-start | bytes 24584 | tf_op jit(solution)/shard_map/ppermute | solution.py:24
  48.7 7.2 %collective-permute-start.8 = (f32[8,256]{1,0:T(8,128)}, f32[8,256]{1,0:T(8,128)S(1)}, u32[]{:S(2)}, u32[]{:S(2)}) collective-permute-start(f32[8,256]{1,0:T(8,128)} %get-tuple-element.11.refs_6_), channel_id=1, source_target_pairs={{16,0},{20,4},{24,8},{28,12},{17,1},{21,5},{25,9},{29,13},{18,2},{... | collective-permute-start | bytes 24584 | tf_op jit(solution)/shard_map/ppermute | solution.py:24
  55.9 0.8 %copy-start.9 = (bf16[256,1024]{1,0:T(8,128)(2,1)}, bf16[256,1024]{1,0:T(8,128)(2,1)S(1)}, u32[]{:S(2)}) copy-start(bf16[256,1024]{1,0:T(8,128)(2,1)S(1)} %collective-permute-done.7.refs_9_) | copy-start | bytes 1572868
  55.9 0.8 %copy-start.11 = (f32[8,256]{1,0:T(8,128)}, f32[8,256]{1,0:T(8,128)S(1)}, u32[]{:S(2)}) copy-start(f32[8,256]{1,0:T(8,128)S(1)} %collective-permute-done.5.refs_7_) | copy-start | bytes 24580
  55.9 0.8 %copy-start.12 = (f32[8,256]{1,0:T(8,128)}, f32[8,256]{1,0:T(8,128)S(1)}, u32[]{:S(2)}) copy-start(f32[8,256]{1,0:T(8,128)S(1)} %collective-permute-done.6.refs_8_) | copy-start | bytes 24580
  56.7 0.6 copy-start.13

commit v11 on v9

--- a/solution.py
+++ b/solution.py
@@ -531,10 +531,13 @@
     ahead2 = passed_along(queries_grads, "seq", -2)
     swap_one = lax.ppermute(jnp.where(odd, queries_grads, keys_values), "seq", pairs)
     back4 = passed_along(back2, "seq", 2)
+    from_right = [(source, source - 1) for source in range(1, devices, 2)]
+    back_side = lax.ppermute(back2, "seq", from_right)
     ahead4 = passed_along(ahead2, "seq", -2)
-    swap_two = lax.ppermute(jnp.where(odd, back2, ahead2), "seq", pairs)
-    back1 = jnp.where(odd, swap_one, swap_two)
-    ahead1 = jnp.where(odd, swap_two, swap_one)
+    from_left = [(source, source + 1) for source in range(0, devices - 1, 2)]
+    ahead_side = lax.ppermute(ahead2, "seq", from_left)
+    back1 = jnp.where(odd, swap_one, back_side)
+    ahead1 = jnp.where(odd, ahead_side, swap_one)
     far_back = [back4] + [passed_along(keys_values, "seq", shift) for shift in far_shifts[1:]]
     far_ahead = [ahead4] + [passed_along(queries_grads, "seq", -shift) for shift in far_shifts[1:]]
     far_back = far_back[: len(far_shifts)]

time: 62 us -> 63.6 us (1.026)
  starting transfers between devices: 18.2 us -> 22.6 us
  waiting for transfers between devices: 21.4 us -> 19 us
    ppermute x7, waiting for transfers between devices: 15.3 us -> 10.7 us  [passed_along(): lax.ppermute(value, axis, [(source, source + steps) for source in range(f...]
    ppermute x1 -> x2, starting transfers between devices: 1.58 us -> 4.89 us  [the longest x1 3.6 us: body(): ahead_side = lax.ppermute(ahead2, 'seq', from_left)]
    ppermute x1 -> x2, waiting for transfers between devices: 6.15 us -> 8.27 us  [the longest x1 4.36 us: body(): ahead_side = lax.ppermute(ahead2, 'seq', from_left)]
    ppermute x7, starting transfers between devices: 15 us -> 15.7 us  [passed_along(): lax.ppermute(value, axis, [(source, source + steps) for source in range(f...]
  transfers between devices with their start and end apart: 9 -> 10, of which waited for: 5 -> 4; matrix products, arithmetic and copies ran while one was open for 2% -> 2% of each run, Pallas kernels for 19% -> 18%
where the time goes in v11:
time: 63.6 us; the launch traced here: 63.1 us
  starting transfers between devices  22.6 us (36%)
  waiting for transfers between devices  19 us (30%)
  Pallas kernels  17 us (27%)
  local copies, waits for them, and re-layouts  2.51 us (4%)
  other arithmetic  1.11 us (2%)
  between operations  0.91 us (1%)
    ppermute x7, starting transfers between devices, passed_along(): lax.ppermute(value, axis, [(source, source + steps) for source in range(f...  15.7 us
    pallas_call x2, Pallas kernels, body(): pl.pallas_call(functools.partial(row_kernel, len(near_list), far_offsets,...  11.6 us
    ppermute x7, waiting for transfers between devices, passed_along(): lax.ppermute(value, axis, [(source, source + steps) for source in range(f...  10.7 us
    pallas_call x1, Pallas kernels, body(): pl.pallas_call(functools.partial(key_kernel, len(near_list), far_offsets,...  5.42 us
    ppermute x1, waiting for transfers between devices, body(): ahead_side = lax.ppermute(ahead2, 'seq', from_left)  4.36 us
    ppermute x1, waiting for transfers between devices, body(): back_side = lax.ppermute(back2, 'seq', from_right)  3.92 us
    ppermute x1, starting transfers between devices, body(): ahead_side = lax.ppermute(ahead2, 'seq', from_left)  3.6 us
    unnamed x26, local copies, waits for them, and re-layouts  2.46 us
  transfers between devices with their start and end apart: 10, of which 4 were waited for; matrix products, arithmetic and copies ran while one was open for 2% of the time, Pallas kernels for 18%

profile of v11, /device:TPU:0, one launch (start us, length us, event | category | flops | bytes accessed | tf_op | source)
XLA Modules:
  0.0 63.1 jit_solution(13187812039241335473)
XLA Ops:
  0.6 0.0 copy-start.1
  0.6 1.0 %constant_dynamic-update-slice_fusion.3 = bf16[256,1024]{1,0:T(8,128)(2,1)S(1)} fusion(bf16[256,512]{1,0:T(8,128)(2,1)} %refs_1_.3), kind=kLoop, calls=%fused_computation.6 | loop fusion | bytes 524288
  1.7 0.0 copy-start.5
  1.7 1.4 %collective-permute-start.4 = (bf16[256,1024]{1,0:T(8,128)(2,1)S(1)}, bf16[256,1024]{1,0:T(8,128)(2,1)S(1)}, u32[]{:S(2)}, u32[]{:S(2)}) collective-permute-start(bf16[256,1024]{1,0:T(8,128)(2,1)S(1)} %constant_dynamic-update-slice_fusion.2.refs_2_), channel_id=1, source_target_pairs={{8,0},{12,4},{16,8},{20,12},{24,16},{28,20},{9,1},{13,5},{17,9},{2... | collective-permute-start | bytes 1572872 | tf_op jit(solution)/shard_map/ppermute | solution.py:24
  3.3 5.6 %collective-permute-start = (bf16[256,1024]{1,0:T(8,128)(2,1)S(1)}, bf16[256,1024]{1,0:T(8,128)(2,1)S(1)}, u32[]{:S(2)}, u32[]{:S(2)}) collective-permute-start(bf16[256,1024]{1,0:T(8,128)(2,1)S(1)} %constant_dynamic-update-slice_fusion.refs_5_.refs_1_), channel_id=1, source_target_pairs={{0,8},{4,12},{8,16},{12,20},{16,24},{20,28},{1,9},{5,13},{9,17},{1... | collective-permute-start | bytes 1572872 | tf_op jit(solution)/shard_map/ppermute | solution.py:24
  8.9 0.1 broadcast_select_fusion.2
  9.0 2.0 %collective-permute-start.1 = (bf16[256,1024]{1,0:T(8,128)(2,1)S(1)}, bf16[256,1024]{1,0:T(8,128)(2,1)S(1)}, u32[]{:S(2)}, u32[]{:S(2)}) collective-permute-start(bf16[256,1024]{1,0:T(8,128)(2,1)S(1)} %broadcast_select_fusion.2), channel_id=1, source_target_pairs={{0,4},{4,0},{8,12},{12,8},{16,20},{20,16},{24,28},{28,24},{1,5},{5... | collective-permute-start | bytes 1572872 | tf_op jit(solution)/shard_map/ppermute | solution.py:532
  11.0 7.7 %collective-permute-done.4.refs_4_ = bf16[256,1024]{1,0:T(8,128)(2,1)S(1)} collective-permute-done((bf16[256,1024]{1,0:T(8,128)(2,1)S(1)}, bf16[256,1024]{1,0:T(8,128)(2,1)S(1)}, u32[]{:S(2)}, u32[]{:S(2)}) %collective-permute-start.4) | collective-permute-done | bytes 524320 | tf_op jit(solution)/shard_map/ppermute | solution.py:24
  18.7 3.6 %collective-permute-start.5 = (bf16[256,1024]{1,0:T(8,128)(2,1)S(1)}, bf16[256,1024]{1,0:T(8,128)(2,1)S(1)}, u32[]{:S(2)}, u32[]{:S(2)}) collective-permute-start(bf16[256,1024]{1,0:T(8,128)(2,1)S(1)} %collective-permute-done.4.refs_4_), channel_id=1, source_target_pairs={{0,4},{8,12},{16,20},{24,28},{1,5},{9,13},{17,21},{25,29},{2,6},{1... | collective-permute-start | bytes 1572872 | tf_op jit(solution)/shard_map/ppermute | solution.py:538
  22.4 1.3 %collective-permute-start.2 = (bf16[256,1024]{1,0:T(8,128)(2,1)S(1)}, bf16[256,1024]{1,0:T(8,128)(2,1)S(1)}, u32[]{:S(2)}, u32[]{:S(2)}) collective-permute-start(bf16[256,1024]{1,0:T(8,128)(2,1)S(1)} %collective-permute-done.refs_3_), channel_id=1, source_target_pairs={{4,0},{12,8},{20,16},{28,24},{5,1},{13,9},{21,17},{29,25},{6,2},{1... | collective-permute-start | bytes 1572872 | tf_op jit(solution)/shard_map/ppermute | solution.py:535
  23.7 3.5 %collective-permute-start.3 = (bf16[256,1024]{1,0:T(8,128)(2,1)S(1)}, bf16[256,1024]{1,0:T(8,128)(2,1)S(1)}, u32[]{:S(2)}, u32[]{:S(2)}) collective-permute-start(bf16[256,1024]{1,0:T(8,128)(2,1)S(1)} %collective-permute-done.refs_3_), channel_id=1, source_target_pairs={{0,8},{4,12},{8,16},{12,20},{16,24},{20,28},{1,9},{5,13},{9,17},{1... | collective-permute-start | bytes 1572872 | tf_op jit(solution)/shard_map/ppermute | solution.py:24
  27.2 1.3 %collective-permute-start.8 = (bf16[256,1024]{1,0:T(8,128)(2,1)S(1)}, bf16[256,1024]{1,0:T(8,128)(2,1)S(1)}, u32[]{:S(2)}, u32[]{:S(2)}) collective-permute-start(bf16[256,1024]{1,0:T(8,128)(2,1)S(1)} %collective-permute-done.4.refs_4_), channel_id=1, source_target_pairs={{8,0},{12,4},{16,8},{20,12},{24,16},{28,20},{9,1},{13,5},{17,9},{2... | collective-permute-start | bytes 1572872 | tf_op jit(solution)/shard_map/ppermute | solution.py:24
  28.5 4.4 %collective-permute-done.5 = bf16[256,1024]{1,0:T(8,128)(2,1)S(1)} collective-permute-done((bf16[256,1024]{1,0:T(8,128)(2,1)S(1)}, bf16[256,1024]{1,0:T(8,128)(2,1)S(1)}, u32[]{:S(2)}, u32[]{:S(2)}) %collective-permute-start.5) | collective-permute-done | bytes 524320 | tf_op jit(solution)/shard_map/ppermute | solution.py:538
  32.8 3.9 %collective-permute-done.2 = bf16[256,1024]{1,0:T(8,128)(2,1)S(1)} collective-permute-done((bf16[256,1024]{1,0:T(8,128)(2,1)S(1)}, bf16[256,1024]{1,0:T(8,128)(2,1)S(1)}, u32[]{:S(2)}, u32[]{:S(2)}) %collective-permute-start.2) | collective-permute-done | bytes 524320 | tf_op jit(solution)/shard_map/ppermute | solution.py:535
  36.8 1.1 %broadcast_select_fusion = (bf16[256,1024]{1,0:T(8,128)(2,1)}, bf16[256,1024]{1,0:T(8,128)(2,1)}) fusion(bf16[256,1024]{1,0:T(8,128)(2,1)S(1)} %collective-permute-done.5, bf16[256,1024]{1,0:T(8,128)(2,1)S(1)} %collective-permute-done.1, pred[]{:T(512)S(6)} %eq.5, bf16[256,1024]{1,0:T(8,128)(2,1)S(1)} %collective-permute-done.2), kind=kLoop, calls=%fused_computation | loop fusion | flops 524288 | bytes 2621441 | tf_op jit(solution)/shard_map/jit(_where)/select_n | solution.py:540
  37.8 0.8 %copy-done.3 = bf16[256,1024]{1,0:T(8,128)(2,1)} copy-done((bf16[256,1024]{1,0:T(8,128)(2,1)}, bf16[256,1024]{1,0:T(8,128)(2,1)S(1)}, u32[]{:S(2)}) %copy-start.3) | copy-done | bytes 524312
  38.6 6.4 %rows_stats.1 = (bf16[256,512]{1,0:T(8,128)(2,1)}, f32[256,8]{1,0:T(8,128)}, f32[8,256]{1,0:T(8,128)}) custom-call(s32[1]{0:T(128)} %bitcast.refs_0_, bf16[256,512]{1,0:T(8,128)(2,1)} %refs_1_.3, bf16[256,512]{1,0:T(8,128)(2,1)} %refs_2_.3, bf16[256,1024]{1,0:T(8,128)(2,1)} %copy-done.2, bf16[256,1024]{1,0:T(8,128)(2,1)} %get-tuple-element.15.refs_4_, ...), custom_call_target="tpu_custom_call" | custom-call | flops 402653184 | bytes 4194304 | tf_op jit(solution)/shard_map/rows_stats/pallas_call | solution.py:550
  45.1 1.3 %collective-permute-start.6 = (f32[8,256]{1,0:T(8,128)}, f32[8,256]{1,0:T(8,128)S(1)}, u32[]{:S(2)}, u32[]{:S(2)}) collective-permute-start(f32[8,256]{1,0:T(8,128)} %get-tuple-element.11.refs_5_), channel_id=1, source_target_pairs={{4,0},{8,4},{12,8},{16,12},{20,16},{24,20},{28,24},{5,1},{9,5},{13... | collective-permute-start | bytes 24584 | tf_op jit(solution)/shard_map/ppermute | solution.py:24
  46.3 1.3 %collective-permute-start.7 = (f32[8,256]{1,0:T(8,128)}, f32[8,256]{1,0:T(8,128)S(1)}, u32[]{:S(2)}, u32[]{:S(2)}) collective-permute-start(f32[8,256]{1,0:T(8,128)} %get-tuple-element.11.refs_5_), channel_id=1, source_target_pairs={{8,0},{12,4},{16,8},{20,12},{24,16},{28,20},{9,1},{13,5},{17,9},{2... | collective-permute-start | bytes 24584 | tf_op jit(solution)/shard_map/ppermute | solution.py:24
  47.6 1.3 %collective-permute-start.9 = (f32[8,256]{1,0:T(8,128)}, f32[8,256]{1,0:T(8,128)S(1)}, u32[]{:S(2)}, u32[]{:S(2)}) collective-permute-start(f32[8,256]{1,0:T(8,128)} %get-tuple-element.11.refs_5_), channel_id=1, source_target_pairs={{16,0},{20,4},{24,8},{28,12},{17,1},{21,5},{25,9},{29,13},{18,2},{... | collective-permute-start | bytes 24584 | tf_op jit(solution)/shard_map/ppermute | solution.py:24
  48.9 5.2 %rows_grad.1 = bf16[256,512]{1,0:T(8,128)(2,1)} custom-call(s32[1]{0:T(128)} %bitcast.refs_0_, bf16[256,512]{1,0:T(8,128)(2,1)} %refs_1_.3, bf16[256,512]{1,0:T(8,128)(2,1)} %refs_2_.3, bf16[256,1024]{1,0:T(8,128)(2,1)} %copy-done.2, bf16[256,1024]{1,0:T(8,128)(2,1)} %get-tuple-element.15.refs_4_, bf16[256,1024]{1,0:T(8,128)(2,1)} %copy-done, ...), custom_call_target="tpu_custom_call" | custom-call | flops 603979776 | bytes 4194304 | tf_op jit(solution)/shard_map/rows_grad/pallas_call | solution.py:565
  54.1 3.0 %collective-permute-done.9.refs_9_ = f32[8,256]{1,0:T(8,128)S(1)} collective-permute-done((f32[8,256]{1,0:T(8,128)}, f32[8,256]{1,0:T(8,128)S(1)}, u32[]{:S(2)}, u32[]{:S(2)}) %collective-permute-start.9) | collective-permute-done | bytes 8224 | tf_op jit(solution)/shard_map/ppermute | solution.py:24
  57.1 0.6 copy-done.11
  57.7 5.4 %keys_pass.1 = (bf16[256,512]{1,0:T(8,128)(2,1)}, bf16[256,512]{1,0:T(8,128)(2,1)}) custom-call(s32[1]{0:T(128)} %bitcast.refs_0_, bf16[256,1024]{1,0:T(8,128)(2,1)} %copy-done, bf16[256,1024]{1,0:T(8,128)(2,1)} %copy-done.4, bf16[256,1024]{1,0:T(8,128)(2,1)} %get-tuple-element.14.refs_3_, bf16[256,1024]{1,0:T(8,128)(2,1)} %copy-done.7, ...), custom_call_target="tpu_custom_call" | custom-call | flops 805306368 | bytes 4194304 | tf_op jit(solution)/shard_map/keys_pass/pallas_call | solution.py:573
  (29 shorter events, 0.1 us)
Async XLA Ops:
  0.6 1.0 %copy-start.1 = (bf16[256,512]{1,0:T(8,128)(2,1)S(1)}, bf16[256,512]{1,0:T(8,128)(2,1)}, u32[]{:S(2)}) copy-start(bf16[256,512]{1,0:T(8,128)(2,1)} %refs_2_.3) | copy-start | bytes 786436
  1.7 1.5 %copy-start.5 = (bf16[256,512]{1,0:T(8,128)(2,1)S(1)}, bf16[256,512]{1,0:T(8,128)(2,1)}, u32[]{:S(2)}) copy-start(bf16[256,512]{1,0:T(8,128)(2,1)} %param.5) | copy-start | bytes 786436
  1.7 7.2 %copy-start.4 = (bf16[256,1024]{1,0:T(8,128)(2,1)}, bf16[256,1024]{1,0:T(8,128)(2,1)S(1)}, u32[]{:S(2)}) copy-start(bf16[256,1024]{1,0:T(8,128)(2,1)S(1)} %constant_dynamic-update-slice_fusion.2.refs_2_) | copy-start | bytes 1572868
  1.7 1.5 %copy-start.6 = (bf16[256,512]{1,0:T(8,128)(2,1)S(1)}, bf16[256,512]{1,0:T(8,128)(2,1)}, u32[]{:S(2)}) copy-start(bf16[256,512]{1,0:T(8,128)(2,1)} %param.6) | copy-start | bytes 786436
  1.7 17.0 %collective-permute-start.4 = (bf16[256,1024]{1,0:T(8,128)(2,1)S(1)}, bf16[256,1024]{1,0:T(8,128)(2,1)S(1)}, u32[]{:S(2)}, u32[]{:S(2)}) collective-permute-start(bf16[256,1024]{1,0:T(8,128)(2,1)S(1)} %constant_dynamic-update-slice_fusion.2.refs_2_), channel_id=1, source_target_pairs={{8,0},{12,4},{16,8},{20,12},{24,16},{28,20},{9,1},{13,5},{17,9},{2... | collective-permute-start | bytes 1572872 | tf_op jit(solution)/shard_map/ppermute | solution.py:24
  3.3 5.7 %copy-start = (bf16[256,1024]{1,0:T(8,128)(2,1)}, bf16[256,1024]{1,0:T(8,128)(2,1)S(1)}, u32[]{:S(2)}) copy-start(bf16[256,1024]{1,0:T(8,128)(2,1)S(1)} %constant_dynamic-update-slice_fusion.refs_5_.refs_1_) | copy-start | bytes 1572868
  3.3 19.1 %collective-permute-start = (bf16[256,1024]{1,0:T(8,128)(2,1)S(1)}, bf16[256,1024]{1,0:T(8,128)(2,1)S(1)}, u32[]{:S(2)}, u32[]{:S(2)}) collective-permute-start(bf16[256,1024]{1,0:T(8,128)(2,1)S(1)} %constant_dynamic-update-slice_fusion.refs_5_.refs_1_), channel_id=1, source_target_pairs={{0,8},{4,12},{8,16},{12,20},{16,24},{20,28},{1,9},{5,13},{9,17},{1... | collective-permute-start | bytes 1572872 | tf_op jit(solution)/shard_map/ppermute | solution.py:24
  9.0 19.5 %collective-permute-start.1 = (bf16[256,1024]{1,0:T(8,128)(2,1)S(1)}, bf16[256,1024]{1,0:T(8,128)(2,1)S(1)}, u32[]{:S(2)}, u32[]{:S(2)}) collective-permute-start(bf16[256,1024]{1,0:T(8,128)(2,1)S(1)} %broadcast_select_fusion.2), channel_id=1, source_target_pairs={{0,4},{4,0},{8,12},{12,8},{16,20},{20,16},{24,28},{28,24},{1,5},{5... | collective-permute-start | bytes 1572872 | tf_op jit(solution)/shard_map/ppermute | solution.py:532
  18.7 19.1 %copy-start.7 = (bf16[256,1024]{1,0:T(8,128)(2,1)}, bf16[256,1024]{1,0:T(8,128)(2,1)S(1)}, u32[]{:S(2)}) copy-start(bf16[256,1024]{1,0:T(8,128)(2,1)S(1)} %collective-permute-done.4.refs_4_) | copy-start | bytes 1572868
  18.7 14.1 %collective-permute-start.5 = (bf16[256,1024]{1,0:T(8,128)(2,1)S(1)}, bf16[256,1024]{1,0:T(8,128)(2,1)S(1)}, u32[]{:S(2)}, u32[]{:S(2)}) collective-permute-start(bf16[256,1024]{1,0:T(8,128)(2,1)S(1)} %collective-permute-done.4.refs_4_), channel_id=1, source_target_pairs={{0,4},{8,12},{16,20},{24,28},{1,5},{9,13},{17,21},{25,29},{2,6},{1... | collective-permute-start | bytes 1572872 | tf_op jit(solution)/shard_map/ppermute | solution.py:538
  22.3 15.5 %copy-start.2 = (bf16[256,1024]{1,0:T(8,128)(2,1)}, bf16[256,1024]{1,0:T(8,128)(2,1)S(1)}, u32[]{:S(2)}) copy-start(bf16[256,1024]{1,0:T(8,128)(2,1)S(1)} %collective-permute-done.refs_3_) | copy-start | bytes 1572868
  22.4 14.4 %collective-permute-start.2 = (bf16[256,1024]{1,0:T(8,128)(2,1)S(1)}, bf16[256,1024]{1,0:T(8,128)(2,1)S(1)}, u32[]{:S(2)}, u32[]{:S(2)}) collective-permute-start(bf16[256,1024]{1,0:T(8,128)(2,1)S(1)} %collective-permute-done.refs_3_), channel_id=1, source_target_pairs={{4,0},{12,8},{20,16},{28,24},{5,1},{13,9},{21,17},{29,25},{6,2},{1... | collective-permute-start | bytes 1572872 | tf_op jit(solution)/shard_map/ppermute | solution.py:535
  23.7 14.2 %collective-permute-start.3 = (bf16[256,1024]{1,0:T(8,128)(2,1)S(1)}, bf16[256,1024]{1,0:T(8,128)(2,1)S(1)}, u32[]{:S(2)}, u32[]{:S(2)}) collective-permute-start(bf16[256,1024]{1,0:T(8,128)(2,1)S(1)} %collective-permute-done.refs_3_), channel_id=1, source_target_pairs={{0,8},{4,12},{8,16},{12,20},{16,24},{20,28},{1,9},{5,13},{9,17},{1... | collective-permute-start | bytes 1572872 | tf_op jit(solution)/shard_map/ppermute | solution.py:24
  27.2 26.9 %collective-permute-start.8 = (bf16[256,1024]{1,0:T(8,128)(2,1)S(1)}, bf16[256,1024]{1,0:T(8,128)(2,1)S(1)}, u32[]{:S(2)}, u32[]{:S(2)}) collective-permute-start(bf16[256,1024]{1,0:T(8,128)(2,1)S(1)} %collective-permute-done.4.refs_4_), channel_id=1, source_target_pairs={{8,0},{12,4},{16,8},{20,12},{24,16},{28,20},{9,1},{13,5},{17,9},{2... | collective-permute-start | bytes 1572872 | tf_op jit(solution)/shard_map/ppermute | solution.py:24
  37.8 0.8 %copy-start.3 = (bf16[256,1024]{1,0:T(8,128)(2,1)}, bf16[256,1024]{1,0:T(8,128)(2,1)S(1)}, u32[]{:S(2)}) copy-start(bf16[256,1024]{1,0:T(8,128)(2,1)S(1)} %collective-permute-done.3.refs_6_) | copy-start | bytes 1572868
  45.1 9.1 %collective-permute-start.6 = (f32[8,256]{1,0:T(8,128)}, f32[8,256]{1,0:T(8,128)S(1)}, u32[]{:S(2)}, u32[]{:S(2)}) collective-permute-start(f32[8,256]{1,0:T(8,128)} %get-tuple-element.11.refs_5_), channel_id=1, source_target_pairs={{4,0},{8,4},{12,8},{16,12},{20,16},{24,20},{28,24},{5,1},{9,5},{13... | collective-permute-start | bytes 24584 | tf_op jit(solution)/shard_map/ppermute | solution.py:24
  46.3 7.8 %collective-permute-start.7 = (f32[8,256]{1,0:T(8,128)}, f32[8,256]{1,0:T(8,128)S(1)}, u32[]{:S(2)}, u32[]{:S(2)}) collective-permute-start(f32[8,256]{1,0:T(8,128)} %get-tuple-element.11.refs_5_), channel_id=1, source_target_pairs={{8,0},{12,4},{16,8},{20,12},{24,16},{28,20},{9,1},{13,5},{17,9},{2... | collective-permute-start | bytes 24584 | tf_op jit(solution)/shard_map/ppermute | solution.py:24
  47.6 9.5 %collective-permute-start.9 = (f32[8,256]{1,0:T(8,128)}, f32[8,256]{1,0:T(8,128)S(1)}, u32[]{:S(2)}, u32[]{:S(2)}) collective-permute-start(f32[8,256]{1,0:T(8,128)} %get-tuple-element.11.refs_5_), channel_id=1, source_target_pairs={{16,0},{20,4},{24,8},{28,12},{17,1},{21,5},{25,9},{29,13},{18,2},{... | collective-permute-start | bytes 24584 | tf_op jit(solution)/shard_map/ppermute | solution.py:24
  54.1 3.0 %copy-start.8 = (bf16[256,1024]{1,0:T(8,128)(2,1)}, bf16[256,1024]{1,0:T(8,128)(2,1)S(1)}, u32[]{:S(2)}) copy-start(bf16[256,1024]{1,0:T(8,128)(2,1)S(1)} %collective-permute-done.8.refs_8_) | copy-start | bytes 1572868
  54.1 3.0 %copy-start.9 = (f32[8,256]{1,0:T(8,128)}, f32[8,256]{1,0:T(8,128)S(1)}, u32[]{:S(2)}) copy-start(f32[8,256]{1,0:T(8,128)S(1)} %collective-permute-done.6.refs_6_) | copy-start | bytes 24580
  54.1 3.0 %copy-start.10 = (f32[8,256]{1,0:T(8,128)}, f32[8,256]{1,0:T(8,128)S(1)}, u32[]{:S(2)}) copy-start(f32[8,256]{1,0:T(8,128)S(1)} %collective-permute-done.7.refs_7_) | copy-start | bytes 24580
  57.1 0.6 copy-start.11

commit v12 on v9

--- a/solution.py
+++ b/solution.py
@@ -454,10 +454,16 @@
     far_count = len(far_list)
     position_ref, own_ref = refs[:2]
     span_refs = refs[2:5]
-    stats_refs = refs[5:8]
-    far_rows = refs[8 : 8 + far_count]
-    far_stats = refs[8 + far_count : 8 + 2 * far_count]
-    grad_key_ref, grad_value_ref = refs[8 + 2 * far_count :]
+    gathered_ref = refs[5]
+    far_rows = refs[6 : 6 + far_count]
+    grad_key_ref, grad_value_ref = refs[6 + far_count :]
+    segments = gathered_ref.shape[0]
+
+    def segment_stats(step):
+        return gathered_ref.at[jnp.minimum(position_ref[0] + step, segments - 1)]
+
+    stats_refs = tuple(segment_stats(step) for step in range(3))
+    far_stats = [segment_stats(offset // 2) for offset in far_list]
     width = heads * HD
     near_rows = near_count * BLK
     scale = 1.0 / math.sqrt(HD)
@@ -556,9 +562,7 @@
         cost_estimate=estimate(tok_count, row_width, slab_rows, 2, 1),
         name="rows_stats",
     )(*row_inputs)
-    stats_one = passed_along(stats_rows, "seq", -1)
-    stats_two = passed_along(stats_rows, "seq", -2)
-    far_stats = [passed_along(stats_rows, "seq", -shift) for shift in far_shifts]
+    gathered = lax.all_gather(stats_rows, "seq")
     grad_queries = pl.pallas_call(
         functools.partial(row_kernel, len(near_list), far_offsets, heads, "grad"),
         out_shape=jax.ShapeDtypeStruct((tok_count, row_width), jnp.bfloat16),
@@ -573,7 +577,7 @@
             jax.ShapeDtypeStruct((tok_count, row_width), jnp.bfloat16),
             jax.ShapeDtypeStruct((tok_count, row_width), jnp.bfloat16),
         ),
-        in_specs=[smem_spec()] + [vmem_spec()] * (7 + 2 * len(far_ahead)),
+        in_specs=[smem_spec()] + [vmem_spec()] * (5 + len(far_ahead)),
         out_specs=(vmem_spec(), vmem_spec()),
         cost_estimate=estimate(tok_count, row_width, slab_rows, 4, 1),
         name="keys_pass",
@@ -583,11 +587,8 @@
         queries_grads,
         ahead1,
         ahead2,
-        stats_rows,
-        stats_one,
-        stats_two,
+        gathered,
         *far_ahead,
-        *far_stats,
     )
     return attended, grad_queries, grad_keys, grad_values
 

time: 62 us -> 88.6 us (1.43)
  blocking collectives: 0 us -> 32.6 us
  starting transfers between devices: 18.2 us -> 14.3 us
  waiting for transfers between devices: 21.4 us -> 19.6 us
    all_gather x0 -> x1, blocking collectives: none -> 32.6 us  [body(): gathered = lax.all_gather(stats_rows, 'seq')]
    ppermute x7 -> x4, starting transfers between devices: 15 us -> 11.1 us  [passed_along(): lax.ppermute(value, axis, [(source, source + steps) for source in range(f...]
    ppermute x7 -> x4, waiting for transfers between devices: 15.3 us -> 13.4 us  [passed_along(): lax.ppermute(value, axis, [(source, source + steps) for source in range(f...]
    unnamed x26 -> x20, local copies, waits for them, and re-layouts: 2.44 us -> 2.68 us
  transfers between devices with their start and end apart: 9 -> 6, of which waited for: 5 -> 4; matrix products, arithmetic and copies ran while one was open for 2% -> 1% of each run, Pallas kernels for 19% -> 13%
where the time goes in v12:
time: 88.6 us; the launch traced here: 88.3 us
  blocking collectives  32.6 us (37%)
  waiting for transfers between devices  19.6 us (22%)
  Pallas kernels  17 us (19%)
  starting transfers between devices  14.3 us (16%)
  local copies, waits for them, and re-layouts  2.72 us (3%)
  other arithmetic  1.16 us (1%)
    all_gather x1, blocking collectives, body(): gathered = lax.all_gather(stats_rows, 'seq')  32.6 us
    ppermute x4, waiting for transfers between devices, passed_along(): lax.ppermute(value, axis, [(source, source + steps) for source in range(f...  13.4 us
    pallas_call x2, Pallas kernels, body(): pl.pallas_call(functools.partial(row_kernel, len(near_list), far_offsets,...  11.6 us
    ppermute x4, starting transfers between devices, passed_along(): lax.ppermute(value, axis, [(source, source + steps) for source in range(f...  11.1 us
    ppermute x1, waiting for transfers between devices, body(): swap_two = lax.ppermute(jnp.where(odd, back2, ahead2), 'seq', pairs)  6.15 us
    pallas_call x1, Pallas kernels, body(): pl.pallas_call(functools.partial(key_kernel, len(near_list), far_offsets,...  5.42 us
    unnamed x20, local copies, waits for them, and re-layouts  2.68 us
  transfers between devices with their start and end apart: 6, of which 4 were waited for; matrix products, arithmetic and copies ran while one was open for 1% of the time, Pallas kernels for 13%

profile of v12, /device:TPU:0, one launch (start us, length us, event | category | flops | bytes accessed | tf_op | source)
XLA Modules:
  0.0 88.3 jit_solution(5614619885086459156)
XLA Ops:
  0.6 1.0 %constant_dynamic-update-slice_fusion.1 = bf16[256,1024]{1,0:T(8,128)(2,1)S(1)} fusion(bf16[256,512]{1,0:T(8,128)(2,1)} %param.5), kind=kLoop, calls=%fused_computation.5 | loop fusion | bytes 524288
  1.7 0.0 copy-start.2
  1.7 0.0 copy-start.3
  1.7 5.1 %collective-permute-start = (bf16[256,1024]{1,0:T(8,128)(2,1)S(1)}, bf16[256,1024]{1,0:T(8,128)(2,1)S(1)}, u32[]{:S(2)}, u32[]{:S(2)}) collective-permute-start(bf16[256,1024]{1,0:T(8,128)(2,1)S(1)} %constant_dynamic-update-slice_fusion.refs_5_.refs_1_), channel_id=1, source_target_pairs={{0,8},{4,12},{8,16},{12,20},{16,24},{20,28},{1,9},{5,13},{9,17},{1... | collective-permute-start | bytes 1572872 | tf_op jit(solution)/shard_map/ppermute | solution.py:24
  6.9 1.3 %collective-permute-start.2 = (bf16[256,1024]{1,0:T(8,128)(2,1)S(1)}, bf16[256,1024]{1,0:T(8,128)(2,1)S(1)}, u32[]{:S(2)}, u32[]{:S(2)}) collective-permute-start(bf16[256,1024]{1,0:T(8,128)(2,1)S(1)} %constant_dynamic-update-slice_fusion.2.refs_2_), channel_id=1, source_target_pairs={{8,0},{12,4},{16,8},{20,12},{24,16},{28,20},{9,1},{13,5},{17,9},{2... | collective-permute-start | bytes 1572872 | tf_op jit(solution)/shard_map/ppermute | solution.py:24
  8.3 0.1 broadcast_select_fusion.3
  8.3 1.6 %collective-permute-start.1 = (bf16[256,1024]{1,0:T(8,128)(2,1)S(1)}, bf16[256,1024]{1,0:T(8,128)(2,1)S(1)}, u32[]{:S(2)}, u32[]{:S(2)}) collective-permute-start(bf16[256,1024]{1,0:T(8,128)(2,1)S(1)} %broadcast_select_fusion.3), channel_id=1, source_target_pairs={{0,4},{4,0},{8,12},{12,8},{16,20},{20,16},{24,28},{28,24},{1,5},{5... | collective-permute-start | bytes 1572872 | tf_op jit(solution)/shard_map/ppermute | solution.py:538
  9.9 8.1 %collective-permute-done.refs_3_ = bf16[256,1024]{1,0:T(8,128)(2,1)S(1)} collective-permute-done((bf16[256,1024]{1,0:T(8,128)(2,1)S(1)}, bf16[256,1024]{1,0:T(8,128)(2,1)S(1)}, u32[]{:S(2)}, u32[]{:S(2)}) %collective-permute-start) | collective-permute-done | bytes 524320 | tf_op jit(solution)/shard_map/ppermute | solution.py:24
  18.0 4.2 %collective-permute-done.2.refs_4_ = bf16[256,1024]{1,0:T(8,128)(2,1)S(1)} collective-permute-done((bf16[256,1024]{1,0:T(8,128)(2,1)S(1)}, bf16[256,1024]{1,0:T(8,128)(2,1)S(1)}, u32[]{:S(2)}, u32[]{:S(2)}) %collective-permute-start.2) | collective-permute-done | bytes 524320 | tf_op jit(solution)/shard_map/ppermute | solution.py:24
  22.2 0.1 broadcast_select_fusion.2
  22.3 1.6 %collective-permute-start.3 = (bf16[256,1024]{1,0:T(8,128)(2,1)S(1)}, bf16[256,1024]{1,0:T(8,128)(2,1)S(1)}, u32[]{:S(2)}, u32[]{:S(2)}) collective-permute-start(bf16[256,1024]{1,0:T(8,128)(2,1)S(1)} %broadcast_select_fusion.2), channel_id=1, source_target_pairs={{0,4},{4,0},{8,12},{12,8},{16,20},{20,16},{24,28},{28,24},{1,5},{5... | collective-permute-start | bytes 1572872 | tf_op jit(solution)/shard_map/ppermute | solution.py:541
  23.9 3.5 %collective-permute-start.4 = (bf16[256,1024]{1,0:T(8,128)(2,1)S(1)}, bf16[256,1024]{1,0:T(8,128)(2,1)S(1)}, u32[]{:S(2)}, u32[]{:S(2)}) collective-permute-start(bf16[256,1024]{1,0:T(8,128)(2,1)S(1)} %collective-permute-done.refs_3_), channel_id=1, source_target_pairs={{0,8},{4,12},{8,16},{12,20},{16,24},{20,28},{1,9},{5,13},{9,17},{1... | collective-permute-start | bytes 1572872 | tf_op jit(solution)/shard_map/ppermute | solution.py:24
  27.3 1.3 %collective-permute-start.5 = (bf16[256,1024]{1,0:T(8,128)(2,1)S(1)}, bf16[256,1024]{1,0:T(8,128)(2,1)S(1)}, u32[]{:S(2)}, u32[]{:S(2)}) collective-permute-start(bf16[256,1024]{1,0:T(8,128)(2,1)S(1)} %collective-permute-done.2.refs_4_), channel_id=1, source_target_pairs={{8,0},{12,4},{16,8},{20,12},{24,16},{28,20},{9,1},{13,5},{17,9},{2... | collective-permute-start | bytes 1572872 | tf_op jit(solution)/shard_map/ppermute | solution.py:24
  28.6 0.0 collective-permute-done.1
  28.7 6.1 %collective-permute-done.3 = bf16[256,1024]{1,0:T(8,128)(2,1)S(1)} collective-permute-done((bf16[256,1024]{1,0:T(8,128)(2,1)S(1)}, bf16[256,1024]{1,0:T(8,128)(2,1)S(1)}, u32[]{:S(2)}, u32[]{:S(2)}) %collective-permute-start.3) | collective-permute-done | bytes 524320 | tf_op jit(solution)/shard_map/ppermute | solution.py:541
  34.8 1.0 %broadcast_select_fusion = (bf16[256,1024]{1,0:T(8,128)(2,1)}, bf16[256,1024]{1,0:T(8,128)(2,1)}) fusion(bf16[256,1024]{1,0:T(8,128)(2,1)S(1)} %collective-permute-done.3, bf16[256,1024]{1,0:T(8,128)(2,1)S(1)} %collective-permute-done.1, pred[]{:T(512)S(6)} %eq.5), kind=kLoop, calls=%fused_computation | loop fusion | flops 524288 | bytes 2097153 | tf_op jit(solution)/shard_map/jit(_where)/select_n | solution.py:543
  35.9 1.1 %collective-permute-done.4.refs_6_ = bf16[256,1024]{1,0:T(8,128)(2,1)S(1)} collective-permute-done((bf16[256,1024]{1,0:T(8,128)(2,1)S(1)}, bf16[256,1024]{1,0:T(8,128)(2,1)S(1)}, u32[]{:S(2)}, u32[]{:S(2)}) %collective-permute-start.4) | collective-permute-done | bytes 524320 | tf_op jit(solution)/shard_map/ppermute | solution.py:24
  37.0 0.8 copy-done.4
  37.8 6.4 %rows_stats.1 = (bf16[256,512]{1,0:T(8,128)(2,1)}, f32[256,8]{1,0:T(8,128)}, f32[8,256]{1,0:T(8,128)}) custom-call(s32[1]{0:T(128)} %bitcast.refs_0_, bf16[256,512]{1,0:T(8,128)(2,1)} %refs_1_.3, bf16[256,512]{1,0:T(8,128)(2,1)} %refs_2_.3, bf16[256,1024]{1,0:T(8,128)(2,1)} %copy-done.1, bf16[256,1024]{1,0:T(8,128)(2,1)} %get-tuple-element.15.refs_4_, ...), custom_call_target="tpu_custom_call" | custom-call | flops 402653184 | bytes 4194304 | tf_op jit(solution)/shard_map/rows_stats/pallas_call | solution.py:553
  44.2 32.6 %all-gather = f32[64,256]{1,0:T(8,128)} all-gather(f32[8,256]{1,0:T(8,128)} %get-tuple-element.11), channel_id=2, replica_groups=mesh['seq'=8,'rep'=4] {'seq'}, dimensions={0}, use_global_device_ids=true | all-gather | bytes 73728 | tf_op jit(solution)/shard_map/all_gather | solution.py:565
  76.9 5.2 %rows_grad.1 = bf16[256,512]{1,0:T(8,128)(2,1)} custom-call(s32[1]{0:T(128)} %bitcast.refs_0_, bf16[256,512]{1,0:T(8,128)(2,1)} %refs_1_.3, bf16[256,512]{1,0:T(8,128)(2,1)} %refs_2_.3, bf16[256,1024]{1,0:T(8,128)(2,1)} %copy-done.1, bf16[256,1024]{1,0:T(8,128)(2,1)} %get-tuple-element.15.refs_4_, bf16[256,1024]{1,0:T(8,128)(2,1)} %copy-done, ...), custom_call_target="tpu_custom_call" | custom-call | flops 603979776 | bytes 4194304 | tf_op jit(solution)/shard_map/rows_grad/pallas_call | solution.py:566
  82.0 0.0 collective-permute-done.5.refs_6_
  82.0 0.8 copy-done.8
  82.9 5.4 %keys_pass.1 = (bf16[256,512]{1,0:T(8,128)(2,1)}, bf16[256,512]{1,0:T(8,128)(2,1)}) custom-call(s32[1]{0:T(128)} %bitcast.refs_0_, bf16[256,1024]{1,0:T(8,128)(2,1)} %copy-done, bf16[256,1024]{1,0:T(8,128)(2,1)} %copy-done.5, bf16[256,1024]{1,0:T(8,128)(2,1)} %get-tuple-element.14.refs_3_, bf16[256,1024]{1,0:T(8,128)(2,1)} %copy-done.6, ...), custom_call_target="tpu_custom_call" | custom-call | flops 805306368 | bytes 4194304 | tf_op jit(solution)/shard_map/keys_pass/pallas_call | solution.py:574
  (17 shorter events, 0.1 us)
Async XLA Ops:
  0.6 1.0 %copy-start.7 = (bf16[256,512]{1,0:T(8,128)(2,1)S(1)}, bf16[256,512]{1,0:T(8,128)(2,1)}, u32[]{:S(2)}) copy-start(bf16[256,512]{1,0:T(8,128)(2,1)} %param.6) | copy-start | bytes 786436
  1.7 5.2 %copy-start.2 = (bf16[256,512]{1,0:T(8,128)(2,1)S(1)}, bf16[256,512]{1,0:T(8,128)(2,1)}, u32[]{:S(2)}) copy-start(bf16[256,512]{1,0:T(8,128)(2,1)} %refs_1_.3) | copy-start | bytes 786436
  1.7 6.5 %copy-start = (bf16[256,1024]{1,0:T(8,128)(2,1)}, bf16[256,1024]{1,0:T(8,128)(2,1)S(1)}, u32[]{:S(2)}) copy-start(bf16[256,1024]{1,0:T(8,128)(2,1)S(1)} %constant_dynamic-update-slice_fusion.refs_5_.refs_1_) | copy-start | bytes 1572868
  1.7 5.2 %copy-start.3 = (bf16[256,512]{1,0:T(8,128)(2,1)S(1)}, bf16[256,512]{1,0:T(8,128)(2,1)}, u32[]{:S(2)}) copy-start(bf16[256,512]{1,0:T(8,128)(2,1)} %refs_2_.3) | copy-start | bytes 786436
  1.7 16.2 %collective-permute-start = (bf16[256,1024]{1,0:T(8,128)(2,1)S(1)}, bf16[256,1024]{1,0:T(8,128)(2,1)S(1)}, u32[]{:S(2)}, u32[]{:S(2)}) collective-permute-start(bf16[256,1024]{1,0:T(8,128)(2,1)S(1)} %constant_dynamic-update-slice_fusion.refs_5_.refs_1_), channel_id=1, source_target_pairs={{0,8},{4,12},{8,16},{12,20},{16,24},{20,28},{1,9},{5,13},{9,17},{1... | collective-permute-start | bytes 1572872 | tf_op jit(solution)/shard_map/ppermute | solution.py:24
  6.9 1.4 %copy-start.5 = (bf16[256,1024]{1,0:T(8,128)(2,1)}, bf16[256,1024]{1,0:T(8,128)(2,1)S(1)}, u32[]{:S(2)}) copy-start(bf16[256,1024]{1,0:T(8,128)(2,1)S(1)} %constant_dynamic-update-slice_fusion.2.refs_2_) | copy-start | bytes 1572868
  6.9 15.3 %collective-permute-start.2 = (bf16[256,1024]{1,0:T(8,128)(2,1)S(1)}, bf16[256,1024]{1,0:T(8,128)(2,1)S(1)}, u32[]{:S(2)}, u32[]{:S(2)}) collective-permute-start(bf16[256,1024]{1,0:T(8,128)(2,1)S(1)} %constant_dynamic-update-slice_fusion.2.refs_2_), channel_id=1, source_target_pairs={{8,0},{12,4},{16,8},{20,12},{24,16},{28,20},{9,1},{13,5},{17,9},{2... | collective-permute-start | bytes 1572872 | tf_op jit(solution)/shard_map/ppermute | solution.py:24
  8.3 20.3 %collective-permute-start.1 = (bf16[256,1024]{1,0:T(8,128)(2,1)S(1)}, bf16[256,1024]{1,0:T(8,128)(2,1)S(1)}, u32[]{:S(2)}, u32[]{:S(2)}) collective-permute-start(bf16[256,1024]{1,0:T(8,128)(2,1)S(1)} %broadcast_select_fusion.3), channel_id=1, source_target_pairs={{0,4},{4,0},{8,12},{12,8},{16,20},{20,16},{24,28},{28,24},{1,5},{5... | collective-permute-start | bytes 1572872 | tf_op jit(solution)/shard_map/ppermute | solution.py:538
  18.0 5.9 %copy-start.1 = (bf16[256,1024]{1,0:T(8,128)(2,1)}, bf16[256,1024]{1,0:T(8,128)(2,1)S(1)}, u32[]{:S(2)}) copy-start(bf16[256,1024]{1,0:T(8,128)(2,1)S(1)} %collective-permute-done.refs_3_) | copy-start | bytes 1572868
  22.2 5.1 %copy-start.6 = (bf16[256,1024]{1,0:T(8,128)(2,1)}, bf16[256,1024]{1,0:T(8,128)(2,1)S(1)}, u32[]{:S(2)}) copy-start(bf16[256,1024]{1,0:T(8,128)(2,1)S(1)} %collective-permute-done.2.refs_4_) | copy-start | bytes 1572868
  22.3 12.5 %collective-permute-start.3 = (bf16[256,1024]{1,0:T(8,128)(2,1)S(1)}, bf16[256,1024]{1,0:T(8,128)(2,1)S(1)}, u32[]{:S(2)}, u32[]{:S(2)}) collective-permute-start(bf16[256,1024]{1,0:T(8,128)(2,1)S(1)} %broadcast_select_fusion.2), channel_id=1, source_target_pairs={{0,4},{4,0},{8,12},{12,8},{16,20},{20,16},{24,28},{28,24},{1,5},{5... | collective-permute-start | bytes 1572872 | tf_op jit(solution)/shard_map/ppermute | solution.py:541
  23.9 13.1 %collective-permute-start.4 = (bf16[256,1024]{1,0:T(8,128)(2,1)S(1)}, bf16[256,1024]{1,0:T(8,128)(2,1)S(1)}, u32[]{:S(2)}, u32[]{:S(2)}) collective-permute-start(bf16[256,1024]{1,0:T(8,128)(2,1)S(1)} %collective-permute-done.refs_3_), channel_id=1, source_target_pairs={{0,8},{4,12},{8,16},{12,20},{16,24},{20,28},{1,9},{5,13},{9,17},{1... | collective-permute-start | bytes 1572872 | tf_op jit(solution)/shard_map/ppermute | solution.py:24
  27.3 54.7 %collective-permute-start.5 = (bf16[256,1024]{1,0:T(8,128)(2,1)S(1)}, bf16[256,1024]{1,0:T(8,128)(2,1)S(1)}, u32[]{:S(2)}, u32[]{:S(2)}) collective-permute-start(bf16[256,1024]{1,0:T(8,128)(2,1)S(1)} %collective-permute-done.2.refs_4_), channel_id=1, source_target_pairs={{8,0},{12,4},{16,8},{20,12},{24,16},{28,20},{9,1},{13,5},{17,9},{2... | collective-permute-start | bytes 1572872 | tf_op jit(solution)/shard_map/ppermute | solution.py:24
  37.0 0.8 copy-start.4
  82.0 0.8 copy-start.8

commit v13 on v9

--- a/solution.py
+++ b/solution.py
@@ -246,7 +246,7 @@
 
 
 def relay_ok(count, blocks_dev, rim, far_shifts):
-    return count % 2 == 0 and blocks_dev == 2 and rim == 2 and (not far_shifts or far_shifts[0] == 4)
+    return count % 2 == 0 and blocks_dev == 2 and rim == 2 and bool(far_shifts) and far_shifts[0] == 4
 
 
 def plan(tok_count, devices):
@@ -335,28 +335,28 @@
 
 
 def span_load(refs, start, length, other, axis):
-    size = refs[0].shape[axis]
     pieces = []
-    at = start
-    while length > 0:
-        index, offset = at // size, at % size
-        count = min(size - offset, length)
-        window = pl.ds(offset, count)
-        pieces.append(refs[index][window, other] if axis == 0 else refs[index][other, window])
-        at += count
-        length -= count
+    base = 0
+    for ref in refs:
+        size = ref.shape[axis]
+        low = max(start, base)
+        high = min(start + length, base + size)
+        if low < high:
+            window = pl.ds(low - base, high - low)
+            pieces.append(ref[window, other] if axis == 0 else ref[other, window])
+        base += size
     return pieces[0] if len(pieces) == 1 else jnp.concatenate(pieces, axis=axis)
 
 
 def row_kernel(near_count, far_list, heads, phase, *refs):
     far_count = len(far_list)
     position_ref, query_ref, grad_ref = refs[:3]
-    span_refs = refs[3:6]
-    far_refs = refs[6 : 6 + far_count]
+    span_refs = refs[3:7]
+    far_items = refs[7 : 8 + far_count]
     if phase == "stats":
-        attended_ref, stats_ref, stats_rows_ref = refs[6 + far_count :]
+        attended_ref, stats_ref, stats_rows_ref = refs[8 + far_count :]
     else:
-        stats_in_ref, grad_query_ref = refs[6 + far_count :]
+        stats_in_ref, grad_query_ref = refs[8 + far_count :]
     width = heads * HD
     near_rows = near_count * BLK
     scale = 1.0 / math.sqrt(HD)
@@ -382,9 +382,12 @@
             query = query_ref[rows, cols]
             grad = grad_ref[rows, cols]
             keys = [span_load(span_refs, block * BLK, near_rows, cols, 0)]
-            keys = keys + [item[rows, cols] for item in far_refs]
+            far_views = [(far_items[block], pl.ds(0, BLK))] + [
+                (item, rows) for item in far_items[2:]
+            ]
+            keys = keys + [item[window, cols] for item, window in far_views]
             values = [span_load(span_refs, block * BLK, near_rows, value_cols, 0)]
-            values = values + [item[rows, value_cols] for item in far_refs]
+            values = values + [item[window, value_cols] for item, window in far_views]
             scores = [
                 lax.dot_general(query, key, TRANS_B, preferred_element_type=jnp.float32) * scale
                 for key in keys
@@ -527,23 +530,27 @@
     pairs = swap_pairs(devices)
     keys_values = jnp.concatenate([key_tokens, value_tokens], axis=1)
     queries_grads = jnp.concatenate([queries, grad_out], axis=1)
-    back2 = passed_along(keys_values, "seq", 2)
+    back2_top = passed_along(keys_values[:BLK], "seq", 2)
+    back2_bottom = passed_along(keys_values[BLK:], "seq", 2)
+    back2 = jnp.concatenate([back2_top, back2_bottom], axis=0)
     ahead2 = passed_along(queries_grads, "seq", -2)
     swap_one = lax.ppermute(jnp.where(odd, queries_grads, keys_values), "seq", pairs)
-    back4 = passed_along(back2, "seq", 2)
+    back4_top = passed_along(back2_top, "seq", 2)
+    back4_bottom = passed_along(back2_bottom, "seq", 2)
     ahead4 = passed_along(ahead2, "seq", -2)
     swap_two = lax.ppermute(jnp.where(odd, back2, ahead2), "seq", pairs)
     back1 = jnp.where(odd, swap_one, swap_two)
     ahead1 = jnp.where(odd, swap_two, swap_one)
-    far_back = [back4] + [passed_along(keys_values, "seq", shift) for shift in far_shifts[1:]]
+    far_back = [back4_top, back4_bottom] + [
+        passed_along(keys_values, "seq", shift) for shift in far_shifts[1:]
+    ]
     far_ahead = [ahead4] + [passed_along(queries_grads, "seq", -shift) for shift in far_shifts[1:]]
-    far_back = far_back[: len(far_shifts)]
     far_ahead = far_ahead[: len(far_shifts)]
 
     position_arr = jnp.reshape(position, (1,)).astype(jnp.int32)
     far_offsets = list(far_list)
     slab_rows = (len(near_list) + len(far_list)) * BLK
-    row_inputs = (position_arr, queries, grad_out, back2, back1, keys_values, *far_back)
+    row_inputs = (position_arr, queries, grad_out, back2_top, back2_bottom, back1, keys_values, *far_back)
     attended, stats, stats_rows = pl.pallas_call(
         functools.partial(row_kernel, len(near_list), far_offsets, heads, "stats"),
         out_shape=(
@@ -551,7 +558,7 @@
             jax.ShapeDtypeStruct((tok_count, 2 * heads), jnp.float32),
             jax.ShapeDtypeStruct((2 * heads, tok_count), jnp.float32),
         ),
-        in_specs=[smem_spec()] + [vmem_spec()] * (5 + len(far_back)),
+        in_specs=[smem_spec()] + [vmem_spec()] * (6 + len(far_back)),
         out_specs=(vmem_spec(), vmem_spec(), vmem_spec()),
         cost_estimate=estimate(tok_count, row_width, slab_rows, 2, 1),
         name="rows_stats",
@@ -562,7 +569,7 @@
     grad_queries = pl.pallas_call(
         functools.partial(row_kernel, len(near_list), far_offsets, heads, "grad"),
         out_shape=jax.ShapeDtypeStruct((tok_count, row_width), jnp.bfloat16),
-        in_specs=[smem_spec()] + [vmem_spec()] * (6 + len(far_back)),
+        in_specs=[smem_spec()] + [vmem_spec()] * (7 + len(far_back)),
         out_specs=vmem_spec(),
         cost_estimate=estimate(tok_count, row_width, slab_rows, 3, 1),
         name="rows_grad",

time: 62 us -> 63.2 us (1.019)
  starting transfers between devices: 18.2 us -> 28.3 us
  waiting for transfers between devices: 21.4 us -> 12.6 us
    ppermute x7 -> x9, starting transfers between devices: 15 us -> 25 us  [passed_along(): lax.ppermute(value, axis, [(source, source + steps) for source in range(f...]
    ppermute x7 -> x9, waiting for transfers between devices: 15.3 us -> 7.84 us  [passed_along(): lax.ppermute(value, axis, [(source, source + steps) for source in range(f...]
    ppermute x1, waiting for transfers between devices: 6.15 us -> 4.77 us  [body(): swap_two = lax.ppermute(jnp.where(odd, back2, ahead2), 'seq', pairs)]
    unnamed x26 -> x30, local copies, waits for them, and re-layouts: 2.44 us -> 2.47 us
  transfers between devices with their start and end apart: 9 -> 11, of which waited for: 5 -> 4; matrix products, arithmetic and copies ran while one was open for 2% -> 2% of each run, Pallas kernels for 19% -> 18%
where the time goes in v13:
time: 63.2 us; the launch traced here: 62.7 us
  starting transfers between devices  28.3 us (45%)
  Pallas kernels  17 us (27%)
  waiting for transfers between devices  12.6 us (20%)
  local copies, waits for them, and re-layouts  2.55 us (4%)
  other arithmetic  1.3 us (2%)
  between operations  0.93 us (1%)
    ppermute x9, starting transfers between devices, passed_along(): lax.ppermute(value, axis, [(source, source + steps) for source in range(f...  25 us
    pallas_call x2, Pallas kernels, body(): pl.pallas_call(functools.partial(row_kernel, len(near_list), far_offsets,...  11.6 us
    ppermute x9, waiting for transfers between devices, passed_along(): lax.ppermute(value, axis, [(source, source + steps) for source in range(f...  7.84 us
    pallas_call x1, Pallas kernels, body(): pl.pallas_call(functools.partial(key_kernel, len(near_list), far_offsets,...  5.42 us
    ppermute x1, waiting for transfers between devices, body(): swap_two = lax.ppermute(jnp.where(odd, back2, ahead2), 'seq', pairs)  4.77 us
    unnamed x30, local copies, waits for them, and re-layouts  2.47 us
    ppermute x1, starting transfers between devices, body(): swap_two = lax.ppermute(jnp.where(odd, back2, ahead2), 'seq', pairs)  1.74 us
    ppermute x1, starting transfers between devices, body(): lax.ppermute(jnp.where(odd, queries_grads, keys_values), 'seq', pairs)  1.58 us
  transfers between devices with their start and end apart: 11, of which 4 were waited for; matrix products, arithmetic and copies ran while one was open for 2% of the time, Pallas kernels for 18%

profile of v13, /device:TPU:0, one launch (start us, length us, event | category | flops | bytes accessed | tf_op | source)
XLA Modules:
  0.0 62.7 jit_solution(380530545030921634)
XLA Ops:
  0.6 1.0 %constant_dynamic-update-slice_fusion.3 = bf16[256,1024]{1,0:T(8,128)(2,1)S(1)} fusion(bf16[256,512]{1,0:T(8,128)(2,1)} %refs_1_.3), kind=kLoop, calls=%fused_computation.7 | loop fusion | bytes 524288
  1.7 1.4 %collective-permute-start.3 = (bf16[256,1024]{1,0:T(8,128)(2,1)S(1)}, bf16[256,1024]{1,0:T(8,128)(2,1)S(1)}, u32[]{:S(2)}, u32[]{:S(2)}) collective-permute-start(bf16[256,1024]{1,0:T(8,128)(2,1)S(1)} %constant_dynamic-update-slice_fusion.2.refs_2_), channel_id=1, source_target_pairs={{8,0},{12,4},{16,8},{20,12},{24,16},{28,20},{9,1},{13,5},{17,9},{2... | collective-permute-start | bytes 1572872 | tf_op jit(solution)/shard_map/ppermute | solution.py:24
  3.3 5.6 %collective-permute-start = (bf16[128,1024]{1,0:T(8,128)(2,1)S(1)}, bf16[128,1024]{1,0:T(8,128)(2,1)S(1)}, u32[]{:S(2)}, u32[]{:S(2)}) collective-permute-start(bf16[128,1024]{1,0:T(8,128)(2,1)S(1)} %get-tuple-element.17), channel_id=1, source_target_pairs={{0,8},{4,12},{8,16},{12,20},{16,24},{20,28},{1,9},{5,13},{9,17},{1... | collective-permute-start | bytes 786440 | tf_op jit(solution)/shard_map/ppermute | solution.py:24
  8.9 3.9 %collective-permute-start.1 = (bf16[128,1024]{1,0:T(8,128)(2,1)S(1)}, bf16[128,1024]{1,0:T(8,128)(2,1)S(1)}, u32[]{:S(2)}, u32[]{:S(2)}) collective-permute-start(bf16[128,1024]{1,0:T(8,128)(2,1)S(1)} %get-tuple-element.16), channel_id=1, source_target_pairs={{0,8},{4,12},{8,16},{12,20},{16,24},{20,28},{1,9},{5,13},{9,17},{1... | collective-permute-start | bytes 786440 | tf_op jit(solution)/shard_map/ppermute | solution.py:24
  12.9 1.6 %collective-permute-start.2 = (bf16[256,1024]{1,0:T(8,128)(2,1)S(1)}, bf16[256,1024]{1,0:T(8,128)(2,1)S(1)}, u32[]{:S(2)}, u32[]{:S(2)}) collective-permute-start(bf16[256,1024]{1,0:T(8,128)(2,1)S(1)} %broadcast_select_fusion.2), channel_id=1, source_target_pairs={{0,4},{4,0},{8,12},{12,8},{16,20},{20,16},{24,28},{28,24},{1,5},{5... | collective-permute-start | bytes 1572872 | tf_op jit(solution)/shard_map/ppermute | solution.py:537
  14.5 1.1 %collective-permute-done.refs_3_ = bf16[128,1024]{1,0:T(8,128)(2,1)S(1)} collective-permute-done((bf16[128,1024]{1,0:T(8,128)(2,1)S(1)}, bf16[128,1024]{1,0:T(8,128)(2,1)S(1)}, u32[]{:S(2)}, u32[]{:S(2)}) %collective-permute-start) | collective-permute-done | bytes 262176 | tf_op jit(solution)/shard_map/ppermute | solution.py:24
  15.6 4.5 %collective-permute-done.1.refs_4_ = bf16[128,1024]{1,0:T(8,128)(2,1)S(1)} collective-permute-done((bf16[128,1024]{1,0:T(8,128)(2,1)S(1)}, bf16[128,1024]{1,0:T(8,128)(2,1)S(1)}, u32[]{:S(2)}, u32[]{:S(2)}) %collective-permute-start.1) | collective-permute-done | bytes 262176 | tf_op jit(solution)/shard_map/ppermute | solution.py:24
  20.0 0.2 maximum_select_fusion
  20.2 1.7 %collective-permute-start.4 = (bf16[256,1024]{1,0:T(8,128)(2,1)S(1)}, bf16[256,1024]{1,0:T(8,128)(2,1)S(1)}, u32[]{:S(2)}, u32[]{:S(2)}) collective-permute-start(bf16[256,1024]{1,0:T(8,128)(2,1)S(1)} %maximum_select_fusion), channel_id=1, source_target_pairs={{0,4},{4,0},{8,12},{12,8},{16,20},{20,16},{24,28},{28,24},{1,5},{5... | collective-permute-start | bytes 1572872 | tf_op jit(solution)/shard_map/ppermute | solution.py:541
  22.0 1.3 %collective-permute-start.9 = (bf16[256,1024]{1,0:T(8,128)(2,1)S(1)}, bf16[256,1024]{1,0:T(8,128)(2,1)S(1)}, u32[]{:S(2)}, u32[]{:S(2)}) collective-permute-start(bf16[256,1024]{1,0:T(8,128)(2,1)S(1)} %collective-permute-done.3.refs_4_), channel_id=1, source_target_pairs={{8,0},{12,4},{16,8},{20,12},{24,16},{28,20},{9,1},{13,5},{17,9},{2... | collective-permute-start | bytes 1572872 | tf_op jit(solution)/shard_map/ppermute | solution.py:24
  23.3 5.0 %collective-permute-start.5 = (bf16[128,1024]{1,0:T(8,128)(2,1)S(1)}, bf16[128,1024]{1,0:T(8,128)(2,1)S(1)}, u32[]{:S(2)}, u32[]{:S(2)}) collective-permute-start(bf16[128,1024]{1,0:T(8,128)(2,1)S(1)} %collective-permute-done.refs_3_), channel_id=1, source_target_pairs={{0,8},{4,12},{8,16},{12,20},{16,24},{20,28},{1,9},{5,13},{9,17},{1... | collective-permute-start | bytes 786440 | tf_op jit(solution)/shard_map/ppermute | solution.py:24
  28.3 3.9 %collective-permute-start.6 = (bf16[128,1024]{1,0:T(8,128)(2,1)S(1)}, bf16[128,1024]{1,0:T(8,128)(2,1)S(1)}, u32[]{:S(2)}, u32[]{:S(2)}) collective-permute-start(bf16[128,1024]{1,0:T(8,128)(2,1)S(1)} %collective-permute-done.1.refs_4_), channel_id=1, source_target_pairs={{0,8},{4,12},{8,16},{12,20},{16,24},{20,28},{1,9},{5,13},{9,17},{1... | collective-permute-start | bytes 786440 | tf_op jit(solution)/shard_map/ppermute | solution.py:24
  32.3 4.8 %collective-permute-done.4 = bf16[256,1024]{1,0:T(8,128)(2,1)S(1)} collective-permute-done((bf16[256,1024]{1,0:T(8,128)(2,1)S(1)}, bf16[256,1024]{1,0:T(8,128)(2,1)S(1)}, u32[]{:S(2)}, u32[]{:S(2)}) %collective-permute-start.4) | collective-permute-done | bytes 524320 | tf_op jit(solution)/shard_map/ppermute | solution.py:541
  37.0 1.1 %broadcast_select_fusion = (bf16[256,1024]{1,0:T(8,128)(2,1)}, bf16[256,1024]{1,0:T(8,128)(2,1)}) fusion(bf16[256,1024]{1,0:T(8,128)(2,1)S(1)} %collective-permute-done.4, bf16[256,1024]{1,0:T(8,128)(2,1)S(1)} %collective-permute-done.2, pred[]{:T(512)S(6)} %eq.5), kind=kLoop, calls=%fused_computation.1 | loop fusion | flops 524288 | bytes 2097153 | tf_op jit(solution)/shard_map/jit(_where)/select_n | solution.py:543
  38.1 0.7 %copy-done.5 = bf16[128,1024]{1,0:T(8,128)(2,1)} copy-done((bf16[128,1024]{1,0:T(8,128)(2,1)}, bf16[128,1024]{1,0:T(8,128)(2,1)S(1)}, u32[]{:S(2)}) %copy-start.5) | copy-done | bytes 262168
  38.8 0.1 copy-done.6
  38.9 6.4 %rows_stats.1 = (bf16[256,512]{1,0:T(8,128)(2,1)}, f32[256,8]{1,0:T(8,128)}, f32[8,256]{1,0:T(8,128)}) custom-call(s32[1]{0:T(128)} %bitcast.refs_0_, bf16[256,512]{1,0:T(8,128)(2,1)} %refs_1_.3, bf16[256,512]{1,0:T(8,128)(2,1)} %refs_2_.3, bf16[128,1024]{1,0:T(8,128)(2,1)} %copy-done.2, bf16[128,1024]{1,0:T(8,128)(2,1)} %copy-done.3, ...), custom_call_target="tpu_custom_call" | custom-call | flops 402653184 | bytes 4194304 | tf_op jit(solution)/shard_map/rows_stats/pallas_call | solution.py:554
  45.3 1.3 %collective-permute-start.7 = (f32[8,256]{1,0:T(8,128)}, f32[8,256]{1,0:T(8,128)S(1)}, u32[]{:S(2)}, u32[]{:S(2)}) collective-permute-start(f32[8,256]{1,0:T(8,128)} %get-tuple-element.11.refs_5_), channel_id=1, source_target_pairs={{4,0},{8,4},{12,8},{16,12},{20,16},{24,20},{28,24},{5,1},{9,5},{13... | collective-permute-start | bytes 24584 | tf_op jit(solution)/shard_map/ppermute | solution.py:24
  46.6 1.3 %collective-permute-start.8 = (f32[8,256]{1,0:T(8,128)}, f32[8,256]{1,0:T(8,128)S(1)}, u32[]{:S(2)}, u32[]{:S(2)}) collective-permute-start(f32[8,256]{1,0:T(8,128)} %get-tuple-element.11.refs_5_), channel_id=1, source_target_pairs={{8,0},{12,4},{16,8},{20,12},{24,16},{28,20},{9,1},{13,5},{17,9},{2... | collective-permute-start | bytes 24584 | tf_op jit(solution)/shard_map/ppermute | solution.py:24
  47.9 1.3 %collective-permute-start.10 = (f32[8,256]{1,0:T(8,128)}, f32[8,256]{1,0:T(8,128)S(1)}, u32[]{:S(2)}, u32[]{:S(2)}) collective-permute-start(f32[8,256]{1,0:T(8,128)} %get-tuple-element.11.refs_5_), channel_id=1, source_target_pairs={{16,0},{20,4},{24,8},{28,12},{17,1},{21,5},{25,9},{29,13},{18,2},{... | collective-permute-start | bytes 24584 | tf_op jit(solution)/shard_map/ppermute | solution.py:24
  49.2 5.2 %rows_grad.1 = bf16[256,512]{1,0:T(8,128)(2,1)} custom-call(s32[1]{0:T(128)} %bitcast.refs_0_, bf16[256,512]{1,0:T(8,128)(2,1)} %refs_1_.3, bf16[256,512]{1,0:T(8,128)(2,1)} %refs_2_.3, bf16[128,1024]{1,0:T(8,128)(2,1)} %copy-done.2, bf16[128,1024]{1,0:T(8,128)(2,1)} %copy-done.3, bf16[256,1024]{1,0:T(8,128)(2,1)} %get-tuple-element.15.refs_5_, ...), custom_call_target="tpu_custom_call" | custom-call | flops 603979776 | bytes 4194304 | tf_op jit(solution)/shard_map/rows_grad/pallas_call | solution.py:569
  54.4 2.3 %collective-permute-done.10.refs_9_ = f32[8,256]{1,0:T(8,128)S(1)} collective-permute-done((f32[8,256]{1,0:T(8,128)}, f32[8,256]{1,0:T(8,128)S(1)}, u32[]{:S(2)}, u32[]{:S(2)}) %collective-permute-start.10) | collective-permute-done | bytes 8224 | tf_op jit(solution)/shard_map/ppermute | solution.py:24
  56.7 0.6 copy-done.13
  57.3 5.4 %keys_pass.1 = (bf16[256,512]{1,0:T(8,128)(2,1)}, bf16[256,512]{1,0:T(8,128)(2,1)}) custom-call(s32[1]{0:T(128)} %bitcast.refs_0_, bf16[256,1024]{1,0:T(8,128)(2,1)} %copy-done, bf16[256,1024]{1,0:T(8,128)(2,1)} %copy-done.4, bf16[256,1024]{1,0:T(8,128)(2,1)} %get-tuple-element.14.refs_3_, bf16[256,1024]{1,0:T(8,128)(2,1)} %copy-done.7, ...), custom_call_target="tpu_custom_call" | custom-call | flops 805306368 | bytes 4194304 | tf_op jit(solution)/shard_map/keys_pass/pallas_call | solution.py:577
  (37 shorter events, 0.2 us)
Async XLA Ops:
  0.6 1.0 %copy-start.1 = (bf16[256,512]{1,0:T(8,128)(2,1)S(1)}, bf16[256,512]{1,0:T(8,128)(2,1)}, u32[]{:S(2)}) copy-start(bf16[256,512]{1,0:T(8,128)(2,1)} %refs_2_.3) | copy-start | bytes 786436
  1.7 1.5 %copy-start.8 = (bf16[256,512]{1,0:T(8,128)(2,1)S(1)}, bf16[256,512]{1,0:T(8,128)(2,1)}, u32[]{:S(2)}) copy-start(bf16[256,512]{1,0:T(8,128)(2,1)} %param.5) | copy-start | bytes 786436
  1.7 11.1 %copy-start.4 = (bf16[256,1024]{1,0:T(8,128)(2,1)}, bf16[256,1024]{1,0:T(8,128)(2,1)S(1)}, u32[]{:S(2)}) copy-start(bf16[256,1024]{1,0:T(8,128)(2,1)S(1)} %constant_dynamic-update-slice_fusion.2.refs_2_) | copy-start | bytes 1572868
  1.7 1.5 %copy-start.9 = (bf16[256,512]{1,0:T(8,128)(2,1)S(1)}, bf16[256,512]{1,0:T(8,128)(2,1)}, u32[]{:S(2)}) copy-start(bf16[256,512]{1,0:T(8,128)(2,1)} %param.6) | copy-start | bytes 786436
  1.7 18.3 %collective-permute-start.3 = (bf16[256,1024]{1,0:T(8,128)(2,1)S(1)}, bf16[256,1024]{1,0:T(8,128)(2,1)S(1)}, u32[]{:S(2)}, u32[]{:S(2)}) collective-permute-start(bf16[256,1024]{1,0:T(8,128)(2,1)S(1)} %constant_dynamic-update-slice_fusion.2.refs_2_), channel_id=1, source_target_pairs={{8,0},{12,4},{16,8},{20,12},{24,16},{28,20},{9,1},{13,5},{17,9},{2... | collective-permute-start | bytes 1572872 | tf_op jit(solution)/shard_map/ppermute | solution.py:24
  3.3 9.6 %copy-start = (bf16[256,1024]{1,0:T(8,128)(2,1)}, bf16[256,1024]{1,0:T(8,128)(2,1)S(1)}, u32[]{:S(2)}) copy-start(bf16[256,1024]{1,0:T(8,128)(2,1)S(1)} %constant_dynamic-update-slice_fusion.refs_6_.refs_1_) | copy-start | bytes 1572868
  3.3 12.3 %collective-permute-start = (bf16[128,1024]{1,0:T(8,128)(2,1)S(1)}, bf16[128,1024]{1,0:T(8,128)(2,1)S(1)}, u32[]{:S(2)}, u32[]{:S(2)}) collective-permute-start(bf16[128,1024]{1,0:T(8,128)(2,1)S(1)} %get-tuple-element.17), channel_id=1, source_target_pairs={{0,8},{4,12},{8,16},{12,20},{16,24},{20,28},{1,9},{5,13},{9,17},{1... | collective-permute-start | bytes 786440 | tf_op jit(solution)/shard_map/ppermute | solution.py:24
  8.9 11.1 %collective-permute-start.1 = (bf16[128,1024]{1,0:T(8,128)(2,1)S(1)}, bf16[128,1024]{1,0:T(8,128)(2,1)S(1)}, u32[]{:S(2)}, u32[]{:S(2)}) collective-permute-start(bf16[128,1024]{1,0:T(8,128)(2,1)S(1)} %get-tuple-element.16), channel_id=1, source_target_pairs={{0,8},{4,12},{8,16},{12,20},{16,24},{20,28},{1,9},{5,13},{9,17},{1... | collective-permute-start | bytes 786440 | tf_op jit(solution)/shard_map/ppermute | solution.py:24
  12.9 19.3 %collective-permute-start.2 = (bf16[256,1024]{1,0:T(8,128)(2,1)S(1)}, bf16[256,1024]{1,0:T(8,128)(2,1)S(1)}, u32[]{:S(2)}, u32[]{:S(2)}) collective-permute-start(bf16[256,1024]{1,0:T(8,128)(2,1)S(1)} %broadcast_select_fusion.2), channel_id=1, source_target_pairs={{0,4},{4,0},{8,12},{12,8},{16,20},{20,16},{24,28},{28,24},{1,5},{5... | collective-permute-start | bytes 1572872 | tf_op jit(solution)/shard_map/ppermute | solution.py:537
  15.6 7.7 %copy-start.2 = (bf16[128,1024]{1,0:T(8,128)(2,1)}, bf16[128,1024]{1,0:T(8,128)(2,1)S(1)}, u32[]{:S(2)}) copy-start(bf16[128,1024]{1,0:T(8,128)(2,1)S(1)} %collective-permute-done.refs_3_) | copy-start | bytes 786436
  20.0 8.3 %copy-start.3 = (bf16[128,1024]{1,0:T(8,128)(2,1)}, bf16[128,1024]{1,0:T(8,128)(2,1)S(1)}, u32[]{:S(2)}) copy-start(bf16[128,1024]{1,0:T(8,128)(2,1)S(1)} %collective-permute-done.1.refs_4_) | copy-start | bytes 786436
  20.0 1.9 %copy-start.7 = (bf16[256,1024]{1,0:T(8,128)(2,1)}, bf16[256,1024]{1,0:T(8,128)(2,1)S(1)}, u32[]{:S(2)}) copy-start(bf16[256,1024]{1,0:T(8,128)(2,1)S(1)} %collective-permute-done.3.refs_4_) | copy-start | bytes 1572868
  20.2 16.8 %collective-permute-start.4 = (bf16[256,1024]{1,0:T(8,128)(2,1)S(1)}, bf16[256,1024]{1,0:T(8,128)(2,1)S(1)}, u32[]{:S(2)}, u32[]{:S(2)}) collective-permute-start(bf16[256,1024]{1,0:T(8,128)(2,1)S(1)} %maximum_select_fusion), channel_id=1, source_target_pairs={{0,4},{4,0},{8,12},{12,8},{16,20},{20,16},{24,28},{28,24},{1,5},{5... | collective-permute-start | bytes 1572872 | tf_op jit(solution)/shard_map/ppermute | solution.py:541
  22.0 32.4 %collective-permute-start.9 = (bf16[256,1024]{1,0:T(8,128)(2,1)S(1)}, bf16[256,1024]{1,0:T(8,128)(2,1)S(1)}, u32[]{:S(2)}, u32[]{:S(2)}) collective-permute-start(bf16[256,1024]{1,0:T(8,128)(2,1)S(1)} %collective-permute-done.3.refs_4_), channel_id=1, source_target_pairs={{8,0},{12,4},{16,8},{20,12},{24,16},{28,20},{9,1},{13,5},{17,9},{2... | collective-permute-start | bytes 1572872 | tf_op jit(solution)/shard_map/ppermute | solution.py:24
  23.3 14.8 %collective-permute-start.5 = (bf16[128,1024]{1,0:T(8,128)(2,1)S(1)}, bf16[128,1024]{1,0:T(8,128)(2,1)S(1)}, u32[]{:S(2)}, u32[]{:S(2)}) collective-permute-start(bf16[128,1024]{1,0:T(8,128)(2,1)S(1)} %collective-permute-done.refs_3_), channel_id=1, source_target_pairs={{0,8},{4,12},{8,16},{12,20},{16,24},{20,28},{1,9},{5,13},{9,17},{1... | collective-permute-start | bytes 786440 | tf_op jit(solution)/shard_map/ppermute | solution.py:24
  28.3 9.8 %collective-permute-start.6 = (bf16[128,1024]{1,0:T(8,128)(2,1)S(1)}, bf16[128,1024]{1,0:T(8,128)(2,1)S(1)}, u32[]{:S(2)}, u32[]{:S(2)}) collective-permute-start(bf16[128,1024]{1,0:T(8,128)(2,1)S(1)} %collective-permute-done.1.refs_4_), channel_id=1, source_target_pairs={{0,8},{4,12},{8,16},{12,20},{16,24},{20,28},{1,9},{5,13},{9,17},{1... | collective-permute-start | bytes 786440 | tf_op jit(solution)/shard_map/ppermute | solution.py:24
  38.1 0.7 %copy-start.5 = (bf16[128,1024]{1,0:T(8,128)(2,1)}, bf16[128,1024]{1,0:T(8,128)(2,1)S(1)}, u32[]{:S(2)}) copy-start(bf16[128,1024]{1,0:T(8,128)(2,1)S(1)} %collective-permute-done.5.refs_7_) | copy-start | bytes 786436
  38.1 0.8 %copy-start.6 = (bf16[128,1024]{1,0:T(8,128)(2,1)}, bf16[128,1024]{1,0:T(8,128)(2,1)S(1)}, u32[]{:S(2)}) copy-start(bf16[128,1024]{1,0:T(8,128)(2,1)S(1)} %collective-permute-done.6.refs_8_) | copy-start | bytes 786436
  45.3 9.1 %collective-permute-start.7 = (f32[8,256]{1,0:T(8,128)}, f32[8,256]{1,0:T(8,128)S(1)}, u32[]{:S(2)}, u32[]{:S(2)}) collective-permute-start(f32[8,256]{1,0:T(8,128)} %get-tuple-element.11.refs_5_), channel_id=1, source_target_pairs={{4,0},{8,4},{12,8},{16,12},{20,16},{24,20},{28,24},{5,1},{9,5},{13... | collective-permute-start | bytes 24584 | tf_op jit(solution)/shard_map/ppermute | solution.py:24
  46.6 7.8 %collective-permute-start.8 = (f32[8,256]{1,0:T(8,128)}, f32[8,256]{1,0:T(8,128)S(1)}, u32[]{:S(2)}, u32[]{:S(2)}) collective-permute-start(f32[8,256]{1,0:T(8,128)} %get-tuple-element.11.refs_5_), channel_id=1, source_target_pairs={{8,0},{12,4},{16,8},{20,12},{24,16},{28,20},{9,1},{13,5},{17,9},{2... | collective-permute-start | bytes 24584 | tf_op jit(solution)/shard_map/ppermute | solution.py:24
  47.9 8.8 %collective-permute-start.10 = (f32[8,256]{1,0:T(8,128)}, f32[8,256]{1,0:T(8,128)S(1)}, u32[]{:S(2)}, u32[]{:S(2)}) collective-permute-start(f32[8,256]{1,0:T(8,128)} %get-tuple-element.11.refs_5_), channel_id=1, source_target_pairs={{16,0},{20,4},{24,8},{28,12},{17,1},{21,5},{25,9},{29,13},{18,2},{... | collective-permute-start | bytes 24584 | tf_op jit(solution)/shard_map/ppermute | solution.py:24
  54.4 2.3 %copy-start.10 = (bf16[256,1024]{1,0:T(8,128)(2,1)}, bf16[256,1024]{1,0:T(8,128)(2,1)S(1)}, u32[]{:S(2)}) copy-start(bf16[256,1024]{1,0:T(8,128)(2,1)S(1)} %collective-permute-done.9.refs_8_) | copy-start | bytes 1572868
  54.4 2.3 %copy-start.11 = (f32[8,256]{1,0:T(8,128)}, f32[8,256]{1,0:T(8,128)S(1)}, u32[]{:S(2)}) copy-start(f32[8,256]{1,0:T(8,128)S(1)} %collective-permute-done.7.refs_6_) | copy-start | bytes 24580
  54.4 2.3 %copy-start.12 = (f32[8,256]{1,0:T(8,128)}, f32[8,256]{1,0:T(8,128)S(1)}, u32[]{:S(2)}) copy-start(f32[8,256]{1,0:T(8,128)S(1)} %collective-permute-done.8.refs_7_) | copy-start | bytes 24580
  (1 other events, 0.6 us)

commit v14 on v9

--- a/solution.py
+++ b/solution.py
@@ -371,7 +371,12 @@
         near_span = pl.ds(block * BLK, near_rows)
         near_mask = jnp.logical_and(near_causal, first + block - near_offset >= 0)
         far_live = [first + block - offset >= 0 for offset in far_list]
-        masks = [near_mask] + far_live
+        masks = [
+            jnp.concatenate(
+                [near_mask] + [jnp.logical_and(near_row_ids[:, :BLK] >= 0, live) for live in far_live],
+                axis=1,
+            )
+        ]
         if phase == "stats":
             stats_tile = jnp.zeros((BLK, 2 * heads), jnp.float32)
         else:
@@ -382,9 +387,9 @@
             query = query_ref[rows, cols]
             grad = grad_ref[rows, cols]
             keys = [span_load(span_refs, block * BLK, near_rows, cols, 0)]
-            keys = keys + [item[rows, cols] for item in far_refs]
+            keys = [jnp.concatenate(keys + [item[rows, cols] for item in far_refs], axis=0)]
             values = [span_load(span_refs, block * BLK, near_rows, value_cols, 0)]
-            values = values + [item[rows, value_cols] for item in far_refs]
+            values = [jnp.concatenate(values + [item[rows, value_cols] for item in far_refs], axis=0)]
             scores = [
                 lax.dot_general(query, key, TRANS_B, preferred_element_type=jnp.float32) * scale
                 for key in keys
@@ -471,22 +476,29 @@
         near_span = pl.ds(block * BLK, near_rows)
         near_mask = jnp.logical_and(near_causal, first + block + near_offset < block_total)
         far_live = [first + block + offset < block_total for offset in far_list]
-        masks = [near_mask] + far_live
+        masks = [
+            jnp.concatenate(
+                [near_mask] + [jnp.logical_and(near_key_ids[:, :BLK] >= 0, live) for live in far_live],
+                axis=1,
+            )
+        ]
         for head in range(heads):
             cols = pl.ds(head * HD, HD)
             value_cols = pl.ds(width + head * HD, HD)
             key = own_ref[rows, cols]
             value = own_ref[rows, value_cols]
             queries = [span_load(span_refs, block * BLK, near_rows, cols, 0)]
-            queries = queries + [item[rows, cols] for item in far_rows]
+            queries = [jnp.concatenate(queries + [item[rows, cols] for item in far_rows], axis=0)]
             grads = [span_load(span_refs, block * BLK, near_rows, value_cols, 0)]
-            grads = grads + [item[rows, value_cols] for item in far_rows]
+            grads = [jnp.concatenate(grads + [item[rows, value_cols] for item in far_rows], axis=0)]
             totals = [span_load(stats_refs, block * BLK, near_rows, pl.ds(head, 1), 1)] + [
                 item[pl.ds(head, 1), rows] for item in far_stats
             ]
             dots = [span_load(stats_refs, block * BLK, near_rows, pl.ds(heads + head, 1), 1)] + [
                 item[pl.ds(heads + head, 1), rows] for item in far_stats
             ]
+            totals = [jnp.concatenate(totals, axis=1)]
+            dots = [jnp.concatenate(dots, axis=1)]
             grad_key = jnp.zeros((BLK, HD), jnp.float32)
             grad_value = jnp.zeros((BLK, HD), jnp.float32)
             for query, grad, log_total, out_dot, mask in zip(queries, grads, totals, dots, masks):

time: 62 us -> 60.4 us (0.974)
  Pallas kernels: 17 us -> 15.3 us
  waiting for transfers between devices: 21.4 us -> 22.1 us
    pallas_call x2, Pallas kernels: 11.6 us -> 10.5 us  [body(): pl.pallas_call(functools.partial(row_kernel, len(near_list), far_offsets,...]
    pallas_call x1, Pallas kernels: 5.42 us -> 4.74 us  [body(): pl.pallas_call(functools.partial(key_kernel, len(near_list), far_offsets,...]
    ppermute x7, waiting for transfers between devices: 15.3 us -> 15.9 us  [passed_along(): lax.ppermute(value, axis, [(source, source + steps) for source in range(f...]
  transfers between devices with their start and end apart: 9 -> 9, of which waited for: 5 -> 5; matrix products, arithmetic and copies ran while one was open for 2% -> 2% of each run, Pallas kernels for 19% -> 18%
where the time goes in v14:
time: 60.4 us; the launch traced here: 60 us
  waiting for transfers between devices  22.1 us (37%)
  starting transfers between devices  18.2 us (30%)
  Pallas kernels  15.3 us (25%)
  local copies, waits for them, and re-layouts  2.49 us (4%)
  other arithmetic  1.15 us (2%)
  between operations  0.88 us (1%)
    ppermute x7, waiting for transfers between devices, passed_along(): lax.ppermute(value, axis, [(source, source + steps) for source in range(f...  15.9 us
    ppermute x7, starting transfers between devices, passed_along(): lax.ppermute(value, axis, [(source, source + steps) for source in range(f...  15 us
    pallas_call x2, Pallas kernels, body(): pl.pallas_call(functools.partial(row_kernel, len(near_list), far_offsets,...  10.5 us
    ppermute x1, waiting for transfers between devices, body(): swap_two = lax.ppermute(jnp.where(odd, back2, ahead2), 'seq', pairs)  6.15 us
    pallas_call x1, Pallas kernels, body(): pl.pallas_call(functools.partial(key_kernel, len(near_list), far_offsets,...  4.74 us
    unnamed x26, local copies, waits for them, and re-layouts  2.44 us
    ppermute x1, starting transfers between devices, body(): lax.ppermute(jnp.where(odd, queries_grads, keys_values), 'seq', pairs)  1.58 us
    ppermute x1, starting transfers between devices, body(): swap_two = lax.ppermute(jnp.where(odd, back2, ahead2), 'seq', pairs)  1.58 us
  transfers between devices with their start and end apart: 9, of which 5 were waited for; matrix products, arithmetic and copies ran while one was open for 2% of the time, Pallas kernels for 18%

profile of v14, /device:TPU:0, one launch (start us, length us, event | category | flops | bytes accessed | tf_op | source)
XLA Modules:
  0.0 60.0 jit_solution(11559256538212809651)
XLA Ops:
  0.6 1.0 %constant_dynamic-update-slice_fusion.1 = bf16[256,1024]{1,0:T(8,128)(2,1)S(1)} fusion(bf16[256,512]{1,0:T(8,128)(2,1)} %param.5), kind=kLoop, calls=%fused_computation.5 | loop fusion | bytes 524288
  1.7 0.0 copy-start.2
  1.7 5.1 %collective-permute-start = (bf16[256,1024]{1,0:T(8,128)(2,1)S(1)}, bf16[256,1024]{1,0:T(8,128)(2,1)S(1)}, u32[]{:S(2)}, u32[]{:S(2)}) collective-permute-start(bf16[256,1024]{1,0:T(8,128)(2,1)S(1)} %constant_dynamic-update-slice_fusion.refs_5_.refs_1_), channel_id=1, source_target_pairs={{0,8},{4,12},{8,16},{12,20},{16,24},{20,28},{1,9},{5,13},{9,17},{1... | collective-permute-start | bytes 1572872 | tf_op jit(solution)/shard_map/ppermute | solution.py:24
  6.9 1.3 %collective-permute-start.2 = (bf16[256,1024]{1,0:T(8,128)(2,1)S(1)}, bf16[256,1024]{1,0:T(8,128)(2,1)S(1)}, u32[]{:S(2)}, u32[]{:S(2)}) collective-permute-start(bf16[256,1024]{1,0:T(8,128)(2,1)S(1)} %constant_dynamic-update-slice_fusion.2.refs_2_), channel_id=1, source_target_pairs={{8,0},{12,4},{16,8},{20,12},{24,16},{28,20},{9,1},{13,5},{17,9},{2... | collective-permute-start | bytes 1572872 | tf_op jit(solution)/shard_map/ppermute | solution.py:24
  8.3 0.1 broadcast_select_fusion.3
  8.3 1.6 %collective-permute-start.1 = (bf16[256,1024]{1,0:T(8,128)(2,1)S(1)}, bf16[256,1024]{1,0:T(8,128)(2,1)S(1)}, u32[]{:S(2)}, u32[]{:S(2)}) collective-permute-start(bf16[256,1024]{1,0:T(8,128)(2,1)S(1)} %broadcast_select_fusion.3), channel_id=1, source_target_pairs={{0,4},{4,0},{8,12},{12,8},{16,20},{20,16},{24,28},{28,24},{1,5},{5... | collective-permute-start | bytes 1572872 | tf_op jit(solution)/shard_map/ppermute | solution.py:544
  9.9 8.1 %collective-permute-done.refs_3_ = bf16[256,1024]{1,0:T(8,128)(2,1)S(1)} collective-permute-done((bf16[256,1024]{1,0:T(8,128)(2,1)S(1)}, bf16[256,1024]{1,0:T(8,128)(2,1)S(1)}, u32[]{:S(2)}, u32[]{:S(2)}) %collective-permute-start) | collective-permute-done | bytes 524320 | tf_op jit(solution)/shard_map/ppermute | solution.py:24
  18.0 4.2 %collective-permute-done.2.refs_4_ = bf16[256,1024]{1,0:T(8,128)(2,1)S(1)} collective-permute-done((bf16[256,1024]{1,0:T(8,128)(2,1)S(1)}, bf16[256,1024]{1,0:T(8,128)(2,1)S(1)}, u32[]{:S(2)}, u32[]{:S(2)}) %collective-permute-start.2) | collective-permute-done | bytes 524320 | tf_op jit(solution)/shard_map/ppermute | solution.py:24
  22.2 0.1 broadcast_select_fusion.2
  22.3 1.6 %collective-permute-start.3 = (bf16[256,1024]{1,0:T(8,128)(2,1)S(1)}, bf16[256,1024]{1,0:T(8,128)(2,1)S(1)}, u32[]{:S(2)}, u32[]{:S(2)}) collective-permute-start(bf16[256,1024]{1,0:T(8,128)(2,1)S(1)} %broadcast_select_fusion.2), channel_id=1, source_target_pairs={{0,4},{4,0},{8,12},{12,8},{16,20},{20,16},{24,28},{28,24},{1,5},{5... | collective-permute-start | bytes 1572872 | tf_op jit(solution)/shard_map/ppermute | solution.py:547
  23.9 3.5 %collective-permute-start.4 = (bf16[256,1024]{1,0:T(8,128)(2,1)S(1)}, bf16[256,1024]{1,0:T(8,128)(2,1)S(1)}, u32[]{:S(2)}, u32[]{:S(2)}) collective-permute-start(bf16[256,1024]{1,0:T(8,128)(2,1)S(1)} %collective-permute-done.refs_3_), channel_id=1, source_target_pairs={{0,8},{4,12},{8,16},{12,20},{16,24},{20,28},{1,9},{5,13},{9,17},{1... | collective-permute-start | bytes 1572872 | tf_op jit(solution)/shard_map/ppermute | solution.py:24
  27.3 1.3 %collective-permute-start.7 = (bf16[256,1024]{1,0:T(8,128)(2,1)S(1)}, bf16[256,1024]{1,0:T(8,128)(2,1)S(1)}, u32[]{:S(2)}, u32[]{:S(2)}) collective-permute-start(bf16[256,1024]{1,0:T(8,128)(2,1)S(1)} %collective-permute-done.2.refs_4_), channel_id=1, source_target_pairs={{8,0},{12,4},{16,8},{20,12},{24,16},{28,20},{9,1},{13,5},{17,9},{2... | collective-permute-start | bytes 1572872 | tf_op jit(solution)/shard_map/ppermute | solution.py:24
  28.7 6.1 %collective-permute-done.3 = bf16[256,1024]{1,0:T(8,128)(2,1)S(1)} collective-permute-done((bf16[256,1024]{1,0:T(8,128)(2,1)S(1)}, bf16[256,1024]{1,0:T(8,128)(2,1)S(1)}, u32[]{:S(2)}, u32[]{:S(2)}) %collective-permute-start.3) | collective-permute-done | bytes 524320 | tf_op jit(solution)/shard_map/ppermute | solution.py:547
  34.8 1.0 %broadcast_select_fusion = (bf16[256,1024]{1,0:T(8,128)(2,1)}, bf16[256,1024]{1,0:T(8,128)(2,1)}) fusion(bf16[256,1024]{1,0:T(8,128)(2,1)S(1)} %collective-permute-done.3, bf16[256,1024]{1,0:T(8,128)(2,1)S(1)} %collective-permute-done.1, pred[]{:T(512)S(6)} %eq.5), kind=kLoop, calls=%fused_computation | loop fusion | flops 524288 | bytes 2097153 | tf_op jit(solution)/shard_map/jit(_where)/select_n | solution.py:549
  35.8 1.2 %collective-permute-done.4.refs_6_ = bf16[256,1024]{1,0:T(8,128)(2,1)S(1)} collective-permute-done((bf16[256,1024]{1,0:T(8,128)(2,1)S(1)}, bf16[256,1024]{1,0:T(8,128)(2,1)S(1)}, u32[]{:S(2)}, u32[]{:S(2)}) %collective-permute-start.4) | collective-permute-done | bytes 524320 | tf_op jit(solution)/shard_map/ppermute | solution.py:24
  37.0 0.8 %copy-done.4 = bf16[256,1024]{1,0:T(8,128)(2,1)} copy-done((bf16[256,1024]{1,0:T(8,128)(2,1)}, bf16[256,1024]{1,0:T(8,128)(2,1)S(1)}, u32[]{:S(2)}) %copy-start.4) | copy-done | bytes 524312
  37.8 6.0 %rows_stats.1 = (bf16[256,512]{1,0:T(8,128)(2,1)}, f32[256,8]{1,0:T(8,128)}, f32[8,256]{1,0:T(8,128)}) custom-call(s32[1]{0:T(128)} %bitcast.refs_0_, bf16[256,512]{1,0:T(8,128)(2,1)} %refs_1_.3, bf16[256,512]{1,0:T(8,128)(2,1)} %refs_2_.3, bf16[256,1024]{1,0:T(8,128)(2,1)} %copy-done.1, bf16[256,1024]{1,0:T(8,128)(2,1)} %get-tuple-element.15.refs_4_, ...), custom_call_target="tpu_custom_call" | custom-call | flops 402653184 | bytes 4194304 | tf_op jit(solution)/shard_map/rows_stats/pallas_call | solution.py:559
  43.8 1.3 %collective-permute-start.5 = (f32[8,256]{1,0:T(8,128)}, f32[8,256]{1,0:T(8,128)S(1)}, u32[]{:S(2)}, u32[]{:S(2)}) collective-permute-start(f32[8,256]{1,0:T(8,128)} %get-tuple-element.11.refs_5_), channel_id=1, source_target_pairs={{4,0},{8,4},{12,8},{16,12},{20,16},{24,20},{28,24},{5,1},{9,5},{13... | collective-permute-start | bytes 24584 | tf_op jit(solution)/shard_map/ppermute | solution.py:24
  45.1 1.3 %collective-permute-start.6 = (f32[8,256]{1,0:T(8,128)}, f32[8,256]{1,0:T(8,128)S(1)}, u32[]{:S(2)}, u32[]{:S(2)}) collective-permute-start(f32[8,256]{1,0:T(8,128)} %get-tuple-element.11.refs_5_), channel_id=1, source_target_pairs={{8,0},{12,4},{16,8},{20,12},{24,16},{28,20},{9,1},{13,5},{17,9},{2... | collective-permute-start | bytes 24584 | tf_op jit(solution)/shard_map/ppermute | solution.py:24
  46.4 1.3 %collective-permute-start.8 = (f32[8,256]{1,0:T(8,128)}, f32[8,256]{1,0:T(8,128)S(1)}, u32[]{:S(2)}, u32[]{:S(2)}) collective-permute-start(f32[8,256]{1,0:T(8,128)} %get-tuple-element.11.refs_5_), channel_id=1, source_target_pairs={{16,0},{20,4},{24,8},{28,12},{17,1},{21,5},{25,9},{29,13},{18,2},{... | collective-permute-start | bytes 24584 | tf_op jit(solution)/shard_map/ppermute | solution.py:24
  47.7 4.5 %rows_grad.1 = bf16[256,512]{1,0:T(8,128)(2,1)} custom-call(s32[1]{0:T(128)} %bitcast.refs_0_, bf16[256,512]{1,0:T(8,128)(2,1)} %refs_1_.3, bf16[256,512]{1,0:T(8,128)(2,1)} %refs_2_.3, bf16[256,1024]{1,0:T(8,128)(2,1)} %copy-done.1, bf16[256,1024]{1,0:T(8,128)(2,1)} %get-tuple-element.15.refs_4_, bf16[256,1024]{1,0:T(8,128)(2,1)} %copy-done, ...), custom_call_target="tpu_custom_call" | custom-call | flops 603979776 | bytes 4194304 | tf_op jit(solution)/shard_map/rows_grad/pallas_call | solution.py:574
  52.3 2.5 %collective-permute-done.8.refs_9_ = f32[8,256]{1,0:T(8,128)S(1)} collective-permute-done((f32[8,256]{1,0:T(8,128)}, f32[8,256]{1,0:T(8,128)S(1)}, u32[]{:S(2)}, u32[]{:S(2)}) %collective-permute-start.8) | collective-permute-done | bytes 8224 | tf_op jit(solution)/shard_map/ppermute | solution.py:24
  54.7 0.6 copy-done.11
  55.3 4.7 %keys_pass.1 = (bf16[256,512]{1,0:T(8,128)(2,1)}, bf16[256,512]{1,0:T(8,128)(2,1)}) custom-call(s32[1]{0:T(128)} %bitcast.refs_0_, bf16[256,1024]{1,0:T(8,128)(2,1)} %copy-done, bf16[256,1024]{1,0:T(8,128)(2,1)} %copy-done.5, bf16[256,1024]{1,0:T(8,128)(2,1)} %get-tuple-element.14.refs_3_, bf16[256,1024]{1,0:T(8,128)(2,1)} %copy-done.6, ...), custom_call_target="tpu_custom_call" | custom-call | flops 805306368 | bytes 4194304 | tf_op jit(solution)/shard_map/keys_pass/pallas_call | solution.py:582
  (28 shorter events, 0.1 us)
Async XLA Ops:
  0.6 1.0 %copy-start.7 = (bf16[256,512]{1,0:T(8,128)(2,1)S(1)}, bf16[256,512]{1,0:T(8,128)(2,1)}, u32[]{:S(2)}) copy-start(bf16[256,512]{1,0:T(8,128)(2,1)} %param.6) | copy-start | bytes 786436
  1.7 5.2 %copy-start.2 = (bf16[256,512]{1,0:T(8,128)(2,1)S(1)}, bf16[256,512]{1,0:T(8,128)(2,1)}, u32[]{:S(2)}) copy-start(bf16[256,512]{1,0:T(8,128)(2,1)} %refs_1_.3) | copy-start | bytes 786436
  1.7 6.5 %copy-start = (bf16[256,1024]{1,0:T(8,128)(2,1)}, bf16[256,1024]{1,0:T(8,128)(2,1)S(1)}, u32[]{:S(2)}) copy-start(bf16[256,1024]{1,0:T(8,128)(2,1)S(1)} %constant_dynamic-update-slice_fusion.refs_5_.refs_1_) | copy-start | bytes 1572868
  1.7 5.2 %copy-start.3 = (bf16[256,512]{1,0:T(8,128)(2,1)S(1)}, bf16[256,512]{1,0:T(8,128)(2,1)}, u32[]{:S(2)}) copy-start(bf16[256,512]{1,0:T(8,128)(2,1)} %refs_2_.3) | copy-start | bytes 786436
  1.7 16.2 %collective-permute-start = (bf16[256,1024]{1,0:T(8,128)(2,1)S(1)}, bf16[256,1024]{1,0:T(8,128)(2,1)S(1)}, u32[]{:S(2)}, u32[]{:S(2)}) collective-permute-start(bf16[256,1024]{1,0:T(8,128)(2,1)S(1)} %constant_dynamic-update-slice_fusion.refs_5_.refs_1_), channel_id=1, source_target_pairs={{0,8},{4,12},{8,16},{12,20},{16,24},{20,28},{1,9},{5,13},{9,17},{1... | collective-permute-start | bytes 1572872 | tf_op jit(solution)/shard_map/ppermute | solution.py:24
  6.9 1.4 %copy-start.5 = (bf16[256,1024]{1,0:T(8,128)(2,1)}, bf16[256,1024]{1,0:T(8,128)(2,1)S(1)}, u32[]{:S(2)}) copy-start(bf16[256,1024]{1,0:T(8,128)(2,1)S(1)} %constant_dynamic-update-slice_fusion.2.refs_2_) | copy-start | bytes 1572868
  6.9 15.3 %collective-permute-start.2 = (bf16[256,1024]{1,0:T(8,128)(2,1)S(1)}, bf16[256,1024]{1,0:T(8,128)(2,1)S(1)}, u32[]{:S(2)}, u32[]{:S(2)}) collective-permute-start(bf16[256,1024]{1,0:T(8,128)(2,1)S(1)} %constant_dynamic-update-slice_fusion.2.refs_2_), channel_id=1, source_target_pairs={{8,0},{12,4},{16,8},{20,12},{24,16},{28,20},{9,1},{13,5},{17,9},{2... | collective-permute-start | bytes 1572872 | tf_op jit(solution)/shard_map/ppermute | solution.py:24
  8.3 20.3 %collective-permute-start.1 = (bf16[256,1024]{1,0:T(8,128)(2,1)S(1)}, bf16[256,1024]{1,0:T(8,128)(2,1)S(1)}, u32[]{:S(2)}, u32[]{:S(2)}) collective-permute-start(bf16[256,1024]{1,0:T(8,128)(2,1)S(1)} %broadcast_select_fusion.3), channel_id=1, source_target_pairs={{0,4},{4,0},{8,12},{12,8},{16,20},{20,16},{24,28},{28,24},{1,5},{5... | collective-permute-start | bytes 1572872 | tf_op jit(solution)/shard_map/ppermute | solution.py:544
  18.0 5.9 %copy-start.1 = (bf16[256,1024]{1,0:T(8,128)(2,1)}, bf16[256,1024]{1,0:T(8,128)(2,1)S(1)}, u32[]{:S(2)}) copy-start(bf16[256,1024]{1,0:T(8,128)(2,1)S(1)} %collective-permute-done.refs_3_) | copy-start | bytes 1572868
  22.2 5.1 %copy-start.6 = (bf16[256,1024]{1,0:T(8,128)(2,1)}, bf16[256,1024]{1,0:T(8,128)(2,1)S(1)}, u32[]{:S(2)}) copy-start(bf16[256,1024]{1,0:T(8,128)(2,1)S(1)} %collective-permute-done.2.refs_4_) | copy-start | bytes 1572868
  22.3 12.5 %collective-permute-start.3 = (bf16[256,1024]{1,0:T(8,128)(2,1)S(1)}, bf16[256,1024]{1,0:T(8,128)(2,1)S(1)}, u32[]{:S(2)}, u32[]{:S(2)}) collective-permute-start(bf16[256,1024]{1,0:T(8,128)(2,1)S(1)} %broadcast_select_fusion.2), channel_id=1, source_target_pairs={{0,4},{4,0},{8,12},{12,8},{16,20},{20,16},{24,28},{28,24},{1,5},{5... | collective-permute-start | bytes 1572872 | tf_op jit(solution)/shard_map/ppermute | solution.py:547
  23.9 13.1 %collective-permute-start.4 = (bf16[256,1024]{1,0:T(8,128)(2,1)S(1)}, bf16[256,1024]{1,0:T(8,128)(2,1)S(1)}, u32[]{:S(2)}, u32[]{:S(2)}) collective-permute-start(bf16[256,1024]{1,0:T(8,128)(2,1)S(1)} %collective-permute-done.refs_3_), channel_id=1, source_target_pairs={{0,8},{4,12},{8,16},{12,20},{16,24},{20,28},{1,9},{5,13},{9,17},{1... | collective-permute-start | bytes 1572872 | tf_op jit(solution)/shard_map/ppermute | solution.py:24
  27.3 24.9 %collective-permute-start.7 = (bf16[256,1024]{1,0:T(8,128)(2,1)S(1)}, bf16[256,1024]{1,0:T(8,128)(2,1)S(1)}, u32[]{:S(2)}, u32[]{:S(2)}) collective-permute-start(bf16[256,1024]{1,0:T(8,128)(2,1)S(1)} %collective-permute-done.2.refs_4_), channel_id=1, source_target_pairs={{8,0},{12,4},{16,8},{20,12},{24,16},{28,20},{9,1},{13,5},{17,9},{2... | collective-permute-start | bytes 1572872 | tf_op jit(solution)/shard_map/ppermute | solution.py:24
  37.0 0.8 %copy-start.4 = (bf16[256,1024]{1,0:T(8,128)(2,1)}, bf16[256,1024]{1,0:T(8,128)(2,1)S(1)}, u32[]{:S(2)}) copy-start(bf16[256,1024]{1,0:T(8,128)(2,1)S(1)} %collective-permute-done.4.refs_6_) | copy-start | bytes 1572868
  43.8 8.4 %collective-permute-start.5 = (f32[8,256]{1,0:T(8,128)}, f32[8,256]{1,0:T(8,128)S(1)}, u32[]{:S(2)}, u32[]{:S(2)}) collective-permute-start(f32[8,256]{1,0:T(8,128)} %get-tuple-element.11.refs_5_), channel_id=1, source_target_pairs={{4,0},{8,4},{12,8},{16,12},{20,16},{24,20},{28,24},{5,1},{9,5},{13... | collective-permute-start | bytes 24584 | tf_op jit(solution)/shard_map/ppermute | solution.py:24
  45.1 7.1 %collective-permute-start.6 = (f32[8,256]{1,0:T(8,128)}, f32[8,256]{1,0:T(8,128)S(1)}, u32[]{:S(2)}, u32[]{:S(2)}) collective-permute-start(f32[8,256]{1,0:T(8,128)} %get-tuple-element.11.refs_5_), channel_id=1, source_target_pairs={{8,0},{12,4},{16,8},{20,12},{24,16},{28,20},{9,1},{13,5},{17,9},{2... | collective-permute-start | bytes 24584 | tf_op jit(solution)/shard_map/ppermute | solution.py:24
  46.4 8.3 %collective-permute-start.8 = (f32[8,256]{1,0:T(8,128)}, f32[8,256]{1,0:T(8,128)S(1)}, u32[]{:S(2)}, u32[]{:S(2)}) collective-permute-start(f32[8,256]{1,0:T(8,128)} %get-tuple-element.11.refs_5_), channel_id=1, source_target_pairs={{16,0},{20,4},{24,8},{28,12},{17,1},{21,5},{25,9},{29,13},{18,2},{... | collective-permute-start | bytes 24584 | tf_op jit(solution)/shard_map/ppermute | solution.py:24
  52.2 2.5 %copy-start.8 = (bf16[256,1024]{1,0:T(8,128)(2,1)}, bf16[256,1024]{1,0:T(8,128)(2,1)S(1)}, u32[]{:S(2)}) copy-start(bf16[256,1024]{1,0:T(8,128)(2,1)S(1)} %collective-permute-done.7.refs_8_) | copy-start | bytes 1572868
  52.2 2.5 %copy-start.9 = (f32[8,256]{1,0:T(8,128)}, f32[8,256]{1,0:T(8,128)S(1)}, u32[]{:S(2)}) copy-start(f32[8,256]{1,0:T(8,128)S(1)} %collective-permute-done.5.refs_6_) | copy-start | bytes 24580
  52.2 2.5 %copy-start.10 = (f32[8,256]{1,0:T(8,128)}, f32[8,256]{1,0:T(8,128)S(1)}, u32[]{:S(2)}) copy-start(f32[8,256]{1,0:T(8,128)S(1)} %collective-permute-done.6.refs_7_) | copy-start | bytes 24580
  54.7 0.6 copy-start.11

commit v15 on v14

--- a/solution.py
+++ b/solution.py
@@ -427,9 +427,9 @@
             attended = jnp.zeros((BLK, HD), jnp.float32)
             for item, value in zip(shifted, values):
                 attended = attended + jnp.dot(
-                    (item * inverse).astype(jnp.bfloat16), value, preferred_element_type=jnp.float32
+                    item.astype(jnp.bfloat16), value, preferred_element_type=jnp.float32
                 )
-            attended = attended.astype(jnp.bfloat16)
+            attended = (attended * inverse).astype(jnp.bfloat16)
             attended_ref[rows, cols] = attended
             out_dot = jnp.sum(
                 grad.astype(jnp.float32) * attended.astype(jnp.float32), axis=-1, keepdims=True

time: 60.4 us -> 60.1 us (level)
  transfers between devices with their start and end apart: 9 -> 9, of which waited for: 5 -> 5; matrix products, arithmetic and copies ran while one was open for 2% -> 2% of each run, Pallas kernels for 18% -> 17%
where the time goes in v15:
time: 60.1 us; the launch traced here: 59.7 us
  waiting for transfers between devices  22.1 us (37%)
  starting transfers between devices  18.2 us (30%)
  Pallas kernels  15 us (25%)
  local copies, waits for them, and re-layouts  2.49 us (4%)
  other arithmetic  1.15 us (2%)
  between operations  0.88 us (1%)
    ppermute x7, waiting for transfers between devices, passed_along(): lax.ppermute(value, axis, [(source, source + steps) for source in range(f...  15.9 us
    ppermute x7, starting transfers between devices, passed_along(): lax.ppermute(value, axis, [(source, source + steps) for source in range(f...  15 us
    pallas_call x2, Pallas kernels, body(): pl.pallas_call(functools.partial(row_kernel, len(near_list), far_offsets,...  10.2 us
    ppermute x1, waiting for transfers between devices, body(): swap_two = lax.ppermute(jnp.where(odd, back2, ahead2), 'seq', pairs)  6.15 us
    pallas_call x1, Pallas kernels, body(): pl.pallas_call(functools.partial(key_kernel, len(near_list), far_offsets,...  4.75 us
    unnamed x26, local copies, waits for them, and re-layouts  2.44 us
    ppermute x1, starting transfers between devices, body(): lax.ppermute(jnp.where(odd, queries_grads, keys_values), 'seq', pairs)  1.58 us
    ppermute x1, starting transfers between devices, body(): swap_two = lax.ppermute(jnp.where(odd, back2, ahead2), 'seq', pairs)  1.58 us
  transfers between devices with their start and end apart: 9, of which 5 were waited for; matrix products, arithmetic and copies ran while one was open for 2% of the time, Pallas kernels for 17%

profile of v15, /device:TPU:0, one launch (start us, length us, event | category | flops | bytes accessed | tf_op | source)
XLA Modules:
  0.0 59.7 jit_solution(4582023214208475095)
XLA Ops:
  0.6 1.0 %constant_dynamic-update-slice_fusion.1 = bf16[256,1024]{1,0:T(8,128)(2,1)S(1)} fusion(bf16[256,512]{1,0:T(8,128)(2,1)} %param.5), kind=kLoop, calls=%fused_computation.5 | loop fusion | bytes 524288
  1.7 0.0 copy-start.2
  1.7 5.1 %collective-permute-start = (bf16[256,1024]{1,0:T(8,128)(2,1)S(1)}, bf16[256,1024]{1,0:T(8,128)(2,1)S(1)}, u32[]{:S(2)}, u32[]{:S(2)}) collective-permute-start(bf16[256,1024]{1,0:T(8,128)(2,1)S(1)} %constant_dynamic-update-slice_fusion.refs_5_.refs_1_), channel_id=1, source_target_pairs={{0,8},{4,12},{8,16},{12,20},{16,24},{20,28},{1,9},{5,13},{9,17},{1... | collective-permute-start | bytes 1572872 | tf_op jit(solution)/shard_map/ppermute | solution.py:24
  6.9 1.3 %collective-permute-start.2 = (bf16[256,1024]{1,0:T(8,128)(2,1)S(1)}, bf16[256,1024]{1,0:T(8,128)(2,1)S(1)}, u32[]{:S(2)}, u32[]{:S(2)}) collective-permute-start(bf16[256,1024]{1,0:T(8,128)(2,1)S(1)} %constant_dynamic-update-slice_fusion.2.refs_2_), channel_id=1, source_target_pairs={{8,0},{12,4},{16,8},{20,12},{24,16},{28,20},{9,1},{13,5},{17,9},{2... | collective-permute-start | bytes 1572872 | tf_op jit(solution)/shard_map/ppermute | solution.py:24
  8.3 0.1 broadcast_select_fusion.3
  8.3 1.6 %collective-permute-start.1 = (bf16[256,1024]{1,0:T(8,128)(2,1)S(1)}, bf16[256,1024]{1,0:T(8,128)(2,1)S(1)}, u32[]{:S(2)}, u32[]{:S(2)}) collective-permute-start(bf16[256,1024]{1,0:T(8,128)(2,1)S(1)} %broadcast_select_fusion.3), channel_id=1, source_target_pairs={{0,4},{4,0},{8,12},{12,8},{16,20},{20,16},{24,28},{28,24},{1,5},{5... | collective-permute-start | bytes 1572872 | tf_op jit(solution)/shard_map/ppermute | solution.py:544
  9.9 8.1 %collective-permute-done.refs_3_ = bf16[256,1024]{1,0:T(8,128)(2,1)S(1)} collective-permute-done((bf16[256,1024]{1,0:T(8,128)(2,1)S(1)}, bf16[256,1024]{1,0:T(8,128)(2,1)S(1)}, u32[]{:S(2)}, u32[]{:S(2)}) %collective-permute-start) | collective-permute-done | bytes 524320 | tf_op jit(solution)/shard_map/ppermute | solution.py:24
  18.0 4.2 %collective-permute-done.2.refs_4_ = bf16[256,1024]{1,0:T(8,128)(2,1)S(1)} collective-permute-done((bf16[256,1024]{1,0:T(8,128)(2,1)S(1)}, bf16[256,1024]{1,0:T(8,128)(2,1)S(1)}, u32[]{:S(2)}, u32[]{:S(2)}) %collective-permute-start.2) | collective-permute-done | bytes 524320 | tf_op jit(solution)/shard_map/ppermute | solution.py:24
  22.2 0.1 broadcast_select_fusion.2
  22.3 1.6 %collective-permute-start.3 = (bf16[256,1024]{1,0:T(8,128)(2,1)S(1)}, bf16[256,1024]{1,0:T(8,128)(2,1)S(1)}, u32[]{:S(2)}, u32[]{:S(2)}) collective-permute-start(bf16[256,1024]{1,0:T(8,128)(2,1)S(1)} %broadcast_select_fusion.2), channel_id=1, source_target_pairs={{0,4},{4,0},{8,12},{12,8},{16,20},{20,16},{24,28},{28,24},{1,5},{5... | collective-permute-start | bytes 1572872 | tf_op jit(solution)/shard_map/ppermute | solution.py:547
  23.9 3.5 %collective-permute-start.4 = (bf16[256,1024]{1,0:T(8,128)(2,1)S(1)}, bf16[256,1024]{1,0:T(8,128)(2,1)S(1)}, u32[]{:S(2)}, u32[]{:S(2)}) collective-permute-start(bf16[256,1024]{1,0:T(8,128)(2,1)S(1)} %collective-permute-done.refs_3_), channel_id=1, source_target_pairs={{0,8},{4,12},{8,16},{12,20},{16,24},{20,28},{1,9},{5,13},{9,17},{1... | collective-permute-start | bytes 1572872 | tf_op jit(solution)/shard_map/ppermute | solution.py:24
  27.3 1.3 %collective-permute-start.7 = (bf16[256,1024]{1,0:T(8,128)(2,1)S(1)}, bf16[256,1024]{1,0:T(8,128)(2,1)S(1)}, u32[]{:S(2)}, u32[]{:S(2)}) collective-permute-start(bf16[256,1024]{1,0:T(8,128)(2,1)S(1)} %collective-permute-done.2.refs_4_), channel_id=1, source_target_pairs={{8,0},{12,4},{16,8},{20,12},{24,16},{28,20},{9,1},{13,5},{17,9},{2... | collective-permute-start | bytes 1572872 | tf_op jit(solution)/shard_map/ppermute | solution.py:24
  28.7 6.1 %collective-permute-done.3 = bf16[256,1024]{1,0:T(8,128)(2,1)S(1)} collective-permute-done((bf16[256,1024]{1,0:T(8,128)(2,1)S(1)}, bf16[256,1024]{1,0:T(8,128)(2,1)S(1)}, u32[]{:S(2)}, u32[]{:S(2)}) %collective-permute-start.3) | collective-permute-done | bytes 524320 | tf_op jit(solution)/shard_map/ppermute | solution.py:547
  34.8 1.0 %broadcast_select_fusion = (bf16[256,1024]{1,0:T(8,128)(2,1)}, bf16[256,1024]{1,0:T(8,128)(2,1)}) fusion(bf16[256,1024]{1,0:T(8,128)(2,1)S(1)} %collective-permute-done.3, bf16[256,1024]{1,0:T(8,128)(2,1)S(1)} %collective-permute-done.1, pred[]{:T(512)S(6)} %eq.5), kind=kLoop, calls=%fused_computation | loop fusion | flops 524288 | bytes 2097153 | tf_op jit(solution)/shard_map/jit(_where)/select_n | solution.py:549
  35.8 1.2 %collective-permute-done.4.refs_6_ = bf16[256,1024]{1,0:T(8,128)(2,1)S(1)} collective-permute-done((bf16[256,1024]{1,0:T(8,128)(2,1)S(1)}, bf16[256,1024]{1,0:T(8,128)(2,1)S(1)}, u32[]{:S(2)}, u32[]{:S(2)}) %collective-permute-start.4) | collective-permute-done | bytes 524320 | tf_op jit(solution)/shard_map/ppermute | solution.py:24
  37.0 0.8 %copy-done.4 = bf16[256,1024]{1,0:T(8,128)(2,1)} copy-done((bf16[256,1024]{1,0:T(8,128)(2,1)}, bf16[256,1024]{1,0:T(8,128)(2,1)S(1)}, u32[]{:S(2)}) %copy-start.4) | copy-done | bytes 524312
  37.8 5.7 %rows_stats.1 = (bf16[256,512]{1,0:T(8,128)(2,1)}, f32[256,8]{1,0:T(8,128)}, f32[8,256]{1,0:T(8,128)}) custom-call(s32[1]{0:T(128)} %bitcast.refs_0_, bf16[256,512]{1,0:T(8,128)(2,1)} %refs_1_.3, bf16[256,512]{1,0:T(8,128)(2,1)} %refs_2_.3, bf16[256,1024]{1,0:T(8,128)(2,1)} %copy-done.1, bf16[256,1024]{1,0:T(8,128)(2,1)} %get-tuple-element.15.refs_4_, ...), custom_call_target="tpu_custom_call" | custom-call | flops 402653184 | bytes 4194304 | tf_op jit(solution)/shard_map/rows_stats/pallas_call | solution.py:559
  43.5 1.3 %collective-permute-start.5 = (f32[8,256]{1,0:T(8,128)}, f32[8,256]{1,0:T(8,128)S(1)}, u32[]{:S(2)}, u32[]{:S(2)}) collective-permute-start(f32[8,256]{1,0:T(8,128)} %get-tuple-element.11.refs_5_), channel_id=1, source_target_pairs={{4,0},{8,4},{12,8},{16,12},{20,16},{24,20},{28,24},{5,1},{9,5},{13... | collective-permute-start | bytes 24584 | tf_op jit(solution)/shard_map/ppermute | solution.py:24
  44.8 1.3 %collective-permute-start.6 = (f32[8,256]{1,0:T(8,128)}, f32[8,256]{1,0:T(8,128)S(1)}, u32[]{:S(2)}, u32[]{:S(2)}) collective-permute-start(f32[8,256]{1,0:T(8,128)} %get-tuple-element.11.refs_5_), channel_id=1, source_target_pairs={{8,0},{12,4},{16,8},{20,12},{24,16},{28,20},{9,1},{13,5},{17,9},{2... | collective-permute-start | bytes 24584 | tf_op jit(solution)/shard_map/ppermute | solution.py:24
  46.1 1.3 %collective-permute-start.8 = (f32[8,256]{1,0:T(8,128)}, f32[8,256]{1,0:T(8,128)S(1)}, u32[]{:S(2)}, u32[]{:S(2)}) collective-permute-start(f32[8,256]{1,0:T(8,128)} %get-tuple-element.11.refs_5_), channel_id=1, source_target_pairs={{16,0},{20,4},{24,8},{28,12},{17,1},{21,5},{25,9},{29,13},{18,2},{... | collective-permute-start | bytes 24584 | tf_op jit(solution)/shard_map/ppermute | solution.py:24
  47.4 4.5 %rows_grad.1 = bf16[256,512]{1,0:T(8,128)(2,1)} custom-call(s32[1]{0:T(128)} %bitcast.refs_0_, bf16[256,512]{1,0:T(8,128)(2,1)} %refs_1_.3, bf16[256,512]{1,0:T(8,128)(2,1)} %refs_2_.3, bf16[256,1024]{1,0:T(8,128)(2,1)} %copy-done.1, bf16[256,1024]{1,0:T(8,128)(2,1)} %get-tuple-element.15.refs_4_, bf16[256,1024]{1,0:T(8,128)(2,1)} %copy-done, ...), custom_call_target="tpu_custom_call" | custom-call | flops 603979776 | bytes 4194304 | tf_op jit(solution)/shard_map/rows_grad/pallas_call | solution.py:574
  51.9 2.5 %collective-permute-done.8.refs_9_ = f32[8,256]{1,0:T(8,128)S(1)} collective-permute-done((f32[8,256]{1,0:T(8,128)}, f32[8,256]{1,0:T(8,128)S(1)}, u32[]{:S(2)}, u32[]{:S(2)}) %collective-permute-start.8) | collective-permute-done | bytes 8224 | tf_op jit(solution)/shard_map/ppermute | solution.py:24
  54.4 0.6 copy-done.11
  55.0 4.8 %keys_pass.1 = (bf16[256,512]{1,0:T(8,128)(2,1)}, bf16[256,512]{1,0:T(8,128)(2,1)}) custom-call(s32[1]{0:T(128)} %bitcast.refs_0_, bf16[256,1024]{1,0:T(8,128)(2,1)} %copy-done, bf16[256,1024]{1,0:T(8,128)(2,1)} %copy-done.5, bf16[256,1024]{1,0:T(8,128)(2,1)} %get-tuple-element.14.refs_3_, bf16[256,1024]{1,0:T(8,128)(2,1)} %copy-done.6, ...), custom_call_target="tpu_custom_call" | custom-call | flops 805306368 | bytes 4194304 | tf_op jit(solution)/shard_map/keys_pass/pallas_call | solution.py:582
  (28 shorter events, 0.1 us)
Async XLA Ops:
  0.6 1.0 %copy-start.7 = (bf16[256,512]{1,0:T(8,128)(2,1)S(1)}, bf16[256,512]{1,0:T(8,128)(2,1)}, u32[]{:S(2)}) copy-start(bf16[256,512]{1,0:T(8,128)(2,1)} %param.6) | copy-start | bytes 786436
  1.7 5.2 %copy-start.2 = (bf16[256,512]{1,0:T(8,128)(2,1)S(1)}, bf16[256,512]{1,0:T(8,128)(2,1)}, u32[]{:S(2)}) copy-start(bf16[256,512]{1,0:T(8,128)(2,1)} %refs_1_.3) | copy-start | bytes 786436
  1.7 6.5 %copy-start = (bf16[256,1024]{1,0:T(8,128)(2,1)}, bf16[256,1024]{1,0:T(8,128)(2,1)S(1)}, u32[]{:S(2)}) copy-start(bf16[256,1024]{1,0:T(8,128)(2,1)S(1)} %constant_dynamic-update-slice_fusion.refs_5_.refs_1_) | copy-start | bytes 1572868
  1.7 5.2 %copy-start.3 = (bf16[256,512]{1,0:T(8,128)(2,1)S(1)}, bf16[256,512]{1,0:T(8,128)(2,1)}, u32[]{:S(2)}) copy-start(bf16[256,512]{1,0:T(8,128)(2,1)} %refs_2_.3) | copy-start | bytes 786436
  1.7 16.2 %collective-permute-start = (bf16[256,1024]{1,0:T(8,128)(2,1)S(1)}, bf16[256,1024]{1,0:T(8,128)(2,1)S(1)}, u32[]{:S(2)}, u32[]{:S(2)}) collective-permute-start(bf16[256,1024]{1,0:T(8,128)(2,1)S(1)} %constant_dynamic-update-slice_fusion.refs_5_.refs_1_), channel_id=1, source_target_pairs={{0,8},{4,12},{8,16},{12,20},{16,24},{20,28},{1,9},{5,13},{9,17},{1... | collective-permute-start | bytes 1572872 | tf_op jit(solution)/shard_map/ppermute | solution.py:24
  6.9 1.4 %copy-start.5 = (bf16[256,1024]{1,0:T(8,128)(2,1)}, bf16[256,1024]{1,0:T(8,128)(2,1)S(1)}, u32[]{:S(2)}) copy-start(bf16[256,1024]{1,0:T(8,128)(2,1)S(1)} %constant_dynamic-update-slice_fusion.2.refs_2_) | copy-start | bytes 1572868
  6.9 15.3 %collective-permute-start.2 = (bf16[256,1024]{1,0:T(8,128)(2,1)S(1)}, bf16[256,1024]{1,0:T(8,128)(2,1)S(1)}, u32[]{:S(2)}, u32[]{:S(2)}) collective-permute-start(bf16[256,1024]{1,0:T(8,128)(2,1)S(1)} %constant_dynamic-update-slice_fusion.2.refs_2_), channel_id=1, source_target_pairs={{8,0},{12,4},{16,8},{20,12},{24,16},{28,20},{9,1},{13,5},{17,9},{2... | collective-permute-start | bytes 1572872 | tf_op jit(solution)/shard_map/ppermute | solution.py:24
  8.3 20.3 %collective-permute-start.1 = (bf16[256,1024]{1,0:T(8,128)(2,1)S(1)}, bf16[256,1024]{1,0:T(8,128)(2,1)S(1)}, u32[]{:S(2)}, u32[]{:S(2)}) collective-permute-start(bf16[256,1024]{1,0:T(8,128)(2,1)S(1)} %broadcast_select_fusion.3), channel_id=1, source_target_pairs={{0,4},{4,0},{8,12},{12,8},{16,20},{20,16},{24,28},{28,24},{1,5},{5... | collective-permute-start | bytes 1572872 | tf_op jit(solution)/shard_map/ppermute | solution.py:544
  18.0 5.9 %copy-start.1 = (bf16[256,1024]{1,0:T(8,128)(2,1)}, bf16[256,1024]{1,0:T(8,128)(2,1)S(1)}, u32[]{:S(2)}) copy-start(bf16[256,1024]{1,0:T(8,128)(2,1)S(1)} %collective-permute-done.refs_3_) | copy-start | bytes 1572868
  22.2 5.1 %copy-start.6 = (bf16[256,1024]{1,0:T(8,128)(2,1)}, bf16[256,1024]{1,0:T(8,128)(2,1)S(1)}, u32[]{:S(2)}) copy-start(bf16[256,1024]{1,0:T(8,128)(2,1)S(1)} %collective-permute-done.2.refs_4_) | copy-start | bytes 1572868
  22.3 12.5 %collective-permute-start.3 = (bf16[256,1024]{1,0:T(8,128)(2,1)S(1)}, bf16[256,1024]{1,0:T(8,128)(2,1)S(1)}, u32[]{:S(2)}, u32[]{:S(2)}) collective-permute-start(bf16[256,1024]{1,0:T(8,128)(2,1)S(1)} %broadcast_select_fusion.2), channel_id=1, source_target_pairs={{0,4},{4,0},{8,12},{12,8},{16,20},{20,16},{24,28},{28,24},{1,5},{5... | collective-permute-start | bytes 1572872 | tf_op jit(solution)/shard_map/ppermute | solution.py:547
  23.9 13.1 %collective-permute-start.4 = (bf16[256,1024]{1,0:T(8,128)(2,1)S(1)}, bf16[256,1024]{1,0:T(8,128)(2,1)S(1)}, u32[]{:S(2)}, u32[]{:S(2)}) collective-permute-start(bf16[256,1024]{1,0:T(8,128)(2,1)S(1)} %collective-permute-done.refs_3_), channel_id=1, source_target_pairs={{0,8},{4,12},{8,16},{12,20},{16,24},{20,28},{1,9},{5,13},{9,17},{1... | collective-permute-start | bytes 1572872 | tf_op jit(solution)/shard_map/ppermute | solution.py:24
  27.3 24.5 %collective-permute-start.7 = (bf16[256,1024]{1,0:T(8,128)(2,1)S(1)}, bf16[256,1024]{1,0:T(8,128)(2,1)S(1)}, u32[]{:S(2)}, u32[]{:S(2)}) collective-permute-start(bf16[256,1024]{1,0:T(8,128)(2,1)S(1)} %collective-permute-done.2.refs_4_), channel_id=1, source_target_pairs={{8,0},{12,4},{16,8},{20,12},{24,16},{28,20},{9,1},{13,5},{17,9},{2... | collective-permute-start | bytes 1572872 | tf_op jit(solution)/shard_map/ppermute | solution.py:24
  37.0 0.8 %copy-start.4 = (bf16[256,1024]{1,0:T(8,128)(2,1)}, bf16[256,1024]{1,0:T(8,128)(2,1)S(1)}, u32[]{:S(2)}) copy-start(bf16[256,1024]{1,0:T(8,128)(2,1)S(1)} %collective-permute-done.4.refs_6_) | copy-start | bytes 1572868
  43.5 8.4 %collective-permute-start.5 = (f32[8,256]{1,0:T(8,128)}, f32[8,256]{1,0:T(8,128)S(1)}, u32[]{:S(2)}, u32[]{:S(2)}) collective-permute-start(f32[8,256]{1,0:T(8,128)} %get-tuple-element.11.refs_5_), channel_id=1, source_target_pairs={{4,0},{8,4},{12,8},{16,12},{20,16},{24,20},{28,24},{5,1},{9,5},{13... | collective-permute-start | bytes 24584 | tf_op jit(solution)/shard_map/ppermute | solution.py:24
  44.8 7.1 %collective-permute-start.6 = (f32[8,256]{1,0:T(8,128)}, f32[8,256]{1,0:T(8,128)S(1)}, u32[]{:S(2)}, u32[]{:S(2)}) collective-permute-start(f32[8,256]{1,0:T(8,128)} %get-tuple-element.11.refs_5_), channel_id=1, source_target_pairs={{8,0},{12,4},{16,8},{20,12},{24,16},{28,20},{9,1},{13,5},{17,9},{2... | collective-permute-start | bytes 24584 | tf_op jit(solution)/shard_map/ppermute | solution.py:24
  46.1 8.3 %collective-permute-start.8 = (f32[8,256]{1,0:T(8,128)}, f32[8,256]{1,0:T(8,128)S(1)}, u32[]{:S(2)}, u32[]{:S(2)}) collective-permute-start(f32[8,256]{1,0:T(8,128)} %get-tuple-element.11.refs_5_), channel_id=1, source_target_pairs={{16,0},{20,4},{24,8},{28,12},{17,1},{21,5},{25,9},{29,13},{18,2},{... | collective-permute-start | bytes 24584 | tf_op jit(solution)/shard_map/ppermute | solution.py:24
  51.9 2.5 %copy-start.8 = (bf16[256,1024]{1,0:T(8,128)(2,1)}, bf16[256,1024]{1,0:T(8,128)(2,1)S(1)}, u32[]{:S(2)}) copy-start(bf16[256,1024]{1,0:T(8,128)(2,1)S(1)} %collective-permute-done.7.refs_8_) | copy-start | bytes 1572868
  51.9 2.5 %copy-start.9 = (f32[8,256]{1,0:T(8,128)}, f32[8,256]{1,0:T(8,128)S(1)}, u32[]{:S(2)}) copy-start(f32[8,256]{1,0:T(8,128)S(1)} %collective-permute-done.5.refs_6_) | copy-start | bytes 24580
  51.9 2.5 %copy-start.10 = (f32[8,256]{1,0:T(8,128)}, f32[8,256]{1,0:T(8,128)S(1)}, u32[]{:S(2)}) copy-start(f32[8,256]{1,0:T(8,128)S(1)} %collective-permute-done.6.refs_7_) | copy-start | bytes 24580
  54.4 0.6 copy-start.11
